TPU v7x, 128 devices: a whole 4x4x4 slice. The times are simulated.
128 devices in a mesh: depth: 8 (over z, core), plane: 16 (over x, y).
Axes of the slice: x: 4, y: 4, z: 4, core: 2. Of those that a mesh axis runs over, the one named last changes fastest.
Arguments:
- toar: bfloat16 [8, 8, 2, 32768], P('depth', None, None, 'plane'), may hold values from -6 to 6
- pml_coeff: float32 [8, 2, 32768], P('depth', None, 'plane'), may hold values from -1.5 to 1.5
- coupling: float32 [8, 32768], P('depth', 'plane'), may hold values from 0.5 to 1
- inverse: bfloat16 [8, 512, 16, 64, 128], P('depth', 'plane'), may hold values from -0.125 to 0.125
- pattern: int32 [8, 512, 16], P('depth', 'plane'), may hold values from 0 to 511
- patch_map: int32 [8, 32768], P('depth', 'plane'), may hold values from 0 to 16383, as said below
Outputs:
- precond: bfloat16 [8, 8, 2, 32768], P('depth', None, None, 'plane')
- patch_sens: float32 [8, 16384], P(None, ('depth', 'plane'))
Inputs may be any that keep to these rules, and one draw needn't show every extreme that they name: `patch_map`: patch p belongs to owner p // 128. Among the cells of one device (one layer, one block of 2048 cells), at most 32 name patches of any one owner, and in every such block some owner is named exactly 32 times. `pattern`: block columns of the whole layer.
All inputs are finite; a program needn't handle non-finite values.
Results may differ from a plain program's by a relative error of at most 0.018.
Values may be sent and summed in bfloat16 or wider, within the bound.
No kernel may reach another device: no remote copies, remote signals or barrier semaphores. Data moves between devices by JAX's collectives and lax.ppermute only.
A program may use at most 128 MiB of HBM per device.

v0:
```python
import jax
import jax.numpy as jnp
from jax import lax
from jax.sharding import PartitionSpec as P

PATCH_DEV = 128


def passed_along(value, axis, steps):
    count = lax.axis_size(axis)
    first, last = (max(0, -steps), min(count, count - steps))
    return lax.ppermute(value, axis, [(source, source + steps) for source in range(first, last)])


def shards(toar, pml_coeff, coupling, inverse, pattern, patch_map):
    toar_local = toar[0]
    coeff = pml_coeff[0]
    coupler = coupling[0]
    inv_local = inverse[0]
    pattern_flat = pattern[0].reshape(-1)
    block_rows = inv_local.shape[0]
    per_row = inv_local.shape[1]
    block_cells = inv_local.shape[2]
    depth_count = lax.axis_size("depth")
    factor = inv_local.reshape(block_rows, per_row, block_cells, 2, block_cells)
    toar_f32 = toar_local.astype(jnp.float32)
    real_part = coeff[0] * toar_f32[:, 0] - coeff[1] * toar_f32[:, 1]
    imag_part = coeff[0] * toar_f32[:, 1] + coeff[1] * toar_f32[:, 0]
    source = jnp.stack([real_part, imag_part], axis=1)

    def apply_layer(incoming):
        gathered = lax.all_gather(incoming, "plane", axis=2, tiled=True)
        rows_here = gathered.shape[0]
        blocks = gathered.reshape(rows_here, 2, -1, block_cells)
        chosen = jnp.take(blocks, pattern_flat, axis=2)
        chosen = chosen.reshape(rows_here, 2, block_rows, per_row, block_cells)
        partial_value = jnp.einsum(
            "rkiaj,vbrkj->vabri", factor, chosen, preferred_element_type=jnp.float32
        )
        real_out = partial_value[:, 0, 0] - partial_value[:, 1, 1]
        imag_out = partial_value[:, 0, 1] + partial_value[:, 1, 0]
        return jnp.stack([real_out, imag_out], axis=1).reshape(
            rows_here, 2, block_rows * block_cells
        )

    def down_turn(turn_index, current):
        arrived = passed_along(current, "depth", 1)
        down_in = (source + coupler * arrived.astype(jnp.float32)).astype(jnp.bfloat16)
        return apply_layer(down_in).astype(jnp.bfloat16)

    first = apply_layer(source.astype(jnp.bfloat16)).astype(jnp.bfloat16)
    swept = lax.fori_loop(0, depth_count - 1, down_turn, first)

    def up_turn(turn_index, current):
        outgoing = (coupler * current.astype(jnp.float32)).astype(jnp.bfloat16)
        arrived = passed_along(outgoing, "depth", -1)
        return (swept.astype(jnp.float32) + apply_layer(arrived)).astype(jnp.bfloat16)

    precond = lax.fori_loop(0, depth_count - 1, up_turn, swept)
    product = precond.astype(jnp.float32) * toar_f32
    contrib = product[:, 0] + product[:, 1]
    cell_patch = patch_map[0]
    owner_count = depth_count * lax.axis_size("plane")
    patch_total = PATCH_DEV * owner_count
    local_sums = jax.ops.segment_sum(contrib.T, cell_patch, num_segments=patch_total).T
    owned = lax.psum_scatter(local_sums, ("depth", "plane"), scatter_dimension=1, tiled=True)
    return (precond[None], owned)


def solution(mesh):
    return jax.shard_map(
        shards,
        mesh=mesh,
        in_specs=(
            P("depth", None, None, "plane"),
            P("depth", None, "plane"),
            P("depth", "plane"),
            P("depth", "plane", None, None, None),
            P("depth", "plane", None),
            P("depth", "plane"),
        ),
        out_specs=(P("depth", None, None, "plane"), P(None, ("depth", "plane"))),
        check_vma=False,
    )
```

profile of v0, /device:TPU:1, one launch (start us, length us, event | category | flops | bytes accessed | tf_op | source)
XLA Modules:
  0.0 1724.1 jit_solution(11908913365908243737)
XLA Ops:
  10.4 27.9 %reshape_squeeze.7 = bf16[32,16,64,2,64]{4,3,2,1,0:T(2,128)(2,1)} reshape(bf16[1,32,16,64,128]{4,3,2,1,0:T(8,128)(2,1)} %param.15) | data formatting | bytes 16777216 | tf_op jit(solution)/shard_map/reshape;squeeze | solution.py:25
  38.3 15.2 copy.28
  66.4 13.0 fusion.24
  79.8 501.8 %while.20 = (s32[]{:T(128)}, bf16[8,2,2048]{2,0,1:T(8,128)(2,1)S(1)}, f32[1,2048]{1,0:T(1,128)S(1)}, f32[8,2,2048]{2,0,1:T(8,128)S(1)}, s32[512]{0:T(512)S(1)}, /*index=5*/bf16[32,16,64,2,64]{4,2,1,3,0:T(8,128)(2,1)}, s32[]{:T(128)}) while((s32[]{:T(128)}, bf16[8,2,2048]{2,0,1:T(8,128)(2,1)S(1)}, f32[1,2048]{1,0:T(1,128)S(1)}, ...), condition=%wide.region_1.3_spmd, body=%wide.region_0.0_spmd.sunk | while | flops 134977024 | bytes 22699164 | solution.py:52
  87.3 42.0 %all-gather.6.cloned.1.call-done = bf16[8,2,32768]{2,0,1:T(8,128)(2,1)} async-done(((bf16[8,2,2048]{2,0,1:T(8,128)(2,1)}), bf16[8,2,32768]{2,0,1:T(8,128)(2,1)}) %all-gather.6.cloned.1.call-update) | async-done | bytes 1048592 | tf_op jit(solution)/shard_map/while/body/eval_jaxpr/all_gather | solution.py:32
  142.0 10.1 fusion.44
  159.7 41.0 %all-gather.6.cloned.1.call-done = bf16[8,2,32768]{2,0,1:T(8,128)(2,1)} async-done(((bf16[8,2,2048]{2,0,1:T(8,128)(2,1)}), bf16[8,2,32768]{2,0,1:T(8,128)(2,1)}) %all-gather.6.cloned.1.call-update) | async-done | bytes 1048592 | tf_op jit(solution)/shard_map/while/body/eval_jaxpr/all_gather | solution.py:32
  213.5 10.1 fusion.44
  231.2 41.0 %all-gather.6.cloned.1.call-done = bf16[8,2,32768]{2,0,1:T(8,128)(2,1)} async-done(((bf16[8,2,2048]{2,0,1:T(8,128)(2,1)}), bf16[8,2,32768]{2,0,1:T(8,128)(2,1)}) %all-gather.6.cloned.1.call-update) | async-done | bytes 1048592 | tf_op jit(solution)/shard_map/while/body/eval_jaxpr/all_gather | solution.py:32
  285.0 10.1 fusion.44
  302.8 41.0 %all-gather.6.cloned.1.call-done = bf16[8,2,32768]{2,0,1:T(8,128)(2,1)} async-done(((bf16[8,2,2048]{2,0,1:T(8,128)(2,1)}), bf16[8,2,32768]{2,0,1:T(8,128)(2,1)}) %all-gather.6.cloned.1.call-update) | async-done | bytes 1048592 | tf_op jit(solution)/shard_map/while/body/eval_jaxpr/all_gather | solution.py:32
  374.3 41.0 %all-gather.6.cloned.1.call-done = bf16[8,2,32768]{2,0,1:T(8,128)(2,1)} async-done(((bf16[8,2,2048]{2,0,1:T(8,128)(2,1)}), bf16[8,2,32768]{2,0,1:T(8,128)(2,1)}) %all-gather.6.cloned.1.call-update) | async-done | bytes 1048592 | tf_op jit(solution)/shard_map/while/body/eval_jaxpr/all_gather | solution.py:32
  445.8 41.0 %all-gather.6.cloned.1.call-done = bf16[8,2,32768]{2,0,1:T(8,128)(2,1)} async-done(((bf16[8,2,2048]{2,0,1:T(8,128)(2,1)}), bf16[8,2,32768]{2,0,1:T(8,128)(2,1)}) %all-gather.6.cloned.1.call-update) | async-done | bytes 1048592 | tf_op jit(solution)/shard_map/while/body/eval_jaxpr/all_gather | solution.py:32
  517.3 41.0 %all-gather.6.cloned.1.call-done = bf16[8,2,32768]{2,0,1:T(8,128)(2,1)} async-done(((bf16[8,2,2048]{2,0,1:T(8,128)(2,1)}), bf16[8,2,32768]{2,0,1:T(8,128)(2,1)}) %all-gather.6.cloned.1.call-update) | async-done | bytes 1048592 | tf_op jit(solution)/shard_map/while/body/eval_jaxpr/all_gather | solution.py:32
  581.6 495.5 %while.21 = (s32[]{:T(128)}, bf16[8,2,2048]{2,0,1:T(8,128)(2,1)S(1)}, bf16[8,2,2048]{2,0,1:T(8,128)(2,1)S(1)}, f32[1,2048]{1,0:T(1,128)S(1)}, s32[512]{0:T(512)S...) while((s32[]{:T(128)}, bf16[8,2,2048]{2,0,1:T(8,128)(2,1)S(1)}, bf16[8,2,2048]{2,0,1:T(8,128)(2,1)S(1)}, ...), condition=%wide.region_3.5_spmd, body=%wide.region_2.4_spmd.sunk | while | flops 135009792 | bytes 23289016 | solution.py:59
  589.5 39.7 %all-gather.8.cloned.1.call-done = bf16[8,2,32768]{2,0,1:T(8,128)(2,1)} async-done(((bf16[8,2,2048]{2,0,1:T(8,128)(2,1)}), bf16[8,2,32768]{2,0,1:T(8,128)(2,1)}) %all-gather.8.cloned.1.call-update) | async-done | bytes 1048592 | tf_op jit(solution)/shard_map/while/body/eval_jaxpr/all_gather | solution.py:32
  660.3 39.7 %all-gather.8.cloned.1.call-done = bf16[8,2,32768]{2,0,1:T(8,128)(2,1)} async-done(((bf16[8,2,2048]{2,0,1:T(8,128)(2,1)}), bf16[8,2,32768]{2,0,1:T(8,128)(2,1)}) %all-gather.8.cloned.1.call-update) | async-done | bytes 1048592 | tf_op jit(solution)/shard_map/while/body/eval_jaxpr/all_gather | solution.py:32
  731.1 39.7 %all-gather.8.cloned.1.call-done = bf16[8,2,32768]{2,0,1:T(8,128)(2,1)} async-done(((bf16[8,2,2048]{2,0,1:T(8,128)(2,1)}), bf16[8,2,32768]{2,0,1:T(8,128)(2,1)}) %all-gather.8.cloned.1.call-update) | async-done | bytes 1048592 | tf_op jit(solution)/shard_map/while/body/eval_jaxpr/all_gather | solution.py:32
  801.9 39.7 %all-gather.8.cloned.1.call-done = bf16[8,2,32768]{2,0,1:T(8,128)(2,1)} async-done(((bf16[8,2,2048]{2,0,1:T(8,128)(2,1)}), bf16[8,2,32768]{2,0,1:T(8,128)(2,1)}) %all-gather.8.cloned.1.call-update) | async-done | bytes 1048592 | tf_op jit(solution)/shard_map/while/body/eval_jaxpr/all_gather | solution.py:32
  872.7 39.7 %all-gather.8.cloned.1.call-done = bf16[8,2,32768]{2,0,1:T(8,128)(2,1)} async-done(((bf16[8,2,2048]{2,0,1:T(8,128)(2,1)}), bf16[8,2,32768]{2,0,1:T(8,128)(2,1)}) %all-gather.8.cloned.1.call-update) | async-done | bytes 1048592 | tf_op jit(solution)/shard_map/while/body/eval_jaxpr/all_gather | solution.py:32
  943.4 39.7 %all-gather.8.cloned.1.call-done = bf16[8,2,32768]{2,0,1:T(8,128)(2,1)} async-done(((bf16[8,2,2048]{2,0,1:T(8,128)(2,1)}), bf16[8,2,32768]{2,0,1:T(8,128)(2,1)}) %all-gather.8.cloned.1.call-update) | async-done | bytes 1048592 | tf_op jit(solution)/shard_map/while/body/eval_jaxpr/all_gather | solution.py:32
  1014.2 39.7 %all-gather.8.cloned.1.call-done = bf16[8,2,32768]{2,0,1:T(8,128)(2,1)} async-done(((bf16[8,2,2048]{2,0,1:T(8,128)(2,1)}), bf16[8,2,32768]{2,0,1:T(8,128)(2,1)}) %all-gather.8.cloned.1.call-update) | async-done | bytes 1048592 | tf_op jit(solution)/shard_map/while/body/eval_jaxpr/all_gather | solution.py:32
  1077.6 15.5 scatter_custom_fusion
  1093.8 622.2 %reduce-scatter.2.cloned.1.call-done = f32[8,128]{0,1:T(8,128)} async-done(((f32[8,16384]{0,1:T(8,128)}), f32[8,128]{0,1:T(8,128)}) %reduce-scatter.2.cloned.1.call-update) | async-done | bytes 4112 | tf_op jit(solution)/shard_map/reduce_scatter | solution.py:66
  (312 shorter events, 418.2 us)
Async XLA Ops:
  7.2 48.0 %all-gather.4.cloned.1.call-start = ((), (), s32[]{:S(2)}) async-start(), calls=%async_computation.1 | async-start | bytes 1114112 | tf_op jit(solution)/shard_map/all_gather | solution.py:32
  80.0 49.2 %all-gather.6.cloned.1.call-start = ((), (), s32[]{:S(2)}) async-start(), calls=%async_computation.3 | async-start | bytes 1114112 | tf_op jit(solution)/shard_map/while/body/eval_jaxpr/all_gather | solution.py:32
  80.1 6.5 collective-permute-start
  152.4 48.3 %all-gather.6.cloned.1.call-start = ((), (), s32[]{:S(2)}) async-start(), calls=%async_computation.3 | async-start | bytes 1114112 | tf_op jit(solution)/shard_map/while/body/eval_jaxpr/all_gather | solution.py:32
  224.0 48.3 %all-gather.6.cloned.1.call-start = ((), (), s32[]{:S(2)}) async-start(), calls=%async_computation.3 | async-start | bytes 1114112 | tf_op jit(solution)/shard_map/while/body/eval_jaxpr/all_gather | solution.py:32
  295.5 48.3 %all-gather.6.cloned.1.call-start = ((), (), s32[]{:S(2)}) async-start(), calls=%async_computation.3 | async-start | bytes 1114112 | tf_op jit(solution)/shard_map/while/body/eval_jaxpr/all_gather | solution.py:32
  367.0 48.3 %all-gather.6.cloned.1.call-start = ((), (), s32[]{:S(2)}) async-start(), calls=%async_computation.3 | async-start | bytes 1114112 | tf_op jit(solution)/shard_map/while/body/eval_jaxpr/all_gather | solution.py:32
  438.6 48.3 %all-gather.6.cloned.1.call-start = ((), (), s32[]{:S(2)}) async-start(), calls=%async_computation.3 | async-start | bytes 1114112 | tf_op jit(solution)/shard_map/while/body/eval_jaxpr/all_gather | solution.py:32
  510.1 48.3 %all-gather.6.cloned.1.call-start = ((), (), s32[]{:S(2)}) async-start(), calls=%async_computation.3 | async-start | bytes 1114112 | tf_op jit(solution)/shard_map/while/body/eval_jaxpr/all_gather | solution.py:32
  581.6 47.6 %all-gather.8.cloned.1.call-start = ((), (), s32[]{:S(2)}) async-start(), calls=%async_computation.4 | async-start | bytes 1114112 | tf_op jit(solution)/shard_map/while/body/eval_jaxpr/all_gather | solution.py:32
  581.7 7.1 collective-permute-start.1
  652.4 47.6 %all-gather.8.cloned.1.call-start = ((), (), s32[]{:S(2)}) async-start(), calls=%async_computation.4 | async-start | bytes 1114112 | tf_op jit(solution)/shard_map/while/body/eval_jaxpr/all_gather | solution.py:32
  652.5 7.1 collective-permute-start.1
  723.2 47.6 %all-gather.8.cloned.1.call-start = ((), (), s32[]{:S(2)}) async-start(), calls=%async_computation.4 | async-start | bytes 1114112 | tf_op jit(solution)/shard_map/while/body/eval_jaxpr/all_gather | solution.py:32
  723.3 7.1 collective-permute-start.1
  794.0 47.6 %all-gather.8.cloned.1.call-start = ((), (), s32[]{:S(2)}) async-start(), calls=%async_computation.4 | async-start | bytes 1114112 | tf_op jit(solution)/shard_map/while/body/eval_jaxpr/all_gather | solution.py:32
  794.1 7.1 collective-permute-start.1
  864.8 47.6 %all-gather.8.cloned.1.call-start = ((), (), s32[]{:S(2)}) async-start(), calls=%async_computation.4 | async-start | bytes 1114112 | tf_op jit(solution)/shard_map/while/body/eval_jaxpr/all_gather | solution.py:32
  864.9 7.1 collective-permute-start.1
  935.6 47.6 %all-gather.8.cloned.1.call-start = ((), (), s32[]{:S(2)}) async-start(), calls=%async_computation.4 | async-start | bytes 1114112 | tf_op jit(solution)/shard_map/while/body/eval_jaxpr/all_gather | solution.py:32
  935.6 7.1 collective-permute-start.1
  1006.3 47.6 %all-gather.8.cloned.1.call-start = ((), (), s32[]{:S(2)}) async-start(), calls=%async_computation.4 | async-start | bytes 1114112 | tf_op jit(solution)/shard_map/while/body/eval_jaxpr/all_gather | solution.py:32
  1006.4 7.1 collective-permute-start.1
  1077.1 638.9 %reduce-scatter.2.cloned.1.call-start = ((), (), s32[]{:S(2)}) async-start(), calls=%async_computation.2 | async-start | bytes 8454144 | tf_op jit(solution)/shard_map/reduce_scatter | solution.py:66
  (15 other events, 552.3 us)
Sparse Core Ops, SparseCore 0:
  10.8 44.3 all-gather.3
  87.4 41.8 all-gather.5
  159.8 40.9 all-gather.5
  231.3 40.9 all-gather.5
  302.8 40.9 all-gather.5
  374.4 40.9 all-gather.5
  445.9 40.9 all-gather.5
  517.4 40.9 all-gather.5
  589.6 39.5 all-gather.7
  660.4 39.5 all-gather.7
  731.2 39.5 all-gather.7
  802.0 39.5 all-gather.7
  872.7 39.5 all-gather.7
  943.5 39.5 all-gather.7
  1014.3 39.5 all-gather.7
  1093.3 622.7 reduce-scatter.1
where the time goes:
time: 1760 us; the launch traced here: 1720 us
  waiting for transfers between devices  1220 us (69%)
  local copies, waits for them, and re-layouts  202 us (11%)
  matrix products  154 us (9%)
  other arithmetic  66 us (4%)
  starting transfers between devices  65 us (4%)
    reduce_scatter x1, waiting for transfers between devices, shards(): lax.psum_scatter(local_sums, ('depth', 'plane'), scatter_dimension=1, til...  622 us
    all_gather x15, waiting for transfers between devices, apply_layer(): gathered = lax.all_gather(incoming, 'plane', axis=2, tiled=True)  568 us
    dot_general x15, matrix products, apply_layer(): jnp.einsum('rkiaj,vbrkj->vabri', factor, chosen, preferred_element_type=j...  154 us
    reshape x30, local copies, waits for them, and re-layouts, apply_layer(): blocks = gathered.reshape(rows_here, 2, -1, block_cells)  85.8 us
    ppermute x14, starting transfers between devices, passed_along(): lax.ppermute(value, axis, [(source, source + steps) for source in range(f...  64.3 us
    gather x15, local copies, waits for them, and re-layouts, apply_layer(): chosen = jnp.take(blocks, pattern_flat, axis=2)  60.9 us
    select_n x30, other arithmetic, apply_layer(): chosen = jnp.take(blocks, pattern_flat, axis=2)  43 us
  transfers between devices with their start and end apart: 30, of which 30 were waited for; matrix products, arithmetic and copies ran while one was open for 3% of the time, Pallas kernels for 0%

commit v1 on v0

v1 whole, which is shorter than its diff:
```python
import jax
import jax.numpy as jnp
from jax import lax
from jax.sharding import PartitionSpec as P

PATCH_DEV = 128
CAP = 32


def passed_along(value, axis, steps):
    count = lax.axis_size(axis)
    first, last = (max(0, -steps), min(count, count - steps))
    return lax.ppermute(value, axis, [(source, source + steps) for source in range(first, last)])


def shards(toar, pml_coeff, coupling, inverse, pattern, patch_map):
    toar_local = toar[0]
    coeff = pml_coeff[0]
    coupler = coupling[0]
    factor = inverse[0]
    pattern_flat = pattern[0].reshape(-1)
    block_rows = factor.shape[0]
    block_cells = factor.shape[2]
    depth_count = lax.axis_size("depth")
    plane_count = lax.axis_size("plane")
    vec_count = toar_local.shape[0]
    toar_f32 = toar_local.astype(jnp.float32)
    real_part = coeff[0] * toar_f32[:, 0] - coeff[1] * toar_f32[:, 1]
    imag_part = coeff[0] * toar_f32[:, 1] + coeff[1] * toar_f32[:, 0]
    source = jnp.stack([real_part, imag_part], axis=1)

    def apply_layer(incoming):
        local_blocks = incoming.reshape(vec_count, 2, block_rows, block_cells).transpose(2, 0, 1, 3)
        gathered = lax.all_gather(local_blocks, "plane", axis=0, tiled=True)
        chosen = jnp.take(gathered, pattern_flat, axis=0)
        chosen = chosen.reshape(block_rows, -1, vec_count, 2, block_cells)
        x_re = chosen[:, :, :, 0]
        x_im = chosen[:, :, :, 1]
        expanded = jnp.stack(
            [jnp.concatenate([x_re, -x_im], axis=-1), jnp.concatenate([x_im, x_re], axis=-1)],
            axis=3,
        )
        out = jnp.einsum(
            "rkic,rkvwc->vwri", factor, expanded, preferred_element_type=jnp.float32
        )
        return out.reshape(vec_count, 2, block_rows * block_cells)

    def down_turn(turn_index, current):
        arrived = passed_along(current, "depth", 1)
        down_in = (source + coupler * arrived.astype(jnp.float32)).astype(jnp.bfloat16)
        return apply_layer(down_in).astype(jnp.bfloat16)

    first = apply_layer(source.astype(jnp.bfloat16)).astype(jnp.bfloat16)
    swept = lax.fori_loop(0, depth_count - 1, down_turn, first)

    def up_turn(turn_index, current):
        outgoing = (coupler * current.astype(jnp.float32)).astype(jnp.bfloat16)
        arrived = passed_along(outgoing, "depth", -1)
        return (swept.astype(jnp.float32) + apply_layer(arrived)).astype(jnp.bfloat16)

    precond = lax.fori_loop(0, depth_count - 1, up_turn, swept)
    product = precond.astype(jnp.float32) * toar_f32
    contrib = product[:, 0] + product[:, 1]

    cell_patch = patch_map[0]
    cell_count = cell_patch.shape[0]
    owner_count = depth_count * plane_count
    owner = cell_patch // PATCH_DEV
    hits = (owner[:, None] == jnp.arange(owner_count, dtype=owner.dtype)[None, :]).astype(jnp.int32)
    rank = jnp.take_along_axis(jnp.cumsum(hits, axis=0), owner[:, None], axis=1)[:, 0] - 1
    slot = owner * CAP + rank
    cells = jnp.arange(cell_count, dtype=jnp.int32)
    perm = jnp.full((owner_count * CAP,), cell_count, jnp.int32).at[slot].set(cells)
    local_patch = (cell_patch % PATCH_DEV).astype(jnp.float32)
    padded = jnp.concatenate(
        [jnp.concatenate([contrib.T, local_patch[:, None]], axis=1),
         jnp.zeros((1, vec_count + 1), jnp.float32)],
        axis=0,
    )
    packed = jnp.take(padded, perm, axis=0).reshape(owner_count, CAP, vec_count + 1)
    received = lax.all_to_all(packed, ("depth", "plane"), 0, 0, tiled=True)
    received = received.reshape(owner_count * CAP, vec_count + 1)
    target = received[:, vec_count].astype(jnp.int32)
    owned = jax.ops.segment_sum(received[:, :vec_count], target, num_segments=PATCH_DEV).T
    return (precond[None], owned)


def solution(mesh):
    return jax.shard_map(
        shards,
        mesh=mesh,
        in_specs=(
            P("depth", None, None, "plane"),
            P("depth", None, "plane"),
            P("depth", "plane"),
            P("depth", "plane", None, None, None),
            P("depth", "plane", None),
            P("depth", "plane"),
        ),
        out_specs=(P("depth", None, None, "plane"), P(None, ("depth", "plane"))),
        check_vma=False,
    )
```

time: 1760 us -> 991 us (0.56); the launches traced: 1720 us -> 990 us
  waiting for transfers between devices: 1220 us -> 666 us
  matrix products: 154 us -> 34 us
  local copies, waits for them, and re-layouts: 202 us -> 134 us
    reduce_scatter x1 -> x0, waiting for transfers between devices: 622 us -> none  [shards(): lax.psum_scatter(local_sums, ('depth', 'plane'), scatter_dimension=1, til...]
    dot_general x15, matrix products: 154 us -> 34 us  [apply_layer(): jnp.einsum('rkic,rkvwc->vwri', factor, expanded, preferred_element_type=j...]
    reshape x30 -> x22, local copies, waits for them, and re-layouts: 85.8 us -> 3.54 us  [the longest x14 2.44 us: apply_layer(): incoming.reshape(vec_count, 2, block_rows, block_cells)]
    all_gather x15, waiting for transfers between devices: 568 us -> 625 us  [apply_layer(): gathered = lax.all_gather(local_blocks, 'plane', axis=0, tiled=True)]
    another operation x17 -> x6, local copies, waits for them, and re-layouts: 28 us -> 0.93 us  [the longest x1 27.9 us: shards(): factor = inv_local.reshape(block_rows, per_row, block_cells, 2, block_cells)]
    select_n x30 -> x33, other arithmetic: 43 us -> 27.9 us  [the longest x30 26.4 us: apply_layer(): chosen = jnp.take(gathered, pattern_flat, axis=0)]
    gather x15 -> x18, local copies, waits for them, and re-layouts: 60.9 us -> 70 us  [the longest x15 41.6 us: apply_layer(): chosen = jnp.take(gathered, pattern_flat, axis=0)]
where the time goes in v1:
time: 991 us; the launch traced here: 990 us
  waiting for transfers between devices  666 us (67%)
  local copies, waits for them, and re-layouts  134 us (14%)
  other arithmetic  73.8 us (7%)
  starting transfers between devices  65 us (7%)
  matrix products  34 us (3%)
  between operations  14.1 us (1%)
    all_gather x15, waiting for transfers between devices, apply_layer(): gathered = lax.all_gather(local_blocks, 'plane', axis=0, tiled=True)  625 us
    ppermute x14, starting transfers between devices, passed_along(): lax.ppermute(value, axis, [(source, source + steps) for source in range(f...  55.9 us
    gather x15, local copies, waits for them, and re-layouts, apply_layer(): chosen = jnp.take(gathered, pattern_flat, axis=0)  41.6 us
    dot_general x15, matrix products, apply_layer(): jnp.einsum('rkic,rkvwc->vwri', factor, expanded, preferred_element_type=j...  34 us
    ppermute x14, waiting for transfers between devices, passed_along(): lax.ppermute(value, axis, [(source, source + steps) for source in range(f...  30.8 us
    select_n x30, other arithmetic, apply_layer(): chosen = jnp.take(gathered, pattern_flat, axis=0)  26.4 us
    while x56, local copies, waits for them, and re-layouts  24.8 us
    scatter-add x1, other arithmetic, shards(): jax.ops.segment_sum(received[:, :vec_count], target, num_segments=PATCH_DEV)  22.8 us
  transfers between devices with their start and end apart: 30, of which 30 were waited for; matrix products, arithmetic and copies ran while one was open for 3% of the time, Pallas kernels for 0%

profile of v1, /device:TPU:1, one launch (start us, length us, event | category | flops | bytes accessed | tf_op | source)
XLA Modules:
  0.0 989.7 jit_solution(395873803658313803)
XLA Ops:
  13.6 16.8 %gather_fusion.3 = s32[2048]{0:T(1024)S(1)} fusion(s32[2048,128]{0,1:T(8,128)S(1)} %bitcast.223, s32[2048]{0:T(1024)S(1)} %bitcast.222), kind=kCustom, calls=%fused_computation.4 | custom fusion | bytes 32768 | tf_op jit(solution)/shard_map/jit(take_along_axis)/gather | solution.py:70
  30.5 8.2 scatter_custom_fusion
  39.0 18.4 %all-gather.4.cloned.1.call-done = bf16[512,8,2,64]{3,1,2,0:T(8,128)(2,1)} async-done(((bf16[32,8,2,64]{3,1,2,0:T(8,128)(2,1)}), bf16[512,8,2,64]{3,1,2,0:T(8,128)(2,1)}) %all-gather.4.cloned.1.call-update) | async-done | bytes 1048592 | tf_op jit(solution)/shard_map/all_gather | solution.py:34
  67.9 430.4 %while.20 = (s32[]{:T(128)}, bf16[8,2,2048]{2,0,1:T(8,128)(2,1)S(1)}, f32[1,2048]{1,0:T(1,128)S(1)}, f32[8,2,2048]{2,0,1:T(8,128)S(1)}, s32[512]{0:T(512)S(1)}, /*index=5*/bf16[32,16,64,128]{3,2,1,0:T(8,128)(2,1)}, s32[]{:T(128)}) while((s32[]{:T(128)}, bf16[8,2,2048]{2,0,1:T(8,128)(2,1)S(1)}, f32[1,2048]{1,0:T(1,128)S(1)}, ...), condition=%wide.region_1.3_spmd, body=%wide.region_0.0_spmd.sunk | while | flops 140416512 | bytes 54353100 | solution.py:54
  68.0 4.6 collective-permute-start
  74.8 44.0 %all-gather.6.cloned.1.call-done = bf16[512,8,2,64]{3,1,2,0:T(8,128)(2,1)} async-done(((bf16[32,8,2,64]{3,1,2,0:T(8,128)(2,1)}), bf16[512,8,2,64]{3,1,2,0:T(8,128)(2,1)}) %all-gather.6.cloned.1.call-update) | async-done | bytes 1048592 | tf_op jit(solution)/shard_map/while/body/eval_jaxpr/all_gather | solution.py:34
  136.3 44.0 %all-gather.6.cloned.1.call-done = bf16[512,8,2,64]{3,1,2,0:T(8,128)(2,1)} async-done(((bf16[32,8,2,64]{3,1,2,0:T(8,128)(2,1)}), bf16[512,8,2,64]{3,1,2,0:T(8,128)(2,1)}) %all-gather.6.cloned.1.call-update) | async-done | bytes 1048592 | tf_op jit(solution)/shard_map/while/body/eval_jaxpr/all_gather | solution.py:34
  197.8 44.0 %all-gather.6.cloned.1.call-done = bf16[512,8,2,64]{3,1,2,0:T(8,128)(2,1)} async-done(((bf16[32,8,2,64]{3,1,2,0:T(8,128)(2,1)}), bf16[512,8,2,64]{3,1,2,0:T(8,128)(2,1)}) %all-gather.6.cloned.1.call-update) | async-done | bytes 1048592 | tf_op jit(solution)/shard_map/while/body/eval_jaxpr/all_gather | solution.py:34
  259.3 44.0 %all-gather.6.cloned.1.call-done = bf16[512,8,2,64]{3,1,2,0:T(8,128)(2,1)} async-done(((bf16[32,8,2,64]{3,1,2,0:T(8,128)(2,1)}), bf16[512,8,2,64]{3,1,2,0:T(8,128)(2,1)}) %all-gather.6.cloned.1.call-update) | async-done | bytes 1048592 | tf_op jit(solution)/shard_map/while/body/eval_jaxpr/all_gather | solution.py:34
  320.8 44.0 %all-gather.6.cloned.1.call-done = bf16[512,8,2,64]{3,1,2,0:T(8,128)(2,1)} async-done(((bf16[32,8,2,64]{3,1,2,0:T(8,128)(2,1)}), bf16[512,8,2,64]{3,1,2,0:T(8,128)(2,1)}) %all-gather.6.cloned.1.call-update) | async-done | bytes 1048592 | tf_op jit(solution)/shard_map/while/body/eval_jaxpr/all_gather | solution.py:34
  382.3 44.0 %all-gather.6.cloned.1.call-done = bf16[512,8,2,64]{3,1,2,0:T(8,128)(2,1)} async-done(((bf16[32,8,2,64]{3,1,2,0:T(8,128)(2,1)}), bf16[512,8,2,64]{3,1,2,0:T(8,128)(2,1)}) %all-gather.6.cloned.1.call-update) | async-done | bytes 1048592 | tf_op jit(solution)/shard_map/while/body/eval_jaxpr/all_gather | solution.py:34
  443.8 44.0 %all-gather.6.cloned.1.call-done = bf16[512,8,2,64]{3,1,2,0:T(8,128)(2,1)} async-done(((bf16[32,8,2,64]{3,1,2,0:T(8,128)(2,1)}), bf16[512,8,2,64]{3,1,2,0:T(8,128)(2,1)}) %all-gather.6.cloned.1.call-update) | async-done | bytes 1048592 | tf_op jit(solution)/shard_map/while/body/eval_jaxpr/all_gather | solution.py:34
  498.4 425.7 %while.21 = (s32[]{:T(128)}, bf16[8,2,2048]{2,0,1:T(8,128)(2,1)S(1)}, bf16[8,2,2048]{2,0,1:T(8,128)(2,1)S(1)}, f32[1,2048]{1,0:T(1,128)S(1)}, s32[512]{0:T(512)S...) while((s32[]{:T(128)}, bf16[8,2,2048]{2,0,1:T(8,128)(2,1)S(1)}, bf16[8,2,2048]{2,0,1:T(8,128)(2,1)S(1)}, ...), condition=%wide.region_3.5_spmd, body=%wide.region_2.4_spmd.sunk | while | flops 140449280 | bytes 54811852 | solution.py:61
  506.2 42.7 %all-gather.8.cloned.1.call-done = bf16[512,8,2,64]{3,1,2,0:T(8,128)(2,1)} async-done(((bf16[32,8,2,64]{3,1,2,0:T(8,128)(2,1)}), bf16[512,8,2,64]{3,1,2,0:T(8,128)(2,1)}) %all-gather.8.cloned.1.call-update) | async-done | bytes 1048592 | tf_op jit(solution)/shard_map/while/body/eval_jaxpr/all_gather | solution.py:34
  567.0 42.7 %all-gather.8.cloned.1.call-done = bf16[512,8,2,64]{3,1,2,0:T(8,128)(2,1)} async-done(((bf16[32,8,2,64]{3,1,2,0:T(8,128)(2,1)}), bf16[512,8,2,64]{3,1,2,0:T(8,128)(2,1)}) %all-gather.8.cloned.1.call-update) | async-done | bytes 1048592 | tf_op jit(solution)/shard_map/while/body/eval_jaxpr/all_gather | solution.py:34
  627.7 42.7 %all-gather.8.cloned.1.call-done = bf16[512,8,2,64]{3,1,2,0:T(8,128)(2,1)} async-done(((bf16[32,8,2,64]{3,1,2,0:T(8,128)(2,1)}), bf16[512,8,2,64]{3,1,2,0:T(8,128)(2,1)}) %all-gather.8.cloned.1.call-update) | async-done | bytes 1048592 | tf_op jit(solution)/shard_map/while/body/eval_jaxpr/all_gather | solution.py:34
  688.5 42.7 %all-gather.8.cloned.1.call-done = bf16[512,8,2,64]{3,1,2,0:T(8,128)(2,1)} async-done(((bf16[32,8,2,64]{3,1,2,0:T(8,128)(2,1)}), bf16[512,8,2,64]{3,1,2,0:T(8,128)(2,1)}) %all-gather.8.cloned.1.call-update) | async-done | bytes 1048592 | tf_op jit(solution)/shard_map/while/body/eval_jaxpr/all_gather | solution.py:34
  749.3 42.7 %all-gather.8.cloned.1.call-done = bf16[512,8,2,64]{3,1,2,0:T(8,128)(2,1)} async-done(((bf16[32,8,2,64]{3,1,2,0:T(8,128)(2,1)}), bf16[512,8,2,64]{3,1,2,0:T(8,128)(2,1)}) %all-gather.8.cloned.1.call-update) | async-done | bytes 1048592 | tf_op jit(solution)/shard_map/while/body/eval_jaxpr/all_gather | solution.py:34
  810.1 42.7 %all-gather.8.cloned.1.call-done = bf16[512,8,2,64]{3,1,2,0:T(8,128)(2,1)} async-done(((bf16[32,8,2,64]{3,1,2,0:T(8,128)(2,1)}), bf16[512,8,2,64]{3,1,2,0:T(8,128)(2,1)}) %all-gather.8.cloned.1.call-update) | async-done | bytes 1048592 | tf_op jit(solution)/shard_map/while/body/eval_jaxpr/all_gather | solution.py:34
  870.9 42.7 %all-gather.8.cloned.1.call-done = bf16[512,8,2,64]{3,1,2,0:T(8,128)(2,1)} async-done(((bf16[32,8,2,64]{3,1,2,0:T(8,128)(2,1)}), bf16[512,8,2,64]{3,1,2,0:T(8,128)(2,1)}) %all-gather.8.cloned.1.call-update) | async-done | bytes 1048592 | tf_op jit(solution)/shard_map/while/body/eval_jaxpr/all_gather | solution.py:34
  924.7 10.8 %gather_fusion.2 = f32[4096,9]{1,0:T(8,128)S(1)} fusion(f32[2049,9]{1,0:T(8,128)S(1)} %concatenate.29, s32[4096]{0:T(1024)S(1)} %fusion.60), kind=kCustom, calls=%fused_computation.3 | custom fusion | bytes 311296 | tf_op jit(solution)/shard_map/jit(_take)/gather | solution.py:80
  937.6 8.5 all-to-all-start
  946.8 9.9 all-to-all-done
  959.7 22.8 %scatter_custom_fusion.1 = f32[128,8]{1,0:T(8,128)S(1)} fusion(s32[4096]{0:T(1024)S(1)} %bitcast.239, f32[4096,8]{1,0:T(8,128)S(1)} %copy.101, f32[]{:T(128)} %constant.77.clone.1), kind=kCustom, calls=%fused_computation.77 | custom fusion | flops 32768 | bytes 4100 | tf_op jit(solution)/shard_map/scatter-add | solution.py:84
  (414 shorter events, 266.7 us)
Async XLA Ops:
  7.2 50.2 %all-gather.4.cloned.1.call-start = ((), (), s32[]{:S(2)}) async-start(), calls=%async_computation.1 | async-start | bytes 2228224 | tf_op jit(solution)/shard_map/all_gather | solution.py:34
  67.9 50.9 %all-gather.6.cloned.1.call-start = ((), (), s32[]{:S(2)}) async-start(), calls=%async_computation.2 | async-start | bytes 2228224 | tf_op jit(solution)/shard_map/while/body/eval_jaxpr/all_gather | solution.py:34
  129.4 50.9 %all-gather.6.cloned.1.call-start = ((), (), s32[]{:S(2)}) async-start(), calls=%async_computation.2 | async-start | bytes 2228224 | tf_op jit(solution)/shard_map/while/body/eval_jaxpr/all_gather | solution.py:34
  129.5 5.9 collective-permute-start
  190.9 50.9 %all-gather.6.cloned.1.call-start = ((), (), s32[]{:S(2)}) async-start(), calls=%async_computation.2 | async-start | bytes 2228224 | tf_op jit(solution)/shard_map/while/body/eval_jaxpr/all_gather | solution.py:34
  252.4 50.9 %all-gather.6.cloned.1.call-start = ((), (), s32[]{:S(2)}) async-start(), calls=%async_computation.2 | async-start | bytes 2228224 | tf_op jit(solution)/shard_map/while/body/eval_jaxpr/all_gather | solution.py:34
  313.9 50.9 %all-gather.6.cloned.1.call-start = ((), (), s32[]{:S(2)}) async-start(), calls=%async_computation.2 | async-start | bytes 2228224 | tf_op jit(solution)/shard_map/while/body/eval_jaxpr/all_gather | solution.py:34
  375.4 50.9 %all-gather.6.cloned.1.call-start = ((), (), s32[]{:S(2)}) async-start(), calls=%async_computation.2 | async-start | bytes 2228224 | tf_op jit(solution)/shard_map/while/body/eval_jaxpr/all_gather | solution.py:34
  436.9 50.9 %all-gather.6.cloned.1.call-start = ((), (), s32[]{:S(2)}) async-start(), calls=%async_computation.2 | async-start | bytes 2228224 | tf_op jit(solution)/shard_map/while/body/eval_jaxpr/all_gather | solution.py:34
  498.6 50.2 %all-gather.8.cloned.1.call-start = ((), (), s32[]{:S(2)}) async-start(), calls=%async_computation.3 | async-start | bytes 2228224 | tf_op jit(solution)/shard_map/while/body/eval_jaxpr/all_gather | solution.py:34
  498.7 6.5 collective-permute-start.1
  559.4 50.2 %all-gather.8.cloned.1.call-start = ((), (), s32[]{:S(2)}) async-start(), calls=%async_computation.3 | async-start | bytes 2228224 | tf_op jit(solution)/shard_map/while/body/eval_jaxpr/all_gather | solution.py:34
  559.5 6.5 collective-permute-start.1
  620.2 50.2 %all-gather.8.cloned.1.call-start = ((), (), s32[]{:S(2)}) async-start(), calls=%async_computation.3 | async-start | bytes 2228224 | tf_op jit(solution)/shard_map/while/body/eval_jaxpr/all_gather | solution.py:34
  620.3 6.5 collective-permute-start.1
  681.0 50.2 %all-gather.8.cloned.1.call-start = ((), (), s32[]{:S(2)}) async-start(), calls=%async_computation.3 | async-start | bytes 2228224 | tf_op jit(solution)/shard_map/while/body/eval_jaxpr/all_gather | solution.py:34
  681.1 6.5 collective-permute-start.1
  741.8 50.2 %all-gather.8.cloned.1.call-start = ((), (), s32[]{:S(2)}) async-start(), calls=%async_computation.3 | async-start | bytes 2228224 | tf_op jit(solution)/shard_map/while/body/eval_jaxpr/all_gather | solution.py:34
  741.8 6.5 collective-permute-start.1
  802.6 50.2 %all-gather.8.cloned.1.call-start = ((), (), s32[]{:S(2)}) async-start(), calls=%async_computation.3 | async-start | bytes 2228224 | tf_op jit(solution)/shard_map/while/body/eval_jaxpr/all_gather | solution.py:34
  802.6 6.5 collective-permute-start.1
  863.3 50.2 %all-gather.8.cloned.1.call-start = ((), (), s32[]{:S(2)}) async-start(), calls=%async_computation.3 | async-start | bytes 2228224 | tf_op jit(solution)/shard_map/while/body/eval_jaxpr/all_gather | solution.py:34
  863.4 6.5 collective-permute-start.1
  937.6 19.1 %all-to-all-start = ((f32[128,1,288]{2,1,0:T(1,128)}), f32[128,1,288]{2,1,0:T(1,128)S(1)}, u32[]{:S(2)}, u32[]{:S(2)}) async-start(f32[128,1,288]{2,1,0:T(1,128)} %reshape.447), calls=%async_computation | async-start | bytes 393216 | tf_op jit(solution)/shard_map/all_to_all | solution.py:81
  (39 other events, 563.5 us)
Sparse Core Ops, SparseCore 0:
  10.1 47.1 all-gather.3
  74.9 43.8 all-gather.5
  136.4 43.8 all-gather.5
  197.9 43.8 all-gather.5
  259.4 43.8 all-gather.5
  320.9 43.8 all-gather.5
  382.4 43.8 all-gather.5
  443.9 43.8 all-gather.5
  506.2 42.5 all-gather.7
  567.0 42.5 all-gather.7
  627.8 42.5 all-gather.7
  688.6 42.5 all-gather.7
  749.4 42.5 all-gather.7
  810.2 42.5 all-gather.7
  871.0 42.5 all-gather.7

commit v2 on v1

--- a/solution.py
+++ b/solution.py
@@ -29,10 +29,29 @@
     imag_part = coeff[0] * toar_f32[:, 1] + coeff[1] * toar_f32[:, 0]
     source = jnp.stack([real_part, imag_part], axis=1)
 
+    side_a = next(n for n in range(int(plane_count ** 0.5), 0, -1) if plane_count % n == 0)
+    side_b = plane_count // side_a
+    plane_routes = {}
+    for offset in range(1, plane_count):
+        step_a, step_b = divmod(offset, side_b)
+        plane_routes[offset] = [
+            (a * side_b + b, ((a + step_a) % side_a) * side_b + (b + step_b) % side_b)
+            for a in range(side_a)
+            for b in range(side_b)
+        ]
+    here = lax.axis_index("plane")
+    origin = pattern_flat // block_rows
+    slot_a = (here // side_b - origin // side_b) % side_a
+    slot_b = (here % side_b - origin % side_b) % side_b
+    remapped = (slot_a * side_b + slot_b) * block_rows + pattern_flat % block_rows
+
     def apply_layer(incoming):
         local_blocks = incoming.reshape(vec_count, 2, block_rows, block_cells).transpose(2, 0, 1, 3)
-        gathered = lax.all_gather(local_blocks, "plane", axis=0, tiled=True)
-        chosen = jnp.take(gathered, pattern_flat, axis=0)
+        pieces = [local_blocks]
+        for offset in range(1, plane_count):
+            pieces.append(lax.ppermute(local_blocks, "plane", plane_routes[offset]))
+        gathered = jnp.concatenate(pieces, axis=0)
+        chosen = jnp.take(gathered, remapped, axis=0)
         chosen = chosen.reshape(block_rows, -1, vec_count, 2, block_cells)
         x_re = chosen[:, :, :, 0]
         x_im = chosen[:, :, :, 1]

time: 991 us -> 982 us (level); the launches traced: 990 us -> 969 us
  waiting for transfers between devices: 666 us -> 99.3 us
  starting transfers between devices: 65 us -> 476 us
  local copies, waits for them, and re-layouts: 134 us -> 281 us
  between operations: 14.1 us -> 1.55 us
    all_gather x15 -> x0, waiting for transfers between devices: 625 us -> none  [apply_layer(): gathered = lax.all_gather(local_blocks, 'plane', axis=0, tiled=True)]
    ppermute x0 -> x225, starting transfers between devices: none -> 412 us  [apply_layer(): pieces.append(lax.ppermute(local_blocks, 'plane', plane_routes[offset]))]
    while x56 -> x266, local copies, waits for them, and re-layouts: 24.8 us -> 163 us
    ppermute x0 -> x225, waiting for transfers between devices: none -> 50.5 us  [apply_layer(): pieces.append(lax.ppermute(local_blocks, 'plane', plane_routes[offset]))]
    transpose x15 -> x0, local copies, waits for them, and re-layouts: 10.8 us -> none  [apply_layer(): incoming.reshape(vec_count, 2, block_rows, block_cells)]
    concatenate x0 -> x15, local copies, waits for them, and re-layouts: none -> 9.92 us  [apply_layer(): gathered = jnp.concatenate(pieces, axis=0)]
  transfers between devices with their start and end apart: 30 -> 240, of which waited for: 30 -> 46; matrix products, arithmetic and copies ran while one was open for 3% -> 18% of each run, Pallas kernels for 0% -> 0%
where the time goes in v2:
time: 982 us; the launch traced here: 969 us
  starting transfers between devices  476 us (48%)
  local copies, waits for them, and re-layouts  281 us (29%)
  waiting for transfers between devices  99.3 us (10%)
  other arithmetic  74.5 us (8%)
  matrix products  34 us (3%)
    ppermute x225, starting transfers between devices, apply_layer(): pieces.append(lax.ppermute(local_blocks, 'plane', plane_routes[offset]))  412 us
    while x266, local copies, waits for them, and re-layouts  163 us
    ppermute x14, starting transfers between devices, passed_along(): lax.ppermute(value, axis, [(source, source + steps) for source in range(f...  55.8 us
    ppermute x225, waiting for transfers between devices, apply_layer(): pieces.append(lax.ppermute(local_blocks, 'plane', plane_routes[offset]))  50.5 us
    gather x15, local copies, waits for them, and re-layouts, apply_layer(): chosen = jnp.take(gathered, remapped, axis=0)  41.7 us
    ppermute x14, waiting for transfers between devices, passed_along(): lax.ppermute(value, axis, [(source, source + steps) for source in range(f...  38.9 us
    dot_general x15, matrix products, apply_layer(): jnp.einsum('rkic,rkvwc->vwri', factor, expanded, preferred_element_type=j...  34 us
    select_n x30, other arithmetic, apply_layer(): chosen = jnp.take(gathered, remapped, axis=0)  26.3 us
  transfers between devices with their start and end apart: 240, of which 46 were waited for; matrix products, arithmetic and copies ran while one was open for 18% of the time, Pallas kernels for 0%

profile of v2, /device:TPU:1, one launch (start us, length us, event | category | flops | bytes accessed | tf_op | source)
XLA Modules:
  0.0 968.7 jit_solution(5904884703422739265)
XLA Ops:
  13.3 16.8 %gather_fusion.3 = s32[2048]{0:T(1024)S(1)} fusion(s32[2048,128]{0,1:T(8,128)S(1)} %bitcast.237, s32[2048]{0:T(1024)S(1)} %bitcast.236), kind=kCustom, calls=%fused_computation.4 | custom fusion | bytes 32768 | tf_op jit(solution)/shard_map/jit(take_along_axis)/gather | solution.py:89
  30.2 8.1 scatter_custom_fusion
  82.6 419.8 %while.20 = (s32[]{:T(128)}, bf16[8,2,2048]{2,0,1:T(8,128)(2,1)S(1)}, f32[1,2048]{1,0:T(1,128)S(1)}, f32[8,2,2048]{2,0,1:T(8,128)S(1)}, s32[512]{0:T(512)S(1)}, /*index=5*/bf16[32,16,64,128]{3,2,1,0:T(8,128)(2,1)}, s32[]{:T(128)}) while((s32[]{:T(128)}, bf16[8,2,2048]{2,0,1:T(8,128)(2,1)S(1)}, f32[1,2048]{1,0:T(1,128)S(1)}, ...), condition=%wide.region_1.3_spmd, body=%wide.region_0.2_spmd.sunk | while | flops 140416512 | bytes 56975100 | solution.py:73
  82.6 7.4 collective-permute-start
  144.0 5.8 collective-permute-start
  177.6 6.9 collective-permute-start.13
  203.3 8.1 collective-permute-start
  263.8 8.7 collective-permute-start
  324.9 5.0 collective-permute-start
  482.7 6.6 collective-permute-done.13
  502.4 407.9 %while.21 = (s32[]{:T(128)}, bf16[8,2,2048]{2,0,1:T(8,128)(2,1)S(1)}, bf16[8,2,2048]{2,0,1:T(8,128)(2,1)S(1)}, f32[1,2048]{1,0:T(1,128)S(1)}, s32[512]{0:T(512)S...) while((s32[]{:T(128)}, bf16[8,2,2048]{2,0,1:T(8,128)(2,1)S(1)}, bf16[8,2,2048]{2,0,1:T(8,128)(2,1)S(1)}, ...), condition=%wide.region_3.5_spmd, body=%wide.region_2.4_spmd.sunk | while | flops 140449280 | bytes 57433852 | solution.py:80
  535.7 8.2 collective-permute-start.30
  596.3 5.8 collective-permute-start.31
  620.3 5.2 collective-permute-done.16
  651.5 7.9 collective-permute-start.30
  701.0 5.7 collective-permute-start.26
  738.0 5.1 collective-permute-done.16
  766.6 5.6 collective-permute-done.23
  829.8 7.5 collective-permute-start.30
  855.9 5.3 collective-permute-done.16
  910.9 10.8 %gather_fusion.2 = f32[4096,9]{1,0:T(8,128)S(1)} fusion(f32[2049,9]{1,0:T(8,128)S(1)} %concatenate.39, s32[4096]{0:T(1024)S(1)} %fusion.60), kind=kCustom, calls=%fused_computation.3 | custom fusion | bytes 311296 | tf_op jit(solution)/shard_map/jit(_take)/gather | solution.py:99
  923.8 7.4 all-to-all-start
  931.9 9.9 %all-to-all-done = f32[128,1,288]{2,1,0:T(1,128)S(1)} async-done(((f32[128,1,288]{2,1,0:T(1,128)}), f32[128,1,288]{2,1,0:T(1,128)S(1)}, u32[]{:S(2)}, u32[]{:S(2)}) %all-to-all-start) | async-done | bytes 147488 | tf_op jit(solution)/shard_map/all_to_all | solution.py:100
  944.8 22.8 %scatter_custom_fusion.1 = f32[128,8]{1,0:T(8,128)S(1)} fusion(s32[4096]{0:T(1024)S(1)} %bitcast.281, f32[4096,8]{1,0:T(8,128)S(1)} %copy.102, f32[]{:T(128)} %constant.155.clone.1), kind=kCustom, calls=%fused_computation.127 | custom fusion | flops 32768 | bytes 4100 | tf_op jit(solution)/shard_map/scatter-add | solution.py:103
  (1062 shorter events, 784.2 us)
Async XLA Ops:
  2.7 37.4 %collective-permute-start.32 = (bf16[32,8,2,64]{3,1,2,0:T(8,128)(2,1)S(1)}, bf16[32,8,2,64]{3,1,2,0:T(8,128)(2,1)S(1)}, u32[]{:S(2)}, u32[]{:S(2)}) collective-permute-start(bf16[32,8,2,64]{3,1,2,0:T(8,128)(2,1)S(1)} %maximum_bitcast_fusion.6), channel_id=1, source_target_pairs={{0,1},{1,2},{2,3},{3,0},{4,5},{5,6},{6,7},{7,4},{8,9},{9,10},{10,1... | collective-permute-start | bytes 196616 | tf_op jit(solution)/shard_map/ppermute | solution.py:52
  4.9 37.2 %collective-permute-start.33 = (bf16[32,8,2,64]{3,1,2,0:T(8,128)(2,1)S(1)}, bf16[32,8,2,64]{3,1,2,0:T(8,128)(2,1)S(1)}, u32[]{:S(2)}, u32[]{:S(2)}) collective-permute-start(bf16[32,8,2,64]{3,1,2,0:T(8,128)(2,1)S(1)} %maximum_bitcast_fusion.6), channel_id=1, source_target_pairs={{0,2},{1,3},{2,0},{3,1},{4,6},{5,7},{6,4},{7,5},{8,10},{9,11},{10,... | collective-permute-start | bytes 196616 | tf_op jit(solution)/shard_map/ppermute | solution.py:52
  7.5 36.9 %collective-permute-start.34 = (bf16[32,8,2,64]{3,1,2,0:T(8,128)(2,1)S(1)}, bf16[32,8,2,64]{3,1,2,0:T(8,128)(2,1)S(1)}, u32[]{:S(2)}, u32[]{:S(2)}) collective-permute-start(bf16[32,8,2,64]{3,1,2,0:T(8,128)(2,1)S(1)} %maximum_bitcast_fusion.6), channel_id=1, source_target_pairs={{0,3},{1,0},{2,1},{3,2},{4,7},{5,4},{6,5},{7,6},{8,11},{9,8},{10,9... | collective-permute-start | bytes 196616 | tf_op jit(solution)/shard_map/ppermute | solution.py:52
  8.6 38.6 %collective-permute-start.35 = (bf16[32,8,2,64]{3,1,2,0:T(8,128)(2,1)S(1)}, bf16[32,8,2,64]{3,1,2,0:T(8,128)(2,1)S(1)}, u32[]{:S(2)}, u32[]{:S(2)}) collective-permute-start(bf16[32,8,2,64]{3,1,2,0:T(8,128)(2,1)S(1)} %maximum_bitcast_fusion.6), channel_id=1, source_target_pairs={{0,4},{1,5},{2,6},{3,7},{4,8},{5,9},{6,10},{7,11},{8,12},{9,13},{1... | collective-permute-start | bytes 196616 | tf_op jit(solution)/shard_map/ppermute | solution.py:52
  106.6 17.7 %collective-permute-start.9 = (bf16[32,8,2,64]{3,1,2,0:T(8,128)(2,1)S(1)}, bf16[32,8,2,64]{3,1,2,0:T(8,128)(2,1)S(1)}, u32[]{:S(2)}, u32[]{:S(2)}) collective-permute-start(bf16[32,8,2,64]{3,1,2,0:T(8,128)(2,1)S(1)} %bitcast.251), channel_id=1, source_target_pairs={{0,9},{1,10},{2,11},{3,8},{4,13},{5,14},{6,15},{7,12},{8,1},{9,2},... | collective-permute-start | bytes 196616 | tf_op jit(solution)/shard_map/while/body/eval_jaxpr/ppermute | solution.py:52
  108.4 18.7 %collective-permute-start.10 = (bf16[32,8,2,64]{3,1,2,0:T(8,128)(2,1)S(1)}, bf16[32,8,2,64]{3,1,2,0:T(8,128)(2,1)S(1)}, u32[]{:S(2)}, u32[]{:S(2)}) collective-permute-start(bf16[32,8,2,64]{3,1,2,0:T(8,128)(2,1)S(1)} %bitcast.252), channel_id=1, source_target_pairs={{0,10},{1,11},{2,8},{3,9},{4,14},{5,15},{6,12},{7,13},{8,2},{9,3},... | collective-permute-start | bytes 196616 | tf_op jit(solution)/shard_map/while/body/eval_jaxpr/ppermute | solution.py:52
  167.2 18.0 %collective-permute-start.9 = (bf16[32,8,2,64]{3,1,2,0:T(8,128)(2,1)S(1)}, bf16[32,8,2,64]{3,1,2,0:T(8,128)(2,1)S(1)}, u32[]{:S(2)}, u32[]{:S(2)}) collective-permute-start(bf16[32,8,2,64]{3,1,2,0:T(8,128)(2,1)S(1)} %bitcast.251), channel_id=1, source_target_pairs={{0,9},{1,10},{2,11},{3,8},{4,13},{5,14},{6,15},{7,12},{8,1},{9,2},... | collective-permute-start | bytes 196616 | tf_op jit(solution)/shard_map/while/body/eval_jaxpr/ppermute | solution.py:52
  167.9 18.0 %collective-permute-start.10 = (bf16[32,8,2,64]{3,1,2,0:T(8,128)(2,1)S(1)}, bf16[32,8,2,64]{3,1,2,0:T(8,128)(2,1)S(1)}, u32[]{:S(2)}, u32[]{:S(2)}) collective-permute-start(bf16[32,8,2,64]{3,1,2,0:T(8,128)(2,1)S(1)} %bitcast.252), channel_id=1, source_target_pairs={{0,10},{1,11},{2,8},{3,9},{4,14},{5,15},{6,12},{7,13},{8,2},{9,3},... | collective-permute-start | bytes 196616 | tf_op jit(solution)/shard_map/while/body/eval_jaxpr/ppermute | solution.py:52
  172.7 15.9 %collective-permute-start.11 = (bf16[32,8,2,64]{3,1,2,0:T(8,128)(2,1)S(1)}, bf16[32,8,2,64]{3,1,2,0:T(8,128)(2,1)S(1)}, u32[]{:S(2)}, u32[]{:S(2)}) collective-permute-start(bf16[32,8,2,64]{3,1,2,0:T(8,128)(2,1)S(1)} %bitcast.253), channel_id=1, source_target_pairs={{0,11},{1,8},{2,9},{3,10},{4,15},{5,12},{6,13},{7,14},{8,3},{9,0},... | collective-permute-start | bytes 196616 | tf_op jit(solution)/shard_map/while/body/eval_jaxpr/ppermute | solution.py:52
  229.9 16.7 %collective-permute-start.10 = (bf16[32,8,2,64]{3,1,2,0:T(8,128)(2,1)S(1)}, bf16[32,8,2,64]{3,1,2,0:T(8,128)(2,1)S(1)}, u32[]{:S(2)}, u32[]{:S(2)}) collective-permute-start(bf16[32,8,2,64]{3,1,2,0:T(8,128)(2,1)S(1)} %bitcast.252), channel_id=1, source_target_pairs={{0,10},{1,11},{2,8},{3,9},{4,14},{5,15},{6,12},{7,13},{8,2},{9,3},... | collective-permute-start | bytes 196616 | tf_op jit(solution)/shard_map/while/body/eval_jaxpr/ppermute | solution.py:52
  284.0 18.6 %collective-permute-start.7 = (bf16[32,8,2,64]{3,1,2,0:T(8,128)(2,1)S(1)}, bf16[32,8,2,64]{3,1,2,0:T(8,128)(2,1)S(1)}, u32[]{:S(2)}, u32[]{:S(2)}) collective-permute-start(bf16[32,8,2,64]{3,1,2,0:T(8,128)(2,1)S(1)} %bitcast.249), channel_id=1, source_target_pairs={{0,7},{1,4},{2,5},{3,6},{4,11},{5,8},{6,9},{7,10},{8,15},{9,12},{1... | collective-permute-start | bytes 196616 | tf_op jit(solution)/shard_map/while/body/eval_jaxpr/ppermute | solution.py:52
  287.1 16.2 %collective-permute-start.8 = (bf16[32,8,2,64]{3,1,2,0:T(8,128)(2,1)S(1)}, bf16[32,8,2,64]{3,1,2,0:T(8,128)(2,1)S(1)}, u32[]{:S(2)}, u32[]{:S(2)}) collective-permute-start(bf16[32,8,2,64]{3,1,2,0:T(8,128)(2,1)S(1)} %bitcast.250), channel_id=1, source_target_pairs={{0,8},{1,9},{2,10},{3,11},{4,12},{5,13},{6,14},{7,15},{8,0},{9,1},... | collective-permute-start | bytes 196616 | tf_op jit(solution)/shard_map/while/body/eval_jaxpr/ppermute | solution.py:52
  292.4 15.9 %collective-permute-start.10 = (bf16[32,8,2,64]{3,1,2,0:T(8,128)(2,1)S(1)}, bf16[32,8,2,64]{3,1,2,0:T(8,128)(2,1)S(1)}, u32[]{:S(2)}, u32[]{:S(2)}) collective-permute-start(bf16[32,8,2,64]{3,1,2,0:T(8,128)(2,1)S(1)} %bitcast.252), channel_id=1, source_target_pairs={{0,10},{1,11},{2,8},{3,9},{4,14},{5,15},{6,12},{7,13},{8,2},{9,3},... | collective-permute-start | bytes 196616 | tf_op jit(solution)/shard_map/while/body/eval_jaxpr/ppermute | solution.py:52
  347.3 16.6 %collective-permute-start.9 = (bf16[32,8,2,64]{3,1,2,0:T(8,128)(2,1)S(1)}, bf16[32,8,2,64]{3,1,2,0:T(8,128)(2,1)S(1)}, u32[]{:S(2)}, u32[]{:S(2)}) collective-permute-start(bf16[32,8,2,64]{3,1,2,0:T(8,128)(2,1)S(1)} %bitcast.251), channel_id=1, source_target_pairs={{0,9},{1,10},{2,11},{3,8},{4,13},{5,14},{6,15},{7,12},{8,1},{9,2},... | collective-permute-start | bytes 196616 | tf_op jit(solution)/shard_map/while/body/eval_jaxpr/ppermute | solution.py:52
  525.2 19.2 %collective-permute-start.26 = (bf16[32,8,2,64]{3,1,2,0:T(8,128)(2,1)S(1)}, bf16[32,8,2,64]{3,1,2,0:T(8,128)(2,1)S(1)}, u32[]{:S(2)}, u32[]{:S(2)}) collective-permute-start(bf16[32,8,2,64]{3,1,2,0:T(8,128)(2,1)S(1)} %bitcast.267), channel_id=1, source_target_pairs={{0,10},{1,11},{2,8},{3,9},{4,14},{5,15},{6,12},{7,13},{8,2},{9,3},... | collective-permute-start | bytes 196616 | tf_op jit(solution)/shard_map/while/body/eval_jaxpr/ppermute | solution.py:52
  529.0 16.1 %collective-permute-start.27 = (bf16[32,8,2,64]{3,1,2,0:T(8,128)(2,1)S(1)}, bf16[32,8,2,64]{3,1,2,0:T(8,128)(2,1)S(1)}, u32[]{:S(2)}, u32[]{:S(2)}) collective-permute-start(bf16[32,8,2,64]{3,1,2,0:T(8,128)(2,1)S(1)} %bitcast.268), channel_id=1, source_target_pairs={{0,11},{1,8},{2,9},{3,10},{4,15},{5,12},{6,13},{7,14},{8,3},{9,0},... | collective-permute-start | bytes 196616 | tf_op jit(solution)/shard_map/while/body/eval_jaxpr/ppermute | solution.py:52
  642.1 17.9 %collective-permute-start.26 = (bf16[32,8,2,64]{3,1,2,0:T(8,128)(2,1)S(1)}, bf16[32,8,2,64]{3,1,2,0:T(8,128)(2,1)S(1)}, u32[]{:S(2)}, u32[]{:S(2)}) collective-permute-start(bf16[32,8,2,64]{3,1,2,0:T(8,128)(2,1)S(1)} %bitcast.267), channel_id=1, source_target_pairs={{0,10},{1,11},{2,8},{3,9},{4,14},{5,15},{6,12},{7,13},{8,2},{9,3},... | collective-permute-start | bytes 196616 | tf_op jit(solution)/shard_map/while/body/eval_jaxpr/ppermute | solution.py:52
  645.3 18.4 %collective-permute-start.27 = (bf16[32,8,2,64]{3,1,2,0:T(8,128)(2,1)S(1)}, bf16[32,8,2,64]{3,1,2,0:T(8,128)(2,1)S(1)}, u32[]{:S(2)}, u32[]{:S(2)}) collective-permute-start(bf16[32,8,2,64]{3,1,2,0:T(8,128)(2,1)S(1)} %bitcast.268), channel_id=1, source_target_pairs={{0,11},{1,8},{2,9},{3,10},{4,15},{5,12},{6,13},{7,14},{8,3},{9,0},... | collective-permute-start | bytes 196616 | tf_op jit(solution)/shard_map/while/body/eval_jaxpr/ppermute | solution.py:52
  701.0 19.0 %collective-permute-start.26 = (bf16[32,8,2,64]{3,1,2,0:T(8,128)(2,1)S(1)}, bf16[32,8,2,64]{3,1,2,0:T(8,128)(2,1)S(1)}, u32[]{:S(2)}, u32[]{:S(2)}) collective-permute-start(bf16[32,8,2,64]{3,1,2,0:T(8,128)(2,1)S(1)} %bitcast.267), channel_id=1, source_target_pairs={{0,10},{1,11},{2,8},{3,9},{4,14},{5,15},{6,12},{7,13},{8,2},{9,3},... | collective-permute-start | bytes 196616 | tf_op jit(solution)/shard_map/while/body/eval_jaxpr/ppermute | solution.py:52
  751.7 20.4 %collective-permute-start.23 = (bf16[32,8,2,64]{3,1,2,0:T(8,128)(2,1)S(1)}, bf16[32,8,2,64]{3,1,2,0:T(8,128)(2,1)S(1)}, u32[]{:S(2)}, u32[]{:S(2)}) collective-permute-start(bf16[32,8,2,64]{3,1,2,0:T(8,128)(2,1)S(1)} %bitcast.264), channel_id=1, source_target_pairs={{0,7},{1,4},{2,5},{3,6},{4,11},{5,8},{6,9},{7,10},{8,15},{9,12},{1... | collective-permute-start | bytes 196616 | tf_op jit(solution)/shard_map/while/body/eval_jaxpr/ppermute | solution.py:52
  755.2 17.6 %collective-permute-start.24 = (bf16[32,8,2,64]{3,1,2,0:T(8,128)(2,1)S(1)}, bf16[32,8,2,64]{3,1,2,0:T(8,128)(2,1)S(1)}, u32[]{:S(2)}, u32[]{:S(2)}) collective-permute-start(bf16[32,8,2,64]{3,1,2,0:T(8,128)(2,1)S(1)} %bitcast.265), channel_id=1, source_target_pairs={{0,8},{1,9},{2,10},{3,11},{4,12},{5,13},{6,14},{7,15},{8,0},{9,1},... | collective-permute-start | bytes 196616 | tf_op jit(solution)/shard_map/while/body/eval_jaxpr/ppermute | solution.py:52
  819.9 18.0 %collective-permute-start.26 = (bf16[32,8,2,64]{3,1,2,0:T(8,128)(2,1)S(1)}, bf16[32,8,2,64]{3,1,2,0:T(8,128)(2,1)S(1)}, u32[]{:S(2)}, u32[]{:S(2)}) collective-permute-start(bf16[32,8,2,64]{3,1,2,0:T(8,128)(2,1)S(1)} %bitcast.267), channel_id=1, source_target_pairs={{0,10},{1,11},{2,8},{3,9},{4,14},{5,15},{6,12},{7,13},{8,2},{9,3},... | collective-permute-start | bytes 196616 | tf_op jit(solution)/shard_map/while/body/eval_jaxpr/ppermute | solution.py:52
  870.1 16.2 %collective-permute-start.23 = (bf16[32,8,2,64]{3,1,2,0:T(8,128)(2,1)S(1)}, bf16[32,8,2,64]{3,1,2,0:T(8,128)(2,1)S(1)}, u32[]{:S(2)}, u32[]{:S(2)}) collective-permute-start(bf16[32,8,2,64]{3,1,2,0:T(8,128)(2,1)S(1)} %bitcast.264), channel_id=1, source_target_pairs={{0,7},{1,4},{2,5},{3,6},{4,11},{5,8},{6,9},{7,10},{8,15},{9,12},{1... | collective-permute-start | bytes 196616 | tf_op jit(solution)/shard_map/while/body/eval_jaxpr/ppermute | solution.py:52
  923.8 18.0 %all-to-all-start = ((f32[128,1,288]{2,1,0:T(1,128)}), f32[128,1,288]{2,1,0:T(1,128)S(1)}, u32[]{:S(2)}, u32[]{:S(2)}) async-start(f32[128,1,288]{2,1,0:T(1,128)} %reshape.447), calls=%async_computation | async-start | bytes 393216 | tf_op jit(solution)/shard_map/all_to_all | solution.py:100
  (250 other events, 2833.2 us)

commit v3 on v1

--- a/solution.py
+++ b/solution.py
@@ -31,11 +31,14 @@
 
     def apply_layer(incoming):
         local_blocks = incoming.reshape(vec_count, 2, block_rows, block_cells).transpose(2, 0, 1, 3)
-        gathered = lax.all_gather(local_blocks, "plane", axis=0, tiled=True)
+        local_blocks = local_blocks.reshape(block_rows, vec_count, 2 * block_cells)
+        copies = jnp.broadcast_to(local_blocks[None], (plane_count,) + local_blocks.shape)
+        gathered = lax.all_to_all(copies, "plane", 0, 0, tiled=True)
+        gathered = gathered.reshape(plane_count * block_rows, vec_count, 2 * block_cells)
         chosen = jnp.take(gathered, pattern_flat, axis=0)
-        chosen = chosen.reshape(block_rows, -1, vec_count, 2, block_cells)
-        x_re = chosen[:, :, :, 0]
-        x_im = chosen[:, :, :, 1]
+        chosen = chosen.reshape(block_rows, -1, vec_count, 2 * block_cells)
+        x_re = chosen[..., :block_cells]
+        x_im = chosen[..., block_cells:]
         expanded = jnp.stack(
             [jnp.concatenate([x_re, -x_im], axis=-1), jnp.concatenate([x_im, x_re], axis=-1)],
             axis=3,

time: 991 us -> 663 us (0.67)
  waiting for transfers between devices: 666 us -> 265 us
  starting transfers between devices: 65 us -> 131 us
  matrix products: 34 us -> 84.9 us
  local copies, waits for them, and re-layouts: 134 us -> 98.2 us
  between operations: 14.1 us -> 1.04 us
    all_gather x15 -> x0, waiting for transfers between devices: 625 us -> none  [apply_layer(): gathered = lax.all_gather(local_blocks, 'plane', axis=0, tiled=True)]
    all_to_all x0 -> x15, waiting for transfers between devices: none -> 192 us  [apply_layer(): gathered = lax.all_to_all(copies, 'plane', 0, 0, tiled=True)]
    all_to_all x0 -> x15, starting transfers between devices: none -> 59.8 us  [apply_layer(): gathered = lax.all_to_all(copies, 'plane', 0, 0, tiled=True)]
    dot_general x15, matrix products: 34 us -> 84.9 us  [apply_layer(): jnp.einsum('rkic,rkvwc->vwri', factor, expanded, preferred_element_type=j...]
    ppermute x14, waiting for transfers between devices: 30.8 us -> 63 us  [passed_along(): lax.ppermute(value, axis, [(source, source + steps) for source in range(f...]
    while x56 -> x0, local copies, waits for them, and re-layouts: 24.8 us -> none
    broadcast_in_dim x0 -> x30, local copies, waits for them, and re-layouts: none -> 19.3 us  [apply_layer(): jnp.broadcast_to(local_blocks[None], (plane_count,) + local_blocks.shape)]
    gather x15, local copies, waits for them, and re-layouts: 41.6 us -> 27 us  [apply_layer(): chosen = jnp.take(gathered, pattern_flat, axis=0)]
  transfers between devices with their start and end apart: 30 -> 30, of which waited for: 30 -> 30; matrix products, arithmetic and copies ran while one was open for 3% -> 0% of each run, Pallas kernels for 0% -> 0%
where the time goes in v3:
time: 663 us; the launch traced here: 660 us
  waiting for transfers between devices  265 us (40%)
  starting transfers between devices  131 us (20%)
  local copies, waits for them, and re-layouts  98.2 us (15%)
  matrix products  84.9 us (13%)
  other arithmetic  78.4 us (12%)
    all_to_all x15, waiting for transfers between devices, apply_layer(): gathered = lax.all_to_all(copies, 'plane', 0, 0, tiled=True)  192 us
    dot_general x15, matrix products, apply_layer(): jnp.einsum('rkic,rkvwc->vwri', factor, expanded, preferred_element_type=j...  84.9 us
    ppermute x14, waiting for transfers between devices, passed_along(): lax.ppermute(value, axis, [(source, source + steps) for source in range(f...  63 us
    ppermute x14, starting transfers between devices, passed_along(): lax.ppermute(value, axis, [(source, source + steps) for source in range(f...  62.3 us
    all_to_all x15, starting transfers between devices, apply_layer(): gathered = lax.all_to_all(copies, 'plane', 0, 0, tiled=True)  59.8 us
    gather x15, local copies, waits for them, and re-layouts, apply_layer(): chosen = jnp.take(gathered, pattern_flat, axis=0)  27 us
    select_n x30, other arithmetic, apply_layer(): chosen = jnp.take(gathered, pattern_flat, axis=0)  26.4 us
    scatter-add x1, other arithmetic, shards(): jax.ops.segment_sum(received[:, :vec_count], target, num_segments=PATCH_DEV)  22.8 us
  transfers between devices with their start and end apart: 30, of which 30 were waited for; matrix products, arithmetic and copies ran while one was open for 0% of the time, Pallas kernels for 0%

profile of v3, /device:TPU:1, one launch (start us, length us, event | category | flops | bytes accessed | tf_op | source)
XLA Modules:
  0.0 660.4 jit_solution(7788859735526987518)
XLA Ops:
  7.0 16.8 %gather_fusion.3 = s32[2048]{0:T(1024)S(1)} fusion(s32[2048,128]{0,1:T(8,128)S(1)} %bitcast.202, s32[2048]{0:T(1024)S(1)} %bitcast.199), kind=kCustom, calls=%fused_computation.4 | custom fusion | bytes 32768 | tf_op jit(solution)/shard_map/jit(take_along_axis)/gather | solution.py:73
  40.9 15.4 %all-to-all-done.2 = bf16[16,32,8,128]{3,2,1,0:T(8,128)(2,1)S(1)} async-done(((bf16[16,32,8,128]{3,2,1,0:T(8,128)(2,1)}), bf16[16,32,8,128]{3,2,1,0:T(8,128)(2,1)S(1)}, u32[]{:S(2)}, u32[]{:S(2)}) %all-to-all-start.2) | async-done | bytes 1048608 | tf_op jit(solution)/shard_map/all_to_all | solution.py:36
  67.4 265.3 %while.20 = (s32[]{:T(128)}, bf16[8,2,2048]{2,0,1:T(8,128)(2,1)S(1)}, f32[1,2048]{1,0:T(1,128)S(1)}, f32[8,2,2048]{2,0,1:T(8,128)S(1)}, s32[512]{0:T(512)S(1)}, /*index=5*/bf16[32,16,64,128]{3,2,1,0:T(8,128)(2,1)}, s32[]{:T(128)}) while((s32[]{:T(128)}, bf16[8,2,2048]{2,0,1:T(8,128)(2,1)S(1)}, f32[1,2048]{1,0:T(1,128)S(1)}, ...), condition=%wide.region_1.3_spmd, body=%wide.region_0.0_spmd.sunk | while | flops 140416512 | bytes 26500244 | solution.py:57
  80.7 15.4 %all-to-all-done = bf16[16,32,8,128]{3,2,1,0:T(8,128)(2,1)S(1)} async-done(((bf16[16,32,8,128]{3,2,1,0:T(8,128)(2,1)}), bf16[16,32,8,128]{3,2,1,0:T(8,128)(2,1)S(1)}, u32[]{:S(2)}, u32[]{:S(2)}) %all-to-all-start) | async-done | bytes 1048608 | tf_op jit(solution)/shard_map/while/body/eval_jaxpr/all_to_all | solution.py:36
  120.5 13.1 %all-to-all-done = bf16[16,32,8,128]{3,2,1,0:T(8,128)(2,1)S(1)} async-done(((bf16[16,32,8,128]{3,2,1,0:T(8,128)(2,1)}), bf16[16,32,8,128]{3,2,1,0:T(8,128)(2,1)S(1)}, u32[]{:S(2)}, u32[]{:S(2)}) %all-to-all-start) | async-done | bytes 1048608 | tf_op jit(solution)/shard_map/while/body/eval_jaxpr/all_to_all | solution.py:36
  159.6 11.8 %all-to-all-done = bf16[16,32,8,128]{3,2,1,0:T(8,128)(2,1)S(1)} async-done(((bf16[16,32,8,128]{3,2,1,0:T(8,128)(2,1)}), bf16[16,32,8,128]{3,2,1,0:T(8,128)(2,1)S(1)}, u32[]{:S(2)}, u32[]{:S(2)}) %all-to-all-start) | async-done | bytes 1048608 | tf_op jit(solution)/shard_map/while/body/eval_jaxpr/all_to_all | solution.py:36
  196.7 12.3 %all-to-all-done = bf16[16,32,8,128]{3,2,1,0:T(8,128)(2,1)S(1)} async-done(((bf16[16,32,8,128]{3,2,1,0:T(8,128)(2,1)}), bf16[16,32,8,128]{3,2,1,0:T(8,128)(2,1)S(1)}, u32[]{:S(2)}, u32[]{:S(2)}) %all-to-all-start) | async-done | bytes 1048608 | tf_op jit(solution)/shard_map/while/body/eval_jaxpr/all_to_all | solution.py:36
  233.8 12.7 %all-to-all-done = bf16[16,32,8,128]{3,2,1,0:T(8,128)(2,1)S(1)} async-done(((bf16[16,32,8,128]{3,2,1,0:T(8,128)(2,1)}), bf16[16,32,8,128]{3,2,1,0:T(8,128)(2,1)S(1)}, u32[]{:S(2)}, u32[]{:S(2)}) %all-to-all-start) | async-done | bytes 1048608 | tf_op jit(solution)/shard_map/while/body/eval_jaxpr/all_to_all | solution.py:36
  270.9 13.1 %all-to-all-done = bf16[16,32,8,128]{3,2,1,0:T(8,128)(2,1)S(1)} async-done(((bf16[16,32,8,128]{3,2,1,0:T(8,128)(2,1)}), bf16[16,32,8,128]{3,2,1,0:T(8,128)(2,1)S(1)}, u32[]{:S(2)}, u32[]{:S(2)}) %all-to-all-start) | async-done | bytes 1048608 | tf_op jit(solution)/shard_map/while/body/eval_jaxpr/all_to_all | solution.py:36
  308.0 13.7 %all-to-all-done = bf16[16,32,8,128]{3,2,1,0:T(8,128)(2,1)S(1)} async-done(((bf16[16,32,8,128]{3,2,1,0:T(8,128)(2,1)}), bf16[16,32,8,128]{3,2,1,0:T(8,128)(2,1)S(1)}, u32[]{:S(2)}, u32[]{:S(2)}) %all-to-all-start) | async-done | bytes 1048608 | tf_op jit(solution)/shard_map/while/body/eval_jaxpr/all_to_all | solution.py:36
  332.7 267.9 %while.21 = (s32[]{:T(128)}, bf16[8,2,2048]{2,0,1:T(8,128)(2,1)S(1)}, bf16[8,2,2048]{2,0,1:T(8,128)(2,1)S(1)}, f32[1,2048]{1,0:T(1,128)S(1)}, s32[512]{0:T(512)S...) while((s32[]{:T(128)}, bf16[8,2,2048]{2,0,1:T(8,128)(2,1)S(1)}, bf16[8,2,2048]{2,0,1:T(8,128)(2,1)S(1)}, ...), condition=%wide.region_3.5_spmd, body=%wide.region_2.4_spmd.sunk | while | flops 140449280 | bytes 26958996 | solution.py:64
  345.9 13.3 %all-to-all-done.1 = bf16[16,32,8,128]{3,2,1,0:T(8,128)(2,1)S(1)} async-done(((bf16[16,32,8,128]{3,2,1,0:T(8,128)(2,1)}), bf16[16,32,8,128]{3,2,1,0:T(8,128)(2,1)S(1)}, u32[]{:S(2)}, u32[]{:S(2)}) %all-to-all-start.1) | async-done | bytes 1048608 | tf_op jit(solution)/shard_map/while/body/eval_jaxpr/all_to_all | solution.py:36
  384.2 12.5 %all-to-all-done.1 = bf16[16,32,8,128]{3,2,1,0:T(8,128)(2,1)S(1)} async-done(((bf16[16,32,8,128]{3,2,1,0:T(8,128)(2,1)}), bf16[16,32,8,128]{3,2,1,0:T(8,128)(2,1)S(1)}, u32[]{:S(2)}, u32[]{:S(2)}) %all-to-all-start.1) | async-done | bytes 1048608 | tf_op jit(solution)/shard_map/while/body/eval_jaxpr/all_to_all | solution.py:36
  422.8 11.7 %all-to-all-done.1 = bf16[16,32,8,128]{3,2,1,0:T(8,128)(2,1)S(1)} async-done(((bf16[16,32,8,128]{3,2,1,0:T(8,128)(2,1)}), bf16[16,32,8,128]{3,2,1,0:T(8,128)(2,1)S(1)}, u32[]{:S(2)}, u32[]{:S(2)}) %all-to-all-start.1) | async-done | bytes 1048608 | tf_op jit(solution)/shard_map/while/body/eval_jaxpr/all_to_all | solution.py:36
  447.5 9.0 %collective-permute-done.1 = bf16[8,2,2048]{2,0,1:T(8,128)(2,1)S(1)} collective-permute-done((bf16[8,2,2048]{2,0,1:T(8,128)(2,1)S(1)}, bf16[8,2,2048]{2,0,1:T(8,128)(2,1)S(1)}, u32[]{:S(2)}, u32[]{:S(2)}) %collective-permute-start.1) | collective-permute-done | bytes 65568 | tf_op jit(solution)/shard_map/while/body/eval_jaxpr/ppermute | solution.py:13
  461.8 11.7 %all-to-all-done.1 = bf16[16,32,8,128]{3,2,1,0:T(8,128)(2,1)S(1)} async-done(((bf16[16,32,8,128]{3,2,1,0:T(8,128)(2,1)}), bf16[16,32,8,128]{3,2,1,0:T(8,128)(2,1)S(1)}, u32[]{:S(2)}, u32[]{:S(2)}) %all-to-all-start.1) | async-done | bytes 1048608 | tf_op jit(solution)/shard_map/while/body/eval_jaxpr/all_to_all | solution.py:36
  486.5 10.1 %collective-permute-done.1 = bf16[8,2,2048]{2,0,1:T(8,128)(2,1)S(1)} collective-permute-done((bf16[8,2,2048]{2,0,1:T(8,128)(2,1)S(1)}, bf16[8,2,2048]{2,0,1:T(8,128)(2,1)S(1)}, u32[]{:S(2)}, u32[]{:S(2)}) %collective-permute-start.1) | collective-permute-done | bytes 65568 | tf_op jit(solution)/shard_map/while/body/eval_jaxpr/ppermute | solution.py:13
  502.0 11.7 %all-to-all-done.1 = bf16[16,32,8,128]{3,2,1,0:T(8,128)(2,1)S(1)} async-done(((bf16[16,32,8,128]{3,2,1,0:T(8,128)(2,1)}), bf16[16,32,8,128]{3,2,1,0:T(8,128)(2,1)S(1)}, u32[]{:S(2)}, u32[]{:S(2)}) %all-to-all-start.1) | async-done | bytes 1048608 | tf_op jit(solution)/shard_map/while/body/eval_jaxpr/all_to_all | solution.py:36
  539.9 11.7 %all-to-all-done.1 = bf16[16,32,8,128]{3,2,1,0:T(8,128)(2,1)S(1)} async-done(((bf16[16,32,8,128]{3,2,1,0:T(8,128)(2,1)}), bf16[16,32,8,128]{3,2,1,0:T(8,128)(2,1)S(1)}, u32[]{:S(2)}, u32[]{:S(2)}) %all-to-all-start.1) | async-done | bytes 1048608 | tf_op jit(solution)/shard_map/while/body/eval_jaxpr/all_to_all | solution.py:36
  577.9 11.7 %all-to-all-done.1 = bf16[16,32,8,128]{3,2,1,0:T(8,128)(2,1)S(1)} async-done(((bf16[16,32,8,128]{3,2,1,0:T(8,128)(2,1)}), bf16[16,32,8,128]{3,2,1,0:T(8,128)(2,1)S(1)}, u32[]{:S(2)}, u32[]{:S(2)}) %all-to-all-start.1) | async-done | bytes 1048608 | tf_op jit(solution)/shard_map/while/body/eval_jaxpr/all_to_all | solution.py:36
  601.2 10.8 %gather_fusion.2 = f32[4096,9]{1,0:T(8,128)S(1)} fusion(f32[2049,9]{1,0:T(8,128)S(1)} %concatenate.29, s32[4096]{0:T(1024)S(1)} %fusion.58), kind=kCustom, calls=%fused_computation.3 | custom fusion | bytes 311296 | tf_op jit(solution)/shard_map/jit(_take)/gather | solution.py:83
  614.1 9.3 %all-to-all-start.3 = ((f32[128,1,288]{2,1,0:T(1,128)}), f32[128,1,288]{2,1,0:T(1,128)S(1)}, u32[]{:S(2)}, u32[]{:S(2)}) async-start(f32[128,1,288]{2,1,0:T(1,128)} %reshape.462), calls=%async_computation.3 | async-start | bytes 393216 | tf_op jit(solution)/shard_map/all_to_all | solution.py:84
  624.1 9.9 %all-to-all-done.3 = f32[128,1,288]{2,1,0:T(1,128)S(1)} async-done(((f32[128,1,288]{2,1,0:T(1,128)}), f32[128,1,288]{2,1,0:T(1,128)S(1)}, u32[]{:S(2)}, u32[]{:S(2)}) %all-to-all-start.3) | async-done | bytes 147488 | tf_op jit(solution)/shard_map/all_to_all | solution.py:84
  637.0 22.8 %scatter_custom_fusion.1 = f32[128,8]{1,0:T(8,128)S(1)} fusion(s32[4096]{0:T(1024)S(1)} %bitcast.218, f32[4096,8]{1,0:T(8,128)S(1)} %copy.65, f32[]{:T(128)} %constant.77.clone.1), kind=kCustom, calls=%fused_computation.73 | custom fusion | flops 32768 | bytes 4100 | tf_op jit(solution)/shard_map/scatter-add | solution.py:87
  (325 shorter events, 377.1 us)
Async XLA Ops:
  33.2 23.1 %all-to-all-start.2 = ((bf16[16,32,8,128]{3,2,1,0:T(8,128)(2,1)}), bf16[16,32,8,128]{3,2,1,0:T(8,128)(2,1)S(1)}, u32[]{:S(2)}, u32[]{:S(2)}) async-start(bf16[16,32,8,128]{3,2,1,0:T(8,128)(2,1)} %broadcast_in_dim.64), calls=%async_computation.2 | async-start | bytes 2097152 | tf_op jit(solution)/shard_map/all_to_all | solution.py:36
  77.0 19.1 %all-to-all-start = ((bf16[16,32,8,128]{3,2,1,0:T(8,128)(2,1)}), bf16[16,32,8,128]{3,2,1,0:T(8,128)(2,1)S(1)}, u32[]{:S(2)}, u32[]{:S(2)}) async-start(bf16[16,32,8,128]{3,2,1,0:T(8,128)(2,1)} %broadcast_in_dim.114), calls=%async_computation | async-start | bytes 2097152 | tf_op jit(solution)/shard_map/while/body/eval_jaxpr/all_to_all | solution.py:36
  116.8 16.8 %all-to-all-start = ((bf16[16,32,8,128]{3,2,1,0:T(8,128)(2,1)}), bf16[16,32,8,128]{3,2,1,0:T(8,128)(2,1)S(1)}, u32[]{:S(2)}, u32[]{:S(2)}) async-start(bf16[16,32,8,128]{3,2,1,0:T(8,128)(2,1)} %broadcast_in_dim.114), calls=%async_computation | async-start | bytes 2097152 | tf_op jit(solution)/shard_map/while/body/eval_jaxpr/all_to_all | solution.py:36
  144.7 9.6 %collective-permute-start = (bf16[8,2,2048]{2,0,1:T(8,128)(2,1)S(1)}, bf16[8,2,2048]{2,0,1:T(8,128)(2,1)S(1)}, u32[]{:S(2)}, u32[]{:S(2)}) collective-permute-start(bf16[8,2,2048]{2,0,1:T(8,128)(2,1)S(1)} %get-tuple-element.236), channel_id=1, source_target_pairs={{0,16},{16,32},{32,48},{48,64},{64,80},{80,96},{96,112},{1,17},{17... | collective-permute-start | bytes 196616 | tf_op jit(solution)/shard_map/while/body/eval_jaxpr/ppermute | solution.py:13
  155.9 15.5 %all-to-all-start = ((bf16[16,32,8,128]{3,2,1,0:T(8,128)(2,1)}), bf16[16,32,8,128]{3,2,1,0:T(8,128)(2,1)S(1)}, u32[]{:S(2)}, u32[]{:S(2)}) async-start(bf16[16,32,8,128]{3,2,1,0:T(8,128)(2,1)} %broadcast_in_dim.114), calls=%async_computation | async-start | bytes 2097152 | tf_op jit(solution)/shard_map/while/body/eval_jaxpr/all_to_all | solution.py:36
  182.5 8.9 %collective-permute-start = (bf16[8,2,2048]{2,0,1:T(8,128)(2,1)S(1)}, bf16[8,2,2048]{2,0,1:T(8,128)(2,1)S(1)}, u32[]{:S(2)}, u32[]{:S(2)}) collective-permute-start(bf16[8,2,2048]{2,0,1:T(8,128)(2,1)S(1)} %get-tuple-element.236), channel_id=1, source_target_pairs={{0,16},{16,32},{32,48},{48,64},{64,80},{80,96},{96,112},{1,17},{17... | collective-permute-start | bytes 196616 | tf_op jit(solution)/shard_map/while/body/eval_jaxpr/ppermute | solution.py:13
  193.0 16.0 %all-to-all-start = ((bf16[16,32,8,128]{3,2,1,0:T(8,128)(2,1)}), bf16[16,32,8,128]{3,2,1,0:T(8,128)(2,1)S(1)}, u32[]{:S(2)}, u32[]{:S(2)}) async-start(bf16[16,32,8,128]{3,2,1,0:T(8,128)(2,1)} %broadcast_in_dim.114), calls=%async_computation | async-start | bytes 2097152 | tf_op jit(solution)/shard_map/while/body/eval_jaxpr/all_to_all | solution.py:36
  230.1 16.4 %all-to-all-start = ((bf16[16,32,8,128]{3,2,1,0:T(8,128)(2,1)}), bf16[16,32,8,128]{3,2,1,0:T(8,128)(2,1)S(1)}, u32[]{:S(2)}, u32[]{:S(2)}) async-start(bf16[16,32,8,128]{3,2,1,0:T(8,128)(2,1)} %broadcast_in_dim.114), calls=%async_computation | async-start | bytes 2097152 | tf_op jit(solution)/shard_map/while/body/eval_jaxpr/all_to_all | solution.py:36
  267.2 16.8 %all-to-all-start = ((bf16[16,32,8,128]{3,2,1,0:T(8,128)(2,1)}), bf16[16,32,8,128]{3,2,1,0:T(8,128)(2,1)S(1)}, u32[]{:S(2)}, u32[]{:S(2)}) async-start(bf16[16,32,8,128]{3,2,1,0:T(8,128)(2,1)} %broadcast_in_dim.114), calls=%async_computation | async-start | bytes 2097152 | tf_op jit(solution)/shard_map/while/body/eval_jaxpr/all_to_all | solution.py:36
  304.3 17.4 %all-to-all-start = ((bf16[16,32,8,128]{3,2,1,0:T(8,128)(2,1)}), bf16[16,32,8,128]{3,2,1,0:T(8,128)(2,1)S(1)}, u32[]{:S(2)}, u32[]{:S(2)}) async-start(bf16[16,32,8,128]{3,2,1,0:T(8,128)(2,1)} %broadcast_in_dim.114), calls=%async_computation | async-start | bytes 2097152 | tf_op jit(solution)/shard_map/while/body/eval_jaxpr/all_to_all | solution.py:36
  342.2 17.0 %all-to-all-start.1 = ((bf16[16,32,8,128]{3,2,1,0:T(8,128)(2,1)}), bf16[16,32,8,128]{3,2,1,0:T(8,128)(2,1)S(1)}, u32[]{:S(2)}, u32[]{:S(2)}) async-start(bf16[16,32,8,128]{3,2,1,0:T(8,128)(2,1)} %broadcast_in_dim.118), calls=%async_computation.1 | async-start | bytes 2097152 | tf_op jit(solution)/shard_map/while/body/eval_jaxpr/all_to_all | solution.py:36
  370.4 8.6 %collective-permute-start.1 = (bf16[8,2,2048]{2,0,1:T(8,128)(2,1)S(1)}, bf16[8,2,2048]{2,0,1:T(8,128)(2,1)S(1)}, u32[]{:S(2)}, u32[]{:S(2)}) collective-permute-start(bf16[8,2,2048]{2,0,1:T(8,128)(2,1)S(1)} %multiply_convert_fusion.2), channel_id=1, source_target_pairs={{16,0},{32,16},{48,32},{64,48},{80,64},{96,80},{112,96},{17,1},{33... | collective-permute-start | bytes 196616 | tf_op jit(solution)/shard_map/while/body/eval_jaxpr/ppermute | solution.py:13
  380.5 16.2 %all-to-all-start.1 = ((bf16[16,32,8,128]{3,2,1,0:T(8,128)(2,1)}), bf16[16,32,8,128]{3,2,1,0:T(8,128)(2,1)S(1)}, u32[]{:S(2)}, u32[]{:S(2)}) async-start(bf16[16,32,8,128]{3,2,1,0:T(8,128)(2,1)} %broadcast_in_dim.118), calls=%async_computation.1 | async-start | bytes 2097152 | tf_op jit(solution)/shard_map/while/body/eval_jaxpr/all_to_all | solution.py:36
  407.8 9.6 %collective-permute-start.1 = (bf16[8,2,2048]{2,0,1:T(8,128)(2,1)S(1)}, bf16[8,2,2048]{2,0,1:T(8,128)(2,1)S(1)}, u32[]{:S(2)}, u32[]{:S(2)}) collective-permute-start(bf16[8,2,2048]{2,0,1:T(8,128)(2,1)S(1)} %multiply_convert_fusion.2), channel_id=1, source_target_pairs={{16,0},{32,16},{48,32},{64,48},{80,64},{96,80},{112,96},{17,1},{33... | collective-permute-start | bytes 196616 | tf_op jit(solution)/shard_map/while/body/eval_jaxpr/ppermute | solution.py:13
  419.1 15.4 %all-to-all-start.1 = ((bf16[16,32,8,128]{3,2,1,0:T(8,128)(2,1)}), bf16[16,32,8,128]{3,2,1,0:T(8,128)(2,1)S(1)}, u32[]{:S(2)}, u32[]{:S(2)}) async-start(bf16[16,32,8,128]{3,2,1,0:T(8,128)(2,1)} %broadcast_in_dim.118), calls=%async_computation.1 | async-start | bytes 2097152 | tf_op jit(solution)/shard_map/while/body/eval_jaxpr/all_to_all | solution.py:36
  445.6 10.9 %collective-permute-start.1 = (bf16[8,2,2048]{2,0,1:T(8,128)(2,1)S(1)}, bf16[8,2,2048]{2,0,1:T(8,128)(2,1)S(1)}, u32[]{:S(2)}, u32[]{:S(2)}) collective-permute-start(bf16[8,2,2048]{2,0,1:T(8,128)(2,1)S(1)} %multiply_convert_fusion.2), channel_id=1, source_target_pairs={{16,0},{32,16},{48,32},{64,48},{80,64},{96,80},{112,96},{17,1},{33... | collective-permute-start | bytes 196616 | tf_op jit(solution)/shard_map/while/body/eval_jaxpr/ppermute | solution.py:13
  458.1 15.4 %all-to-all-start.1 = ((bf16[16,32,8,128]{3,2,1,0:T(8,128)(2,1)}), bf16[16,32,8,128]{3,2,1,0:T(8,128)(2,1)S(1)}, u32[]{:S(2)}, u32[]{:S(2)}) async-start(bf16[16,32,8,128]{3,2,1,0:T(8,128)(2,1)} %broadcast_in_dim.118), calls=%async_computation.1 | async-start | bytes 2097152 | tf_op jit(solution)/shard_map/while/body/eval_jaxpr/all_to_all | solution.py:36
  484.6 12.1 %collective-permute-start.1 = (bf16[8,2,2048]{2,0,1:T(8,128)(2,1)S(1)}, bf16[8,2,2048]{2,0,1:T(8,128)(2,1)S(1)}, u32[]{:S(2)}, u32[]{:S(2)}) collective-permute-start(bf16[8,2,2048]{2,0,1:T(8,128)(2,1)S(1)} %multiply_convert_fusion.2), channel_id=1, source_target_pairs={{16,0},{32,16},{48,32},{64,48},{80,64},{96,80},{112,96},{17,1},{33... | collective-permute-start | bytes 196616 | tf_op jit(solution)/shard_map/while/body/eval_jaxpr/ppermute | solution.py:13
  498.3 15.4 %all-to-all-start.1 = ((bf16[16,32,8,128]{3,2,1,0:T(8,128)(2,1)}), bf16[16,32,8,128]{3,2,1,0:T(8,128)(2,1)S(1)}, u32[]{:S(2)}, u32[]{:S(2)}) async-start(bf16[16,32,8,128]{3,2,1,0:T(8,128)(2,1)} %broadcast_in_dim.118), calls=%async_computation.1 | async-start | bytes 2097152 | tf_op jit(solution)/shard_map/while/body/eval_jaxpr/all_to_all | solution.py:36
  524.8 9.6 %collective-permute-start.1 = (bf16[8,2,2048]{2,0,1:T(8,128)(2,1)S(1)}, bf16[8,2,2048]{2,0,1:T(8,128)(2,1)S(1)}, u32[]{:S(2)}, u32[]{:S(2)}) collective-permute-start(bf16[8,2,2048]{2,0,1:T(8,128)(2,1)S(1)} %multiply_convert_fusion.2), channel_id=1, source_target_pairs={{16,0},{32,16},{48,32},{64,48},{80,64},{96,80},{112,96},{17,1},{33... | collective-permute-start | bytes 196616 | tf_op jit(solution)/shard_map/while/body/eval_jaxpr/ppermute | solution.py:13
  536.0 15.6 %all-to-all-start.1 = ((bf16[16,32,8,128]{3,2,1,0:T(8,128)(2,1)}), bf16[16,32,8,128]{3,2,1,0:T(8,128)(2,1)S(1)}, u32[]{:S(2)}, u32[]{:S(2)}) async-start(bf16[16,32,8,128]{3,2,1,0:T(8,128)(2,1)} %broadcast_in_dim.118), calls=%async_computation.1 | async-start | bytes 2097152 | tf_op jit(solution)/shard_map/while/body/eval_jaxpr/all_to_all | solution.py:36
  562.8 9.0 %collective-permute-start.1 = (bf16[8,2,2048]{2,0,1:T(8,128)(2,1)S(1)}, bf16[8,2,2048]{2,0,1:T(8,128)(2,1)S(1)}, u32[]{:S(2)}, u32[]{:S(2)}) collective-permute-start(bf16[8,2,2048]{2,0,1:T(8,128)(2,1)S(1)} %multiply_convert_fusion.2), channel_id=1, source_target_pairs={{16,0},{32,16},{48,32},{64,48},{80,64},{96,80},{112,96},{17,1},{33... | collective-permute-start | bytes 196616 | tf_op jit(solution)/shard_map/while/body/eval_jaxpr/ppermute | solution.py:13
  573.3 16.3 %all-to-all-start.1 = ((bf16[16,32,8,128]{3,2,1,0:T(8,128)(2,1)}), bf16[16,32,8,128]{3,2,1,0:T(8,128)(2,1)S(1)}, u32[]{:S(2)}, u32[]{:S(2)}) async-start(bf16[16,32,8,128]{3,2,1,0:T(8,128)(2,1)} %broadcast_in_dim.118), calls=%async_computation.1 | async-start | bytes 2097152 | tf_op jit(solution)/shard_map/while/body/eval_jaxpr/all_to_all | solution.py:36
  614.1 19.9 %all-to-all-start.3 = ((f32[128,1,288]{2,1,0:T(1,128)}), f32[128,1,288]{2,1,0:T(1,128)S(1)}, u32[]{:S(2)}, u32[]{:S(2)}) async-start(f32[128,1,288]{2,1,0:T(1,128)} %reshape.462), calls=%async_computation.3 | async-start | bytes 393216 | tf_op jit(solution)/shard_map/all_to_all | solution.py:84
  (9 other events, 337.9 us)

commit v4 on v3

--- a/solution.py
+++ b/solution.py
@@ -5,6 +5,7 @@
 
 PATCH_DEV = 128
 CAP = 32
+CHAINS = 2
 
 
 def passed_along(value, axis, steps):
@@ -30,13 +31,14 @@
     source = jnp.stack([real_part, imag_part], axis=1)
 
     def apply_layer(incoming):
-        local_blocks = incoming.reshape(vec_count, 2, block_rows, block_cells).transpose(2, 0, 1, 3)
-        local_blocks = local_blocks.reshape(block_rows, vec_count, 2 * block_cells)
+        count = incoming.shape[0]
+        local_blocks = incoming.reshape(count, 2, block_rows, block_cells).transpose(2, 0, 1, 3)
+        local_blocks = local_blocks.reshape(block_rows, count, 2 * block_cells)
         copies = jnp.broadcast_to(local_blocks[None], (plane_count,) + local_blocks.shape)
         gathered = lax.all_to_all(copies, "plane", 0, 0, tiled=True)
-        gathered = gathered.reshape(plane_count * block_rows, vec_count, 2 * block_cells)
+        gathered = gathered.reshape(plane_count * block_rows, count, 2 * block_cells)
         chosen = jnp.take(gathered, pattern_flat, axis=0)
-        chosen = chosen.reshape(block_rows, -1, vec_count, 2 * block_cells)
+        chosen = chosen.reshape(block_rows, -1, count, 2 * block_cells)
         x_re = chosen[..., :block_cells]
         x_im = chosen[..., block_cells:]
         expanded = jnp.stack(
@@ -46,20 +48,32 @@
         out = jnp.einsum(
             "rkic,rkvwc->vwri", factor, expanded, preferred_element_type=jnp.float32
         )
-        return out.reshape(vec_count, 2, block_rows * block_cells)
+        return out.reshape(count, 2, block_rows * block_cells)
+
+    chain = vec_count // CHAINS
+    spans = [slice(index * chain, (index + 1) * chain) for index in range(CHAINS)]
 
     def down_turn(turn_index, current):
-        arrived = passed_along(current, "depth", 1)
-        down_in = (source + coupler * arrived.astype(jnp.float32)).astype(jnp.bfloat16)
-        return apply_layer(down_in).astype(jnp.bfloat16)
+        outs = []
+        for span in spans:
+            arrived = passed_along(current[span], "depth", 1)
+            down_in = (source[span] + coupler * arrived.astype(jnp.float32)).astype(jnp.bfloat16)
+            outs.append(apply_layer(down_in).astype(jnp.bfloat16))
+        return jnp.concatenate(outs, axis=0)
 
-    first = apply_layer(source.astype(jnp.bfloat16)).astype(jnp.bfloat16)
+    source_bf16 = source.astype(jnp.bfloat16)
+    first = jnp.concatenate(
+        [apply_layer(source_bf16[span]).astype(jnp.bfloat16) for span in spans], axis=0
+    )
     swept = lax.fori_loop(0, depth_count - 1, down_turn, first)
 
     def up_turn(turn_index, current):
-        outgoing = (coupler * current.astype(jnp.float32)).astype(jnp.bfloat16)
-        arrived = passed_along(outgoing, "depth", -1)
-        return (swept.astype(jnp.float32) + apply_layer(arrived)).astype(jnp.bfloat16)
+        outs = []
+        for span in spans:
+            outgoing = (coupler * current[span].astype(jnp.float32)).astype(jnp.bfloat16)
+            arrived = passed_along(outgoing, "depth", -1)
+            outs.append((swept[span].astype(jnp.float32) + apply_layer(arrived)).astype(jnp.bfloat16))
+        return jnp.concatenate(outs, axis=0)
 
     precond = lax.fori_loop(0, depth_count - 1, up_turn, swept)
     product = precond.astype(jnp.float32) * toar_f32

time: 663 us -> 945 us (1.43)
  matrix products: 84.9 us -> 179 us
  starting transfers between devices: 131 us -> 224 us
  local copies, waits for them, and re-layouts: 98.2 us -> 149 us
  other arithmetic: 78.4 us -> 121 us
  waiting for transfers between devices: 265 us -> 242 us
  blocking collectives: 0 us -> 17.1 us
    dot_general x15 -> x30, matrix products: 84.9 us -> 179 us  [apply_layer(): jnp.einsum('rkic,rkvwc->vwri', factor, expanded, preferred_element_type=j...]
    all_to_all x15 -> x30, starting transfers between devices: 59.8 us -> 121 us  [apply_layer(): gathered = lax.all_to_all(copies, 'plane', 0, 0, tiled=True)]
    ppermute x14 -> x28, starting transfers between devices: 62.3 us -> 103 us  [passed_along(): lax.ppermute(value, axis, [(source, source + steps) for source in range(f...]
    gather x15 -> x30, local copies, waits for them, and re-layouts: 27 us -> 62.5 us  [apply_layer(): chosen = jnp.take(gathered, pattern_flat, axis=0)]
    ppermute x14 -> x28, waiting for transfers between devices: 63 us -> 36.9 us  [passed_along(): lax.ppermute(value, axis, [(source, source + steps) for source in range(f...]
    another operation x15 -> x30, other arithmetic: 17.3 us -> 42.7 us  [apply_layer(): jnp.stack([jnp.concatenate([x_re, -x_im], axis=-1), jnp.concatenate([x_im...]
    all_to_all x0 -> x1, blocking collectives: none -> 17.1 us  [shards(): received = lax.all_to_all(packed, ('depth', 'plane'), 0, 0, tiled=True)]
    broadcast_in_dim x30 -> x90, local copies, waits for them, and re-layouts: 19.3 us -> 34 us  [apply_layer(): jnp.broadcast_to(local_blocks[None], (plane_count,) + local_blocks.shape)]
  transfers between devices with their start and end apart: 30 -> 58, of which waited for: 30 -> 51; matrix products, arithmetic and copies ran while one was open for 0% -> 5% of each run, Pallas kernels for 0% -> 0%
where the time goes in v4:
time: 945 us; the launch traced here: 936 us
  waiting for transfers between devices  242 us (26%)
  starting transfers between devices  224 us (24%)
  matrix products  179 us (19%)
  local copies, waits for them, and re-layouts  149 us (16%)
  other arithmetic  121 us (13%)
  blocking collectives  17.1 us (2%)
    all_to_all x30, waiting for transfers between devices, apply_layer(): gathered = lax.all_to_all(copies, 'plane', 0, 0, tiled=True)  205 us
    dot_general x30, matrix products, apply_layer(): jnp.einsum('rkic,rkvwc->vwri', factor, expanded, preferred_element_type=j...  179 us
    all_to_all x30, starting transfers between devices, apply_layer(): gathered = lax.all_to_all(copies, 'plane', 0, 0, tiled=True)  121 us
    ppermute x28, starting transfers between devices, passed_along(): lax.ppermute(value, axis, [(source, source + steps) for source in range(f...  103 us
    gather x30, local copies, waits for them, and re-layouts, apply_layer(): chosen = jnp.take(gathered, pattern_flat, axis=0)  62.5 us
    another operation x30, other arithmetic, apply_layer(): jnp.stack([jnp.concatenate([x_re, -x_im], axis=-1), jnp.concatenate([x_im...  42.7 us
    ppermute x28, waiting for transfers between devices, passed_along(): lax.ppermute(value, axis, [(source, source + steps) for source in range(f...  36.9 us
    broadcast_in_dim x90, local copies, waits for them, and re-layouts, apply_layer(): jnp.broadcast_to(local_blocks[None], (plane_count,) + local_blocks.shape)  34 us
  transfers between devices with their start and end apart: 58, of which 51 were waited for; matrix products, arithmetic and copies ran while one was open for 5% of the time, Pallas kernels for 0%

profile of v4, /device:TPU:1, one launch (start us, length us, event | category | flops | bytes accessed | tf_op | source)
XLA Modules:
  0.0 935.9 jit_solution(1067317028440778619)
XLA Ops:
  6.4 16.8 %gather_fusion.5 = s32[2048]{0:T(1024)S(1)} fusion(s32[2048,128]{0,1:T(8,128)S(1)} %bitcast.311, s32[2048]{0:T(1024)S(1)} %bitcast.306), kind=kCustom, calls=%fused_computation.7 | custom fusion | bytes 32768 | tf_op jit(solution)/shard_map/jit(take_along_axis)/gather | solution.py:87
  24.3 7.6 all-to-all-start.4
  32.2 8.1 scatter_custom_fusion
  77.5 407.9 %while.20 = (s32[]{:T(128)}, bf16[8,2,2048]{2,1,0:T(2,128)(2,1)S(1)}, f32[8,2,2048]{2,1,0:T(2,128)S(1)}, f32[1,2048]{1,0:T(1,128)S(1)}, s32[512]{0:T(512)S(1)}, /*index=5*/bf16[32,16,64,128]{3,2,1,0:T(8,128)(2,1)}, s32[]{:T(128)}) while((s32[]{:T(128)}, bf16[8,2,2048]{2,1,0:T(2,128)(2,1)S(1)}, f32[8,2,2048]{2,1,0:T(2,128)S(1)}, ...), condition=%wide.region_1.3_spmd, body=%wide.region_0.0_spmd.sunk | while | flops 143595008 | bytes 35284188 | solution.py:68
  77.8 7.0 collective-permute-start
  93.2 10.2 %all-to-all-done = bf16[16,32,4,128]{3,2,1,0:T(4,128)(2,1)S(1)} async-done(((bf16[16,32,4,128]{3,2,1,0:T(4,128)(2,1)}), bf16[16,32,4,128]{3,2,1,0:T(4,128)(2,1)S(1)}, u32[]{:S(2)}, u32[]{:S(2)}) %all-to-all-start) | async-done | bytes 524320 | tf_op jit(solution)/shard_map/while/body/eval_jaxpr/all_to_all | solution.py:38
  110.6 6.8 all-to-all-done.1
  152.7 10.2 %all-to-all-done = bf16[16,32,4,128]{3,2,1,0:T(4,128)(2,1)S(1)} async-done(((bf16[16,32,4,128]{3,2,1,0:T(4,128)(2,1)}), bf16[16,32,4,128]{3,2,1,0:T(4,128)(2,1)S(1)}, u32[]{:S(2)}, u32[]{:S(2)}) %all-to-all-start) | async-done | bytes 524320 | tf_op jit(solution)/shard_map/while/body/eval_jaxpr/all_to_all | solution.py:38
  170.2 6.8 all-to-all-done.1
  211.4 10.2 %all-to-all-done = bf16[16,32,4,128]{3,2,1,0:T(4,128)(2,1)S(1)} async-done(((bf16[16,32,4,128]{3,2,1,0:T(4,128)(2,1)}), bf16[16,32,4,128]{3,2,1,0:T(4,128)(2,1)S(1)}, u32[]{:S(2)}, u32[]{:S(2)}) %all-to-all-start) | async-done | bytes 524320 | tf_op jit(solution)/shard_map/while/body/eval_jaxpr/all_to_all | solution.py:38
  228.8 6.8 all-to-all-done.1
  268.7 10.2 %all-to-all-done = bf16[16,32,4,128]{3,2,1,0:T(4,128)(2,1)S(1)} async-done(((bf16[16,32,4,128]{3,2,1,0:T(4,128)(2,1)}), bf16[16,32,4,128]{3,2,1,0:T(4,128)(2,1)S(1)}, u32[]{:S(2)}, u32[]{:S(2)}) %all-to-all-start) | async-done | bytes 524320 | tf_op jit(solution)/shard_map/while/body/eval_jaxpr/all_to_all | solution.py:38
  286.1 6.8 all-to-all-done.1
  326.1 10.2 %all-to-all-done = bf16[16,32,4,128]{3,2,1,0:T(4,128)(2,1)S(1)} async-done(((bf16[16,32,4,128]{3,2,1,0:T(4,128)(2,1)}), bf16[16,32,4,128]{3,2,1,0:T(4,128)(2,1)S(1)}, u32[]{:S(2)}, u32[]{:S(2)}) %all-to-all-start) | async-done | bytes 524320 | tf_op jit(solution)/shard_map/while/body/eval_jaxpr/all_to_all | solution.py:38
  343.5 6.8 all-to-all-done.1
  383.4 10.2 %all-to-all-done = bf16[16,32,4,128]{3,2,1,0:T(4,128)(2,1)S(1)} async-done(((bf16[16,32,4,128]{3,2,1,0:T(4,128)(2,1)}), bf16[16,32,4,128]{3,2,1,0:T(4,128)(2,1)S(1)}, u32[]{:S(2)}, u32[]{:S(2)}) %all-to-all-start) | async-done | bytes 524320 | tf_op jit(solution)/shard_map/while/body/eval_jaxpr/all_to_all | solution.py:38
  400.8 6.8 all-to-all-done.1
  440.8 10.2 %all-to-all-done = bf16[16,32,4,128]{3,2,1,0:T(4,128)(2,1)S(1)} async-done(((bf16[16,32,4,128]{3,2,1,0:T(4,128)(2,1)}), bf16[16,32,4,128]{3,2,1,0:T(4,128)(2,1)S(1)}, u32[]{:S(2)}, u32[]{:S(2)}) %all-to-all-start) | async-done | bytes 524320 | tf_op jit(solution)/shard_map/while/body/eval_jaxpr/all_to_all | solution.py:38
  458.2 6.8 all-to-all-done.1
  485.5 393.8 %while.21 = (s32[]{:T(128)}, bf16[8,2,2048]{2,1,0:T(2,128)(2,1)S(1)}, bf16[8,2,2048]{2,1,0:T(2,128)(2,1)S(1)}, f32[1,2048]{1,0:T(1,128)S(1)}, s32[512]{0:T(512)S...) while((s32[]{:T(128)}, bf16[8,2,2048]{2,1,0:T(2,128)(2,1)S(1)}, bf16[8,2,2048]{2,1,0:T(2,128)(2,1)S(1)}, ...), condition=%wide.region_3.5_spmd, body=%wide.region_2.4_spmd.sunk | while | flops 143627776 | bytes 35611868 | solution.py:78
  514.7 6.7 all-to-all-done.3
  879.9 10.8 %gather_fusion.4 = f32[4096,9]{1,0:T(8,128)S(1)} fusion(f32[2049,9]{1,0:T(8,128)S(1)} %concatenate.57, s32[4096]{0:T(1024)S(1)} %fusion.82), kind=kCustom, calls=%fused_computation.6 | custom fusion | bytes 311296 | tf_op jit(solution)/shard_map/jit(_take)/gather | solution.py:97
  892.2 17.1 %all_to_all.39 = f32[128,1,288]{2,1,0:T(1,128)S(1)} all-to-all(f32[128,1,288]{2,1,0:T(1,128)S(1)} %reshape.539), channel_id=1, replica_groups=mesh['depth'=8,'plane'=16] {'depth','plane'}, dimensions={0} | all-to-all | bytes 294912 | tf_op jit(solution)/shard_map/all_to_all | solution.py:98
  912.3 22.8 %scatter_custom_fusion.1 = f32[128,8]{1,0:T(8,128)S(1)} fusion(s32[4096]{0:T(1024)S(1)} %bitcast.337, f32[4096,8]{1,0:T(8,128)S(1)} %copy.96, f32[]{:T(128)} %constant.77.clone.1), kind=kCustom, calls=%fused_computation.119 | custom fusion | flops 32768 | bytes 4100 | tf_op jit(solution)/shard_map/scatter-add | solution.py:101
  (585 shorter events, 715.0 us)
Async XLA Ops:
  24.3 17.9 %all-to-all-start.4 = ((bf16[16,32,4,128]{3,2,1,0:T(4,128)(2,1)}), bf16[16,32,4,128]{3,2,1,0:T(4,128)(2,1)S(1)}, u32[]{:S(2)}, u32[]{:S(2)}) async-start(bf16[16,32,4,128]{3,2,1,0:T(4,128)(2,1)} %broadcast_in_dim.85), calls=%async_computation.4 | async-start | bytes 1048576 | tf_op jit(solution)/shard_map/all_to_all | solution.py:38
  43.2 13.9 %all-to-all-start.5 = ((bf16[16,32,4,128]{3,2,1,0:T(4,128)(2,1)}), bf16[16,32,4,128]{3,2,1,0:T(4,128)(2,1)S(1)}, u32[]{:S(2)}, u32[]{:S(2)}) async-start(bf16[16,32,4,128]{3,2,1,0:T(4,128)(2,1)} %broadcast_in_dim.87), calls=%async_computation.5 | async-start | bytes 1048576 | tf_op jit(solution)/shard_map/all_to_all | solution.py:38
  89.3 14.1 %all-to-all-start = ((bf16[16,32,4,128]{3,2,1,0:T(4,128)(2,1)}), bf16[16,32,4,128]{3,2,1,0:T(4,128)(2,1)S(1)}, u32[]{:S(2)}, u32[]{:S(2)}) async-start(bf16[16,32,4,128]{3,2,1,0:T(4,128)(2,1)} %broadcast_in_dim.162), calls=%async_computation | async-start | bytes 1048576 | tf_op jit(solution)/shard_map/while/body/eval_jaxpr/all_to_all | solution.py:38
  104.4 13.1 %all-to-all-start.1 = ((bf16[16,32,4,128]{3,2,1,0:T(4,128)(2,1)}), bf16[16,32,4,128]{3,2,1,0:T(4,128)(2,1)S(1)}, u32[]{:S(2)}, u32[]{:S(2)}) async-start(bf16[16,32,4,128]{3,2,1,0:T(4,128)(2,1)} %broadcast_in_dim.164), calls=%async_computation.1 | async-start | bytes 1048576 | tf_op jit(solution)/shard_map/while/body/eval_jaxpr/all_to_all | solution.py:38
  148.9 14.1 %all-to-all-start = ((bf16[16,32,4,128]{3,2,1,0:T(4,128)(2,1)}), bf16[16,32,4,128]{3,2,1,0:T(4,128)(2,1)S(1)}, u32[]{:S(2)}, u32[]{:S(2)}) async-start(bf16[16,32,4,128]{3,2,1,0:T(4,128)(2,1)} %broadcast_in_dim.162), calls=%async_computation | async-start | bytes 1048576 | tf_op jit(solution)/shard_map/while/body/eval_jaxpr/all_to_all | solution.py:38
  163.9 13.1 %all-to-all-start.1 = ((bf16[16,32,4,128]{3,2,1,0:T(4,128)(2,1)}), bf16[16,32,4,128]{3,2,1,0:T(4,128)(2,1)S(1)}, u32[]{:S(2)}, u32[]{:S(2)}) async-start(bf16[16,32,4,128]{3,2,1,0:T(4,128)(2,1)} %broadcast_in_dim.164), calls=%async_computation.1 | async-start | bytes 1048576 | tf_op jit(solution)/shard_map/while/body/eval_jaxpr/all_to_all | solution.py:38
  207.5 14.1 %all-to-all-start = ((bf16[16,32,4,128]{3,2,1,0:T(4,128)(2,1)}), bf16[16,32,4,128]{3,2,1,0:T(4,128)(2,1)S(1)}, u32[]{:S(2)}, u32[]{:S(2)}) async-start(bf16[16,32,4,128]{3,2,1,0:T(4,128)(2,1)} %broadcast_in_dim.162), calls=%async_computation | async-start | bytes 1048576 | tf_op jit(solution)/shard_map/while/body/eval_jaxpr/all_to_all | solution.py:38
  222.5 13.1 %all-to-all-start.1 = ((bf16[16,32,4,128]{3,2,1,0:T(4,128)(2,1)}), bf16[16,32,4,128]{3,2,1,0:T(4,128)(2,1)S(1)}, u32[]{:S(2)}, u32[]{:S(2)}) async-start(bf16[16,32,4,128]{3,2,1,0:T(4,128)(2,1)} %broadcast_in_dim.164), calls=%async_computation.1 | async-start | bytes 1048576 | tf_op jit(solution)/shard_map/while/body/eval_jaxpr/all_to_all | solution.py:38
  264.8 14.1 %all-to-all-start = ((bf16[16,32,4,128]{3,2,1,0:T(4,128)(2,1)}), bf16[16,32,4,128]{3,2,1,0:T(4,128)(2,1)S(1)}, u32[]{:S(2)}, u32[]{:S(2)}) async-start(bf16[16,32,4,128]{3,2,1,0:T(4,128)(2,1)} %broadcast_in_dim.162), calls=%async_computation | async-start | bytes 1048576 | tf_op jit(solution)/shard_map/while/body/eval_jaxpr/all_to_all | solution.py:38
  279.9 13.1 %all-to-all-start.1 = ((bf16[16,32,4,128]{3,2,1,0:T(4,128)(2,1)}), bf16[16,32,4,128]{3,2,1,0:T(4,128)(2,1)S(1)}, u32[]{:S(2)}, u32[]{:S(2)}) async-start(bf16[16,32,4,128]{3,2,1,0:T(4,128)(2,1)} %broadcast_in_dim.164), calls=%async_computation.1 | async-start | bytes 1048576 | tf_op jit(solution)/shard_map/while/body/eval_jaxpr/all_to_all | solution.py:38
  322.2 14.1 %all-to-all-start = ((bf16[16,32,4,128]{3,2,1,0:T(4,128)(2,1)}), bf16[16,32,4,128]{3,2,1,0:T(4,128)(2,1)S(1)}, u32[]{:S(2)}, u32[]{:S(2)}) async-start(bf16[16,32,4,128]{3,2,1,0:T(4,128)(2,1)} %broadcast_in_dim.162), calls=%async_computation | async-start | bytes 1048576 | tf_op jit(solution)/shard_map/while/body/eval_jaxpr/all_to_all | solution.py:38
  337.2 13.1 %all-to-all-start.1 = ((bf16[16,32,4,128]{3,2,1,0:T(4,128)(2,1)}), bf16[16,32,4,128]{3,2,1,0:T(4,128)(2,1)S(1)}, u32[]{:S(2)}, u32[]{:S(2)}) async-start(bf16[16,32,4,128]{3,2,1,0:T(4,128)(2,1)} %broadcast_in_dim.164), calls=%async_computation.1 | async-start | bytes 1048576 | tf_op jit(solution)/shard_map/while/body/eval_jaxpr/all_to_all | solution.py:38
  379.5 14.1 %all-to-all-start = ((bf16[16,32,4,128]{3,2,1,0:T(4,128)(2,1)}), bf16[16,32,4,128]{3,2,1,0:T(4,128)(2,1)S(1)}, u32[]{:S(2)}, u32[]{:S(2)}) async-start(bf16[16,32,4,128]{3,2,1,0:T(4,128)(2,1)} %broadcast_in_dim.162), calls=%async_computation | async-start | bytes 1048576 | tf_op jit(solution)/shard_map/while/body/eval_jaxpr/all_to_all | solution.py:38
  394.6 13.1 %all-to-all-start.1 = ((bf16[16,32,4,128]{3,2,1,0:T(4,128)(2,1)}), bf16[16,32,4,128]{3,2,1,0:T(4,128)(2,1)S(1)}, u32[]{:S(2)}, u32[]{:S(2)}) async-start(bf16[16,32,4,128]{3,2,1,0:T(4,128)(2,1)} %broadcast_in_dim.164), calls=%async_computation.1 | async-start | bytes 1048576 | tf_op jit(solution)/shard_map/while/body/eval_jaxpr/all_to_all | solution.py:38
  436.9 14.1 %all-to-all-start = ((bf16[16,32,4,128]{3,2,1,0:T(4,128)(2,1)}), bf16[16,32,4,128]{3,2,1,0:T(4,128)(2,1)S(1)}, u32[]{:S(2)}, u32[]{:S(2)}) async-start(bf16[16,32,4,128]{3,2,1,0:T(4,128)(2,1)} %broadcast_in_dim.162), calls=%async_computation | async-start | bytes 1048576 | tf_op jit(solution)/shard_map/while/body/eval_jaxpr/all_to_all | solution.py:38
  451.9 13.1 %all-to-all-start.1 = ((bf16[16,32,4,128]{3,2,1,0:T(4,128)(2,1)}), bf16[16,32,4,128]{3,2,1,0:T(4,128)(2,1)S(1)}, u32[]{:S(2)}, u32[]{:S(2)}) async-start(bf16[16,32,4,128]{3,2,1,0:T(4,128)(2,1)} %broadcast_in_dim.164), calls=%async_computation.1 | async-start | bytes 1048576 | tf_op jit(solution)/shard_map/while/body/eval_jaxpr/all_to_all | solution.py:38
  493.6 13.8 %all-to-all-start.2 = ((bf16[16,32,4,128]{3,2,1,0:T(4,128)(2,1)}), bf16[16,32,4,128]{3,2,1,0:T(4,128)(2,1)S(1)}, u32[]{:S(2)}, u32[]{:S(2)}) async-start(bf16[16,32,4,128]{3,2,1,0:T(4,128)(2,1)} %broadcast_in_dim.168), calls=%async_computation.2 | async-start | bytes 1048576 | tf_op jit(solution)/shard_map/while/body/eval_jaxpr/all_to_all | solution.py:38
  508.3 13.1 %all-to-all-start.3 = ((bf16[16,32,4,128]{3,2,1,0:T(4,128)(2,1)}), bf16[16,32,4,128]{3,2,1,0:T(4,128)(2,1)S(1)}, u32[]{:S(2)}, u32[]{:S(2)}) async-start(bf16[16,32,4,128]{3,2,1,0:T(4,128)(2,1)} %broadcast_in_dim.170), calls=%async_computation.3 | async-start | bytes 1048576 | tf_op jit(solution)/shard_map/while/body/eval_jaxpr/all_to_all | solution.py:38
  549.8 13.8 %all-to-all-start.2 = ((bf16[16,32,4,128]{3,2,1,0:T(4,128)(2,1)}), bf16[16,32,4,128]{3,2,1,0:T(4,128)(2,1)S(1)}, u32[]{:S(2)}, u32[]{:S(2)}) async-start(bf16[16,32,4,128]{3,2,1,0:T(4,128)(2,1)} %broadcast_in_dim.168), calls=%async_computation.2 | async-start | bytes 1048576 | tf_op jit(solution)/shard_map/while/body/eval_jaxpr/all_to_all | solution.py:38
  606.0 13.8 %all-to-all-start.2 = ((bf16[16,32,4,128]{3,2,1,0:T(4,128)(2,1)}), bf16[16,32,4,128]{3,2,1,0:T(4,128)(2,1)S(1)}, u32[]{:S(2)}, u32[]{:S(2)}) async-start(bf16[16,32,4,128]{3,2,1,0:T(4,128)(2,1)} %broadcast_in_dim.168), calls=%async_computation.2 | async-start | bytes 1048576 | tf_op jit(solution)/shard_map/while/body/eval_jaxpr/all_to_all | solution.py:38
  662.1 13.8 %all-to-all-start.2 = ((bf16[16,32,4,128]{3,2,1,0:T(4,128)(2,1)}), bf16[16,32,4,128]{3,2,1,0:T(4,128)(2,1)S(1)}, u32[]{:S(2)}, u32[]{:S(2)}) async-start(bf16[16,32,4,128]{3,2,1,0:T(4,128)(2,1)} %broadcast_in_dim.168), calls=%async_computation.2 | async-start | bytes 1048576 | tf_op jit(solution)/shard_map/while/body/eval_jaxpr/all_to_all | solution.py:38
  718.3 13.8 %all-to-all-start.2 = ((bf16[16,32,4,128]{3,2,1,0:T(4,128)(2,1)}), bf16[16,32,4,128]{3,2,1,0:T(4,128)(2,1)S(1)}, u32[]{:S(2)}, u32[]{:S(2)}) async-start(bf16[16,32,4,128]{3,2,1,0:T(4,128)(2,1)} %broadcast_in_dim.168), calls=%async_computation.2 | async-start | bytes 1048576 | tf_op jit(solution)/shard_map/while/body/eval_jaxpr/all_to_all | solution.py:38
  774.5 13.8 %all-to-all-start.2 = ((bf16[16,32,4,128]{3,2,1,0:T(4,128)(2,1)}), bf16[16,32,4,128]{3,2,1,0:T(4,128)(2,1)S(1)}, u32[]{:S(2)}, u32[]{:S(2)}) async-start(bf16[16,32,4,128]{3,2,1,0:T(4,128)(2,1)} %broadcast_in_dim.168), calls=%async_computation.2 | async-start | bytes 1048576 | tf_op jit(solution)/shard_map/while/body/eval_jaxpr/all_to_all | solution.py:38
  830.7 13.8 %all-to-all-start.2 = ((bf16[16,32,4,128]{3,2,1,0:T(4,128)(2,1)}), bf16[16,32,4,128]{3,2,1,0:T(4,128)(2,1)S(1)}, u32[]{:S(2)}, u32[]{:S(2)}) async-start(bf16[16,32,4,128]{3,2,1,0:T(4,128)(2,1)} %broadcast_in_dim.168), calls=%async_computation.2 | async-start | bytes 1048576 | tf_op jit(solution)/shard_map/while/body/eval_jaxpr/all_to_all | solution.py:38
  (38 other events, 660.6 us)

commit v5 on v3

--- a/solution.py
+++ b/solution.py
@@ -35,7 +35,7 @@
         copies = jnp.broadcast_to(local_blocks[None], (plane_count,) + local_blocks.shape)
         gathered = lax.all_to_all(copies, "plane", 0, 0, tiled=True)
         gathered = gathered.reshape(plane_count * block_rows, vec_count, 2 * block_cells)
-        chosen = jnp.take(gathered, pattern_flat, axis=0)
+        chosen = jnp.take(gathered, pattern_flat, axis=0, mode="clip")
         chosen = chosen.reshape(block_rows, -1, vec_count, 2 * block_cells)
         x_re = chosen[..., :block_cells]
         x_im = chosen[..., block_cells:]
@@ -69,10 +69,12 @@
     cell_count = cell_patch.shape[0]
     owner_count = depth_count * plane_count
     owner = cell_patch // PATCH_DEV
-    hits = (owner[:, None] == jnp.arange(owner_count, dtype=owner.dtype)[None, :]).astype(jnp.int32)
-    rank = jnp.take_along_axis(jnp.cumsum(hits, axis=0), owner[:, None], axis=1)[:, 0] - 1
+    hits = (owner[:, None] == jnp.arange(owner_count, dtype=owner.dtype)[None, :]).astype(jnp.bfloat16)
+    cells = jnp.arange(cell_count, dtype=jnp.int32)
+    lower = (cells[:, None] >= cells[None, :]).astype(jnp.bfloat16)
+    running = jnp.dot(lower, hits, preferred_element_type=jnp.float32)
+    rank = jnp.sum(running * hits.astype(jnp.float32), axis=1).astype(jnp.int32) - 1
     slot = owner * CAP + rank
-    cells = jnp.arange(cell_count, dtype=jnp.int32)
     perm = jnp.full((owner_count * CAP,), cell_count, jnp.int32).at[slot].set(cells)
     local_patch = (cell_patch % PATCH_DEV).astype(jnp.float32)
     padded = jnp.concatenate(
@@ -80,11 +82,15 @@
          jnp.zeros((1, vec_count + 1), jnp.float32)],
         axis=0,
     )
-    packed = jnp.take(padded, perm, axis=0).reshape(owner_count, CAP, vec_count + 1)
+    packed = jnp.take(padded, perm, axis=0, mode="clip").reshape(owner_count, CAP, vec_count + 1)
     received = lax.all_to_all(packed, ("depth", "plane"), 0, 0, tiled=True)
     received = received.reshape(owner_count * CAP, vec_count + 1)
     target = received[:, vec_count].astype(jnp.int32)
-    owned = jax.ops.segment_sum(received[:, :vec_count], target, num_segments=PATCH_DEV).T
+    choose = (target[:, None] == jnp.arange(PATCH_DEV, dtype=jnp.int32)[None, :]).astype(jnp.float32)
+    owned = jnp.einsum(
+        "sv,sp->vp", received[:, :vec_count], choose, precision=lax.Precision.HIGHEST,
+        preferred_element_type=jnp.float32,
+    )
     return (precond[None], owned)
 
 

time: 663 us -> 589 us (0.89)
  other arithmetic: 78.4 us -> 27.7 us
  local copies, waits for them, and re-layouts: 98.2 us -> 79.5 us
  waiting for transfers between devices: 265 us -> 257 us
    select_n x31 -> x0, other arithmetic: 27.1 us -> none  [the longest x30 26.4 us: apply_layer(): chosen = jnp.take(gathered, pattern_flat, axis=0)]
    scatter-add x1 -> x0, other arithmetic: 22.8 us -> none  [shards(): jax.ops.segment_sum(received[:, :vec_count], target, num_segments=PATCH_DEV)]
    gather x18 -> x16, local copies, waits for them, and re-layouts: 55.4 us -> 37.8 us  [the longest x15 27 us: apply_layer(): chosen = jnp.take(gathered, pattern_flat, axis=0, mode='clip')]
    all_to_all x15, waiting for transfers between devices: 192 us -> 184 us  [apply_layer(): gathered = lax.all_to_all(copies, 'plane', 0, 0, tiled=True)]
  transfers between devices with their start and end apart: 30 -> 30, of which waited for: 30 -> 30; matrix products, arithmetic and copies ran while one was open for 0% -> 2% of each run, Pallas kernels for 0% -> 0%
where the time goes in v5:
time: 589 us; the launch traced here: 586 us
  waiting for transfers between devices  257 us (44%)
  starting transfers between devices  131 us (22%)
  matrix products  88.4 us (15%)
  local copies, waits for them, and re-layouts  79.5 us (13%)
  other arithmetic  27.7 us (5%)
    all_to_all x15, waiting for transfers between devices, apply_layer(): gathered = lax.all_to_all(copies, 'plane', 0, 0, tiled=True)  184 us
    dot_general x15, matrix products, apply_layer(): jnp.einsum('rkic,rkvwc->vwri', factor, expanded, preferred_element_type=j...  84.9 us
    ppermute x14, waiting for transfers between devices, passed_along(): lax.ppermute(value, axis, [(source, source + steps) for source in range(f...  63 us
    ppermute x14, starting transfers between devices, passed_along(): lax.ppermute(value, axis, [(source, source + steps) for source in range(f...  62.3 us
    all_to_all x15, starting transfers between devices, apply_layer(): gathered = lax.all_to_all(copies, 'plane', 0, 0, tiled=True)  59.8 us
    gather x15, local copies, waits for them, and re-layouts, apply_layer(): chosen = jnp.take(gathered, pattern_flat, axis=0, mode='clip')  27 us
    broadcast_in_dim x30, local copies, waits for them, and re-layouts, apply_layer(): jnp.broadcast_to(local_blocks[None], (plane_count,) + local_blocks.shape)  19.3 us
    another operation x15, other arithmetic, apply_layer(): jnp.stack([jnp.concatenate([x_re, -x_im], axis=-1), jnp.concatenate([x_im...  17.3 us
  transfers between devices with their start and end apart: 30, of which 30 were waited for; matrix products, arithmetic and copies ran while one was open for 2% of the time, Pallas kernels for 0%

profile of v5, /device:TPU:1, one launch (start us, length us, event | category | flops | bytes accessed | tf_op | source)
XLA Modules:
  0.0 586.2 jit_solution(8411036113950040513)
XLA Ops:
  15.7 8.2 %scatter_custom_fusion = s32[4096]{0:T(1024)S(1)} fusion(s32[2048]{0:T(1024)S(1)} %bitcast.197, s32[2048]{0:T(1024)S(1)} %iota.15, s32[]{:T(128)} %constant.43.clone.1), kind=kCustom, calls=%fused_computation.82 | custom fusion | bytes 16388 | tf_op jit(solution)/shard_map/scatter | solution.py:78
  40.5 252.9 %while.20 = (s32[]{:T(128)}, bf16[8,2,2048]{2,0,1:T(8,128)(2,1)S(1)}, f32[1,2048]{1,0:T(1,128)S(1)}, f32[8,2,2048]{2,0,1:T(8,128)S(1)}, s32[512]{0:T(512)S(1)}, /*index=5*/bf16[32,16,64,128]{3,2,1,0:T(8,128)(2,1)}, s32[]{:T(128)}) while((s32[]{:T(128)}, bf16[8,2,2048]{2,0,1:T(8,128)(2,1)S(1)}, f32[1,2048]{1,0:T(1,128)S(1)}, ...), condition=%wide.region_1.2_spmd, body=%wide.region_0.1_spmd.sunk | while | flops 139887616 | bytes 24395924 | solution.py:57
  53.7 15.4 %all-to-all-done = bf16[16,32,8,128]{3,2,1,0:T(8,128)(2,1)S(1)} async-done(((bf16[16,32,8,128]{3,2,1,0:T(8,128)(2,1)}), bf16[16,32,8,128]{3,2,1,0:T(8,128)(2,1)S(1)}, u32[]{:S(2)}, u32[]{:S(2)}) %all-to-all-start) | async-done | bytes 1048608 | tf_op jit(solution)/shard_map/while/body/eval_jaxpr/all_to_all | solution.py:36
  91.8 13.1 %all-to-all-done = bf16[16,32,8,128]{3,2,1,0:T(8,128)(2,1)S(1)} async-done(((bf16[16,32,8,128]{3,2,1,0:T(8,128)(2,1)}), bf16[16,32,8,128]{3,2,1,0:T(8,128)(2,1)S(1)}, u32[]{:S(2)}, u32[]{:S(2)}) %all-to-all-start) | async-done | bytes 1048608 | tf_op jit(solution)/shard_map/while/body/eval_jaxpr/all_to_all | solution.py:36
  114.2 8.2 %collective-permute-start = (bf16[8,2,2048]{2,0,1:T(8,128)(2,1)S(1)}, bf16[8,2,2048]{2,0,1:T(8,128)(2,1)S(1)}, u32[]{:S(2)}, u32[]{:S(2)}) collective-permute-start(bf16[8,2,2048]{2,0,1:T(8,128)(2,1)S(1)} %get-tuple-element.237), channel_id=1, source_target_pairs={{0,16},{16,32},{32,48},{48,64},{64,80},{80,96},{96,112},{1,17},{17... | collective-permute-start | bytes 196616 | tf_op jit(solution)/shard_map/while/body/eval_jaxpr/ppermute | solution.py:13
  129.1 11.8 %all-to-all-done = bf16[16,32,8,128]{3,2,1,0:T(8,128)(2,1)S(1)} async-done(((bf16[16,32,8,128]{3,2,1,0:T(8,128)(2,1)}), bf16[16,32,8,128]{3,2,1,0:T(8,128)(2,1)S(1)}, u32[]{:S(2)}, u32[]{:S(2)}) %all-to-all-start) | async-done | bytes 1048608 | tf_op jit(solution)/shard_map/while/body/eval_jaxpr/all_to_all | solution.py:36
  164.4 12.3 %all-to-all-done = bf16[16,32,8,128]{3,2,1,0:T(8,128)(2,1)S(1)} async-done(((bf16[16,32,8,128]{3,2,1,0:T(8,128)(2,1)}), bf16[16,32,8,128]{3,2,1,0:T(8,128)(2,1)S(1)}, u32[]{:S(2)}, u32[]{:S(2)}) %all-to-all-start) | async-done | bytes 1048608 | tf_op jit(solution)/shard_map/while/body/eval_jaxpr/all_to_all | solution.py:36
  199.8 12.7 %all-to-all-done = bf16[16,32,8,128]{3,2,1,0:T(8,128)(2,1)S(1)} async-done(((bf16[16,32,8,128]{3,2,1,0:T(8,128)(2,1)}), bf16[16,32,8,128]{3,2,1,0:T(8,128)(2,1)S(1)}, u32[]{:S(2)}, u32[]{:S(2)}) %all-to-all-start) | async-done | bytes 1048608 | tf_op jit(solution)/shard_map/while/body/eval_jaxpr/all_to_all | solution.py:36
  235.1 13.2 %all-to-all-done = bf16[16,32,8,128]{3,2,1,0:T(8,128)(2,1)S(1)} async-done(((bf16[16,32,8,128]{3,2,1,0:T(8,128)(2,1)}), bf16[16,32,8,128]{3,2,1,0:T(8,128)(2,1)S(1)}, u32[]{:S(2)}, u32[]{:S(2)}) %all-to-all-start) | async-done | bytes 1048608 | tf_op jit(solution)/shard_map/while/body/eval_jaxpr/all_to_all | solution.py:36
  270.4 13.7 %all-to-all-done = bf16[16,32,8,128]{3,2,1,0:T(8,128)(2,1)S(1)} async-done(((bf16[16,32,8,128]{3,2,1,0:T(8,128)(2,1)}), bf16[16,32,8,128]{3,2,1,0:T(8,128)(2,1)S(1)}, u32[]{:S(2)}, u32[]{:S(2)}) %all-to-all-start) | async-done | bytes 1048608 | tf_op jit(solution)/shard_map/while/body/eval_jaxpr/all_to_all | solution.py:36
  293.5 255.6 %while.21 = (s32[]{:T(128)}, bf16[8,2,2048]{2,0,1:T(8,128)(2,1)S(1)}, bf16[8,2,2048]{2,0,1:T(8,128)(2,1)S(1)}, f32[1,2048]{1,0:T(1,128)S(1)}, s32[512]{0:T(512)S...) while((s32[]{:T(128)}, bf16[8,2,2048]{2,0,1:T(8,128)(2,1)S(1)}, bf16[8,2,2048]{2,0,1:T(8,128)(2,1)S(1)}, ...), condition=%wide.region_3.4_spmd, body=%wide.region_2.3_spmd.sunk | while | flops 139920384 | bytes 24854676 | solution.py:64
  306.6 13.4 %all-to-all-done.1 = bf16[16,32,8,128]{3,2,1,0:T(8,128)(2,1)S(1)} async-done(((bf16[16,32,8,128]{3,2,1,0:T(8,128)(2,1)}), bf16[16,32,8,128]{3,2,1,0:T(8,128)(2,1)S(1)}, u32[]{:S(2)}, u32[]{:S(2)}) %all-to-all-start.1) | async-done | bytes 1048608 | tf_op jit(solution)/shard_map/while/body/eval_jaxpr/all_to_all | solution.py:36
  343.2 12.5 %all-to-all-done.1 = bf16[16,32,8,128]{3,2,1,0:T(8,128)(2,1)S(1)} async-done(((bf16[16,32,8,128]{3,2,1,0:T(8,128)(2,1)}), bf16[16,32,8,128]{3,2,1,0:T(8,128)(2,1)S(1)}, u32[]{:S(2)}, u32[]{:S(2)}) %all-to-all-start.1) | async-done | bytes 1048608 | tf_op jit(solution)/shard_map/while/body/eval_jaxpr/all_to_all | solution.py:36
  367.0 7.7 %collective-permute-done.1 = bf16[8,2,2048]{2,0,1:T(8,128)(2,1)S(1)} collective-permute-done((bf16[8,2,2048]{2,0,1:T(8,128)(2,1)S(1)}, bf16[8,2,2048]{2,0,1:T(8,128)(2,1)S(1)}, u32[]{:S(2)}, u32[]{:S(2)}) %collective-permute-start.1) | collective-permute-done | bytes 65568 | tf_op jit(solution)/shard_map/while/body/eval_jaxpr/ppermute | solution.py:13
  379.9 11.7 %all-to-all-done.1 = bf16[16,32,8,128]{3,2,1,0:T(8,128)(2,1)S(1)} async-done(((bf16[16,32,8,128]{3,2,1,0:T(8,128)(2,1)}), bf16[16,32,8,128]{3,2,1,0:T(8,128)(2,1)S(1)}, u32[]{:S(2)}, u32[]{:S(2)}) %all-to-all-start.1) | async-done | bytes 1048608 | tf_op jit(solution)/shard_map/while/body/eval_jaxpr/all_to_all | solution.py:36
  402.9 9.0 %collective-permute-done.1 = bf16[8,2,2048]{2,0,1:T(8,128)(2,1)S(1)} collective-permute-done((bf16[8,2,2048]{2,0,1:T(8,128)(2,1)S(1)}, bf16[8,2,2048]{2,0,1:T(8,128)(2,1)S(1)}, u32[]{:S(2)}, u32[]{:S(2)}) %collective-permute-start.1) | collective-permute-done | bytes 65568 | tf_op jit(solution)/shard_map/while/body/eval_jaxpr/ppermute | solution.py:13
  417.2 11.7 %all-to-all-done.1 = bf16[16,32,8,128]{3,2,1,0:T(8,128)(2,1)S(1)} async-done(((bf16[16,32,8,128]{3,2,1,0:T(8,128)(2,1)}), bf16[16,32,8,128]{3,2,1,0:T(8,128)(2,1)S(1)}, u32[]{:S(2)}, u32[]{:S(2)}) %all-to-all-start.1) | async-done | bytes 1048608 | tf_op jit(solution)/shard_map/while/body/eval_jaxpr/all_to_all | solution.py:36
  440.2 10.1 %collective-permute-done.1 = bf16[8,2,2048]{2,0,1:T(8,128)(2,1)S(1)} collective-permute-done((bf16[8,2,2048]{2,0,1:T(8,128)(2,1)S(1)}, bf16[8,2,2048]{2,0,1:T(8,128)(2,1)S(1)}, u32[]{:S(2)}, u32[]{:S(2)}) %collective-permute-start.1) | collective-permute-done | bytes 65568 | tf_op jit(solution)/shard_map/while/body/eval_jaxpr/ppermute | solution.py:13
  455.6 11.7 %all-to-all-done.1 = bf16[16,32,8,128]{3,2,1,0:T(8,128)(2,1)S(1)} async-done(((bf16[16,32,8,128]{3,2,1,0:T(8,128)(2,1)}), bf16[16,32,8,128]{3,2,1,0:T(8,128)(2,1)S(1)}, u32[]{:S(2)}, u32[]{:S(2)}) %all-to-all-start.1) | async-done | bytes 1048608 | tf_op jit(solution)/shard_map/while/body/eval_jaxpr/all_to_all | solution.py:36
  491.8 11.7 %all-to-all-done.1 = bf16[16,32,8,128]{3,2,1,0:T(8,128)(2,1)S(1)} async-done(((bf16[16,32,8,128]{3,2,1,0:T(8,128)(2,1)}), bf16[16,32,8,128]{3,2,1,0:T(8,128)(2,1)S(1)}, u32[]{:S(2)}, u32[]{:S(2)}) %all-to-all-start.1) | async-done | bytes 1048608 | tf_op jit(solution)/shard_map/while/body/eval_jaxpr/all_to_all | solution.py:36
  528.0 11.7 %all-to-all-done.1 = bf16[16,32,8,128]{3,2,1,0:T(8,128)(2,1)S(1)} async-done(((bf16[16,32,8,128]{3,2,1,0:T(8,128)(2,1)}), bf16[16,32,8,128]{3,2,1,0:T(8,128)(2,1)S(1)}, u32[]{:S(2)}, u32[]{:S(2)}) %all-to-all-start.1) | async-done | bytes 1048608 | tf_op jit(solution)/shard_map/while/body/eval_jaxpr/all_to_all | solution.py:36
  549.6 10.8 %gather_fusion.3 = f32[4096,9]{1,0:T(8,128)S(1)} fusion(f32[2049,9]{1,0:T(8,128)S(1)} %concatenate.29, s32[4096]{0:T(1024)S(1)} %broadcast_clamp_fusion), kind=kCustom, calls=%fused_computation.3 | custom fusion | bytes 311296 | tf_op jit(solution)/shard_map/jit(_take)/gather | solution.py:85
  562.4 9.3 %all-to-all-start.3 = ((f32[128,1,288]{2,1,0:T(1,128)}), f32[128,1,288]{2,1,0:T(1,128)S(1)}, u32[]{:S(2)}, u32[]{:S(2)}) async-start(f32[128,1,288]{2,1,0:T(1,128)} %reshape.288), calls=%async_computation.3 | async-start | bytes 393216 | tf_op jit(solution)/shard_map/all_to_all | solution.py:86
  572.4 9.9 %all-to-all-done.3 = f32[128,1,288]{2,1,0:T(1,128)S(1)} async-done(((f32[128,1,288]{2,1,0:T(1,128)}), f32[128,1,288]{2,1,0:T(1,128)S(1)}, u32[]{:S(2)}, u32[]{:S(2)}) %all-to-all-start.3) | async-done | bytes 147488 | tf_op jit(solution)/shard_map/all_to_all | solution.py:86
  (263 shorter events, 333.8 us)
Async XLA Ops:
  8.1 23.1 %all-to-all-start.2 = ((bf16[16,32,8,128]{3,2,1,0:T(8,128)(2,1)}), bf16[16,32,8,128]{3,2,1,0:T(8,128)(2,1)S(1)}, u32[]{:S(2)}, u32[]{:S(2)}) async-start(bf16[16,32,8,128]{3,2,1,0:T(8,128)(2,1)} %broadcast_in_dim.50), calls=%async_computation.2 | async-start | bytes 2097152 | tf_op jit(solution)/shard_map/all_to_all | solution.py:36
  50.0 19.1 %all-to-all-start = ((bf16[16,32,8,128]{3,2,1,0:T(8,128)(2,1)}), bf16[16,32,8,128]{3,2,1,0:T(8,128)(2,1)S(1)}, u32[]{:S(2)}, u32[]{:S(2)}) async-start(bf16[16,32,8,128]{3,2,1,0:T(8,128)(2,1)} %broadcast_in_dim.62), calls=%async_computation | async-start | bytes 2097152 | tf_op jit(solution)/shard_map/while/body/eval_jaxpr/all_to_all | solution.py:36
  88.1 16.8 %all-to-all-start = ((bf16[16,32,8,128]{3,2,1,0:T(8,128)(2,1)}), bf16[16,32,8,128]{3,2,1,0:T(8,128)(2,1)S(1)}, u32[]{:S(2)}, u32[]{:S(2)}) async-start(bf16[16,32,8,128]{3,2,1,0:T(8,128)(2,1)} %broadcast_in_dim.62), calls=%async_computation | async-start | bytes 2097152 | tf_op jit(solution)/shard_map/while/body/eval_jaxpr/all_to_all | solution.py:36
  114.2 9.6 %collective-permute-start = (bf16[8,2,2048]{2,0,1:T(8,128)(2,1)S(1)}, bf16[8,2,2048]{2,0,1:T(8,128)(2,1)S(1)}, u32[]{:S(2)}, u32[]{:S(2)}) collective-permute-start(bf16[8,2,2048]{2,0,1:T(8,128)(2,1)S(1)} %get-tuple-element.237), channel_id=1, source_target_pairs={{0,16},{16,32},{32,48},{48,64},{64,80},{80,96},{96,112},{1,17},{17... | collective-permute-start | bytes 196616 | tf_op jit(solution)/shard_map/while/body/eval_jaxpr/ppermute | solution.py:13
  125.4 15.5 %all-to-all-start = ((bf16[16,32,8,128]{3,2,1,0:T(8,128)(2,1)}), bf16[16,32,8,128]{3,2,1,0:T(8,128)(2,1)S(1)}, u32[]{:S(2)}, u32[]{:S(2)}) async-start(bf16[16,32,8,128]{3,2,1,0:T(8,128)(2,1)} %broadcast_in_dim.62), calls=%async_computation | async-start | bytes 2097152 | tf_op jit(solution)/shard_map/while/body/eval_jaxpr/all_to_all | solution.py:36
  150.2 8.9 %collective-permute-start = (bf16[8,2,2048]{2,0,1:T(8,128)(2,1)S(1)}, bf16[8,2,2048]{2,0,1:T(8,128)(2,1)S(1)}, u32[]{:S(2)}, u32[]{:S(2)}) collective-permute-start(bf16[8,2,2048]{2,0,1:T(8,128)(2,1)S(1)} %get-tuple-element.237), channel_id=1, source_target_pairs={{0,16},{16,32},{32,48},{48,64},{64,80},{80,96},{96,112},{1,17},{17... | collective-permute-start | bytes 196616 | tf_op jit(solution)/shard_map/while/body/eval_jaxpr/ppermute | solution.py:13
  160.8 16.0 %all-to-all-start = ((bf16[16,32,8,128]{3,2,1,0:T(8,128)(2,1)}), bf16[16,32,8,128]{3,2,1,0:T(8,128)(2,1)S(1)}, u32[]{:S(2)}, u32[]{:S(2)}) async-start(bf16[16,32,8,128]{3,2,1,0:T(8,128)(2,1)} %broadcast_in_dim.62), calls=%async_computation | async-start | bytes 2097152 | tf_op jit(solution)/shard_map/while/body/eval_jaxpr/all_to_all | solution.py:36
  196.1 16.4 %all-to-all-start = ((bf16[16,32,8,128]{3,2,1,0:T(8,128)(2,1)}), bf16[16,32,8,128]{3,2,1,0:T(8,128)(2,1)S(1)}, u32[]{:S(2)}, u32[]{:S(2)}) async-start(bf16[16,32,8,128]{3,2,1,0:T(8,128)(2,1)} %broadcast_in_dim.62), calls=%async_computation | async-start | bytes 2097152 | tf_op jit(solution)/shard_map/while/body/eval_jaxpr/all_to_all | solution.py:36
  231.4 16.8 %all-to-all-start = ((bf16[16,32,8,128]{3,2,1,0:T(8,128)(2,1)}), bf16[16,32,8,128]{3,2,1,0:T(8,128)(2,1)S(1)}, u32[]{:S(2)}, u32[]{:S(2)}) async-start(bf16[16,32,8,128]{3,2,1,0:T(8,128)(2,1)} %broadcast_in_dim.62), calls=%async_computation | async-start | bytes 2097152 | tf_op jit(solution)/shard_map/while/body/eval_jaxpr/all_to_all | solution.py:36
  266.7 17.4 %all-to-all-start = ((bf16[16,32,8,128]{3,2,1,0:T(8,128)(2,1)}), bf16[16,32,8,128]{3,2,1,0:T(8,128)(2,1)S(1)}, u32[]{:S(2)}, u32[]{:S(2)}) async-start(bf16[16,32,8,128]{3,2,1,0:T(8,128)(2,1)} %broadcast_in_dim.62), calls=%async_computation | async-start | bytes 2097152 | tf_op jit(solution)/shard_map/while/body/eval_jaxpr/all_to_all | solution.py:36
  302.9 17.0 %all-to-all-start.1 = ((bf16[16,32,8,128]{3,2,1,0:T(8,128)(2,1)}), bf16[16,32,8,128]{3,2,1,0:T(8,128)(2,1)S(1)}, u32[]{:S(2)}, u32[]{:S(2)}) async-start(bf16[16,32,8,128]{3,2,1,0:T(8,128)(2,1)} %broadcast_in_dim.64), calls=%async_computation.1 | async-start | bytes 2097152 | tf_op jit(solution)/shard_map/while/body/eval_jaxpr/all_to_all | solution.py:36
  329.3 8.6 %collective-permute-start.1 = (bf16[8,2,2048]{2,0,1:T(8,128)(2,1)S(1)}, bf16[8,2,2048]{2,0,1:T(8,128)(2,1)S(1)}, u32[]{:S(2)}, u32[]{:S(2)}) collective-permute-start(bf16[8,2,2048]{2,0,1:T(8,128)(2,1)S(1)} %multiply_convert_fusion.2), channel_id=1, source_target_pairs={{16,0},{32,16},{48,32},{64,48},{80,64},{96,80},{112,96},{17,1},{33... | collective-permute-start | bytes 196616 | tf_op jit(solution)/shard_map/while/body/eval_jaxpr/ppermute | solution.py:13
  339.5 16.2 %all-to-all-start.1 = ((bf16[16,32,8,128]{3,2,1,0:T(8,128)(2,1)}), bf16[16,32,8,128]{3,2,1,0:T(8,128)(2,1)S(1)}, u32[]{:S(2)}, u32[]{:S(2)}) async-start(bf16[16,32,8,128]{3,2,1,0:T(8,128)(2,1)} %broadcast_in_dim.64), calls=%async_computation.1 | async-start | bytes 2097152 | tf_op jit(solution)/shard_map/while/body/eval_jaxpr/all_to_all | solution.py:36
  365.0 9.6 %collective-permute-start.1 = (bf16[8,2,2048]{2,0,1:T(8,128)(2,1)S(1)}, bf16[8,2,2048]{2,0,1:T(8,128)(2,1)S(1)}, u32[]{:S(2)}, u32[]{:S(2)}) collective-permute-start(bf16[8,2,2048]{2,0,1:T(8,128)(2,1)S(1)} %multiply_convert_fusion.2), channel_id=1, source_target_pairs={{16,0},{32,16},{48,32},{64,48},{80,64},{96,80},{112,96},{17,1},{33... | collective-permute-start | bytes 196616 | tf_op jit(solution)/shard_map/while/body/eval_jaxpr/ppermute | solution.py:13
  376.3 15.4 %all-to-all-start.1 = ((bf16[16,32,8,128]{3,2,1,0:T(8,128)(2,1)}), bf16[16,32,8,128]{3,2,1,0:T(8,128)(2,1)S(1)}, u32[]{:S(2)}, u32[]{:S(2)}) async-start(bf16[16,32,8,128]{3,2,1,0:T(8,128)(2,1)} %broadcast_in_dim.64), calls=%async_computation.1 | async-start | bytes 2097152 | tf_op jit(solution)/shard_map/while/body/eval_jaxpr/all_to_all | solution.py:36
  401.0 10.9 %collective-permute-start.1 = (bf16[8,2,2048]{2,0,1:T(8,128)(2,1)S(1)}, bf16[8,2,2048]{2,0,1:T(8,128)(2,1)S(1)}, u32[]{:S(2)}, u32[]{:S(2)}) collective-permute-start(bf16[8,2,2048]{2,0,1:T(8,128)(2,1)S(1)} %multiply_convert_fusion.2), channel_id=1, source_target_pairs={{16,0},{32,16},{48,32},{64,48},{80,64},{96,80},{112,96},{17,1},{33... | collective-permute-start | bytes 196616 | tf_op jit(solution)/shard_map/while/body/eval_jaxpr/ppermute | solution.py:13
  413.5 15.4 %all-to-all-start.1 = ((bf16[16,32,8,128]{3,2,1,0:T(8,128)(2,1)}), bf16[16,32,8,128]{3,2,1,0:T(8,128)(2,1)S(1)}, u32[]{:S(2)}, u32[]{:S(2)}) async-start(bf16[16,32,8,128]{3,2,1,0:T(8,128)(2,1)} %broadcast_in_dim.64), calls=%async_computation.1 | async-start | bytes 2097152 | tf_op jit(solution)/shard_map/while/body/eval_jaxpr/all_to_all | solution.py:36
  438.3 12.1 %collective-permute-start.1 = (bf16[8,2,2048]{2,0,1:T(8,128)(2,1)S(1)}, bf16[8,2,2048]{2,0,1:T(8,128)(2,1)S(1)}, u32[]{:S(2)}, u32[]{:S(2)}) collective-permute-start(bf16[8,2,2048]{2,0,1:T(8,128)(2,1)S(1)} %multiply_convert_fusion.2), channel_id=1, source_target_pairs={{16,0},{32,16},{48,32},{64,48},{80,64},{96,80},{112,96},{17,1},{33... | collective-permute-start | bytes 196616 | tf_op jit(solution)/shard_map/while/body/eval_jaxpr/ppermute | solution.py:13
  452.0 15.4 %all-to-all-start.1 = ((bf16[16,32,8,128]{3,2,1,0:T(8,128)(2,1)}), bf16[16,32,8,128]{3,2,1,0:T(8,128)(2,1)S(1)}, u32[]{:S(2)}, u32[]{:S(2)}) async-start(bf16[16,32,8,128]{3,2,1,0:T(8,128)(2,1)} %broadcast_in_dim.64), calls=%async_computation.1 | async-start | bytes 2097152 | tf_op jit(solution)/shard_map/while/body/eval_jaxpr/all_to_all | solution.py:36
  476.7 9.6 %collective-permute-start.1 = (bf16[8,2,2048]{2,0,1:T(8,128)(2,1)S(1)}, bf16[8,2,2048]{2,0,1:T(8,128)(2,1)S(1)}, u32[]{:S(2)}, u32[]{:S(2)}) collective-permute-start(bf16[8,2,2048]{2,0,1:T(8,128)(2,1)S(1)} %multiply_convert_fusion.2), channel_id=1, source_target_pairs={{16,0},{32,16},{48,32},{64,48},{80,64},{96,80},{112,96},{17,1},{33... | collective-permute-start | bytes 196616 | tf_op jit(solution)/shard_map/while/body/eval_jaxpr/ppermute | solution.py:13
  487.9 15.6 %all-to-all-start.1 = ((bf16[16,32,8,128]{3,2,1,0:T(8,128)(2,1)}), bf16[16,32,8,128]{3,2,1,0:T(8,128)(2,1)S(1)}, u32[]{:S(2)}, u32[]{:S(2)}) async-start(bf16[16,32,8,128]{3,2,1,0:T(8,128)(2,1)} %broadcast_in_dim.64), calls=%async_computation.1 | async-start | bytes 2097152 | tf_op jit(solution)/shard_map/while/body/eval_jaxpr/all_to_all | solution.py:36
  512.9 9.0 %collective-permute-start.1 = (bf16[8,2,2048]{2,0,1:T(8,128)(2,1)S(1)}, bf16[8,2,2048]{2,0,1:T(8,128)(2,1)S(1)}, u32[]{:S(2)}, u32[]{:S(2)}) collective-permute-start(bf16[8,2,2048]{2,0,1:T(8,128)(2,1)S(1)} %multiply_convert_fusion.2), channel_id=1, source_target_pairs={{16,0},{32,16},{48,32},{64,48},{80,64},{96,80},{112,96},{17,1},{33... | collective-permute-start | bytes 196616 | tf_op jit(solution)/shard_map/while/body/eval_jaxpr/ppermute | solution.py:13
  523.5 16.3 %all-to-all-start.1 = ((bf16[16,32,8,128]{3,2,1,0:T(8,128)(2,1)}), bf16[16,32,8,128]{3,2,1,0:T(8,128)(2,1)S(1)}, u32[]{:S(2)}, u32[]{:S(2)}) async-start(bf16[16,32,8,128]{3,2,1,0:T(8,128)(2,1)} %broadcast_in_dim.64), calls=%async_computation.1 | async-start | bytes 2097152 | tf_op jit(solution)/shard_map/while/body/eval_jaxpr/all_to_all | solution.py:36
  562.4 19.9 %all-to-all-start.3 = ((f32[128,1,288]{2,1,0:T(1,128)}), f32[128,1,288]{2,1,0:T(1,128)S(1)}, u32[]{:S(2)}, u32[]{:S(2)}) async-start(f32[128,1,288]{2,1,0:T(1,128)} %reshape.288), calls=%async_computation.3 | async-start | bytes 393216 | tf_op jit(solution)/shard_map/all_to_all | solution.py:86
  (9 other events, 317.6 us)

commit v6 on v5

--- a/solution.py
+++ b/solution.py
@@ -75,14 +75,18 @@
     running = jnp.dot(lower, hits, preferred_element_type=jnp.float32)
     rank = jnp.sum(running * hits.astype(jnp.float32), axis=1).astype(jnp.int32) - 1
     slot = owner * CAP + rank
-    perm = jnp.full((owner_count * CAP,), cell_count, jnp.int32).at[slot].set(cells)
+    placed = (slot[:, None] == jnp.arange(owner_count * CAP, dtype=jnp.int32)[None, :]).astype(jnp.bfloat16)
     local_patch = (cell_patch % PATCH_DEV).astype(jnp.float32)
-    padded = jnp.concatenate(
-        [jnp.concatenate([contrib.T, local_patch[:, None]], axis=1),
-         jnp.zeros((1, vec_count + 1), jnp.float32)],
-        axis=0,
-    )
-    packed = jnp.take(padded, perm, axis=0, mode="clip").reshape(owner_count, CAP, vec_count + 1)
+    rows = jnp.concatenate([contrib.T, local_patch[:, None]], axis=1)
+    high = rows.astype(jnp.bfloat16)
+    rest = rows - high.astype(jnp.float32)
+    middle = rest.astype(jnp.bfloat16)
+    low = (rest - middle.astype(jnp.float32)).astype(jnp.bfloat16)
+    parts = jnp.concatenate([high, middle, low], axis=1)
+    moved = jnp.einsum("cs,cq->sq", placed, parts, preferred_element_type=jnp.float32)
+    width = vec_count + 1
+    packed = (moved[:, :width] + moved[:, width:2 * width]) + moved[:, 2 * width:]
+    packed = packed.reshape(owner_count, CAP, width)
     received = lax.all_to_all(packed, ("depth", "plane"), 0, 0, tiled=True)
     received = received.reshape(owner_count * CAP, vec_count + 1)
     target = received[:, vec_count].astype(jnp.int32)

time: 589 us -> 583 us (0.990)
  local copies, waits for them, and re-layouts: 79.5 us -> 59.8 us
  waiting for transfers between devices: 257 us -> 265 us
  matrix products: 88.4 us -> 94.9 us
    gather x1 -> x0, local copies, waits for them, and re-layouts: 10.8 us -> none  [shards(): jnp.take(padded, perm, axis=0, mode='clip')]
    all_to_all x15, waiting for transfers between devices: 184 us -> 192 us  [apply_layer(): gathered = lax.all_to_all(copies, 'plane', 0, 0, tiled=True)]
    scatter x1 -> x0, local copies, waits for them, and re-layouts: 8.24 us -> none  [shards(): jnp.full((owner_count * CAP,), cell_count, jnp.int32).at[slot].set(cells)]
    dot_general x0 -> x1, matrix products: none -> 6.47 us  [shards(): jnp.einsum('cs,cq->sq', placed, parts, preferred_element_type=jnp.float32)]
  transfers between devices with their start and end apart: 30 -> 30, of which waited for: 30 -> 30; matrix products, arithmetic and copies ran while one was open for 2% -> 0% of each run, Pallas kernels for 0% -> 0%
where the time goes in v6:
time: 583 us; the launch traced here: 581 us
  waiting for transfers between devices  265 us (45%)
  starting transfers between devices  131 us (22%)
  matrix products  94.9 us (16%)
  local copies, waits for them, and re-layouts  59.8 us (10%)
  other arithmetic  27.4 us (5%)
    all_to_all x15, waiting for transfers between devices, apply_layer(): gathered = lax.all_to_all(copies, 'plane', 0, 0, tiled=True)  192 us
    dot_general x15, matrix products, apply_layer(): jnp.einsum('rkic,rkvwc->vwri', factor, expanded, preferred_element_type=j...  84.9 us
    ppermute x14, waiting for transfers between devices, passed_along(): lax.ppermute(value, axis, [(source, source + steps) for source in range(f...  62.9 us
    ppermute x14, starting transfers between devices, passed_along(): lax.ppermute(value, axis, [(source, source + steps) for source in range(f...  62.3 us
    all_to_all x15, starting transfers between devices, apply_layer(): gathered = lax.all_to_all(copies, 'plane', 0, 0, tiled=True)  59.8 us
    gather x15, local copies, waits for them, and re-layouts, apply_layer(): chosen = jnp.take(gathered, pattern_flat, axis=0, mode='clip')  27 us
    broadcast_in_dim x30, local copies, waits for them, and re-layouts, apply_layer(): jnp.broadcast_to(local_blocks[None], (plane_count,) + local_blocks.shape)  19.4 us
    another operation x15, other arithmetic, apply_layer(): jnp.stack([jnp.concatenate([x_re, -x_im], axis=-1), jnp.concatenate([x_im...  17.3 us
  transfers between devices with their start and end apart: 30, of which 30 were waited for; matrix products, arithmetic and copies ran while one was open for 0% of the time, Pallas kernels for 0%

profile of v6, /device:TPU:1, one launch (start us, length us, event | category | flops | bytes accessed | tf_op | source)
XLA Modules:
  0.0 580.9 jit_solution(7029474008969403511)
XLA Ops:
  15.3 15.4 %all-to-all-done.2 = bf16[16,32,8,128]{3,2,1,0:T(8,128)(2,1)S(1)} async-done(((bf16[16,32,8,128]{3,2,1,0:T(8,128)(2,1)}), bf16[16,32,8,128]{3,2,1,0:T(8,128)(2,1)S(1)}, u32[]{:S(2)}, u32[]{:S(2)}) %all-to-all-start.2) | async-done | bytes 1048608 | tf_op jit(solution)/shard_map/all_to_all | solution.py:36
  40.1 253.0 %while.20 = (s32[]{:T(128)}, bf16[8,2,2048]{2,0,1:T(8,128)(2,1)S(1)}, f32[1,2048]{1,0:T(1,128)S(1)}, f32[8,2,2048]{2,0,1:T(8,128)S(1)}, s32[512]{0:T(512)S(1)}, /*index=5*/bf16[32,16,64,128]{3,2,1,0:T(8,128)(2,1)}, s32[]{:T(128)}) while((s32[]{:T(128)}, bf16[8,2,2048]{2,0,1:T(8,128)(2,1)S(1)}, f32[1,2048]{1,0:T(1,128)S(1)}, ...), condition=%wide.region_1.2_spmd, body=%wide.region_0.1_spmd.sunk | while | flops 139887616 | bytes 24395924 | solution.py:57
  53.3 15.4 %all-to-all-done = bf16[16,32,8,128]{3,2,1,0:T(8,128)(2,1)S(1)} async-done(((bf16[16,32,8,128]{3,2,1,0:T(8,128)(2,1)}), bf16[16,32,8,128]{3,2,1,0:T(8,128)(2,1)S(1)}, u32[]{:S(2)}, u32[]{:S(2)}) %all-to-all-start) | async-done | bytes 1048608 | tf_op jit(solution)/shard_map/while/body/eval_jaxpr/all_to_all | solution.py:36
  91.4 13.1 %all-to-all-done = bf16[16,32,8,128]{3,2,1,0:T(8,128)(2,1)S(1)} async-done(((bf16[16,32,8,128]{3,2,1,0:T(8,128)(2,1)}), bf16[16,32,8,128]{3,2,1,0:T(8,128)(2,1)S(1)}, u32[]{:S(2)}, u32[]{:S(2)}) %all-to-all-start) | async-done | bytes 1048608 | tf_op jit(solution)/shard_map/while/body/eval_jaxpr/all_to_all | solution.py:36
  113.8 8.3 %collective-permute-start = (bf16[8,2,2048]{2,0,1:T(8,128)(2,1)S(1)}, bf16[8,2,2048]{2,0,1:T(8,128)(2,1)S(1)}, u32[]{:S(2)}, u32[]{:S(2)}) collective-permute-start(bf16[8,2,2048]{2,0,1:T(8,128)(2,1)S(1)} %get-tuple-element.219), channel_id=1, source_target_pairs={{0,16},{16,32},{32,48},{48,64},{64,80},{80,96},{96,112},{1,17},{17... | collective-permute-start | bytes 196616 | tf_op jit(solution)/shard_map/while/body/eval_jaxpr/ppermute | solution.py:13
  128.7 11.8 %all-to-all-done = bf16[16,32,8,128]{3,2,1,0:T(8,128)(2,1)S(1)} async-done(((bf16[16,32,8,128]{3,2,1,0:T(8,128)(2,1)}), bf16[16,32,8,128]{3,2,1,0:T(8,128)(2,1)S(1)}, u32[]{:S(2)}, u32[]{:S(2)}) %all-to-all-start) | async-done | bytes 1048608 | tf_op jit(solution)/shard_map/while/body/eval_jaxpr/all_to_all | solution.py:36
  164.0 12.3 %all-to-all-done = bf16[16,32,8,128]{3,2,1,0:T(8,128)(2,1)S(1)} async-done(((bf16[16,32,8,128]{3,2,1,0:T(8,128)(2,1)}), bf16[16,32,8,128]{3,2,1,0:T(8,128)(2,1)S(1)}, u32[]{:S(2)}, u32[]{:S(2)}) %all-to-all-start) | async-done | bytes 1048608 | tf_op jit(solution)/shard_map/while/body/eval_jaxpr/all_to_all | solution.py:36
  199.4 12.7 %all-to-all-done = bf16[16,32,8,128]{3,2,1,0:T(8,128)(2,1)S(1)} async-done(((bf16[16,32,8,128]{3,2,1,0:T(8,128)(2,1)}), bf16[16,32,8,128]{3,2,1,0:T(8,128)(2,1)S(1)}, u32[]{:S(2)}, u32[]{:S(2)}) %all-to-all-start) | async-done | bytes 1048608 | tf_op jit(solution)/shard_map/while/body/eval_jaxpr/all_to_all | solution.py:36
  234.7 13.2 %all-to-all-done = bf16[16,32,8,128]{3,2,1,0:T(8,128)(2,1)S(1)} async-done(((bf16[16,32,8,128]{3,2,1,0:T(8,128)(2,1)}), bf16[16,32,8,128]{3,2,1,0:T(8,128)(2,1)S(1)}, u32[]{:S(2)}, u32[]{:S(2)}) %all-to-all-start) | async-done | bytes 1048608 | tf_op jit(solution)/shard_map/while/body/eval_jaxpr/all_to_all | solution.py:36
  270.0 13.7 %all-to-all-done = bf16[16,32,8,128]{3,2,1,0:T(8,128)(2,1)S(1)} async-done(((bf16[16,32,8,128]{3,2,1,0:T(8,128)(2,1)}), bf16[16,32,8,128]{3,2,1,0:T(8,128)(2,1)S(1)}, u32[]{:S(2)}, u32[]{:S(2)}) %all-to-all-start) | async-done | bytes 1048608 | tf_op jit(solution)/shard_map/while/body/eval_jaxpr/all_to_all | solution.py:36
  293.1 255.6 %while.21 = (s32[]{:T(128)}, bf16[8,2,2048]{2,0,1:T(8,128)(2,1)S(1)}, bf16[8,2,2048]{2,0,1:T(8,128)(2,1)S(1)}, f32[1,2048]{1,0:T(1,128)S(1)}, s32[512]{0:T(512)S...) while((s32[]{:T(128)}, bf16[8,2,2048]{2,0,1:T(8,128)(2,1)S(1)}, bf16[8,2,2048]{2,0,1:T(8,128)(2,1)S(1)}, ...), condition=%wide.region_3.4_spmd, body=%wide.region_2.3_spmd.sunk | while | flops 139920384 | bytes 24854676 | solution.py:64
  306.2 13.4 %all-to-all-done.1 = bf16[16,32,8,128]{3,2,1,0:T(8,128)(2,1)S(1)} async-done(((bf16[16,32,8,128]{3,2,1,0:T(8,128)(2,1)}), bf16[16,32,8,128]{3,2,1,0:T(8,128)(2,1)S(1)}, u32[]{:S(2)}, u32[]{:S(2)}) %all-to-all-start.1) | async-done | bytes 1048608 | tf_op jit(solution)/shard_map/while/body/eval_jaxpr/all_to_all | solution.py:36
  342.8 12.5 %all-to-all-done.1 = bf16[16,32,8,128]{3,2,1,0:T(8,128)(2,1)S(1)} async-done(((bf16[16,32,8,128]{3,2,1,0:T(8,128)(2,1)}), bf16[16,32,8,128]{3,2,1,0:T(8,128)(2,1)S(1)}, u32[]{:S(2)}, u32[]{:S(2)}) %all-to-all-start.1) | async-done | bytes 1048608 | tf_op jit(solution)/shard_map/while/body/eval_jaxpr/all_to_all | solution.py:36
  366.6 7.7 %collective-permute-done.1 = bf16[8,2,2048]{2,0,1:T(8,128)(2,1)S(1)} collective-permute-done((bf16[8,2,2048]{2,0,1:T(8,128)(2,1)S(1)}, bf16[8,2,2048]{2,0,1:T(8,128)(2,1)S(1)}, u32[]{:S(2)}, u32[]{:S(2)}) %collective-permute-start.1) | collective-permute-done | bytes 65568 | tf_op jit(solution)/shard_map/while/body/eval_jaxpr/ppermute | solution.py:13
  379.6 11.7 %all-to-all-done.1 = bf16[16,32,8,128]{3,2,1,0:T(8,128)(2,1)S(1)} async-done(((bf16[16,32,8,128]{3,2,1,0:T(8,128)(2,1)}), bf16[16,32,8,128]{3,2,1,0:T(8,128)(2,1)S(1)}, u32[]{:S(2)}, u32[]{:S(2)}) %all-to-all-start.1) | async-done | bytes 1048608 | tf_op jit(solution)/shard_map/while/body/eval_jaxpr/all_to_all | solution.py:36
  402.6 9.0 %collective-permute-done.1 = bf16[8,2,2048]{2,0,1:T(8,128)(2,1)S(1)} collective-permute-done((bf16[8,2,2048]{2,0,1:T(8,128)(2,1)S(1)}, bf16[8,2,2048]{2,0,1:T(8,128)(2,1)S(1)}, u32[]{:S(2)}, u32[]{:S(2)}) %collective-permute-start.1) | collective-permute-done | bytes 65568 | tf_op jit(solution)/shard_map/while/body/eval_jaxpr/ppermute | solution.py:13
  416.8 11.7 %all-to-all-done.1 = bf16[16,32,8,128]{3,2,1,0:T(8,128)(2,1)S(1)} async-done(((bf16[16,32,8,128]{3,2,1,0:T(8,128)(2,1)}), bf16[16,32,8,128]{3,2,1,0:T(8,128)(2,1)S(1)}, u32[]{:S(2)}, u32[]{:S(2)}) %all-to-all-start.1) | async-done | bytes 1048608 | tf_op jit(solution)/shard_map/while/body/eval_jaxpr/all_to_all | solution.py:36
  439.8 10.1 %collective-permute-done.1 = bf16[8,2,2048]{2,0,1:T(8,128)(2,1)S(1)} collective-permute-done((bf16[8,2,2048]{2,0,1:T(8,128)(2,1)S(1)}, bf16[8,2,2048]{2,0,1:T(8,128)(2,1)S(1)}, u32[]{:S(2)}, u32[]{:S(2)}) %collective-permute-start.1) | collective-permute-done | bytes 65568 | tf_op jit(solution)/shard_map/while/body/eval_jaxpr/ppermute | solution.py:13
  455.3 11.7 %all-to-all-done.1 = bf16[16,32,8,128]{3,2,1,0:T(8,128)(2,1)S(1)} async-done(((bf16[16,32,8,128]{3,2,1,0:T(8,128)(2,1)}), bf16[16,32,8,128]{3,2,1,0:T(8,128)(2,1)S(1)}, u32[]{:S(2)}, u32[]{:S(2)}) %all-to-all-start.1) | async-done | bytes 1048608 | tf_op jit(solution)/shard_map/while/body/eval_jaxpr/all_to_all | solution.py:36
  478.2 7.7 %collective-permute-done.1 = bf16[8,2,2048]{2,0,1:T(8,128)(2,1)S(1)} collective-permute-done((bf16[8,2,2048]{2,0,1:T(8,128)(2,1)S(1)}, bf16[8,2,2048]{2,0,1:T(8,128)(2,1)S(1)}, u32[]{:S(2)}, u32[]{:S(2)}) %collective-permute-start.1) | collective-permute-done | bytes 65568 | tf_op jit(solution)/shard_map/while/body/eval_jaxpr/ppermute | solution.py:13
  491.4 11.7 %all-to-all-done.1 = bf16[16,32,8,128]{3,2,1,0:T(8,128)(2,1)S(1)} async-done(((bf16[16,32,8,128]{3,2,1,0:T(8,128)(2,1)}), bf16[16,32,8,128]{3,2,1,0:T(8,128)(2,1)S(1)}, u32[]{:S(2)}, u32[]{:S(2)}) %all-to-all-start.1) | async-done | bytes 1048608 | tf_op jit(solution)/shard_map/while/body/eval_jaxpr/all_to_all | solution.py:36
  527.6 11.7 %all-to-all-done.1 = bf16[16,32,8,128]{3,2,1,0:T(8,128)(2,1)S(1)} async-done(((bf16[16,32,8,128]{3,2,1,0:T(8,128)(2,1)}), bf16[16,32,8,128]{3,2,1,0:T(8,128)(2,1)S(1)}, u32[]{:S(2)}, u32[]{:S(2)}) %all-to-all-start.1) | async-done | bytes 1048608 | tf_op jit(solution)/shard_map/while/body/eval_jaxpr/all_to_all | solution.py:36
  557.1 9.3 %all-to-all-start.3 = ((f32[128,1,288]{2,1,0:T(1,128)}), f32[128,1,288]{2,1,0:T(1,128)S(1)}, u32[]{:S(2)}, u32[]{:S(2)}) async-start(f32[128,1,288]{2,1,0:T(1,128)} %reshape.225), calls=%async_computation.3 | async-start | bytes 393216 | tf_op jit(solution)/shard_map/all_to_all | solution.py:90
  567.1 9.9 %all-to-all-done.3 = f32[128,1,288]{2,1,0:T(1,128)S(1)} async-done(((f32[128,1,288]{2,1,0:T(1,128)}), f32[128,1,288]{2,1,0:T(1,128)S(1)}, u32[]{:S(2)}, u32[]{:S(2)}) %all-to-all-start.3) | async-done | bytes 147488 | tf_op jit(solution)/shard_map/all_to_all | solution.py:90
  (260 shorter events, 324.4 us)
Async XLA Ops:
  7.6 23.1 %all-to-all-start.2 = ((bf16[16,32,8,128]{3,2,1,0:T(8,128)(2,1)}), bf16[16,32,8,128]{3,2,1,0:T(8,128)(2,1)S(1)}, u32[]{:S(2)}, u32[]{:S(2)}) async-start(bf16[16,32,8,128]{3,2,1,0:T(8,128)(2,1)} %broadcast_in_dim.44), calls=%async_computation.2 | async-start | bytes 2097152 | tf_op jit(solution)/shard_map/all_to_all | solution.py:36
  49.6 19.1 %all-to-all-start = ((bf16[16,32,8,128]{3,2,1,0:T(8,128)(2,1)}), bf16[16,32,8,128]{3,2,1,0:T(8,128)(2,1)S(1)}, u32[]{:S(2)}, u32[]{:S(2)}) async-start(bf16[16,32,8,128]{3,2,1,0:T(8,128)(2,1)} %broadcast_in_dim.52), calls=%async_computation | async-start | bytes 2097152 | tf_op jit(solution)/shard_map/while/body/eval_jaxpr/all_to_all | solution.py:36
  87.7 16.8 %all-to-all-start = ((bf16[16,32,8,128]{3,2,1,0:T(8,128)(2,1)}), bf16[16,32,8,128]{3,2,1,0:T(8,128)(2,1)S(1)}, u32[]{:S(2)}, u32[]{:S(2)}) async-start(bf16[16,32,8,128]{3,2,1,0:T(8,128)(2,1)} %broadcast_in_dim.52), calls=%async_computation | async-start | bytes 2097152 | tf_op jit(solution)/shard_map/while/body/eval_jaxpr/all_to_all | solution.py:36
  113.8 9.6 %collective-permute-start = (bf16[8,2,2048]{2,0,1:T(8,128)(2,1)S(1)}, bf16[8,2,2048]{2,0,1:T(8,128)(2,1)S(1)}, u32[]{:S(2)}, u32[]{:S(2)}) collective-permute-start(bf16[8,2,2048]{2,0,1:T(8,128)(2,1)S(1)} %get-tuple-element.219), channel_id=1, source_target_pairs={{0,16},{16,32},{32,48},{48,64},{64,80},{80,96},{96,112},{1,17},{17... | collective-permute-start | bytes 196616 | tf_op jit(solution)/shard_map/while/body/eval_jaxpr/ppermute | solution.py:13
  125.0 15.5 %all-to-all-start = ((bf16[16,32,8,128]{3,2,1,0:T(8,128)(2,1)}), bf16[16,32,8,128]{3,2,1,0:T(8,128)(2,1)S(1)}, u32[]{:S(2)}, u32[]{:S(2)}) async-start(bf16[16,32,8,128]{3,2,1,0:T(8,128)(2,1)} %broadcast_in_dim.52), calls=%async_computation | async-start | bytes 2097152 | tf_op jit(solution)/shard_map/while/body/eval_jaxpr/all_to_all | solution.py:36
  149.9 8.9 %collective-permute-start = (bf16[8,2,2048]{2,0,1:T(8,128)(2,1)S(1)}, bf16[8,2,2048]{2,0,1:T(8,128)(2,1)S(1)}, u32[]{:S(2)}, u32[]{:S(2)}) collective-permute-start(bf16[8,2,2048]{2,0,1:T(8,128)(2,1)S(1)} %get-tuple-element.219), channel_id=1, source_target_pairs={{0,16},{16,32},{32,48},{48,64},{64,80},{80,96},{96,112},{1,17},{17... | collective-permute-start | bytes 196616 | tf_op jit(solution)/shard_map/while/body/eval_jaxpr/ppermute | solution.py:13
  160.4 16.0 %all-to-all-start = ((bf16[16,32,8,128]{3,2,1,0:T(8,128)(2,1)}), bf16[16,32,8,128]{3,2,1,0:T(8,128)(2,1)S(1)}, u32[]{:S(2)}, u32[]{:S(2)}) async-start(bf16[16,32,8,128]{3,2,1,0:T(8,128)(2,1)} %broadcast_in_dim.52), calls=%async_computation | async-start | bytes 2097152 | tf_op jit(solution)/shard_map/while/body/eval_jaxpr/all_to_all | solution.py:36
  195.7 16.4 %all-to-all-start = ((bf16[16,32,8,128]{3,2,1,0:T(8,128)(2,1)}), bf16[16,32,8,128]{3,2,1,0:T(8,128)(2,1)S(1)}, u32[]{:S(2)}, u32[]{:S(2)}) async-start(bf16[16,32,8,128]{3,2,1,0:T(8,128)(2,1)} %broadcast_in_dim.52), calls=%async_computation | async-start | bytes 2097152 | tf_op jit(solution)/shard_map/while/body/eval_jaxpr/all_to_all | solution.py:36
  231.0 16.8 %all-to-all-start = ((bf16[16,32,8,128]{3,2,1,0:T(8,128)(2,1)}), bf16[16,32,8,128]{3,2,1,0:T(8,128)(2,1)S(1)}, u32[]{:S(2)}, u32[]{:S(2)}) async-start(bf16[16,32,8,128]{3,2,1,0:T(8,128)(2,1)} %broadcast_in_dim.52), calls=%async_computation | async-start | bytes 2097152 | tf_op jit(solution)/shard_map/while/body/eval_jaxpr/all_to_all | solution.py:36
  266.4 17.4 %all-to-all-start = ((bf16[16,32,8,128]{3,2,1,0:T(8,128)(2,1)}), bf16[16,32,8,128]{3,2,1,0:T(8,128)(2,1)S(1)}, u32[]{:S(2)}, u32[]{:S(2)}) async-start(bf16[16,32,8,128]{3,2,1,0:T(8,128)(2,1)} %broadcast_in_dim.52), calls=%async_computation | async-start | bytes 2097152 | tf_op jit(solution)/shard_map/while/body/eval_jaxpr/all_to_all | solution.py:36
  302.5 17.0 %all-to-all-start.1 = ((bf16[16,32,8,128]{3,2,1,0:T(8,128)(2,1)}), bf16[16,32,8,128]{3,2,1,0:T(8,128)(2,1)S(1)}, u32[]{:S(2)}, u32[]{:S(2)}) async-start(bf16[16,32,8,128]{3,2,1,0:T(8,128)(2,1)} %broadcast_in_dim.54), calls=%async_computation.1 | async-start | bytes 2097152 | tf_op jit(solution)/shard_map/while/body/eval_jaxpr/all_to_all | solution.py:36
  328.9 8.5 %collective-permute-start.1 = (bf16[8,2,2048]{2,0,1:T(8,128)(2,1)S(1)}, bf16[8,2,2048]{2,0,1:T(8,128)(2,1)S(1)}, u32[]{:S(2)}, u32[]{:S(2)}) collective-permute-start(bf16[8,2,2048]{2,0,1:T(8,128)(2,1)S(1)} %multiply_convert_fusion.2), channel_id=1, source_target_pairs={{16,0},{32,16},{48,32},{64,48},{80,64},{96,80},{112,96},{17,1},{33... | collective-permute-start | bytes 196616 | tf_op jit(solution)/shard_map/while/body/eval_jaxpr/ppermute | solution.py:13
  339.1 16.2 %all-to-all-start.1 = ((bf16[16,32,8,128]{3,2,1,0:T(8,128)(2,1)}), bf16[16,32,8,128]{3,2,1,0:T(8,128)(2,1)S(1)}, u32[]{:S(2)}, u32[]{:S(2)}) async-start(bf16[16,32,8,128]{3,2,1,0:T(8,128)(2,1)} %broadcast_in_dim.54), calls=%async_computation.1 | async-start | bytes 2097152 | tf_op jit(solution)/shard_map/while/body/eval_jaxpr/all_to_all | solution.py:36
  364.6 9.6 %collective-permute-start.1 = (bf16[8,2,2048]{2,0,1:T(8,128)(2,1)S(1)}, bf16[8,2,2048]{2,0,1:T(8,128)(2,1)S(1)}, u32[]{:S(2)}, u32[]{:S(2)}) collective-permute-start(bf16[8,2,2048]{2,0,1:T(8,128)(2,1)S(1)} %multiply_convert_fusion.2), channel_id=1, source_target_pairs={{16,0},{32,16},{48,32},{64,48},{80,64},{96,80},{112,96},{17,1},{33... | collective-permute-start | bytes 196616 | tf_op jit(solution)/shard_map/while/body/eval_jaxpr/ppermute | solution.py:13
  375.9 15.4 %all-to-all-start.1 = ((bf16[16,32,8,128]{3,2,1,0:T(8,128)(2,1)}), bf16[16,32,8,128]{3,2,1,0:T(8,128)(2,1)S(1)}, u32[]{:S(2)}, u32[]{:S(2)}) async-start(bf16[16,32,8,128]{3,2,1,0:T(8,128)(2,1)} %broadcast_in_dim.54), calls=%async_computation.1 | async-start | bytes 2097152 | tf_op jit(solution)/shard_map/while/body/eval_jaxpr/all_to_all | solution.py:36
  400.6 10.9 %collective-permute-start.1 = (bf16[8,2,2048]{2,0,1:T(8,128)(2,1)S(1)}, bf16[8,2,2048]{2,0,1:T(8,128)(2,1)S(1)}, u32[]{:S(2)}, u32[]{:S(2)}) collective-permute-start(bf16[8,2,2048]{2,0,1:T(8,128)(2,1)S(1)} %multiply_convert_fusion.2), channel_id=1, source_target_pairs={{16,0},{32,16},{48,32},{64,48},{80,64},{96,80},{112,96},{17,1},{33... | collective-permute-start | bytes 196616 | tf_op jit(solution)/shard_map/while/body/eval_jaxpr/ppermute | solution.py:13
  413.2 15.4 %all-to-all-start.1 = ((bf16[16,32,8,128]{3,2,1,0:T(8,128)(2,1)}), bf16[16,32,8,128]{3,2,1,0:T(8,128)(2,1)S(1)}, u32[]{:S(2)}, u32[]{:S(2)}) async-start(bf16[16,32,8,128]{3,2,1,0:T(8,128)(2,1)} %broadcast_in_dim.54), calls=%async_computation.1 | async-start | bytes 2097152 | tf_op jit(solution)/shard_map/while/body/eval_jaxpr/all_to_all | solution.py:36
  437.9 12.1 %collective-permute-start.1 = (bf16[8,2,2048]{2,0,1:T(8,128)(2,1)S(1)}, bf16[8,2,2048]{2,0,1:T(8,128)(2,1)S(1)}, u32[]{:S(2)}, u32[]{:S(2)}) collective-permute-start(bf16[8,2,2048]{2,0,1:T(8,128)(2,1)S(1)} %multiply_convert_fusion.2), channel_id=1, source_target_pairs={{16,0},{32,16},{48,32},{64,48},{80,64},{96,80},{112,96},{17,1},{33... | collective-permute-start | bytes 196616 | tf_op jit(solution)/shard_map/while/body/eval_jaxpr/ppermute | solution.py:13
  451.6 15.4 %all-to-all-start.1 = ((bf16[16,32,8,128]{3,2,1,0:T(8,128)(2,1)}), bf16[16,32,8,128]{3,2,1,0:T(8,128)(2,1)S(1)}, u32[]{:S(2)}, u32[]{:S(2)}) async-start(bf16[16,32,8,128]{3,2,1,0:T(8,128)(2,1)} %broadcast_in_dim.54), calls=%async_computation.1 | async-start | bytes 2097152 | tf_op jit(solution)/shard_map/while/body/eval_jaxpr/all_to_all | solution.py:36
  476.3 9.6 %collective-permute-start.1 = (bf16[8,2,2048]{2,0,1:T(8,128)(2,1)S(1)}, bf16[8,2,2048]{2,0,1:T(8,128)(2,1)S(1)}, u32[]{:S(2)}, u32[]{:S(2)}) collective-permute-start(bf16[8,2,2048]{2,0,1:T(8,128)(2,1)S(1)} %multiply_convert_fusion.2), channel_id=1, source_target_pairs={{16,0},{32,16},{48,32},{64,48},{80,64},{96,80},{112,96},{17,1},{33... | collective-permute-start | bytes 196616 | tf_op jit(solution)/shard_map/while/body/eval_jaxpr/ppermute | solution.py:13
  487.5 15.6 %all-to-all-start.1 = ((bf16[16,32,8,128]{3,2,1,0:T(8,128)(2,1)}), bf16[16,32,8,128]{3,2,1,0:T(8,128)(2,1)S(1)}, u32[]{:S(2)}, u32[]{:S(2)}) async-start(bf16[16,32,8,128]{3,2,1,0:T(8,128)(2,1)} %broadcast_in_dim.54), calls=%async_computation.1 | async-start | bytes 2097152 | tf_op jit(solution)/shard_map/while/body/eval_jaxpr/all_to_all | solution.py:36
  512.5 9.0 %collective-permute-start.1 = (bf16[8,2,2048]{2,0,1:T(8,128)(2,1)S(1)}, bf16[8,2,2048]{2,0,1:T(8,128)(2,1)S(1)}, u32[]{:S(2)}, u32[]{:S(2)}) collective-permute-start(bf16[8,2,2048]{2,0,1:T(8,128)(2,1)S(1)} %multiply_convert_fusion.2), channel_id=1, source_target_pairs={{16,0},{32,16},{48,32},{64,48},{80,64},{96,80},{112,96},{17,1},{33... | collective-permute-start | bytes 196616 | tf_op jit(solution)/shard_map/while/body/eval_jaxpr/ppermute | solution.py:13
  523.1 16.3 %all-to-all-start.1 = ((bf16[16,32,8,128]{3,2,1,0:T(8,128)(2,1)}), bf16[16,32,8,128]{3,2,1,0:T(8,128)(2,1)S(1)}, u32[]{:S(2)}, u32[]{:S(2)}) async-start(bf16[16,32,8,128]{3,2,1,0:T(8,128)(2,1)} %broadcast_in_dim.54), calls=%async_computation.1 | async-start | bytes 2097152 | tf_op jit(solution)/shard_map/while/body/eval_jaxpr/all_to_all | solution.py:36
  557.1 19.9 %all-to-all-start.3 = ((f32[128,1,288]{2,1,0:T(1,128)}), f32[128,1,288]{2,1,0:T(1,128)S(1)}, u32[]{:S(2)}, u32[]{:S(2)}) async-start(f32[128,1,288]{2,1,0:T(1,128)} %reshape.225), calls=%async_computation.3 | async-start | bytes 393216 | tf_op jit(solution)/shard_map/all_to_all | solution.py:90
  (9 other events, 317.6 us)

commit v7 on v6

--- a/solution.py
+++ b/solution.py
@@ -78,11 +78,11 @@
     placed = (slot[:, None] == jnp.arange(owner_count * CAP, dtype=jnp.int32)[None, :]).astype(jnp.bfloat16)
     local_patch = (cell_patch % PATCH_DEV).astype(jnp.float32)
     rows = jnp.concatenate([contrib.T, local_patch[:, None]], axis=1)
-    high = rows.astype(jnp.bfloat16)
-    rest = rows - high.astype(jnp.float32)
-    middle = rest.astype(jnp.bfloat16)
-    low = (rest - middle.astype(jnp.float32)).astype(jnp.bfloat16)
-    parts = jnp.concatenate([high, middle, low], axis=1)
+    high = lax.reduce_precision(rows, exponent_bits=8, mantissa_bits=7)
+    rest = rows - high
+    middle = lax.reduce_precision(rest, exponent_bits=8, mantissa_bits=7)
+    low = rest - middle
+    parts = jnp.concatenate([high, middle, low], axis=1).astype(jnp.bfloat16)
     moved = jnp.einsum("cs,cq->sq", placed, parts, preferred_element_type=jnp.float32)
     width = vec_count + 1
     packed = (moved[:, :width] + moved[:, width:2 * width]) + moved[:, 2 * width:]

time: 583 us -> 583 us (level)
  no operation moved by 1% of the time
where the time goes in v7:
time: 583 us; the launch traced here: 581 us
  waiting for transfers between devices  265 us (45%)
  starting transfers between devices  131 us (22%)
  matrix products  94.9 us (16%)
  local copies, waits for them, and re-layouts  59.8 us (10%)
  other arithmetic  27.4 us (5%)
    all_to_all x15, waiting for transfers between devices, apply_layer(): gathered = lax.all_to_all(copies, 'plane', 0, 0, tiled=True)  192 us
    dot_general x15, matrix products, apply_layer(): jnp.einsum('rkic,rkvwc->vwri', factor, expanded, preferred_element_type=j...  84.9 us
    ppermute x14, waiting for transfers between devices, passed_along(): lax.ppermute(value, axis, [(source, source + steps) for source in range(f...  62.9 us
    ppermute x14, starting transfers between devices, passed_along(): lax.ppermute(value, axis, [(source, source + steps) for source in range(f...  62.3 us
    all_to_all x15, starting transfers between devices, apply_layer(): gathered = lax.all_to_all(copies, 'plane', 0, 0, tiled=True)  59.8 us
    gather x15, local copies, waits for them, and re-layouts, apply_layer(): chosen = jnp.take(gathered, pattern_flat, axis=0, mode='clip')  27 us
    broadcast_in_dim x30, local copies, waits for them, and re-layouts, apply_layer(): jnp.broadcast_to(local_blocks[None], (plane_count,) + local_blocks.shape)  19.4 us
    another operation x15, other arithmetic, apply_layer(): jnp.stack([jnp.concatenate([x_re, -x_im], axis=-1), jnp.concatenate([x_im...  17.3 us
  transfers between devices with their start and end apart: 30, of which 30 were waited for; matrix products, arithmetic and copies ran while one was open for 0% of the time, Pallas kernels for 0%

profile of v7, /device:TPU:1, one launch (start us, length us, event | category | flops | bytes accessed | tf_op | source)
XLA Modules:
  0.0 580.9 jit_solution(10560201608022484354)
XLA Ops:
  15.3 15.4 %all-to-all-done.2 = bf16[16,32,8,128]{3,2,1,0:T(8,128)(2,1)S(1)} async-done(((bf16[16,32,8,128]{3,2,1,0:T(8,128)(2,1)}), bf16[16,32,8,128]{3,2,1,0:T(8,128)(2,1)S(1)}, u32[]{:S(2)}, u32[]{:S(2)}) %all-to-all-start.2) | async-done | bytes 1048608 | tf_op jit(solution)/shard_map/all_to_all | solution.py:36
  40.1 253.0 %while.20 = (s32[]{:T(128)}, bf16[8,2,2048]{2,0,1:T(8,128)(2,1)S(1)}, f32[1,2048]{1,0:T(1,128)S(1)}, f32[8,2,2048]{2,0,1:T(8,128)S(1)}, s32[512]{0:T(512)S(1)}, /*index=5*/bf16[32,16,64,128]{3,2,1,0:T(8,128)(2,1)}, s32[]{:T(128)}) while((s32[]{:T(128)}, bf16[8,2,2048]{2,0,1:T(8,128)(2,1)S(1)}, f32[1,2048]{1,0:T(1,128)S(1)}, ...), condition=%wide.region_1.2_spmd, body=%wide.region_0.1_spmd.sunk | while | flops 139887616 | bytes 24395924 | solution.py:57
  53.3 15.4 %all-to-all-done = bf16[16,32,8,128]{3,2,1,0:T(8,128)(2,1)S(1)} async-done(((bf16[16,32,8,128]{3,2,1,0:T(8,128)(2,1)}), bf16[16,32,8,128]{3,2,1,0:T(8,128)(2,1)S(1)}, u32[]{:S(2)}, u32[]{:S(2)}) %all-to-all-start) | async-done | bytes 1048608 | tf_op jit(solution)/shard_map/while/body/eval_jaxpr/all_to_all | solution.py:36
  91.4 13.1 %all-to-all-done = bf16[16,32,8,128]{3,2,1,0:T(8,128)(2,1)S(1)} async-done(((bf16[16,32,8,128]{3,2,1,0:T(8,128)(2,1)}), bf16[16,32,8,128]{3,2,1,0:T(8,128)(2,1)S(1)}, u32[]{:S(2)}, u32[]{:S(2)}) %all-to-all-start) | async-done | bytes 1048608 | tf_op jit(solution)/shard_map/while/body/eval_jaxpr/all_to_all | solution.py:36
  113.8 8.3 %collective-permute-start = (bf16[8,2,2048]{2,0,1:T(8,128)(2,1)S(1)}, bf16[8,2,2048]{2,0,1:T(8,128)(2,1)S(1)}, u32[]{:S(2)}, u32[]{:S(2)}) collective-permute-start(bf16[8,2,2048]{2,0,1:T(8,128)(2,1)S(1)} %get-tuple-element.220), channel_id=1, source_target_pairs={{0,16},{16,32},{32,48},{48,64},{64,80},{80,96},{96,112},{1,17},{17... | collective-permute-start | bytes 196616 | tf_op jit(solution)/shard_map/while/body/eval_jaxpr/ppermute | solution.py:13
  128.7 11.8 %all-to-all-done = bf16[16,32,8,128]{3,2,1,0:T(8,128)(2,1)S(1)} async-done(((bf16[16,32,8,128]{3,2,1,0:T(8,128)(2,1)}), bf16[16,32,8,128]{3,2,1,0:T(8,128)(2,1)S(1)}, u32[]{:S(2)}, u32[]{:S(2)}) %all-to-all-start) | async-done | bytes 1048608 | tf_op jit(solution)/shard_map/while/body/eval_jaxpr/all_to_all | solution.py:36
  164.0 12.3 %all-to-all-done = bf16[16,32,8,128]{3,2,1,0:T(8,128)(2,1)S(1)} async-done(((bf16[16,32,8,128]{3,2,1,0:T(8,128)(2,1)}), bf16[16,32,8,128]{3,2,1,0:T(8,128)(2,1)S(1)}, u32[]{:S(2)}, u32[]{:S(2)}) %all-to-all-start) | async-done | bytes 1048608 | tf_op jit(solution)/shard_map/while/body/eval_jaxpr/all_to_all | solution.py:36
  199.4 12.7 %all-to-all-done = bf16[16,32,8,128]{3,2,1,0:T(8,128)(2,1)S(1)} async-done(((bf16[16,32,8,128]{3,2,1,0:T(8,128)(2,1)}), bf16[16,32,8,128]{3,2,1,0:T(8,128)(2,1)S(1)}, u32[]{:S(2)}, u32[]{:S(2)}) %all-to-all-start) | async-done | bytes 1048608 | tf_op jit(solution)/shard_map/while/body/eval_jaxpr/all_to_all | solution.py:36
  234.7 13.2 %all-to-all-done = bf16[16,32,8,128]{3,2,1,0:T(8,128)(2,1)S(1)} async-done(((bf16[16,32,8,128]{3,2,1,0:T(8,128)(2,1)}), bf16[16,32,8,128]{3,2,1,0:T(8,128)(2,1)S(1)}, u32[]{:S(2)}, u32[]{:S(2)}) %all-to-all-start) | async-done | bytes 1048608 | tf_op jit(solution)/shard_map/while/body/eval_jaxpr/all_to_all | solution.py:36
  270.0 13.7 %all-to-all-done = bf16[16,32,8,128]{3,2,1,0:T(8,128)(2,1)S(1)} async-done(((bf16[16,32,8,128]{3,2,1,0:T(8,128)(2,1)}), bf16[16,32,8,128]{3,2,1,0:T(8,128)(2,1)S(1)}, u32[]{:S(2)}, u32[]{:S(2)}) %all-to-all-start) | async-done | bytes 1048608 | tf_op jit(solution)/shard_map/while/body/eval_jaxpr/all_to_all | solution.py:36
  293.1 255.6 %while.21 = (s32[]{:T(128)}, bf16[8,2,2048]{2,0,1:T(8,128)(2,1)S(1)}, bf16[8,2,2048]{2,0,1:T(8,128)(2,1)S(1)}, f32[1,2048]{1,0:T(1,128)S(1)}, s32[512]{0:T(512)S...) while((s32[]{:T(128)}, bf16[8,2,2048]{2,0,1:T(8,128)(2,1)S(1)}, bf16[8,2,2048]{2,0,1:T(8,128)(2,1)S(1)}, ...), condition=%wide.region_3.4_spmd, body=%wide.region_2.3_spmd.sunk | while | flops 139920384 | bytes 24854676 | solution.py:64
  306.2 13.4 %all-to-all-done.1 = bf16[16,32,8,128]{3,2,1,0:T(8,128)(2,1)S(1)} async-done(((bf16[16,32,8,128]{3,2,1,0:T(8,128)(2,1)}), bf16[16,32,8,128]{3,2,1,0:T(8,128)(2,1)S(1)}, u32[]{:S(2)}, u32[]{:S(2)}) %all-to-all-start.1) | async-done | bytes 1048608 | tf_op jit(solution)/shard_map/while/body/eval_jaxpr/all_to_all | solution.py:36
  342.8 12.5 %all-to-all-done.1 = bf16[16,32,8,128]{3,2,1,0:T(8,128)(2,1)S(1)} async-done(((bf16[16,32,8,128]{3,2,1,0:T(8,128)(2,1)}), bf16[16,32,8,128]{3,2,1,0:T(8,128)(2,1)S(1)}, u32[]{:S(2)}, u32[]{:S(2)}) %all-to-all-start.1) | async-done | bytes 1048608 | tf_op jit(solution)/shard_map/while/body/eval_jaxpr/all_to_all | solution.py:36
  366.6 7.7 %collective-permute-done.1 = bf16[8,2,2048]{2,0,1:T(8,128)(2,1)S(1)} collective-permute-done((bf16[8,2,2048]{2,0,1:T(8,128)(2,1)S(1)}, bf16[8,2,2048]{2,0,1:T(8,128)(2,1)S(1)}, u32[]{:S(2)}, u32[]{:S(2)}) %collective-permute-start.1) | collective-permute-done | bytes 65568 | tf_op jit(solution)/shard_map/while/body/eval_jaxpr/ppermute | solution.py:13
  379.6 11.7 %all-to-all-done.1 = bf16[16,32,8,128]{3,2,1,0:T(8,128)(2,1)S(1)} async-done(((bf16[16,32,8,128]{3,2,1,0:T(8,128)(2,1)}), bf16[16,32,8,128]{3,2,1,0:T(8,128)(2,1)S(1)}, u32[]{:S(2)}, u32[]{:S(2)}) %all-to-all-start.1) | async-done | bytes 1048608 | tf_op jit(solution)/shard_map/while/body/eval_jaxpr/all_to_all | solution.py:36
  402.6 9.0 %collective-permute-done.1 = bf16[8,2,2048]{2,0,1:T(8,128)(2,1)S(1)} collective-permute-done((bf16[8,2,2048]{2,0,1:T(8,128)(2,1)S(1)}, bf16[8,2,2048]{2,0,1:T(8,128)(2,1)S(1)}, u32[]{:S(2)}, u32[]{:S(2)}) %collective-permute-start.1) | collective-permute-done | bytes 65568 | tf_op jit(solution)/shard_map/while/body/eval_jaxpr/ppermute | solution.py:13
  416.8 11.7 %all-to-all-done.1 = bf16[16,32,8,128]{3,2,1,0:T(8,128)(2,1)S(1)} async-done(((bf16[16,32,8,128]{3,2,1,0:T(8,128)(2,1)}), bf16[16,32,8,128]{3,2,1,0:T(8,128)(2,1)S(1)}, u32[]{:S(2)}, u32[]{:S(2)}) %all-to-all-start.1) | async-done | bytes 1048608 | tf_op jit(solution)/shard_map/while/body/eval_jaxpr/all_to_all | solution.py:36
  439.8 10.1 %collective-permute-done.1 = bf16[8,2,2048]{2,0,1:T(8,128)(2,1)S(1)} collective-permute-done((bf16[8,2,2048]{2,0,1:T(8,128)(2,1)S(1)}, bf16[8,2,2048]{2,0,1:T(8,128)(2,1)S(1)}, u32[]{:S(2)}, u32[]{:S(2)}) %collective-permute-start.1) | collective-permute-done | bytes 65568 | tf_op jit(solution)/shard_map/while/body/eval_jaxpr/ppermute | solution.py:13
  455.3 11.7 %all-to-all-done.1 = bf16[16,32,8,128]{3,2,1,0:T(8,128)(2,1)S(1)} async-done(((bf16[16,32,8,128]{3,2,1,0:T(8,128)(2,1)}), bf16[16,32,8,128]{3,2,1,0:T(8,128)(2,1)S(1)}, u32[]{:S(2)}, u32[]{:S(2)}) %all-to-all-start.1) | async-done | bytes 1048608 | tf_op jit(solution)/shard_map/while/body/eval_jaxpr/all_to_all | solution.py:36
  478.2 7.7 %collective-permute-done.1 = bf16[8,2,2048]{2,0,1:T(8,128)(2,1)S(1)} collective-permute-done((bf16[8,2,2048]{2,0,1:T(8,128)(2,1)S(1)}, bf16[8,2,2048]{2,0,1:T(8,128)(2,1)S(1)}, u32[]{:S(2)}, u32[]{:S(2)}) %collective-permute-start.1) | collective-permute-done | bytes 65568 | tf_op jit(solution)/shard_map/while/body/eval_jaxpr/ppermute | solution.py:13
  491.4 11.7 %all-to-all-done.1 = bf16[16,32,8,128]{3,2,1,0:T(8,128)(2,1)S(1)} async-done(((bf16[16,32,8,128]{3,2,1,0:T(8,128)(2,1)}), bf16[16,32,8,128]{3,2,1,0:T(8,128)(2,1)S(1)}, u32[]{:S(2)}, u32[]{:S(2)}) %all-to-all-start.1) | async-done | bytes 1048608 | tf_op jit(solution)/shard_map/while/body/eval_jaxpr/all_to_all | solution.py:36
  527.6 11.7 %all-to-all-done.1 = bf16[16,32,8,128]{3,2,1,0:T(8,128)(2,1)S(1)} async-done(((bf16[16,32,8,128]{3,2,1,0:T(8,128)(2,1)}), bf16[16,32,8,128]{3,2,1,0:T(8,128)(2,1)S(1)}, u32[]{:S(2)}, u32[]{:S(2)}) %all-to-all-start.1) | async-done | bytes 1048608 | tf_op jit(solution)/shard_map/while/body/eval_jaxpr/all_to_all | solution.py:36
  557.1 9.3 %all-to-all-start.3 = ((f32[128,1,288]{2,1,0:T(1,128)}), f32[128,1,288]{2,1,0:T(1,128)S(1)}, u32[]{:S(2)}, u32[]{:S(2)}) async-start(f32[128,1,288]{2,1,0:T(1,128)} %reshape.225), calls=%async_computation.3 | async-start | bytes 393216 | tf_op jit(solution)/shard_map/all_to_all | solution.py:90
  567.1 9.9 %all-to-all-done.3 = f32[128,1,288]{2,1,0:T(1,128)S(1)} async-done(((f32[128,1,288]{2,1,0:T(1,128)}), f32[128,1,288]{2,1,0:T(1,128)S(1)}, u32[]{:S(2)}, u32[]{:S(2)}) %all-to-all-start.3) | async-done | bytes 147488 | tf_op jit(solution)/shard_map/all_to_all | solution.py:90
  (259 shorter events, 324.4 us)
Async XLA Ops:
  7.6 23.1 %all-to-all-start.2 = ((bf16[16,32,8,128]{3,2,1,0:T(8,128)(2,1)}), bf16[16,32,8,128]{3,2,1,0:T(8,128)(2,1)S(1)}, u32[]{:S(2)}, u32[]{:S(2)}) async-start(bf16[16,32,8,128]{3,2,1,0:T(8,128)(2,1)} %broadcast_in_dim.44), calls=%async_computation.2 | async-start | bytes 2097152 | tf_op jit(solution)/shard_map/all_to_all | solution.py:36
  49.6 19.1 %all-to-all-start = ((bf16[16,32,8,128]{3,2,1,0:T(8,128)(2,1)}), bf16[16,32,8,128]{3,2,1,0:T(8,128)(2,1)S(1)}, u32[]{:S(2)}, u32[]{:S(2)}) async-start(bf16[16,32,8,128]{3,2,1,0:T(8,128)(2,1)} %broadcast_in_dim.52), calls=%async_computation | async-start | bytes 2097152 | tf_op jit(solution)/shard_map/while/body/eval_jaxpr/all_to_all | solution.py:36
  87.7 16.8 %all-to-all-start = ((bf16[16,32,8,128]{3,2,1,0:T(8,128)(2,1)}), bf16[16,32,8,128]{3,2,1,0:T(8,128)(2,1)S(1)}, u32[]{:S(2)}, u32[]{:S(2)}) async-start(bf16[16,32,8,128]{3,2,1,0:T(8,128)(2,1)} %broadcast_in_dim.52), calls=%async_computation | async-start | bytes 2097152 | tf_op jit(solution)/shard_map/while/body/eval_jaxpr/all_to_all | solution.py:36
  113.8 9.6 %collective-permute-start = (bf16[8,2,2048]{2,0,1:T(8,128)(2,1)S(1)}, bf16[8,2,2048]{2,0,1:T(8,128)(2,1)S(1)}, u32[]{:S(2)}, u32[]{:S(2)}) collective-permute-start(bf16[8,2,2048]{2,0,1:T(8,128)(2,1)S(1)} %get-tuple-element.220), channel_id=1, source_target_pairs={{0,16},{16,32},{32,48},{48,64},{64,80},{80,96},{96,112},{1,17},{17... | collective-permute-start | bytes 196616 | tf_op jit(solution)/shard_map/while/body/eval_jaxpr/ppermute | solution.py:13
  125.0 15.5 %all-to-all-start = ((bf16[16,32,8,128]{3,2,1,0:T(8,128)(2,1)}), bf16[16,32,8,128]{3,2,1,0:T(8,128)(2,1)S(1)}, u32[]{:S(2)}, u32[]{:S(2)}) async-start(bf16[16,32,8,128]{3,2,1,0:T(8,128)(2,1)} %broadcast_in_dim.52), calls=%async_computation | async-start | bytes 2097152 | tf_op jit(solution)/shard_map/while/body/eval_jaxpr/all_to_all | solution.py:36
  149.9 8.9 %collective-permute-start = (bf16[8,2,2048]{2,0,1:T(8,128)(2,1)S(1)}, bf16[8,2,2048]{2,0,1:T(8,128)(2,1)S(1)}, u32[]{:S(2)}, u32[]{:S(2)}) collective-permute-start(bf16[8,2,2048]{2,0,1:T(8,128)(2,1)S(1)} %get-tuple-element.220), channel_id=1, source_target_pairs={{0,16},{16,32},{32,48},{48,64},{64,80},{80,96},{96,112},{1,17},{17... | collective-permute-start | bytes 196616 | tf_op jit(solution)/shard_map/while/body/eval_jaxpr/ppermute | solution.py:13
  160.4 16.0 %all-to-all-start = ((bf16[16,32,8,128]{3,2,1,0:T(8,128)(2,1)}), bf16[16,32,8,128]{3,2,1,0:T(8,128)(2,1)S(1)}, u32[]{:S(2)}, u32[]{:S(2)}) async-start(bf16[16,32,8,128]{3,2,1,0:T(8,128)(2,1)} %broadcast_in_dim.52), calls=%async_computation | async-start | bytes 2097152 | tf_op jit(solution)/shard_map/while/body/eval_jaxpr/all_to_all | solution.py:36
  195.7 16.4 %all-to-all-start = ((bf16[16,32,8,128]{3,2,1,0:T(8,128)(2,1)}), bf16[16,32,8,128]{3,2,1,0:T(8,128)(2,1)S(1)}, u32[]{:S(2)}, u32[]{:S(2)}) async-start(bf16[16,32,8,128]{3,2,1,0:T(8,128)(2,1)} %broadcast_in_dim.52), calls=%async_computation | async-start | bytes 2097152 | tf_op jit(solution)/shard_map/while/body/eval_jaxpr/all_to_all | solution.py:36
  231.0 16.8 %all-to-all-start = ((bf16[16,32,8,128]{3,2,1,0:T(8,128)(2,1)}), bf16[16,32,8,128]{3,2,1,0:T(8,128)(2,1)S(1)}, u32[]{:S(2)}, u32[]{:S(2)}) async-start(bf16[16,32,8,128]{3,2,1,0:T(8,128)(2,1)} %broadcast_in_dim.52), calls=%async_computation | async-start | bytes 2097152 | tf_op jit(solution)/shard_map/while/body/eval_jaxpr/all_to_all | solution.py:36
  266.4 17.4 %all-to-all-start = ((bf16[16,32,8,128]{3,2,1,0:T(8,128)(2,1)}), bf16[16,32,8,128]{3,2,1,0:T(8,128)(2,1)S(1)}, u32[]{:S(2)}, u32[]{:S(2)}) async-start(bf16[16,32,8,128]{3,2,1,0:T(8,128)(2,1)} %broadcast_in_dim.52), calls=%async_computation | async-start | bytes 2097152 | tf_op jit(solution)/shard_map/while/body/eval_jaxpr/all_to_all | solution.py:36
  302.5 17.0 %all-to-all-start.1 = ((bf16[16,32,8,128]{3,2,1,0:T(8,128)(2,1)}), bf16[16,32,8,128]{3,2,1,0:T(8,128)(2,1)S(1)}, u32[]{:S(2)}, u32[]{:S(2)}) async-start(bf16[16,32,8,128]{3,2,1,0:T(8,128)(2,1)} %broadcast_in_dim.54), calls=%async_computation.1 | async-start | bytes 2097152 | tf_op jit(solution)/shard_map/while/body/eval_jaxpr/all_to_all | solution.py:36
  328.9 8.5 %collective-permute-start.1 = (bf16[8,2,2048]{2,0,1:T(8,128)(2,1)S(1)}, bf16[8,2,2048]{2,0,1:T(8,128)(2,1)S(1)}, u32[]{:S(2)}, u32[]{:S(2)}) collective-permute-start(bf16[8,2,2048]{2,0,1:T(8,128)(2,1)S(1)} %multiply_convert_fusion.2), channel_id=1, source_target_pairs={{16,0},{32,16},{48,32},{64,48},{80,64},{96,80},{112,96},{17,1},{33... | collective-permute-start | bytes 196616 | tf_op jit(solution)/shard_map/while/body/eval_jaxpr/ppermute | solution.py:13
  339.1 16.2 %all-to-all-start.1 = ((bf16[16,32,8,128]{3,2,1,0:T(8,128)(2,1)}), bf16[16,32,8,128]{3,2,1,0:T(8,128)(2,1)S(1)}, u32[]{:S(2)}, u32[]{:S(2)}) async-start(bf16[16,32,8,128]{3,2,1,0:T(8,128)(2,1)} %broadcast_in_dim.54), calls=%async_computation.1 | async-start | bytes 2097152 | tf_op jit(solution)/shard_map/while/body/eval_jaxpr/all_to_all | solution.py:36
  364.6 9.6 %collective-permute-start.1 = (bf16[8,2,2048]{2,0,1:T(8,128)(2,1)S(1)}, bf16[8,2,2048]{2,0,1:T(8,128)(2,1)S(1)}, u32[]{:S(2)}, u32[]{:S(2)}) collective-permute-start(bf16[8,2,2048]{2,0,1:T(8,128)(2,1)S(1)} %multiply_convert_fusion.2), channel_id=1, source_target_pairs={{16,0},{32,16},{48,32},{64,48},{80,64},{96,80},{112,96},{17,1},{33... | collective-permute-start | bytes 196616 | tf_op jit(solution)/shard_map/while/body/eval_jaxpr/ppermute | solution.py:13
  375.9 15.4 %all-to-all-start.1 = ((bf16[16,32,8,128]{3,2,1,0:T(8,128)(2,1)}), bf16[16,32,8,128]{3,2,1,0:T(8,128)(2,1)S(1)}, u32[]{:S(2)}, u32[]{:S(2)}) async-start(bf16[16,32,8,128]{3,2,1,0:T(8,128)(2,1)} %broadcast_in_dim.54), calls=%async_computation.1 | async-start | bytes 2097152 | tf_op jit(solution)/shard_map/while/body/eval_jaxpr/all_to_all | solution.py:36
  400.6 10.9 %collective-permute-start.1 = (bf16[8,2,2048]{2,0,1:T(8,128)(2,1)S(1)}, bf16[8,2,2048]{2,0,1:T(8,128)(2,1)S(1)}, u32[]{:S(2)}, u32[]{:S(2)}) collective-permute-start(bf16[8,2,2048]{2,0,1:T(8,128)(2,1)S(1)} %multiply_convert_fusion.2), channel_id=1, source_target_pairs={{16,0},{32,16},{48,32},{64,48},{80,64},{96,80},{112,96},{17,1},{33... | collective-permute-start | bytes 196616 | tf_op jit(solution)/shard_map/while/body/eval_jaxpr/ppermute | solution.py:13
  413.2 15.4 %all-to-all-start.1 = ((bf16[16,32,8,128]{3,2,1,0:T(8,128)(2,1)}), bf16[16,32,8,128]{3,2,1,0:T(8,128)(2,1)S(1)}, u32[]{:S(2)}, u32[]{:S(2)}) async-start(bf16[16,32,8,128]{3,2,1,0:T(8,128)(2,1)} %broadcast_in_dim.54), calls=%async_computation.1 | async-start | bytes 2097152 | tf_op jit(solution)/shard_map/while/body/eval_jaxpr/all_to_all | solution.py:36
  437.9 12.1 %collective-permute-start.1 = (bf16[8,2,2048]{2,0,1:T(8,128)(2,1)S(1)}, bf16[8,2,2048]{2,0,1:T(8,128)(2,1)S(1)}, u32[]{:S(2)}, u32[]{:S(2)}) collective-permute-start(bf16[8,2,2048]{2,0,1:T(8,128)(2,1)S(1)} %multiply_convert_fusion.2), channel_id=1, source_target_pairs={{16,0},{32,16},{48,32},{64,48},{80,64},{96,80},{112,96},{17,1},{33... | collective-permute-start | bytes 196616 | tf_op jit(solution)/shard_map/while/body/eval_jaxpr/ppermute | solution.py:13
  451.6 15.4 %all-to-all-start.1 = ((bf16[16,32,8,128]{3,2,1,0:T(8,128)(2,1)}), bf16[16,32,8,128]{3,2,1,0:T(8,128)(2,1)S(1)}, u32[]{:S(2)}, u32[]{:S(2)}) async-start(bf16[16,32,8,128]{3,2,1,0:T(8,128)(2,1)} %broadcast_in_dim.54), calls=%async_computation.1 | async-start | bytes 2097152 | tf_op jit(solution)/shard_map/while/body/eval_jaxpr/all_to_all | solution.py:36
  476.3 9.6 %collective-permute-start.1 = (bf16[8,2,2048]{2,0,1:T(8,128)(2,1)S(1)}, bf16[8,2,2048]{2,0,1:T(8,128)(2,1)S(1)}, u32[]{:S(2)}, u32[]{:S(2)}) collective-permute-start(bf16[8,2,2048]{2,0,1:T(8,128)(2,1)S(1)} %multiply_convert_fusion.2), channel_id=1, source_target_pairs={{16,0},{32,16},{48,32},{64,48},{80,64},{96,80},{112,96},{17,1},{33... | collective-permute-start | bytes 196616 | tf_op jit(solution)/shard_map/while/body/eval_jaxpr/ppermute | solution.py:13
  487.5 15.6 %all-to-all-start.1 = ((bf16[16,32,8,128]{3,2,1,0:T(8,128)(2,1)}), bf16[16,32,8,128]{3,2,1,0:T(8,128)(2,1)S(1)}, u32[]{:S(2)}, u32[]{:S(2)}) async-start(bf16[16,32,8,128]{3,2,1,0:T(8,128)(2,1)} %broadcast_in_dim.54), calls=%async_computation.1 | async-start | bytes 2097152 | tf_op jit(solution)/shard_map/while/body/eval_jaxpr/all_to_all | solution.py:36
  512.5 9.0 %collective-permute-start.1 = (bf16[8,2,2048]{2,0,1:T(8,128)(2,1)S(1)}, bf16[8,2,2048]{2,0,1:T(8,128)(2,1)S(1)}, u32[]{:S(2)}, u32[]{:S(2)}) collective-permute-start(bf16[8,2,2048]{2,0,1:T(8,128)(2,1)S(1)} %multiply_convert_fusion.2), channel_id=1, source_target_pairs={{16,0},{32,16},{48,32},{64,48},{80,64},{96,80},{112,96},{17,1},{33... | collective-permute-start | bytes 196616 | tf_op jit(solution)/shard_map/while/body/eval_jaxpr/ppermute | solution.py:13
  523.1 16.3 %all-to-all-start.1 = ((bf16[16,32,8,128]{3,2,1,0:T(8,128)(2,1)}), bf16[16,32,8,128]{3,2,1,0:T(8,128)(2,1)S(1)}, u32[]{:S(2)}, u32[]{:S(2)}) async-start(bf16[16,32,8,128]{3,2,1,0:T(8,128)(2,1)} %broadcast_in_dim.54), calls=%async_computation.1 | async-start | bytes 2097152 | tf_op jit(solution)/shard_map/while/body/eval_jaxpr/all_to_all | solution.py:36
  557.1 19.9 %all-to-all-start.3 = ((f32[128,1,288]{2,1,0:T(1,128)}), f32[128,1,288]{2,1,0:T(1,128)S(1)}, u32[]{:S(2)}, u32[]{:S(2)}) async-start(f32[128,1,288]{2,1,0:T(1,128)} %reshape.225), calls=%async_computation.3 | async-start | bytes 393216 | tf_op jit(solution)/shard_map/all_to_all | solution.py:90
  (9 other events, 317.6 us)

commit v8 on v7

--- a/solution.py
+++ b/solution.py
@@ -29,6 +29,10 @@
     imag_part = coeff[0] * toar_f32[:, 1] + coeff[1] * toar_f32[:, 0]
     source = jnp.stack([real_part, imag_part], axis=1)
 
+    lanes = jnp.arange(2 * block_cells)
+    flip = jnp.where(lanes < block_cells, 1.0, -1.0).astype(factor.dtype)
+    paired = jnp.stack([factor * flip, jnp.roll(factor, block_cells, axis=-1)], axis=2)
+
     def apply_layer(incoming):
         local_blocks = incoming.reshape(vec_count, 2, block_rows, block_cells).transpose(2, 0, 1, 3)
         local_blocks = local_blocks.reshape(block_rows, vec_count, 2 * block_cells)
@@ -37,14 +41,8 @@
         gathered = gathered.reshape(plane_count * block_rows, vec_count, 2 * block_cells)
         chosen = jnp.take(gathered, pattern_flat, axis=0, mode="clip")
         chosen = chosen.reshape(block_rows, -1, vec_count, 2 * block_cells)
-        x_re = chosen[..., :block_cells]
-        x_im = chosen[..., block_cells:]
-        expanded = jnp.stack(
-            [jnp.concatenate([x_re, -x_im], axis=-1), jnp.concatenate([x_im, x_re], axis=-1)],
-            axis=3,
-        )
         out = jnp.einsum(
-            "rkic,rkvwc->vwri", factor, expanded, preferred_element_type=jnp.float32
+            "rkwic,rkvc->vwri", paired, chosen, preferred_element_type=jnp.float32
         )
         return out.reshape(vec_count, 2, block_rows * block_cells)
 

time: 583 us -> 656 us (1.13)
  matrix products: 94.9 us -> 161 us
  local copies, waits for them, and re-layouts: 59.8 us -> 74.7 us
  waiting for transfers between devices: 265 us -> 251 us
    dot_general x15, matrix products: 84.9 us -> 151 us  [apply_layer(): jnp.einsum('rkwic,rkvc->vwri', paired, chosen, preferred_element_type=jnp...]
    all_to_all x15, waiting for transfers between devices: 192 us -> 178 us  [apply_layer(): gathered = lax.all_to_all(copies, 'plane', 0, 0, tiled=True)]
    slice x0 -> x1, local copies, waits for them, and re-layouts: none -> 13.5 us  [shards(): jnp.roll(factor, block_cells, axis=-1)]
    mul x0 -> x1, other arithmetic: none -> 7.16 us  [shards(): factor * flip]
    neg x15 -> x0, other arithmetic: 6.76 us -> none  [apply_layer(): -x_im]
    another operation x17 -> x4, other arithmetic: 17.4 us -> 23.1 us  [the longest x2 23 us: shards(): jnp.stack([factor * flip, jnp.roll(factor, block_cells, axis=-1)], axis=2)]
  transfers between devices with their start and end apart: 30 -> 30, of which waited for: 30 -> 30; matrix products, arithmetic and copies ran while one was open for 0% -> 2% of each run, Pallas kernels for 0% -> 0%
where the time goes in v8:
time: 656 us; the launch traced here: 654 us
  waiting for transfers between devices  251 us (38%)
  matrix products  161 us (25%)
  starting transfers between devices  131 us (20%)
  local copies, waits for them, and re-layouts  74.7 us (11%)
  other arithmetic  32.8 us (5%)
    all_to_all x15, waiting for transfers between devices, apply_layer(): gathered = lax.all_to_all(copies, 'plane', 0, 0, tiled=True)  178 us
    dot_general x15, matrix products, apply_layer(): jnp.einsum('rkwic,rkvc->vwri', paired, chosen, preferred_element_type=jnp...  151 us
    ppermute x14, waiting for transfers between devices, passed_along(): lax.ppermute(value, axis, [(source, source + steps) for source in range(f...  63 us
    ppermute x14, starting transfers between devices, passed_along(): lax.ppermute(value, axis, [(source, source + steps) for source in range(f...  62.3 us
    all_to_all x15, starting transfers between devices, apply_layer(): gathered = lax.all_to_all(copies, 'plane', 0, 0, tiled=True)  59.8 us
    gather x15, local copies, waits for them, and re-layouts, apply_layer(): chosen = jnp.take(gathered, pattern_flat, axis=0, mode='clip')  27 us
    another operation x2, other arithmetic, shards(): jnp.stack([factor * flip, jnp.roll(factor, block_cells, axis=-1)], axis=2)  23 us
    broadcast_in_dim x30, local copies, waits for them, and re-layouts, apply_layer(): jnp.broadcast_to(local_blocks[None], (plane_count,) + local_blocks.shape)  19.5 us
  transfers between devices with their start and end apart: 30, of which 30 were waited for; matrix products, arithmetic and copies ran while one was open for 2% of the time, Pallas kernels for 0%

profile of v8, /device:TPU:1, one launch (start us, length us, event | category | flops | bytes accessed | tf_op | source)
XLA Modules:
  0.0 654.1 jit_solution(9934731926830685082)
XLA Ops:
  3.8 13.5 %fusion.29 = (bf16[32,16,64,64]{3,2,1,0:T(8,128)(2,1)}, bf16[32,16,64,64]{3,2,1,0:T(8,128)(2,1)}) fusion(bf16[32,16,64,128]{3,2,1,0:T(8,128)(2,1)} %bitcast.141), kind=kLoop, calls=%fused_computation.76 | loop fusion | bytes 16777216 | tf_op jit(solution)/shard_map/jit(_roll_static)/slice | solution.py:34
  45.9 13.7 %pad_maximum_fusion = bf16[32,16,2,64,128]{4,3,1,2,0:T(8,128)(2,1)} fusion(bf16[32,16,1,64,128]{4,3,1,2,0:T(8,128)(2,1)} %maximum_bitcast_fusion, bf16[32,16,1,64,128]{4,3,1,2,0:T(8,128)(2,1)} %bitcast_multiply_fusion), kind=kLoop, calls=%fused_computation.16 | loop fusion | flops 8388608 | bytes 33554432 | tf_op jit(solution)/shard_map/stack | solution.py:34
  63.2 10.2 %fusion.9 = bf16[8,2,32,64]{3,0,1,2:T(8,128)(2,1)S(1)} fusion(bf16[32,16,8,128,1]{3,2,1,4,0:T(8,128)(2,1)S(1)} %bitcast.147, bf16[32,16,1,64,128]{4,3,1,2,0:T(8,128)(2,1)} %maximum_bitcast_fusion, bf16[32,16,1,64,128]{4,3,1,2,0:T(8,128)(2,1)} %bitcast_multiply_fusion), kind=kOutput, calls=%fused_computation.28 | convolution fusion | flops 167804928 | bytes 17891328 | tf_op jit(solution)/shard_map/rkwic,rkvc->vwri/dot_general | solution.py:44
  73.7 272.9 %while.20 = (s32[]{:T(128)}, bf16[8,2,2048]{2,0,1:T(8,128)(2,1)S(1)}, f32[1,2048]{1,0:T(1,128)S(1)}, f32[8,2,2048]{2,0,1:T(8,128)S(1)}, s32[512]{0:T(512)S(1)}, /*index=5*/bf16[32,16,2,64,128]{4,3,1,2,0:T(8,128)(2,1)}, s32[]{:T(128)}) while((s32[]{:T(128)}, bf16[8,2,2048]{2,0,1:T(8,128)(2,1)S(1)}, f32[1,2048]{1,0:T(1,128)S(1)}, ...), condition=%wide.region_1.2_spmd, body=%wide.region_0.1_spmd.sunk | while | flops 134382592 | bytes 25444500 | solution.py:55
  86.9 15.4 %all-to-all-done = bf16[16,32,8,128]{3,2,1,0:T(8,128)(2,1)S(1)} async-done(((bf16[16,32,8,128]{3,2,1,0:T(8,128)(2,1)}), bf16[16,32,8,128]{3,2,1,0:T(8,128)(2,1)S(1)}, u32[]{:S(2)}, u32[]{:S(2)}) %all-to-all-start) | async-done | bytes 1048608 | tf_op jit(solution)/shard_map/while/body/eval_jaxpr/all_to_all | solution.py:40
  104.1 10.1 %fusion.43 = bf16[8,2,32,64]{3,0,1,2:T(8,128)(2,1)S(1)} fusion(bf16[32,16,8,128,1]{3,2,1,4,0:T(8,128)(2,1)S(1)} %bitcast.137, bf16[32,16,2,64,128]{4,3,1,2,0:T(8,128)(2,1)} %get-tuple-element.198), kind=kOutput, calls=%fused_computation.5.clone.1 | convolution fusion | flops 134250496 | bytes 17891328 | tf_op jit(solution)/shard_map/while/body/eval_jaxpr/rkwic,rkvc->vwri/dot_general | solution.py:44
  127.8 13.1 %all-to-all-done = bf16[16,32,8,128]{3,2,1,0:T(8,128)(2,1)S(1)} async-done(((bf16[16,32,8,128]{3,2,1,0:T(8,128)(2,1)}), bf16[16,32,8,128]{3,2,1,0:T(8,128)(2,1)S(1)}, u32[]{:S(2)}, u32[]{:S(2)}) %all-to-all-start) | async-done | bytes 1048608 | tf_op jit(solution)/shard_map/while/body/eval_jaxpr/all_to_all | solution.py:40
  142.7 10.1 %fusion.43 = bf16[8,2,32,64]{3,0,1,2:T(8,128)(2,1)S(1)} fusion(bf16[32,16,8,128,1]{3,2,1,4,0:T(8,128)(2,1)S(1)} %bitcast.137, bf16[32,16,2,64,128]{4,3,1,2,0:T(8,128)(2,1)} %get-tuple-element.198), kind=kOutput, calls=%fused_computation.5.clone.1 | convolution fusion | flops 134250496 | bytes 17891328 | tf_op jit(solution)/shard_map/while/body/eval_jaxpr/rkwic,rkvc->vwri/dot_general | solution.py:44
  168.0 11.8 %all-to-all-done = bf16[16,32,8,128]{3,2,1,0:T(8,128)(2,1)S(1)} async-done(((bf16[16,32,8,128]{3,2,1,0:T(8,128)(2,1)}), bf16[16,32,8,128]{3,2,1,0:T(8,128)(2,1)S(1)}, u32[]{:S(2)}, u32[]{:S(2)}) %all-to-all-start) | async-done | bytes 1048608 | tf_op jit(solution)/shard_map/while/body/eval_jaxpr/all_to_all | solution.py:40
  181.6 10.1 %fusion.43 = bf16[8,2,32,64]{3,0,1,2:T(8,128)(2,1)S(1)} fusion(bf16[32,16,8,128,1]{3,2,1,4,0:T(8,128)(2,1)S(1)} %bitcast.137, bf16[32,16,2,64,128]{4,3,1,2,0:T(8,128)(2,1)} %get-tuple-element.198), kind=kOutput, calls=%fused_computation.5.clone.1 | convolution fusion | flops 134250496 | bytes 17891328 | tf_op jit(solution)/shard_map/while/body/eval_jaxpr/rkwic,rkvc->vwri/dot_general | solution.py:44
  206.2 12.3 %all-to-all-done = bf16[16,32,8,128]{3,2,1,0:T(8,128)(2,1)S(1)} async-done(((bf16[16,32,8,128]{3,2,1,0:T(8,128)(2,1)}), bf16[16,32,8,128]{3,2,1,0:T(8,128)(2,1)S(1)}, u32[]{:S(2)}, u32[]{:S(2)}) %all-to-all-start) | async-done | bytes 1048608 | tf_op jit(solution)/shard_map/while/body/eval_jaxpr/all_to_all | solution.py:40
  244.3 12.7 %all-to-all-done = bf16[16,32,8,128]{3,2,1,0:T(8,128)(2,1)S(1)} async-done(((bf16[16,32,8,128]{3,2,1,0:T(8,128)(2,1)}), bf16[16,32,8,128]{3,2,1,0:T(8,128)(2,1)S(1)}, u32[]{:S(2)}, u32[]{:S(2)}) %all-to-all-start) | async-done | bytes 1048608 | tf_op jit(solution)/shard_map/while/body/eval_jaxpr/all_to_all | solution.py:40
  282.5 13.2 %all-to-all-done = bf16[16,32,8,128]{3,2,1,0:T(8,128)(2,1)S(1)} async-done(((bf16[16,32,8,128]{3,2,1,0:T(8,128)(2,1)}), bf16[16,32,8,128]{3,2,1,0:T(8,128)(2,1)S(1)}, u32[]{:S(2)}, u32[]{:S(2)}) %all-to-all-start) | async-done | bytes 1048608 | tf_op jit(solution)/shard_map/while/body/eval_jaxpr/all_to_all | solution.py:40
  320.7 13.7 %all-to-all-done = bf16[16,32,8,128]{3,2,1,0:T(8,128)(2,1)S(1)} async-done(((bf16[16,32,8,128]{3,2,1,0:T(8,128)(2,1)}), bf16[16,32,8,128]{3,2,1,0:T(8,128)(2,1)S(1)}, u32[]{:S(2)}, u32[]{:S(2)}) %all-to-all-start) | async-done | bytes 1048608 | tf_op jit(solution)/shard_map/while/body/eval_jaxpr/all_to_all | solution.py:40
  336.2 10.1 %fusion.43 = bf16[8,2,32,64]{3,0,1,2:T(8,128)(2,1)S(1)} fusion(bf16[32,16,8,128,1]{3,2,1,4,0:T(8,128)(2,1)S(1)} %bitcast.137, bf16[32,16,2,64,128]{4,3,1,2,0:T(8,128)(2,1)} %get-tuple-element.198), kind=kOutput, calls=%fused_computation.5.clone.1 | convolution fusion | flops 134250496 | bytes 17891328 | tf_op jit(solution)/shard_map/while/body/eval_jaxpr/rkwic,rkvc->vwri/dot_general | solution.py:44
  346.6 275.3 %while.21 = (s32[]{:T(128)}, bf16[8,2,2048]{2,0,1:T(8,128)(2,1)S(1)}, bf16[8,2,2048]{2,0,1:T(8,128)(2,1)S(1)}, f32[1,2048]{1,0:T(1,128)S(1)}, s32[512]{0:T(512)S...) while((s32[]{:T(128)}, bf16[8,2,2048]{2,0,1:T(8,128)(2,1)S(1)}, bf16[8,2,2048]{2,0,1:T(8,128)(2,1)S(1)}, ...), condition=%wide.region_3.4_spmd, body=%wide.region_2.3_spmd.sunk | while | flops 134415360 | bytes 25903252 | solution.py:62
  359.5 13.4 %all-to-all-done.1 = bf16[16,32,8,128]{3,2,1,0:T(8,128)(2,1)S(1)} async-done(((bf16[16,32,8,128]{3,2,1,0:T(8,128)(2,1)}), bf16[16,32,8,128]{3,2,1,0:T(8,128)(2,1)S(1)}, u32[]{:S(2)}, u32[]{:S(2)}) %all-to-all-start.1) | async-done | bytes 1048608 | tf_op jit(solution)/shard_map/while/body/eval_jaxpr/all_to_all | solution.py:40
  398.9 12.5 %all-to-all-done.1 = bf16[16,32,8,128]{3,2,1,0:T(8,128)(2,1)S(1)} async-done(((bf16[16,32,8,128]{3,2,1,0:T(8,128)(2,1)}), bf16[16,32,8,128]{3,2,1,0:T(8,128)(2,1)S(1)}, u32[]{:S(2)}, u32[]{:S(2)}) %all-to-all-start.1) | async-done | bytes 1048608 | tf_op jit(solution)/shard_map/while/body/eval_jaxpr/all_to_all | solution.py:40
  438.5 11.7 %all-to-all-done.1 = bf16[16,32,8,128]{3,2,1,0:T(8,128)(2,1)S(1)} async-done(((bf16[16,32,8,128]{3,2,1,0:T(8,128)(2,1)}), bf16[16,32,8,128]{3,2,1,0:T(8,128)(2,1)S(1)}, u32[]{:S(2)}, u32[]{:S(2)}) %all-to-all-start.1) | async-done | bytes 1048608 | tf_op jit(solution)/shard_map/while/body/eval_jaxpr/all_to_all | solution.py:40
  478.5 11.7 %all-to-all-done.1 = bf16[16,32,8,128]{3,2,1,0:T(8,128)(2,1)S(1)} async-done(((bf16[16,32,8,128]{3,2,1,0:T(8,128)(2,1)}), bf16[16,32,8,128]{3,2,1,0:T(8,128)(2,1)S(1)}, u32[]{:S(2)}, u32[]{:S(2)}) %all-to-all-start.1) | async-done | bytes 1048608 | tf_op jit(solution)/shard_map/while/body/eval_jaxpr/all_to_all | solution.py:40
  504.3 10.1 %collective-permute-done.1 = bf16[8,2,2048]{2,0,1:T(8,128)(2,1)S(1)} collective-permute-done((bf16[8,2,2048]{2,0,1:T(8,128)(2,1)S(1)}, bf16[8,2,2048]{2,0,1:T(8,128)(2,1)S(1)}, u32[]{:S(2)}, u32[]{:S(2)}) %collective-permute-start.1) | collective-permute-done | bytes 65568 | tf_op jit(solution)/shard_map/while/body/eval_jaxpr/ppermute | solution.py:13
  519.8 11.7 %all-to-all-done.1 = bf16[16,32,8,128]{3,2,1,0:T(8,128)(2,1)S(1)} async-done(((bf16[16,32,8,128]{3,2,1,0:T(8,128)(2,1)}), bf16[16,32,8,128]{3,2,1,0:T(8,128)(2,1)S(1)}, u32[]{:S(2)}, u32[]{:S(2)}) %all-to-all-start.1) | async-done | bytes 1048608 | tf_op jit(solution)/shard_map/while/body/eval_jaxpr/all_to_all | solution.py:40
  558.8 11.7 %all-to-all-done.1 = bf16[16,32,8,128]{3,2,1,0:T(8,128)(2,1)S(1)} async-done(((bf16[16,32,8,128]{3,2,1,0:T(8,128)(2,1)}), bf16[16,32,8,128]{3,2,1,0:T(8,128)(2,1)S(1)}, u32[]{:S(2)}, u32[]{:S(2)}) %all-to-all-start.1) | async-done | bytes 1048608 | tf_op jit(solution)/shard_map/while/body/eval_jaxpr/all_to_all | solution.py:40
  597.8 11.7 %all-to-all-done.1 = bf16[16,32,8,128]{3,2,1,0:T(8,128)(2,1)S(1)} async-done(((bf16[16,32,8,128]{3,2,1,0:T(8,128)(2,1)}), bf16[16,32,8,128]{3,2,1,0:T(8,128)(2,1)S(1)}, u32[]{:S(2)}, u32[]{:S(2)}) %all-to-all-start.1) | async-done | bytes 1048608 | tf_op jit(solution)/shard_map/while/body/eval_jaxpr/all_to_all | solution.py:40
  (236 shorter events, 387.0 us)
Async XLA Ops:
  38.3 23.1 %all-to-all-start.2 = ((bf16[16,32,8,128]{3,2,1,0:T(8,128)(2,1)}), bf16[16,32,8,128]{3,2,1,0:T(8,128)(2,1)S(1)}, u32[]{:S(2)}, u32[]{:S(2)}) async-start(bf16[16,32,8,128]{3,2,1,0:T(8,128)(2,1)} %broadcast_in_dim.53), calls=%async_computation.2 | async-start | bytes 2097152 | tf_op jit(solution)/shard_map/all_to_all | solution.py:40
  83.2 19.1 %all-to-all-start = ((bf16[16,32,8,128]{3,2,1,0:T(8,128)(2,1)}), bf16[16,32,8,128]{3,2,1,0:T(8,128)(2,1)S(1)}, u32[]{:S(2)}, u32[]{:S(2)}) async-start(bf16[16,32,8,128]{3,2,1,0:T(8,128)(2,1)} %broadcast_in_dim.65), calls=%async_computation | async-start | bytes 2097152 | tf_op jit(solution)/shard_map/while/body/eval_jaxpr/all_to_all | solution.py:40
  124.1 16.8 %all-to-all-start = ((bf16[16,32,8,128]{3,2,1,0:T(8,128)(2,1)}), bf16[16,32,8,128]{3,2,1,0:T(8,128)(2,1)S(1)}, u32[]{:S(2)}, u32[]{:S(2)}) async-start(bf16[16,32,8,128]{3,2,1,0:T(8,128)(2,1)} %broadcast_in_dim.65), calls=%async_computation | async-start | bytes 2097152 | tf_op jit(solution)/shard_map/while/body/eval_jaxpr/all_to_all | solution.py:40
  153.1 9.6 %collective-permute-start = (bf16[8,2,2048]{2,0,1:T(8,128)(2,1)S(1)}, bf16[8,2,2048]{2,0,1:T(8,128)(2,1)S(1)}, u32[]{:S(2)}, u32[]{:S(2)}) collective-permute-start(bf16[8,2,2048]{2,0,1:T(8,128)(2,1)S(1)} %get-tuple-element.187), channel_id=1, source_target_pairs={{0,16},{16,32},{32,48},{48,64},{64,80},{80,96},{96,112},{1,17},{17... | collective-permute-start | bytes 196616 | tf_op jit(solution)/shard_map/while/body/eval_jaxpr/ppermute | solution.py:13
  164.3 15.5 %all-to-all-start = ((bf16[16,32,8,128]{3,2,1,0:T(8,128)(2,1)}), bf16[16,32,8,128]{3,2,1,0:T(8,128)(2,1)S(1)}, u32[]{:S(2)}, u32[]{:S(2)}) async-start(bf16[16,32,8,128]{3,2,1,0:T(8,128)(2,1)} %broadcast_in_dim.65), calls=%async_computation | async-start | bytes 2097152 | tf_op jit(solution)/shard_map/while/body/eval_jaxpr/all_to_all | solution.py:40
  192.0 8.9 %collective-permute-start = (bf16[8,2,2048]{2,0,1:T(8,128)(2,1)S(1)}, bf16[8,2,2048]{2,0,1:T(8,128)(2,1)S(1)}, u32[]{:S(2)}, u32[]{:S(2)}) collective-permute-start(bf16[8,2,2048]{2,0,1:T(8,128)(2,1)S(1)} %get-tuple-element.187), channel_id=1, source_target_pairs={{0,16},{16,32},{32,48},{48,64},{64,80},{80,96},{96,112},{1,17},{17... | collective-permute-start | bytes 196616 | tf_op jit(solution)/shard_map/while/body/eval_jaxpr/ppermute | solution.py:13
  202.5 16.0 %all-to-all-start = ((bf16[16,32,8,128]{3,2,1,0:T(8,128)(2,1)}), bf16[16,32,8,128]{3,2,1,0:T(8,128)(2,1)S(1)}, u32[]{:S(2)}, u32[]{:S(2)}) async-start(bf16[16,32,8,128]{3,2,1,0:T(8,128)(2,1)} %broadcast_in_dim.65), calls=%async_computation | async-start | bytes 2097152 | tf_op jit(solution)/shard_map/while/body/eval_jaxpr/all_to_all | solution.py:40
  240.7 16.4 %all-to-all-start = ((bf16[16,32,8,128]{3,2,1,0:T(8,128)(2,1)}), bf16[16,32,8,128]{3,2,1,0:T(8,128)(2,1)S(1)}, u32[]{:S(2)}, u32[]{:S(2)}) async-start(bf16[16,32,8,128]{3,2,1,0:T(8,128)(2,1)} %broadcast_in_dim.65), calls=%async_computation | async-start | bytes 2097152 | tf_op jit(solution)/shard_map/while/body/eval_jaxpr/all_to_all | solution.py:40
  278.8 16.8 %all-to-all-start = ((bf16[16,32,8,128]{3,2,1,0:T(8,128)(2,1)}), bf16[16,32,8,128]{3,2,1,0:T(8,128)(2,1)S(1)}, u32[]{:S(2)}, u32[]{:S(2)}) async-start(bf16[16,32,8,128]{3,2,1,0:T(8,128)(2,1)} %broadcast_in_dim.65), calls=%async_computation | async-start | bytes 2097152 | tf_op jit(solution)/shard_map/while/body/eval_jaxpr/all_to_all | solution.py:40
  317.0 17.4 %all-to-all-start = ((bf16[16,32,8,128]{3,2,1,0:T(8,128)(2,1)}), bf16[16,32,8,128]{3,2,1,0:T(8,128)(2,1)S(1)}, u32[]{:S(2)}, u32[]{:S(2)}) async-start(bf16[16,32,8,128]{3,2,1,0:T(8,128)(2,1)} %broadcast_in_dim.65), calls=%async_computation | async-start | bytes 2097152 | tf_op jit(solution)/shard_map/while/body/eval_jaxpr/all_to_all | solution.py:40
  355.8 17.0 %all-to-all-start.1 = ((bf16[16,32,8,128]{3,2,1,0:T(8,128)(2,1)}), bf16[16,32,8,128]{3,2,1,0:T(8,128)(2,1)S(1)}, u32[]{:S(2)}, u32[]{:S(2)}) async-start(bf16[16,32,8,128]{3,2,1,0:T(8,128)(2,1)} %broadcast_in_dim.67), calls=%async_computation.1 | async-start | bytes 2097152 | tf_op jit(solution)/shard_map/while/body/eval_jaxpr/all_to_all | solution.py:40
  385.0 8.6 %collective-permute-start.1 = (bf16[8,2,2048]{2,0,1:T(8,128)(2,1)S(1)}, bf16[8,2,2048]{2,0,1:T(8,128)(2,1)S(1)}, u32[]{:S(2)}, u32[]{:S(2)}) collective-permute-start(bf16[8,2,2048]{2,0,1:T(8,128)(2,1)S(1)} %multiply_convert_fusion.2), channel_id=1, source_target_pairs={{16,0},{32,16},{48,32},{64,48},{80,64},{96,80},{112,96},{17,1},{33... | collective-permute-start | bytes 196616 | tf_op jit(solution)/shard_map/while/body/eval_jaxpr/ppermute | solution.py:13
  395.2 16.2 %all-to-all-start.1 = ((bf16[16,32,8,128]{3,2,1,0:T(8,128)(2,1)}), bf16[16,32,8,128]{3,2,1,0:T(8,128)(2,1)S(1)}, u32[]{:S(2)}, u32[]{:S(2)}) async-start(bf16[16,32,8,128]{3,2,1,0:T(8,128)(2,1)} %broadcast_in_dim.67), calls=%async_computation.1 | async-start | bytes 2097152 | tf_op jit(solution)/shard_map/while/body/eval_jaxpr/all_to_all | solution.py:40
  423.5 9.6 %collective-permute-start.1 = (bf16[8,2,2048]{2,0,1:T(8,128)(2,1)S(1)}, bf16[8,2,2048]{2,0,1:T(8,128)(2,1)S(1)}, u32[]{:S(2)}, u32[]{:S(2)}) collective-permute-start(bf16[8,2,2048]{2,0,1:T(8,128)(2,1)S(1)} %multiply_convert_fusion.2), channel_id=1, source_target_pairs={{16,0},{32,16},{48,32},{64,48},{80,64},{96,80},{112,96},{17,1},{33... | collective-permute-start | bytes 196616 | tf_op jit(solution)/shard_map/while/body/eval_jaxpr/ppermute | solution.py:13
  434.8 15.4 %all-to-all-start.1 = ((bf16[16,32,8,128]{3,2,1,0:T(8,128)(2,1)}), bf16[16,32,8,128]{3,2,1,0:T(8,128)(2,1)S(1)}, u32[]{:S(2)}, u32[]{:S(2)}) async-start(bf16[16,32,8,128]{3,2,1,0:T(8,128)(2,1)} %broadcast_in_dim.67), calls=%async_computation.1 | async-start | bytes 2097152 | tf_op jit(solution)/shard_map/while/body/eval_jaxpr/all_to_all | solution.py:40
  462.3 10.9 %collective-permute-start.1 = (bf16[8,2,2048]{2,0,1:T(8,128)(2,1)S(1)}, bf16[8,2,2048]{2,0,1:T(8,128)(2,1)S(1)}, u32[]{:S(2)}, u32[]{:S(2)}) collective-permute-start(bf16[8,2,2048]{2,0,1:T(8,128)(2,1)S(1)} %multiply_convert_fusion.2), channel_id=1, source_target_pairs={{16,0},{32,16},{48,32},{64,48},{80,64},{96,80},{112,96},{17,1},{33... | collective-permute-start | bytes 196616 | tf_op jit(solution)/shard_map/while/body/eval_jaxpr/ppermute | solution.py:13
  474.9 15.4 %all-to-all-start.1 = ((bf16[16,32,8,128]{3,2,1,0:T(8,128)(2,1)}), bf16[16,32,8,128]{3,2,1,0:T(8,128)(2,1)S(1)}, u32[]{:S(2)}, u32[]{:S(2)}) async-start(bf16[16,32,8,128]{3,2,1,0:T(8,128)(2,1)} %broadcast_in_dim.67), calls=%async_computation.1 | async-start | bytes 2097152 | tf_op jit(solution)/shard_map/while/body/eval_jaxpr/all_to_all | solution.py:40
  502.4 12.1 %collective-permute-start.1 = (bf16[8,2,2048]{2,0,1:T(8,128)(2,1)S(1)}, bf16[8,2,2048]{2,0,1:T(8,128)(2,1)S(1)}, u32[]{:S(2)}, u32[]{:S(2)}) collective-permute-start(bf16[8,2,2048]{2,0,1:T(8,128)(2,1)S(1)} %multiply_convert_fusion.2), channel_id=1, source_target_pairs={{16,0},{32,16},{48,32},{64,48},{80,64},{96,80},{112,96},{17,1},{33... | collective-permute-start | bytes 196616 | tf_op jit(solution)/shard_map/while/body/eval_jaxpr/ppermute | solution.py:13
  516.1 15.4 %all-to-all-start.1 = ((bf16[16,32,8,128]{3,2,1,0:T(8,128)(2,1)}), bf16[16,32,8,128]{3,2,1,0:T(8,128)(2,1)S(1)}, u32[]{:S(2)}, u32[]{:S(2)}) async-start(bf16[16,32,8,128]{3,2,1,0:T(8,128)(2,1)} %broadcast_in_dim.67), calls=%async_computation.1 | async-start | bytes 2097152 | tf_op jit(solution)/shard_map/while/body/eval_jaxpr/all_to_all | solution.py:40
  543.6 9.6 %collective-permute-start.1 = (bf16[8,2,2048]{2,0,1:T(8,128)(2,1)S(1)}, bf16[8,2,2048]{2,0,1:T(8,128)(2,1)S(1)}, u32[]{:S(2)}, u32[]{:S(2)}) collective-permute-start(bf16[8,2,2048]{2,0,1:T(8,128)(2,1)S(1)} %multiply_convert_fusion.2), channel_id=1, source_target_pairs={{16,0},{32,16},{48,32},{64,48},{80,64},{96,80},{112,96},{17,1},{33... | collective-permute-start | bytes 196616 | tf_op jit(solution)/shard_map/while/body/eval_jaxpr/ppermute | solution.py:13
  554.9 15.6 %all-to-all-start.1 = ((bf16[16,32,8,128]{3,2,1,0:T(8,128)(2,1)}), bf16[16,32,8,128]{3,2,1,0:T(8,128)(2,1)S(1)}, u32[]{:S(2)}, u32[]{:S(2)}) async-start(bf16[16,32,8,128]{3,2,1,0:T(8,128)(2,1)} %broadcast_in_dim.67), calls=%async_computation.1 | async-start | bytes 2097152 | tf_op jit(solution)/shard_map/while/body/eval_jaxpr/all_to_all | solution.py:40
  582.7 9.0 %collective-permute-start.1 = (bf16[8,2,2048]{2,0,1:T(8,128)(2,1)S(1)}, bf16[8,2,2048]{2,0,1:T(8,128)(2,1)S(1)}, u32[]{:S(2)}, u32[]{:S(2)}) collective-permute-start(bf16[8,2,2048]{2,0,1:T(8,128)(2,1)S(1)} %multiply_convert_fusion.2), channel_id=1, source_target_pairs={{16,0},{32,16},{48,32},{64,48},{80,64},{96,80},{112,96},{17,1},{33... | collective-permute-start | bytes 196616 | tf_op jit(solution)/shard_map/while/body/eval_jaxpr/ppermute | solution.py:13
  593.2 16.3 %all-to-all-start.1 = ((bf16[16,32,8,128]{3,2,1,0:T(8,128)(2,1)}), bf16[16,32,8,128]{3,2,1,0:T(8,128)(2,1)S(1)}, u32[]{:S(2)}, u32[]{:S(2)}) async-start(bf16[16,32,8,128]{3,2,1,0:T(8,128)(2,1)} %broadcast_in_dim.67), calls=%async_computation.1 | async-start | bytes 2097152 | tf_op jit(solution)/shard_map/while/body/eval_jaxpr/all_to_all | solution.py:40
  630.2 19.9 %all-to-all-start.3 = ((f32[128,1,288]{2,1,0:T(1,128)}), f32[128,1,288]{2,1,0:T(1,128)S(1)}, u32[]{:S(2)}, u32[]{:S(2)}) async-start(f32[128,1,288]{2,1,0:T(1,128)} %reshape.241), calls=%async_computation.3 | async-start | bytes 393216 | tf_op jit(solution)/shard_map/all_to_all | solution.py:88
  (10 other events, 343.6 us)

commit v9 on v7

--- a/solution.py
+++ b/solution.py
@@ -53,15 +53,18 @@
         down_in = (source + coupler * arrived.astype(jnp.float32)).astype(jnp.bfloat16)
         return apply_layer(down_in).astype(jnp.bfloat16)
 
-    first = apply_layer(source.astype(jnp.bfloat16)).astype(jnp.bfloat16)
-    swept = lax.fori_loop(0, depth_count - 1, down_turn, first)
+    swept = apply_layer(source.astype(jnp.bfloat16)).astype(jnp.bfloat16)
+    for turn_index in range(depth_count - 1):
+        swept = down_turn(turn_index, swept)
 
     def up_turn(turn_index, current):
         outgoing = (coupler * current.astype(jnp.float32)).astype(jnp.bfloat16)
         arrived = passed_along(outgoing, "depth", -1)
         return (swept.astype(jnp.float32) + apply_layer(arrived)).astype(jnp.bfloat16)
 
-    precond = lax.fori_loop(0, depth_count - 1, up_turn, swept)
+    precond = swept
+    for turn_index in range(depth_count - 1):
+        precond = up_turn(turn_index, precond)
     product = precond.astype(jnp.float32) * toar_f32
     contrib = product[:, 0] + product[:, 1]
 

time: 583 us -> 566 us (0.971); the launches traced: 581 us -> 557 us
  blocking collectives: 0 us -> 231 us
  waiting for transfers between devices: 265 us -> 78.7 us
  starting transfers between devices: 131 us -> 75.9 us
  local copies, waits for them, and re-layouts: 59.8 us -> 47.4 us
    all_to_all x0 -> x13, blocking collectives: none -> 231 us  [apply_layer(): gathered = lax.all_to_all(copies, 'plane', 0, 0, tiled=True)]
    all_to_all x15 -> x2, waiting for transfers between devices: 192 us -> 25 us  [apply_layer(): gathered = lax.all_to_all(copies, 'plane', 0, 0, tiled=True)]
    all_to_all x15 -> x2, starting transfers between devices: 59.8 us -> 12 us  [apply_layer(): gathered = lax.all_to_all(copies, 'plane', 0, 0, tiled=True)]
    ppermute x14, waiting for transfers between devices: 62.9 us -> 43.9 us  [passed_along(): lax.ppermute(value, axis, [(source, source + steps) for source in range(f...]
    broadcast_in_dim x30, local copies, waits for them, and re-layouts: 19.4 us -> 6.59 us  [apply_layer(): jnp.broadcast_to(local_blocks[None], (plane_count,) + local_blocks.shape)]
    ppermute x14, starting transfers between devices: 62.3 us -> 53.9 us  [passed_along(): lax.ppermute(value, axis, [(source, source + steps) for source in range(f...]
  transfers between devices with their start and end apart: 30 -> 17, of which waited for: 30 -> 17; matrix products, arithmetic and copies ran while one was open for 0% -> 1% of each run, Pallas kernels for 0% -> 0%
where the time goes in v9:
time: 566 us; the launch traced here: 557 us
  blocking collectives  231 us (41%)
  matrix products  94.9 us (17%)
  waiting for transfers between devices  78.7 us (14%)
  starting transfers between devices  75.9 us (13%)
  local copies, waits for them, and re-layouts  47.4 us (8%)
  other arithmetic  26.6 us (5%)
    all_to_all x13, blocking collectives, apply_layer(): gathered = lax.all_to_all(copies, 'plane', 0, 0, tiled=True)  231 us
    dot_general x15, matrix products, apply_layer(): jnp.einsum('rkic,rkvwc->vwri', factor, expanded, preferred_element_type=j...  84.9 us
    ppermute x14, starting transfers between devices, passed_along(): lax.ppermute(value, axis, [(source, source + steps) for source in range(f...  53.9 us
    ppermute x14, waiting for transfers between devices, passed_along(): lax.ppermute(value, axis, [(source, source + steps) for source in range(f...  43.9 us
    gather x15, local copies, waits for them, and re-layouts, apply_layer(): chosen = jnp.take(gathered, pattern_flat, axis=0, mode='clip')  28.1 us
    all_to_all x2, waiting for transfers between devices, apply_layer(): gathered = lax.all_to_all(copies, 'plane', 0, 0, tiled=True)  25 us
    another operation x15, other arithmetic, apply_layer(): jnp.stack([jnp.concatenate([x_re, -x_im], axis=-1), jnp.concatenate([x_im...  17.3 us
    all_to_all x2, starting transfers between devices, apply_layer(): gathered = lax.all_to_all(copies, 'plane', 0, 0, tiled=True)  12 us
  transfers between devices with their start and end apart: 17, of which 17 were waited for; matrix products, arithmetic and copies ran while one was open for 1% of the time, Pallas kernels for 0%

profile of v9, /device:TPU:1, one launch (start us, length us, event | category | flops | bytes accessed | tf_op | source)
XLA Modules:
  0.0 556.7 jit_solution(4717401520003490058)
XLA Ops:
  4.1 7.6 %all-to-all-start = ((bf16[16,32,8,128]{3,2,1,0:T(8,128)(2,1)}), bf16[16,32,8,128]{3,2,1,0:T(8,128)(2,1)S(1)}, u32[]{:S(2)}, u32[]{:S(2)}) async-start(bf16[16,32,8,128]{3,2,1,0:T(8,128)(2,1)} %broadcast_in_dim.134), calls=%async_computation | async-start | bytes 2097152 | tf_op jit(solution)/shard_map/all_to_all | solution.py:36
  11.9 15.3 %all-to-all-done = bf16[16,32,8,128]{3,2,1,0:T(8,128)(2,1)S(1)} async-done(((bf16[16,32,8,128]{3,2,1,0:T(8,128)(2,1)}), bf16[16,32,8,128]{3,2,1,0:T(8,128)(2,1)S(1)}, u32[]{:S(2)}, u32[]{:S(2)}) %all-to-all-start) | async-done | bytes 1048608 | tf_op jit(solution)/shard_map/all_to_all | solution.py:36
  36.5 6.6 %collective-permute-start = (bf16[8,2,2048]{2,0,1:T(8,128)(2,1)S(1)}, bf16[8,2,2048]{2,0,1:T(8,128)(2,1)S(1)}, u32[]{:S(2)}, u32[]{:S(2)}) collective-permute-start(bf16[8,2,2048]{2,0,1:T(8,128)(2,1)S(1)} %convert_element_type.264), channel_id=1, source_target_pairs={{0,16},{16,32},{32,48},{48,64},{64,80},{80,96},{96,112},{1,17},{17... | collective-permute-start | bytes 196616 | tf_op jit(solution)/shard_map/ppermute | solution.py:13
  45.1 18.3 %all_to_all.80 = bf16[16,32,8,128]{3,2,1,0:T(8,128)(2,1)S(1)} all-to-all(bf16[16,32,8,128]{3,2,1,0:T(8,128)(2,1)S(1)} %broadcast_in_dim.137), channel_id=1, replica_groups=mesh['depth'=8,'plane'=16] {'plane'}, dimensions={0} | all-to-all | bytes 2097152 | tf_op jit(solution)/shard_map/all_to_all | solution.py:36
  80.8 17.3 %all_to_all.81 = bf16[16,32,8,128]{3,2,1,0:T(8,128)(2,1)S(1)} all-to-all(bf16[16,32,8,128]{3,2,1,0:T(8,128)(2,1)S(1)} %broadcast_in_dim.139), channel_id=1, replica_groups=mesh['depth'=8,'plane'=16] {'plane'}, dimensions={0} | all-to-all | bytes 2097152 | tf_op jit(solution)/shard_map/all_to_all | solution.py:36
  107.6 7.0 %collective-permute-start.2 = (bf16[8,2,2048]{2,0,1:T(8,128)(2,1)S(1)}, bf16[8,2,2048]{2,0,1:T(8,128)(2,1)S(1)}, u32[]{:S(2)}, u32[]{:S(2)}) collective-permute-start(bf16[8,2,2048]{2,0,1:T(8,128)(2,1)S(1)} %convert_element_type.274), channel_id=1, source_target_pairs={{0,16},{16,32},{32,48},{48,64},{64,80},{80,96},{96,112},{1,17},{17... | collective-permute-start | bytes 196616 | tf_op jit(solution)/shard_map/ppermute | solution.py:13
  116.6 16.0 %all_to_all.82 = bf16[16,32,8,128]{3,2,1,0:T(8,128)(2,1)S(1)} all-to-all(bf16[16,32,8,128]{3,2,1,0:T(8,128)(2,1)S(1)} %broadcast_in_dim.141), channel_id=1, replica_groups=mesh['depth'=8,'plane'=16] {'plane'}, dimensions={0} | all-to-all | bytes 2097152 | tf_op jit(solution)/shard_map/all_to_all | solution.py:36
  142.1 6.3 %collective-permute-start.3 = (bf16[8,2,2048]{2,0,1:T(8,128)(2,1)S(1)}, bf16[8,2,2048]{2,0,1:T(8,128)(2,1)S(1)}, u32[]{:S(2)}, u32[]{:S(2)}) collective-permute-start(bf16[8,2,2048]{2,0,1:T(8,128)(2,1)S(1)} %convert_element_type.279), channel_id=1, source_target_pairs={{0,16},{16,32},{32,48},{48,64},{64,80},{80,96},{96,112},{1,17},{17... | collective-permute-start | bytes 196616 | tf_op jit(solution)/shard_map/ppermute | solution.py:13
  150.4 17.2 %all_to_all.83 = bf16[16,32,8,128]{3,2,1,0:T(8,128)(2,1)S(1)} all-to-all(bf16[16,32,8,128]{3,2,1,0:T(8,128)(2,1)S(1)} %broadcast_in_dim.143), channel_id=1, replica_groups=mesh['depth'=8,'plane'=16] {'plane'}, dimensions={0} | all-to-all | bytes 2097152 | tf_op jit(solution)/shard_map/all_to_all | solution.py:36
  184.6 17.5 %all_to_all.84 = bf16[16,32,8,128]{3,2,1,0:T(8,128)(2,1)S(1)} all-to-all(bf16[16,32,8,128]{3,2,1,0:T(8,128)(2,1)S(1)} %broadcast_in_dim.145), channel_id=1, replica_groups=mesh['depth'=8,'plane'=16] {'plane'}, dimensions={0} | all-to-all | bytes 2097152 | tf_op jit(solution)/shard_map/all_to_all | solution.py:36
  218.4 18.4 %all_to_all.85 = bf16[16,32,8,128]{3,2,1,0:T(8,128)(2,1)S(1)} all-to-all(bf16[16,32,8,128]{3,2,1,0:T(8,128)(2,1)S(1)} %broadcast_in_dim.147), channel_id=1, replica_groups=mesh['depth'=8,'plane'=16] {'plane'}, dimensions={0} | all-to-all | bytes 2097152 | tf_op jit(solution)/shard_map/all_to_all | solution.py:36
  252.4 18.7 %all_to_all.86 = bf16[16,32,8,128]{3,2,1,0:T(8,128)(2,1)S(1)} all-to-all(bf16[16,32,8,128]{3,2,1,0:T(8,128)(2,1)S(1)} %broadcast_in_dim.149), channel_id=1, replica_groups=mesh['depth'=8,'plane'=16] {'plane'}, dimensions={0} | all-to-all | bytes 2097152 | tf_op jit(solution)/shard_map/all_to_all | solution.py:36
  286.8 19.3 %all_to_all.87 = bf16[16,32,8,128]{3,2,1,0:T(8,128)(2,1)S(1)} all-to-all(bf16[16,32,8,128]{3,2,1,0:T(8,128)(2,1)S(1)} %broadcast_in_dim.151), channel_id=1, replica_groups=mesh['depth'=8,'plane'=16] {'plane'}, dimensions={0} | all-to-all | bytes 2097152 | tf_op jit(solution)/shard_map/all_to_all | solution.py:36
  321.6 18.7 %all_to_all.88 = bf16[16,32,8,128]{3,2,1,0:T(8,128)(2,1)S(1)} all-to-all(bf16[16,32,8,128]{3,2,1,0:T(8,128)(2,1)S(1)} %broadcast_in_dim.153), channel_id=1, replica_groups=mesh['depth'=8,'plane'=16] {'plane'}, dimensions={0} | all-to-all | bytes 2097152 | tf_op jit(solution)/shard_map/all_to_all | solution.py:36
  356.0 18.9 %all_to_all.89 = bf16[16,32,8,128]{3,2,1,0:T(8,128)(2,1)S(1)} all-to-all(bf16[16,32,8,128]{3,2,1,0:T(8,128)(2,1)S(1)} %broadcast_in_dim.155), channel_id=1, replica_groups=mesh['depth'=8,'plane'=16] {'plane'}, dimensions={0} | all-to-all | bytes 2097152 | tf_op jit(solution)/shard_map/all_to_all | solution.py:36
  391.5 17.7 %all_to_all.90 = bf16[16,32,8,128]{3,2,1,0:T(8,128)(2,1)S(1)} all-to-all(bf16[16,32,8,128]{3,2,1,0:T(8,128)(2,1)S(1)} %broadcast_in_dim.157), channel_id=1, replica_groups=mesh['depth'=8,'plane'=16] {'plane'}, dimensions={0} | all-to-all | bytes 2097152 | tf_op jit(solution)/shard_map/all_to_all | solution.py:36
  420.4 6.1 %collective-permute-done.11 = bf16[8,2,2048]{2,0,1:T(8,128)(2,1)S(1)} collective-permute-done((bf16[8,2,2048]{2,0,1:T(8,128)(2,1)S(1)}, bf16[8,2,2048]{2,0,1:T(8,128)(2,1)S(1)}, u32[]{:S(2)}, u32[]{:S(2)}) %collective-permute-start.11) | collective-permute-done | bytes 65568 | tf_op jit(solution)/shard_map/ppermute | solution.py:13
  427.2 16.5 %all_to_all.91 = bf16[16,32,8,128]{3,2,1,0:T(8,128)(2,1)S(1)} all-to-all(bf16[16,32,8,128]{3,2,1,0:T(8,128)(2,1)S(1)} %broadcast_in_dim.159), channel_id=1, replica_groups=mesh['depth'=8,'plane'=16] {'plane'}, dimensions={0} | all-to-all | bytes 2097152 | tf_op jit(solution)/shard_map/all_to_all | solution.py:36
  461.5 16.4 %all_to_all.92 = bf16[16,32,8,128]{3,2,1,0:T(8,128)(2,1)S(1)} all-to-all(bf16[16,32,8,128]{3,2,1,0:T(8,128)(2,1)S(1)} %broadcast_in_dim.161), channel_id=1, replica_groups=mesh['depth'=8,'plane'=16] {'plane'}, dimensions={0} | all-to-all | bytes 2097152 | tf_op jit(solution)/shard_map/all_to_all | solution.py:36
  489.2 6.9 %collective-permute-done.13 = bf16[8,2,2048]{2,0,1:T(8,128)(2,1)S(1)} collective-permute-done((bf16[8,2,2048]{2,0,1:T(8,128)(2,1)S(1)}, bf16[8,2,2048]{2,0,1:T(8,128)(2,1)S(1)}, u32[]{:S(2)}, u32[]{:S(2)}) %collective-permute-start.13) | collective-permute-done | bytes 65568 | tf_op jit(solution)/shard_map/ppermute | solution.py:13
  504.3 9.7 %all-to-all-done.14 = bf16[16,32,8,128]{3,2,1,0:T(8,128)(2,1)S(1)} async-done(((bf16[16,32,8,128]{3,2,1,0:T(8,128)(2,1)}), bf16[16,32,8,128]{3,2,1,0:T(8,128)(2,1)S(1)}, u32[]{:S(2)}, u32[]{:S(2)}) %all-to-all-start.14) | async-done | bytes 1048608 | tf_op jit(solution)/shard_map/all_to_all | solution.py:36
  523.6 6.5 %fusion = f32[4096,27]{0,1:T(8,128)S(1)} fusion(s32[2048]{0:T(1024)S(1)} %add_add_fusion, bf16[2048,9]{0,1:T(8,128)(2,1)S(1)} %get-tuple-element.88, bf16[2048,9]{0,1:T(8,128)(2,1)S(1)} %get-tuple-element.89, bf16[2048,9]{0,1:T(8,128)(2,1)S(1)} %get-tuple-element.87), kind=kOutput, calls=%fused_computation.16 | convolution fusion | flops 461705216 | bytes 561152 | tf_op jit(solution)/shard_map/cs,cq->sq/dot_general | solution.py:89
  531.9 10.0 %all-to-all-start.15 = ((f32[128,1,288]{2,1,0:T(1,128)}), f32[128,1,288]{2,1,0:T(1,128)S(1)}, u32[]{:S(2)}, u32[]{:S(2)}) async-start(f32[128,1,288]{2,1,0:T(1,128)} %reshape.573), calls=%async_computation.15 | async-start | bytes 393216 | tf_op jit(solution)/shard_map/all_to_all | solution.py:93
  542.7 9.7 %all-to-all-done.15 = f32[128,1,288]{2,1,0:T(1,128)S(1)} async-done(((f32[128,1,288]{2,1,0:T(1,128)}), f32[128,1,288]{2,1,0:T(1,128)S(1)}, u32[]{:S(2)}, u32[]{:S(2)}) %all-to-all-start.15) | async-done | bytes 147488 | tf_op jit(solution)/shard_map/all_to_all | solution.py:93
  (228 shorter events, 231.8 us)
Async XLA Ops:
  2.3 9.4 %copy-start.5 = (s32[1,32,16]{1,2,0:T(8,128)S(1)}, s32[1,32,16]{1,2,0:T(8,128)}, u32[]{:S(2)}) copy-start(s32[1,32,16]{1,2,0:T(8,128)} %param.10) | copy-start | bytes 6148
  4.1 23.1 %all-to-all-start = ((bf16[16,32,8,128]{3,2,1,0:T(8,128)(2,1)}), bf16[16,32,8,128]{3,2,1,0:T(8,128)(2,1)S(1)}, u32[]{:S(2)}, u32[]{:S(2)}) async-start(bf16[16,32,8,128]{3,2,1,0:T(8,128)(2,1)} %broadcast_in_dim.134), calls=%async_computation | async-start | bytes 2097152 | tf_op jit(solution)/shard_map/all_to_all | solution.py:36
  11.9 17.6 %copy-start.1 = (s32[1024]{0:T(1024)}, s32[1024]{0:T(1024)S(1)}, u32[]{:S(2)}) copy-start(s32[1024]{0:T(1024)S(1)} %pad_clamp_fusion) | copy-start | bytes 12292
  30.6 13.8 %copy-start = (f32[1,2048]{1,0:T(1,128)S(1)}, f32[1,2048]{1,0:T(1,128)}, u32[]{:S(2)}) copy-start(f32[1,2048]{1,0:T(1,128)} %param.8) | copy-start | bytes 24580
  36.5 7.9 %collective-permute-start = (bf16[8,2,2048]{2,0,1:T(8,128)(2,1)S(1)}, bf16[8,2,2048]{2,0,1:T(8,128)(2,1)S(1)}, u32[]{:S(2)}, u32[]{:S(2)}) collective-permute-start(bf16[8,2,2048]{2,0,1:T(8,128)(2,1)S(1)} %convert_element_type.264), channel_id=1, source_target_pairs={{0,16},{16,32},{32,48},{48,64},{64,80},{80,96},{96,112},{1,17},{17... | collective-permute-start | bytes 196616 | tf_op jit(solution)/shard_map/ppermute | solution.py:13
  72.9 7.3 %collective-permute-start.1 = (bf16[8,2,2048]{2,0,1:T(8,128)(2,1)S(1)}, bf16[8,2,2048]{2,0,1:T(8,128)(2,1)S(1)}, u32[]{:S(2)}, u32[]{:S(2)}) collective-permute-start(bf16[8,2,2048]{2,0,1:T(8,128)(2,1)S(1)} %convert_element_type.269), channel_id=1, source_target_pairs={{0,16},{16,32},{32,48},{48,64},{64,80},{80,96},{96,112},{1,17},{17... | collective-permute-start | bytes 196616 | tf_op jit(solution)/shard_map/ppermute | solution.py:13
  107.6 8.4 %collective-permute-start.2 = (bf16[8,2,2048]{2,0,1:T(8,128)(2,1)S(1)}, bf16[8,2,2048]{2,0,1:T(8,128)(2,1)S(1)}, u32[]{:S(2)}, u32[]{:S(2)}) collective-permute-start(bf16[8,2,2048]{2,0,1:T(8,128)(2,1)S(1)} %convert_element_type.274), channel_id=1, source_target_pairs={{0,16},{16,32},{32,48},{48,64},{64,80},{80,96},{96,112},{1,17},{17... | collective-permute-start | bytes 196616 | tf_op jit(solution)/shard_map/ppermute | solution.py:13
  142.1 7.7 %collective-permute-start.3 = (bf16[8,2,2048]{2,0,1:T(8,128)(2,1)S(1)}, bf16[8,2,2048]{2,0,1:T(8,128)(2,1)S(1)}, u32[]{:S(2)}, u32[]{:S(2)}) collective-permute-start(bf16[8,2,2048]{2,0,1:T(8,128)(2,1)S(1)} %convert_element_type.279), channel_id=1, source_target_pairs={{0,16},{16,32},{32,48},{48,64},{64,80},{80,96},{96,112},{1,17},{17... | collective-permute-start | bytes 196616 | tf_op jit(solution)/shard_map/ppermute | solution.py:13
  177.0 6.9 %collective-permute-start.4 = (bf16[8,2,2048]{2,0,1:T(8,128)(2,1)S(1)}, bf16[8,2,2048]{2,0,1:T(8,128)(2,1)S(1)}, u32[]{:S(2)}, u32[]{:S(2)}) collective-permute-start(bf16[8,2,2048]{2,0,1:T(8,128)(2,1)S(1)} %convert_element_type.284), channel_id=1, source_target_pairs={{0,16},{16,32},{32,48},{48,64},{64,80},{80,96},{96,112},{1,17},{17... | collective-permute-start | bytes 196616 | tf_op jit(solution)/shard_map/ppermute | solution.py:13
  211.5 6.2 %collective-permute-start.5 = (bf16[8,2,2048]{2,0,1:T(8,128)(2,1)S(1)}, bf16[8,2,2048]{2,0,1:T(8,128)(2,1)S(1)}, u32[]{:S(2)}, u32[]{:S(2)}) collective-permute-start(bf16[8,2,2048]{2,0,1:T(8,128)(2,1)S(1)} %convert_element_type.289), channel_id=1, source_target_pairs={{0,16},{16,32},{32,48},{48,64},{64,80},{80,96},{96,112},{1,17},{17... | collective-permute-start | bytes 196616 | tf_op jit(solution)/shard_map/ppermute | solution.py:13
  246.3 5.4 collective-permute-start.6
  280.5 25.5 %copy-start.2 = (s32[1024]{0:T(1024)S(1)}, s32[1024]{0:T(1024)}, u32[]{:S(2)}) copy-start(s32[1024]{0:T(1024)} %copy-done.1) | copy-start | bytes 12292
  280.5 5.6 %collective-permute-start.7 = (bf16[8,2,2048]{2,0,1:T(8,128)(2,1)S(1)}, bf16[8,2,2048]{2,0,1:T(8,128)(2,1)S(1)}, u32[]{:S(2)}, u32[]{:S(2)}) collective-permute-start(bf16[8,2,2048]{2,0,1:T(8,128)(2,1)S(1)} %multiply_convert_fusion.6), channel_id=1, source_target_pairs={{16,0},{32,16},{48,32},{64,48},{80,64},{96,80},{112,96},{17,1},{33... | collective-permute-start | bytes 196616 | tf_op jit(solution)/shard_map/ppermute | solution.py:13
  315.4 5.6 %collective-permute-start.8 = (bf16[8,2,2048]{2,0,1:T(8,128)(2,1)S(1)}, bf16[8,2,2048]{2,0,1:T(8,128)(2,1)S(1)}, u32[]{:S(2)}, u32[]{:S(2)}) collective-permute-start(bf16[8,2,2048]{2,0,1:T(8,128)(2,1)S(1)} %multiply_convert_fusion.5), channel_id=1, source_target_pairs={{16,0},{32,16},{48,32},{64,48},{80,64},{96,80},{112,96},{17,1},{33... | collective-permute-start | bytes 196616 | tf_op jit(solution)/shard_map/ppermute | solution.py:13
  349.6 5.7 %collective-permute-start.9 = (bf16[8,2,2048]{2,0,1:T(8,128)(2,1)S(1)}, bf16[8,2,2048]{2,0,1:T(8,128)(2,1)S(1)}, u32[]{:S(2)}, u32[]{:S(2)}) collective-permute-start(bf16[8,2,2048]{2,0,1:T(8,128)(2,1)S(1)} %multiply_convert_fusion.4), channel_id=1, source_target_pairs={{16,0},{32,16},{48,32},{64,48},{80,64},{96,80},{112,96},{17,1},{33... | collective-permute-start | bytes 196616 | tf_op jit(solution)/shard_map/ppermute | solution.py:13
  384.3 6.6 %collective-permute-start.10 = (bf16[8,2,2048]{2,0,1:T(8,128)(2,1)S(1)}, bf16[8,2,2048]{2,0,1:T(8,128)(2,1)S(1)}, u32[]{:S(2)}, u32[]{:S(2)}) collective-permute-start(bf16[8,2,2048]{2,0,1:T(8,128)(2,1)S(1)} %multiply_convert_fusion.3), channel_id=1, source_target_pairs={{16,0},{32,16},{48,32},{64,48},{80,64},{96,80},{112,96},{17,1},{33... | collective-permute-start | bytes 196616 | tf_op jit(solution)/shard_map/ppermute | solution.py:13
  418.5 8.0 %collective-permute-start.11 = (bf16[8,2,2048]{2,0,1:T(8,128)(2,1)S(1)}, bf16[8,2,2048]{2,0,1:T(8,128)(2,1)S(1)}, u32[]{:S(2)}, u32[]{:S(2)}) collective-permute-start(bf16[8,2,2048]{2,0,1:T(8,128)(2,1)S(1)} %multiply_convert_fusion.2), channel_id=1, source_target_pairs={{16,0},{32,16},{48,32},{64,48},{80,64},{96,80},{112,96},{17,1},{33... | collective-permute-start | bytes 196616 | tf_op jit(solution)/shard_map/ppermute | solution.py:13
  453.0 7.9 %collective-permute-start.12 = (bf16[8,2,2048]{2,0,1:T(8,128)(2,1)S(1)}, bf16[8,2,2048]{2,0,1:T(8,128)(2,1)S(1)}, u32[]{:S(2)}, u32[]{:S(2)}) collective-permute-start(bf16[8,2,2048]{2,0,1:T(8,128)(2,1)S(1)} %multiply_convert_fusion.1), channel_id=1, source_target_pairs={{16,0},{32,16},{48,32},{64,48},{80,64},{96,80},{112,96},{17,1},{33... | collective-permute-start | bytes 196616 | tf_op jit(solution)/shard_map/ppermute | solution.py:13
  481.3 7.8 %copy-start.4 = (s32[1,2048]{1,0:T(1,128)S(1)}, s32[1,2048]{1,0:T(1,128)}, u32[]{:S(2)}) copy-start(s32[1,2048]{1,0:T(1,128)} %param.11) | copy-start | bytes 24580
  487.3 8.9 %collective-permute-start.13 = (bf16[8,2,2048]{2,0,1:T(8,128)(2,1)S(1)}, bf16[8,2,2048]{2,0,1:T(8,128)(2,1)S(1)}, u32[]{:S(2)}, u32[]{:S(2)}) collective-permute-start(bf16[8,2,2048]{2,0,1:T(8,128)(2,1)S(1)} %multiply_convert_fusion), channel_id=1, source_target_pairs={{16,0},{32,16},{48,32},{64,48},{80,64},{96,80},{112,96},{17,1},{33... | collective-permute-start | bytes 196616 | tf_op jit(solution)/shard_map/ppermute | solution.py:13
  497.7 16.2 %all-to-all-start.14 = ((bf16[16,32,8,128]{3,2,1,0:T(8,128)(2,1)}), bf16[16,32,8,128]{3,2,1,0:T(8,128)(2,1)S(1)}, u32[]{:S(2)}, u32[]{:S(2)}) async-start(bf16[16,32,8,128]{3,2,1,0:T(8,128)(2,1)} %broadcast_in_dim.163), calls=%async_computation.14 | async-start | bytes 2097152 | tf_op jit(solution)/shard_map/all_to_all | solution.py:36
  517.6 5.9 %copy-start.3 = (bf16[1,8,2,2048]{3,2,1,0:T(2,128)(2,1)S(1)}, bf16[1,8,2,2048]{3,2,1,0:T(2,128)(2,1)}, u32[]{:S(2)}) copy-start(bf16[1,8,2,2048]{3,2,1,0:T(2,128)(2,1)} %param.6) | copy-start | bytes 196612
  531.9 20.6 %all-to-all-start.15 = ((f32[128,1,288]{2,1,0:T(1,128)}), f32[128,1,288]{2,1,0:T(1,128)S(1)}, u32[]{:S(2)}, u32[]{:S(2)}) async-start(f32[128,1,288]{2,1,0:T(1,128)} %reshape.573), calls=%async_computation.15 | async-start | bytes 393216 | tf_op jit(solution)/shard_map/all_to_all | solution.py:93

commit v10 on v9

--- a/solution.py
+++ b/solution.py
@@ -77,8 +77,8 @@
     lower = (cells[:, None] >= cells[None, :]).astype(jnp.bfloat16)
     running = jnp.dot(lower, hits, preferred_element_type=jnp.float32)
     rank = jnp.sum(running * hits.astype(jnp.float32), axis=1).astype(jnp.int32) - 1
-    slot = owner * CAP + rank
-    placed = (slot[:, None] == jnp.arange(owner_count * CAP, dtype=jnp.int32)[None, :]).astype(jnp.bfloat16)
+    by_owner = hits
+    by_rank = (rank[:, None] == jnp.arange(CAP, dtype=jnp.int32)[None, :]).astype(jnp.bfloat16)
     local_patch = (cell_patch % PATCH_DEV).astype(jnp.float32)
     rows = jnp.concatenate([contrib.T, local_patch[:, None]], axis=1)
     high = lax.reduce_precision(rows, exponent_bits=8, mantissa_bits=7)
@@ -86,7 +86,9 @@
     middle = lax.reduce_precision(rest, exponent_bits=8, mantissa_bits=7)
     low = rest - middle
     parts = jnp.concatenate([high, middle, low], axis=1).astype(jnp.bfloat16)
-    moved = jnp.einsum("cs,cq->sq", placed, parts, preferred_element_type=jnp.float32)
+    spread = (by_rank[:, :, None] * parts[:, None, :]).reshape(cell_count, -1)
+    moved = jnp.einsum("co,cq->oq", by_owner, spread, preferred_element_type=jnp.float32)
+    moved = moved.reshape(owner_count * CAP, -1)
     width = vec_count + 1
     packed = (moved[:, :width] + moved[:, width:2 * width]) + moved[:, 2 * width:]
     packed = packed.reshape(owner_count, CAP, width)

time: 566 us -> 577 us (1.019)
  blocking collectives: 231 us -> 215 us
  waiting for transfers between devices: 78.7 us -> 90.8 us
  local copies, waits for them, and re-layouts: 47.4 us -> 57.2 us
    all_to_all x13 -> x12, blocking collectives: 231 us -> 215 us  [apply_layer(): gathered = lax.all_to_all(copies, 'plane', 0, 0, tiled=True)]
    all_to_all x2 -> x3, waiting for transfers between devices: 25 us -> 39.4 us  [apply_layer(): gathered = lax.all_to_all(copies, 'plane', 0, 0, tiled=True)]
    all_to_all x2 -> x3, starting transfers between devices: 12 us -> 16.8 us  [apply_layer(): gathered = lax.all_to_all(copies, 'plane', 0, 0, tiled=True)]
  transfers between devices with their start and end apart: 17 -> 18, of which waited for: 17 -> 18; matrix products, arithmetic and copies ran while one was open for 1% -> 1% of each run, Pallas kernels for 0% -> 0%
where the time goes in v10:
time: 577 us; the launch traced here: 567 us
  blocking collectives  215 us (37%)
  matrix products  91.2 us (16%)
  waiting for transfers between devices  90.8 us (16%)
  starting transfers between devices  80.2 us (14%)
  local copies, waits for them, and re-layouts  57.2 us (10%)
  other arithmetic  31.3 us (5%)
    all_to_all x12, blocking collectives, apply_layer(): gathered = lax.all_to_all(copies, 'plane', 0, 0, tiled=True)  215 us
    dot_general x15, matrix products, apply_layer(): jnp.einsum('rkic,rkvwc->vwri', factor, expanded, preferred_element_type=j...  85.6 us
    ppermute x14, starting transfers between devices, passed_along(): lax.ppermute(value, axis, [(source, source + steps) for source in range(f...  53.9 us
    ppermute x14, waiting for transfers between devices, passed_along(): lax.ppermute(value, axis, [(source, source + steps) for source in range(f...  41.7 us
    all_to_all x3, waiting for transfers between devices, apply_layer(): gathered = lax.all_to_all(copies, 'plane', 0, 0, tiled=True)  39.4 us
    gather x15, local copies, waits for them, and re-layouts, apply_layer(): chosen = jnp.take(gathered, pattern_flat, axis=0, mode='clip')  27.9 us
    another operation x15, other arithmetic, apply_layer(): jnp.stack([jnp.concatenate([x_re, -x_im], axis=-1), jnp.concatenate([x_im...  17.3 us
    all_to_all x3, starting transfers between devices, apply_layer(): gathered = lax.all_to_all(copies, 'plane', 0, 0, tiled=True)  16.8 us
  transfers between devices with their start and end apart: 18, of which 18 were waited for; matrix products, arithmetic and copies ran while one was open for 1% of the time, Pallas kernels for 0%

profile of v10, /device:TPU:1, one launch (start us, length us, event | category | flops | bytes accessed | tf_op | source)
XLA Modules:
  0.0 567.4 jit_solution(6091186313424301739)
XLA Ops:
  4.1 7.6 %all-to-all-start = ((bf16[16,32,8,128]{3,2,1,0:T(8,128)(2,1)}), bf16[16,32,8,128]{3,2,1,0:T(8,128)(2,1)S(1)}, u32[]{:S(2)}, u32[]{:S(2)}) async-start(bf16[16,32,8,128]{3,2,1,0:T(8,128)(2,1)} %broadcast_in_dim.136), calls=%async_computation | async-start | bytes 2097152 | tf_op jit(solution)/shard_map/all_to_all | solution.py:36
  11.9 15.3 %all-to-all-done = bf16[16,32,8,128]{3,2,1,0:T(8,128)(2,1)S(1)} async-done(((bf16[16,32,8,128]{3,2,1,0:T(8,128)(2,1)}), bf16[16,32,8,128]{3,2,1,0:T(8,128)(2,1)S(1)}, u32[]{:S(2)}, u32[]{:S(2)}) %all-to-all-start) | async-done | bytes 1048608 | tf_op jit(solution)/shard_map/all_to_all | solution.py:36
  36.6 6.6 %collective-permute-start = (bf16[8,2,2048]{2,0,1:T(8,128)(2,1)S(1)}, bf16[8,2,2048]{2,0,1:T(8,128)(2,1)S(1)}, u32[]{:S(2)}, u32[]{:S(2)}) collective-permute-start(bf16[8,2,2048]{2,0,1:T(8,128)(2,1)S(1)} %convert_element_type.274), channel_id=1, source_target_pairs={{0,16},{16,32},{32,48},{48,64},{64,80},{80,96},{96,112},{1,17},{17... | collective-permute-start | bytes 196616 | tf_op jit(solution)/shard_map/ppermute | solution.py:13
  45.1 18.3 %all_to_all.80 = bf16[16,32,8,128]{3,2,1,0:T(8,128)(2,1)S(1)} all-to-all(bf16[16,32,8,128]{3,2,1,0:T(8,128)(2,1)S(1)} %broadcast_in_dim.139), channel_id=1, replica_groups=mesh['depth'=8,'plane'=16] {'plane'}, dimensions={0} | all-to-all | bytes 2097152 | tf_op jit(solution)/shard_map/all_to_all | solution.py:36
  72.9 5.9 %collective-permute-start.1 = (bf16[8,2,2048]{2,0,1:T(8,128)(2,1)S(1)}, bf16[8,2,2048]{2,0,1:T(8,128)(2,1)S(1)}, u32[]{:S(2)}, u32[]{:S(2)}) collective-permute-start(bf16[8,2,2048]{2,0,1:T(8,128)(2,1)S(1)} %convert_element_type.279), channel_id=1, source_target_pairs={{0,16},{16,32},{32,48},{48,64},{64,80},{80,96},{96,112},{1,17},{17... | collective-permute-start | bytes 196616 | tf_op jit(solution)/shard_map/ppermute | solution.py:13
  80.8 17.3 %all_to_all.81 = bf16[16,32,8,128]{3,2,1,0:T(8,128)(2,1)S(1)} all-to-all(bf16[16,32,8,128]{3,2,1,0:T(8,128)(2,1)S(1)} %broadcast_in_dim.141), channel_id=1, replica_groups=mesh['depth'=8,'plane'=16] {'plane'}, dimensions={0} | all-to-all | bytes 2097152 | tf_op jit(solution)/shard_map/all_to_all | solution.py:36
  107.6 7.0 %collective-permute-start.2 = (bf16[8,2,2048]{2,0,1:T(8,128)(2,1)S(1)}, bf16[8,2,2048]{2,0,1:T(8,128)(2,1)S(1)}, u32[]{:S(2)}, u32[]{:S(2)}) collective-permute-start(bf16[8,2,2048]{2,0,1:T(8,128)(2,1)S(1)} %convert_element_type.284), channel_id=1, source_target_pairs={{0,16},{16,32},{32,48},{48,64},{64,80},{80,96},{96,112},{1,17},{17... | collective-permute-start | bytes 196616 | tf_op jit(solution)/shard_map/ppermute | solution.py:13
  116.6 16.0 %all_to_all.82 = bf16[16,32,8,128]{3,2,1,0:T(8,128)(2,1)S(1)} all-to-all(bf16[16,32,8,128]{3,2,1,0:T(8,128)(2,1)S(1)} %broadcast_in_dim.143), channel_id=1, replica_groups=mesh['depth'=8,'plane'=16] {'plane'}, dimensions={0} | all-to-all | bytes 2097152 | tf_op jit(solution)/shard_map/all_to_all | solution.py:36
  142.1 6.3 %collective-permute-start.3 = (bf16[8,2,2048]{2,0,1:T(8,128)(2,1)S(1)}, bf16[8,2,2048]{2,0,1:T(8,128)(2,1)S(1)}, u32[]{:S(2)}, u32[]{:S(2)}) collective-permute-start(bf16[8,2,2048]{2,0,1:T(8,128)(2,1)S(1)} %convert_element_type.289), channel_id=1, source_target_pairs={{0,16},{16,32},{32,48},{48,64},{64,80},{80,96},{96,112},{1,17},{17... | collective-permute-start | bytes 196616 | tf_op jit(solution)/shard_map/ppermute | solution.py:13
  150.4 17.2 %all_to_all.83 = bf16[16,32,8,128]{3,2,1,0:T(8,128)(2,1)S(1)} all-to-all(bf16[16,32,8,128]{3,2,1,0:T(8,128)(2,1)S(1)} %broadcast_in_dim.145), channel_id=1, replica_groups=mesh['depth'=8,'plane'=16] {'plane'}, dimensions={0} | all-to-all | bytes 2097152 | tf_op jit(solution)/shard_map/all_to_all | solution.py:36
  184.6 17.5 %all_to_all.84 = bf16[16,32,8,128]{3,2,1,0:T(8,128)(2,1)S(1)} all-to-all(bf16[16,32,8,128]{3,2,1,0:T(8,128)(2,1)S(1)} %broadcast_in_dim.147), channel_id=1, replica_groups=mesh['depth'=8,'plane'=16] {'plane'}, dimensions={0} | all-to-all | bytes 2097152 | tf_op jit(solution)/shard_map/all_to_all | solution.py:36
  218.4 18.4 %all_to_all.85 = bf16[16,32,8,128]{3,2,1,0:T(8,128)(2,1)S(1)} all-to-all(bf16[16,32,8,128]{3,2,1,0:T(8,128)(2,1)S(1)} %broadcast_in_dim.149), channel_id=1, replica_groups=mesh['depth'=8,'plane'=16] {'plane'}, dimensions={0} | all-to-all | bytes 2097152 | tf_op jit(solution)/shard_map/all_to_all | solution.py:36
  252.4 18.7 %all_to_all.86 = bf16[16,32,8,128]{3,2,1,0:T(8,128)(2,1)S(1)} all-to-all(bf16[16,32,8,128]{3,2,1,0:T(8,128)(2,1)S(1)} %broadcast_in_dim.151), channel_id=1, replica_groups=mesh['depth'=8,'plane'=16] {'plane'}, dimensions={0} | all-to-all | bytes 2097152 | tf_op jit(solution)/shard_map/all_to_all | solution.py:36
  286.8 19.3 %all_to_all.87 = bf16[16,32,8,128]{3,2,1,0:T(8,128)(2,1)S(1)} all-to-all(bf16[16,32,8,128]{3,2,1,0:T(8,128)(2,1)S(1)} %broadcast_in_dim.153), channel_id=1, replica_groups=mesh['depth'=8,'plane'=16] {'plane'}, dimensions={0} | all-to-all | bytes 2097152 | tf_op jit(solution)/shard_map/all_to_all | solution.py:36
  321.6 18.7 %all_to_all.88 = bf16[16,32,8,128]{3,2,1,0:T(8,128)(2,1)S(1)} all-to-all(bf16[16,32,8,128]{3,2,1,0:T(8,128)(2,1)S(1)} %broadcast_in_dim.155), channel_id=1, replica_groups=mesh['depth'=8,'plane'=16] {'plane'}, dimensions={0} | all-to-all | bytes 2097152 | tf_op jit(solution)/shard_map/all_to_all | solution.py:36
  356.0 18.9 %all_to_all.89 = bf16[16,32,8,128]{3,2,1,0:T(8,128)(2,1)S(1)} all-to-all(bf16[16,32,8,128]{3,2,1,0:T(8,128)(2,1)S(1)} %broadcast_in_dim.157), channel_id=1, replica_groups=mesh['depth'=8,'plane'=16] {'plane'}, dimensions={0} | all-to-all | bytes 2097152 | tf_op jit(solution)/shard_map/all_to_all | solution.py:36
  391.5 17.7 %all_to_all.90 = bf16[16,32,8,128]{3,2,1,0:T(8,128)(2,1)S(1)} all-to-all(bf16[16,32,8,128]{3,2,1,0:T(8,128)(2,1)S(1)} %broadcast_in_dim.159), channel_id=1, replica_groups=mesh['depth'=8,'plane'=16] {'plane'}, dimensions={0} | all-to-all | bytes 2097152 | tf_op jit(solution)/shard_map/all_to_all | solution.py:36
  420.5 6.1 %collective-permute-done.11 = bf16[8,2,2048]{2,0,1:T(8,128)(2,1)S(1)} collective-permute-done((bf16[8,2,2048]{2,0,1:T(8,128)(2,1)S(1)}, bf16[8,2,2048]{2,0,1:T(8,128)(2,1)S(1)}, u32[]{:S(2)}, u32[]{:S(2)}) %collective-permute-start.11) | collective-permute-done | bytes 65568 | tf_op jit(solution)/shard_map/ppermute | solution.py:13
  427.2 16.5 %all_to_all.91 = bf16[16,32,8,128]{3,2,1,0:T(8,128)(2,1)S(1)} all-to-all(bf16[16,32,8,128]{3,2,1,0:T(8,128)(2,1)S(1)} %broadcast_in_dim.161), channel_id=1, replica_groups=mesh['depth'=8,'plane'=16] {'plane'}, dimensions={0} | all-to-all | bytes 2097152 | tf_op jit(solution)/shard_map/all_to_all | solution.py:36
  467.0 12.3 %all-to-all-done.13 = bf16[16,32,8,128]{3,2,1,0:T(8,128)(2,1)S(1)} async-done(((bf16[16,32,8,128]{3,2,1,0:T(8,128)(2,1)}), bf16[16,32,8,128]{3,2,1,0:T(8,128)(2,1)S(1)}, u32[]{:S(2)}, u32[]{:S(2)}) %all-to-all-start.13) | async-done | bytes 1048608 | tf_op jit(solution)/shard_map/all_to_all | solution.py:36
  503.8 11.7 %all-to-all-done.14 = bf16[16,32,8,128]{3,2,1,0:T(8,128)(2,1)S(1)} async-done(((bf16[16,32,8,128]{3,2,1,0:T(8,128)(2,1)}), bf16[16,32,8,128]{3,2,1,0:T(8,128)(2,1)S(1)}, u32[]{:S(2)}, u32[]{:S(2)}) %all-to-all-start.14) | async-done | bytes 1048608 | tf_op jit(solution)/shard_map/all_to_all | solution.py:36
  518.9 6.3 %add_convert_fusion = (bf16[8,2,32,64]{3,0,1,2:T(8,128)(2,1)}, f32[8,2,32,64]{3,0,1,2:T(8,128)S(1)}) fusion(f32[8,2,32,64]{3,0,1,2:T(8,128)S(1)} %fusion.164, bf16[1,32,16,64,128]{4,3,2,1,0:T(8,128)(2,1)} %param.9, bf16[32,16,8,1,128]{4,2,1,3,0:T(8,128)(2,1)S(1)} %get-tuple-element.13, bf16[32,16,8,1,128]{4,2,1,3,0:T(8,128)(2,1)S(1)} %get-tuple-element.12), kind=kOutput, calls=%fused_computation.168 | convolution fusion | flops 135331840 | bytes 10813440 | tf_op jit(solution)/shard_map/rkic,rkvwc->vwri/dot_general | solution.py:46
  543.2 9.5 %all-to-all-start.15 = ((f32[128,1,288]{2,1,0:T(1,128)}), f32[128,1,288]{2,1,0:T(1,128)S(1)}, u32[]{:S(2)}, u32[]{:S(2)}) async-start(f32[128,1,288]{2,1,0:T(1,128)} %reshape.625), calls=%async_computation.15 | async-start | bytes 393216 | tf_op jit(solution)/shard_map/all_to_all | solution.py:95
  553.5 9.7 %all-to-all-done.15 = f32[128,1,288]{2,1,0:T(1,128)S(1)} async-done(((f32[128,1,288]{2,1,0:T(1,128)}), f32[128,1,288]{2,1,0:T(1,128)S(1)}, u32[]{:S(2)}, u32[]{:S(2)}) %all-to-all-start.15) | async-done | bytes 147488 | tf_op jit(solution)/shard_map/all_to_all | solution.py:95
  (235 shorter events, 246.2 us)
Async XLA Ops:
  2.3 9.4 %copy-start.6 = (s32[1,32,16]{1,2,0:T(8,128)S(1)}, s32[1,32,16]{1,2,0:T(8,128)}, u32[]{:S(2)}) copy-start(s32[1,32,16]{1,2,0:T(8,128)} %param.10) | copy-start | bytes 6148
  4.1 23.1 %all-to-all-start = ((bf16[16,32,8,128]{3,2,1,0:T(8,128)(2,1)}), bf16[16,32,8,128]{3,2,1,0:T(8,128)(2,1)S(1)}, u32[]{:S(2)}, u32[]{:S(2)}) async-start(bf16[16,32,8,128]{3,2,1,0:T(8,128)(2,1)} %broadcast_in_dim.136), calls=%async_computation | async-start | bytes 2097152 | tf_op jit(solution)/shard_map/all_to_all | solution.py:36
  11.9 17.6 %copy-start.2 = (s32[1024]{0:T(1024)}, s32[1024]{0:T(1024)S(1)}, u32[]{:S(2)}) copy-start(s32[1024]{0:T(1024)S(1)} %pad_clamp_fusion) | copy-start | bytes 12292
  30.7 13.8 %copy-start = (f32[1,2048]{1,0:T(1,128)S(1)}, f32[1,2048]{1,0:T(1,128)}, u32[]{:S(2)}) copy-start(f32[1,2048]{1,0:T(1,128)} %param.8) | copy-start | bytes 24580
  36.6 7.9 %collective-permute-start = (bf16[8,2,2048]{2,0,1:T(8,128)(2,1)S(1)}, bf16[8,2,2048]{2,0,1:T(8,128)(2,1)S(1)}, u32[]{:S(2)}, u32[]{:S(2)}) collective-permute-start(bf16[8,2,2048]{2,0,1:T(8,128)(2,1)S(1)} %convert_element_type.274), channel_id=1, source_target_pairs={{0,16},{16,32},{32,48},{48,64},{64,80},{80,96},{96,112},{1,17},{17... | collective-permute-start | bytes 196616 | tf_op jit(solution)/shard_map/ppermute | solution.py:13
  72.9 7.3 %collective-permute-start.1 = (bf16[8,2,2048]{2,0,1:T(8,128)(2,1)S(1)}, bf16[8,2,2048]{2,0,1:T(8,128)(2,1)S(1)}, u32[]{:S(2)}, u32[]{:S(2)}) collective-permute-start(bf16[8,2,2048]{2,0,1:T(8,128)(2,1)S(1)} %convert_element_type.279), channel_id=1, source_target_pairs={{0,16},{16,32},{32,48},{48,64},{64,80},{80,96},{96,112},{1,17},{17... | collective-permute-start | bytes 196616 | tf_op jit(solution)/shard_map/ppermute | solution.py:13
  107.6 8.4 %collective-permute-start.2 = (bf16[8,2,2048]{2,0,1:T(8,128)(2,1)S(1)}, bf16[8,2,2048]{2,0,1:T(8,128)(2,1)S(1)}, u32[]{:S(2)}, u32[]{:S(2)}) collective-permute-start(bf16[8,2,2048]{2,0,1:T(8,128)(2,1)S(1)} %convert_element_type.284), channel_id=1, source_target_pairs={{0,16},{16,32},{32,48},{48,64},{64,80},{80,96},{96,112},{1,17},{17... | collective-permute-start | bytes 196616 | tf_op jit(solution)/shard_map/ppermute | solution.py:13
  142.1 7.7 %collective-permute-start.3 = (bf16[8,2,2048]{2,0,1:T(8,128)(2,1)S(1)}, bf16[8,2,2048]{2,0,1:T(8,128)(2,1)S(1)}, u32[]{:S(2)}, u32[]{:S(2)}) collective-permute-start(bf16[8,2,2048]{2,0,1:T(8,128)(2,1)S(1)} %convert_element_type.289), channel_id=1, source_target_pairs={{0,16},{16,32},{32,48},{48,64},{64,80},{80,96},{96,112},{1,17},{17... | collective-permute-start | bytes 196616 | tf_op jit(solution)/shard_map/ppermute | solution.py:13
  177.1 6.9 %collective-permute-start.4 = (bf16[8,2,2048]{2,0,1:T(8,128)(2,1)S(1)}, bf16[8,2,2048]{2,0,1:T(8,128)(2,1)S(1)}, u32[]{:S(2)}, u32[]{:S(2)}) collective-permute-start(bf16[8,2,2048]{2,0,1:T(8,128)(2,1)S(1)} %convert_element_type.294), channel_id=1, source_target_pairs={{0,16},{16,32},{32,48},{48,64},{64,80},{80,96},{96,112},{1,17},{17... | collective-permute-start | bytes 196616 | tf_op jit(solution)/shard_map/ppermute | solution.py:13
  211.6 6.2 %collective-permute-start.5 = (bf16[8,2,2048]{2,0,1:T(8,128)(2,1)S(1)}, bf16[8,2,2048]{2,0,1:T(8,128)(2,1)S(1)}, u32[]{:S(2)}, u32[]{:S(2)}) collective-permute-start(bf16[8,2,2048]{2,0,1:T(8,128)(2,1)S(1)} %convert_element_type.299), channel_id=1, source_target_pairs={{0,16},{16,32},{32,48},{48,64},{64,80},{80,96},{96,112},{1,17},{17... | collective-permute-start | bytes 196616 | tf_op jit(solution)/shard_map/ppermute | solution.py:13
  246.3 5.4 collective-permute-start.6
  280.5 25.5 %copy-start.3 = (s32[1024]{0:T(1024)S(1)}, s32[1024]{0:T(1024)}, u32[]{:S(2)}) copy-start(s32[1024]{0:T(1024)} %copy-done.2) | copy-start | bytes 12292
  280.6 5.6 collective-permute-start.7
  315.4 5.6 collective-permute-start.8
  349.6 5.7 %collective-permute-start.9 = (bf16[8,2,2048]{2,0,1:T(8,128)(2,1)S(1)}, bf16[8,2,2048]{2,0,1:T(8,128)(2,1)S(1)}, u32[]{:S(2)}, u32[]{:S(2)}) collective-permute-start(bf16[8,2,2048]{2,0,1:T(8,128)(2,1)S(1)} %multiply_convert_fusion.4), channel_id=1, source_target_pairs={{16,0},{32,16},{48,32},{64,48},{80,64},{96,80},{112,96},{17,1},{33... | collective-permute-start | bytes 196616 | tf_op jit(solution)/shard_map/ppermute | solution.py:13
  384.3 6.6 %collective-permute-start.10 = (bf16[8,2,2048]{2,0,1:T(8,128)(2,1)S(1)}, bf16[8,2,2048]{2,0,1:T(8,128)(2,1)S(1)}, u32[]{:S(2)}, u32[]{:S(2)}) collective-permute-start(bf16[8,2,2048]{2,0,1:T(8,128)(2,1)S(1)} %multiply_convert_fusion.3), channel_id=1, source_target_pairs={{16,0},{32,16},{48,32},{64,48},{80,64},{96,80},{112,96},{17,1},{33... | collective-permute-start | bytes 196616 | tf_op jit(solution)/shard_map/ppermute | solution.py:13
  418.5 8.0 %collective-permute-start.11 = (bf16[8,2,2048]{2,0,1:T(8,128)(2,1)S(1)}, bf16[8,2,2048]{2,0,1:T(8,128)(2,1)S(1)}, u32[]{:S(2)}, u32[]{:S(2)}) collective-permute-start(bf16[8,2,2048]{2,0,1:T(8,128)(2,1)S(1)} %multiply_convert_fusion.2), channel_id=1, source_target_pairs={{16,0},{32,16},{48,32},{64,48},{80,64},{96,80},{112,96},{17,1},{33... | collective-permute-start | bytes 196616 | tf_op jit(solution)/shard_map/ppermute | solution.py:13
  453.0 14.0 %copy-start.5 = (s32[1,2048]{1,0:T(1,128)S(1)}, s32[1,2048]{1,0:T(1,128)}, u32[]{:S(2)}) copy-start(s32[1,2048]{1,0:T(1,128)} %param.11) | copy-start | bytes 24580
  453.0 7.9 %collective-permute-start.12 = (bf16[8,2,2048]{2,0,1:T(8,128)(2,1)S(1)}, bf16[8,2,2048]{2,0,1:T(8,128)(2,1)S(1)}, u32[]{:S(2)}, u32[]{:S(2)}) collective-permute-start(bf16[8,2,2048]{2,0,1:T(8,128)(2,1)S(1)} %multiply_convert_fusion.1), channel_id=1, source_target_pairs={{16,0},{32,16},{48,32},{64,48},{80,64},{96,80},{112,96},{17,1},{33... | collective-permute-start | bytes 196616 | tf_op jit(solution)/shard_map/ppermute | solution.py:13
  462.5 16.9 %all-to-all-start.13 = ((bf16[16,32,8,128]{3,2,1,0:T(8,128)(2,1)}), bf16[16,32,8,128]{3,2,1,0:T(8,128)(2,1)S(1)}, u32[]{:S(2)}, u32[]{:S(2)}) async-start(bf16[16,32,8,128]{3,2,1,0:T(8,128)(2,1)} %broadcast_in_dim.163), calls=%async_computation.13 | async-start | bytes 2097152 | tf_op jit(solution)/shard_map/all_to_all | solution.py:36
  488.7 8.6 %collective-permute-start.13 = (bf16[8,2,2048]{2,0,1:T(8,128)(2,1)S(1)}, bf16[8,2,2048]{2,0,1:T(8,128)(2,1)S(1)}, u32[]{:S(2)}, u32[]{:S(2)}) collective-permute-start(bf16[8,2,2048]{2,0,1:T(8,128)(2,1)S(1)} %multiply_convert_fusion), channel_id=1, source_target_pairs={{16,0},{32,16},{48,32},{64,48},{80,64},{96,80},{112,96},{17,1},{33... | collective-permute-start | bytes 196616 | tf_op jit(solution)/shard_map/ppermute | solution.py:13
  499.0 16.5 %all-to-all-start.14 = ((bf16[16,32,8,128]{3,2,1,0:T(8,128)(2,1)}), bf16[16,32,8,128]{3,2,1,0:T(8,128)(2,1)S(1)}, u32[]{:S(2)}, u32[]{:S(2)}) async-start(bf16[16,32,8,128]{3,2,1,0:T(8,128)(2,1)} %broadcast_in_dim.165), calls=%async_computation.14 | async-start | bytes 2097152 | tf_op jit(solution)/shard_map/all_to_all | solution.py:36
  539.5 13.1 %copy-start.1 = (bf16[8,2,32,64]{3,0,1,2:T(8,128)(2,1)S(1)}, bf16[8,2,32,64]{3,0,1,2:T(8,128)(2,1)}, u32[]{:S(2)}) copy-start(bf16[8,2,32,64]{3,0,1,2:T(8,128)(2,1)} %get-tuple-element.94) | copy-start | bytes 196612
  543.2 20.1 %all-to-all-start.15 = ((f32[128,1,288]{2,1,0:T(1,128)}), f32[128,1,288]{2,1,0:T(1,128)S(1)}, u32[]{:S(2)}, u32[]{:S(2)}) async-start(f32[128,1,288]{2,1,0:T(1,128)} %reshape.625), calls=%async_computation.15 | async-start | bytes 393216 | tf_op jit(solution)/shard_map/all_to_all | solution.py:95
  (1 other events, 6.6 us)

commit v11 on v9

--- a/solution.py
+++ b/solution.py
@@ -9,8 +9,10 @@
 
 def passed_along(value, axis, steps):
     count = lax.axis_size(axis)
-    first, last = (max(0, -steps), min(count, count - steps))
-    return lax.ppermute(value, axis, [(source, source + steps) for source in range(first, last)])
+    moved = lax.ppermute(value, axis, [(source, (source + steps) % count) for source in range(count)])
+    target = lax.axis_index(axis) - steps
+    keep = (target >= 0) & (target < count)
+    return jnp.where(keep, moved, jnp.zeros_like(moved))
 
 
 def shards(toar, pml_coeff, coupling, inverse, pattern, patch_map):

time: 566 us -> 547 us (0.966)
  waiting for transfers between devices: 78.7 us -> 52.9 us
  starting transfers between devices: 75.9 us -> 89 us
  blocking collectives: 231 us -> 225 us
    ppermute x14, waiting for transfers between devices: 43.9 us -> 18.2 us  [passed_along(): lax.ppermute(value, axis, [(source, (source + steps) % count) for source...]
    ppermute x14, starting transfers between devices: 53.9 us -> 65.2 us  [passed_along(): lax.ppermute(value, axis, [(source, (source + steps) % count) for source...]
where the time goes in v11:
time: 547 us; the launch traced here: 538 us
  blocking collectives  225 us (41%)
  matrix products  94.9 us (17%)
  starting transfers between devices  89 us (16%)
  waiting for transfers between devices  52.9 us (10%)
  local copies, waits for them, and re-layouts  47.4 us (9%)
  other arithmetic  26.6 us (5%)
    all_to_all x13, blocking collectives, apply_layer(): gathered = lax.all_to_all(copies, 'plane', 0, 0, tiled=True)  225 us
    dot_general x15, matrix products, apply_layer(): jnp.einsum('rkic,rkvwc->vwri', factor, expanded, preferred_element_type=j...  84.9 us
    ppermute x14, starting transfers between devices, passed_along(): lax.ppermute(value, axis, [(source, (source + steps) % count) for source...  65.2 us
    gather x15, local copies, waits for them, and re-layouts, apply_layer(): chosen = jnp.take(gathered, pattern_flat, axis=0, mode='clip')  28.1 us
    all_to_all x2, waiting for transfers between devices, apply_layer(): gathered = lax.all_to_all(copies, 'plane', 0, 0, tiled=True)  25 us
    ppermute x14, waiting for transfers between devices, passed_along(): lax.ppermute(value, axis, [(source, (source + steps) % count) for source...  18.2 us
    another operation x15, other arithmetic, apply_layer(): jnp.stack([jnp.concatenate([x_re, -x_im], axis=-1), jnp.concatenate([x_im...  17.3 us
    all_to_all x1, starting transfers between devices, shards(): received = lax.all_to_all(packed, ('depth', 'plane'), 0, 0, tiled=True)  12.3 us
  transfers between devices with their start and end apart: 17, of which 17 were waited for; matrix products, arithmetic and copies ran while one was open for 1% of the time, Pallas kernels for 0%

profile of v11, /device:TPU:1, one launch (start us, length us, event | category | flops | bytes accessed | tf_op | source)
XLA Modules:
  0.0 538.5 jit_solution(10050234385068426046)
XLA Ops:
  4.1 7.6 %all-to-all-start = ((bf16[16,32,8,128]{3,2,1,0:T(8,128)(2,1)}), bf16[16,32,8,128]{3,2,1,0:T(8,128)(2,1)S(1)}, u32[]{:S(2)}, u32[]{:S(2)}) async-start(bf16[16,32,8,128]{3,2,1,0:T(8,128)(2,1)} %broadcast_in_dim.134), calls=%async_computation | async-start | bytes 2097152 | tf_op jit(solution)/shard_map/all_to_all | solution.py:38
  11.9 15.3 %all-to-all-done = bf16[16,32,8,128]{3,2,1,0:T(8,128)(2,1)S(1)} async-done(((bf16[16,32,8,128]{3,2,1,0:T(8,128)(2,1)}), bf16[16,32,8,128]{3,2,1,0:T(8,128)(2,1)S(1)}, u32[]{:S(2)}, u32[]{:S(2)}) %all-to-all-start) | async-done | bytes 1048608 | tf_op jit(solution)/shard_map/all_to_all | solution.py:38
  30.7 5.7 %fusion.206 = bf16[8,2,32,64]{3,0,1,2:T(8,128)(2,1)S(1)} fusion(bf16[1,32,16,64,128]{4,3,2,1,0:T(8,128)(2,1)} %param.9, bf16[32,16,8,1,128]{4,2,1,3,0:T(8,128)(2,1)S(1)} %get-tuple-element.81, bf16[32,16,8,1,128]{4,2,1,3,0:T(8,128)(2,1)S(1)} %get-tuple-element.80), kind=kOutput, calls=%fused_computation.124 | convolution fusion | flops 135299072 | bytes 10551296 | tf_op jit(solution)/shard_map/rkic,rkvwc->vwri/dot_general | solution.py:48
  43.2 17.7 %all_to_all.80 = bf16[16,32,8,128]{3,2,1,0:T(8,128)(2,1)S(1)} all-to-all(bf16[16,32,8,128]{3,2,1,0:T(8,128)(2,1)S(1)} %broadcast_in_dim.137), channel_id=1, replica_groups=mesh['depth'=8,'plane'=16] {'plane'}, dimensions={0} | all-to-all | bytes 2097152 | tf_op jit(solution)/shard_map/all_to_all | solution.py:38
  77.1 18.1 %all_to_all.81 = bf16[16,32,8,128]{3,2,1,0:T(8,128)(2,1)S(1)} all-to-all(bf16[16,32,8,128]{3,2,1,0:T(8,128)(2,1)S(1)} %broadcast_in_dim.139), channel_id=1, replica_groups=mesh['depth'=8,'plane'=16] {'plane'}, dimensions={0} | all-to-all | bytes 2097152 | tf_op jit(solution)/shard_map/all_to_all | solution.py:38
  111.0 16.3 %all_to_all.82 = bf16[16,32,8,128]{3,2,1,0:T(8,128)(2,1)S(1)} all-to-all(bf16[16,32,8,128]{3,2,1,0:T(8,128)(2,1)S(1)} %broadcast_in_dim.141), channel_id=1, replica_groups=mesh['depth'=8,'plane'=16] {'plane'}, dimensions={0} | all-to-all | bytes 2097152 | tf_op jit(solution)/shard_map/all_to_all | solution.py:38
  142.9 15.1 %all_to_all.83 = bf16[16,32,8,128]{3,2,1,0:T(8,128)(2,1)S(1)} all-to-all(bf16[16,32,8,128]{3,2,1,0:T(8,128)(2,1)S(1)} %broadcast_in_dim.143), channel_id=1, replica_groups=mesh['depth'=8,'plane'=16] {'plane'}, dimensions={0} | all-to-all | bytes 2097152 | tf_op jit(solution)/shard_map/all_to_all | solution.py:38
  167.4 7.3 %collective-permute-start.4 = (bf16[8,2,2048]{2,0,1:T(8,128)(2,1)S(1)}, bf16[8,2,2048]{2,0,1:T(8,128)(2,1)S(1)}, u32[]{:S(2)}, u32[]{:S(2)}) collective-permute-start(bf16[8,2,2048]{2,0,1:T(8,128)(2,1)S(1)} %convert_element_type.284), channel_id=1, source_target_pairs={{0,16},{16,32},{32,48},{48,64},{64,80},{80,96},{96,112},{112,0},{1... | collective-permute-start | bytes 196616 | tf_op jit(solution)/shard_map/ppermute | solution.py:12
  176.8 16.0 %all_to_all.84 = bf16[16,32,8,128]{3,2,1,0:T(8,128)(2,1)S(1)} all-to-all(bf16[16,32,8,128]{3,2,1,0:T(8,128)(2,1)S(1)} %broadcast_in_dim.145), channel_id=1, replica_groups=mesh['depth'=8,'plane'=16] {'plane'}, dimensions={0} | all-to-all | bytes 2097152 | tf_op jit(solution)/shard_map/all_to_all | solution.py:38
  202.3 6.6 %collective-permute-start.5 = (bf16[8,2,2048]{2,0,1:T(8,128)(2,1)S(1)}, bf16[8,2,2048]{2,0,1:T(8,128)(2,1)S(1)}, u32[]{:S(2)}, u32[]{:S(2)}) collective-permute-start(bf16[8,2,2048]{2,0,1:T(8,128)(2,1)S(1)} %convert_element_type.289), channel_id=1, source_target_pairs={{0,16},{16,32},{32,48},{48,64},{64,80},{80,96},{96,112},{112,0},{1... | collective-permute-start | bytes 196616 | tf_op jit(solution)/shard_map/ppermute | solution.py:12
  210.9 18.4 %all_to_all.85 = bf16[16,32,8,128]{3,2,1,0:T(8,128)(2,1)S(1)} all-to-all(bf16[16,32,8,128]{3,2,1,0:T(8,128)(2,1)S(1)} %broadcast_in_dim.147), channel_id=1, replica_groups=mesh['depth'=8,'plane'=16] {'plane'}, dimensions={0} | all-to-all | bytes 2097152 | tf_op jit(solution)/shard_map/all_to_all | solution.py:38
  244.6 16.1 %all_to_all.86 = bf16[16,32,8,128]{3,2,1,0:T(8,128)(2,1)S(1)} all-to-all(bf16[16,32,8,128]{3,2,1,0:T(8,128)(2,1)S(1)} %broadcast_in_dim.149), channel_id=1, replica_groups=mesh['depth'=8,'plane'=16] {'plane'}, dimensions={0} | all-to-all | bytes 2097152 | tf_op jit(solution)/shard_map/all_to_all | solution.py:38
  277.1 17.7 %all_to_all.87 = bf16[16,32,8,128]{3,2,1,0:T(8,128)(2,1)S(1)} all-to-all(bf16[16,32,8,128]{3,2,1,0:T(8,128)(2,1)S(1)} %broadcast_in_dim.151), channel_id=1, replica_groups=mesh['depth'=8,'plane'=16] {'plane'}, dimensions={0} | all-to-all | bytes 2097152 | tf_op jit(solution)/shard_map/all_to_all | solution.py:38
  310.5 16.7 %all_to_all.88 = bf16[16,32,8,128]{3,2,1,0:T(8,128)(2,1)S(1)} all-to-all(bf16[16,32,8,128]{3,2,1,0:T(8,128)(2,1)S(1)} %broadcast_in_dim.153), channel_id=1, replica_groups=mesh['depth'=8,'plane'=16] {'plane'}, dimensions={0} | all-to-all | bytes 2097152 | tf_op jit(solution)/shard_map/all_to_all | solution.py:38
  342.9 19.2 %all_to_all.89 = bf16[16,32,8,128]{3,2,1,0:T(8,128)(2,1)S(1)} all-to-all(bf16[16,32,8,128]{3,2,1,0:T(8,128)(2,1)S(1)} %broadcast_in_dim.155), channel_id=1, replica_groups=mesh['depth'=8,'plane'=16] {'plane'}, dimensions={0} | all-to-all | bytes 2097152 | tf_op jit(solution)/shard_map/all_to_all | solution.py:38
  376.7 19.1 %all_to_all.90 = bf16[16,32,8,128]{3,2,1,0:T(8,128)(2,1)S(1)} all-to-all(bf16[16,32,8,128]{3,2,1,0:T(8,128)(2,1)S(1)} %broadcast_in_dim.157), channel_id=1, replica_groups=mesh['depth'=8,'plane'=16] {'plane'}, dimensions={0} | all-to-all | bytes 2097152 | tf_op jit(solution)/shard_map/all_to_all | solution.py:38
  410.1 17.8 %all_to_all.91 = bf16[16,32,8,128]{3,2,1,0:T(8,128)(2,1)S(1)} all-to-all(bf16[16,32,8,128]{3,2,1,0:T(8,128)(2,1)S(1)} %broadcast_in_dim.159), channel_id=1, replica_groups=mesh['depth'=8,'plane'=16] {'plane'}, dimensions={0} | all-to-all | bytes 2097152 | tf_op jit(solution)/shard_map/all_to_all | solution.py:38
  443.5 17.2 %all_to_all.92 = bf16[16,32,8,128]{3,2,1,0:T(8,128)(2,1)S(1)} all-to-all(bf16[16,32,8,128]{3,2,1,0:T(8,128)(2,1)S(1)} %broadcast_in_dim.161), channel_id=1, replica_groups=mesh['depth'=8,'plane'=16] {'plane'}, dimensions={0} | all-to-all | bytes 2097152 | tf_op jit(solution)/shard_map/all_to_all | solution.py:38
  464.2 5.7 %fusion.146 = f32[8,2,32,64]{3,0,1,2:T(8,128)S(1)} fusion(bf16[1,32,16,64,128]{4,3,2,1,0:T(8,128)(2,1)} %param.9, bf16[32,16,8,1,128]{4,2,1,3,0:T(8,128)(2,1)S(1)} %get-tuple-element.16, bf16[32,16,8,1,128]{4,2,1,3,0:T(8,128)(2,1)S(1)} %get-tuple-element.15), kind=kOutput, calls=%fused_computation.112 | convolution fusion | flops 135266304 | bytes 10616832 | tf_op jit(solution)/shard_map/rkic,rkvwc->vwri/dot_general | solution.py:48
  483.7 9.7 %all-to-all-done.14 = bf16[16,32,8,128]{3,2,1,0:T(8,128)(2,1)S(1)} async-done(((bf16[16,32,8,128]{3,2,1,0:T(8,128)(2,1)}), bf16[16,32,8,128]{3,2,1,0:T(8,128)(2,1)S(1)}, u32[]{:S(2)}, u32[]{:S(2)}) %all-to-all-start.14) | async-done | bytes 1048608 | tf_op jit(solution)/shard_map/all_to_all | solution.py:38
  497.0 5.7 %add_convert_fusion = (bf16[8,2,32,64]{3,0,1,2:T(8,128)(2,1)S(1)}, f32[8,2,32,64]{3,0,1,2:T(8,128)S(1)}) fusion(f32[8,2,32,64]{3,0,1,2:T(8,128)S(1)} %fusion.166, bf16[1,32,16,64,128]{4,3,2,1,0:T(8,128)(2,1)} %param.9, bf16[32,16,8,1,128]{4,2,1,3,0:T(8,128)(2,1)S(1)} %get-tuple-element.11, bf16[32,16,8,1,128]{4,2,1,3,0:T(8,128)(2,1)S(1)} %get-tuple-element.10), kind=kOutput, calls=%fused_computation.167 | convolution fusion | flops 135331840 | bytes 10813440 | tf_op jit(solution)/shard_map/rkic,rkvwc->vwri/dot_general | solution.py:48
  503.1 6.5 %fusion = f32[4096,27]{0,1:T(8,128)S(1)} fusion(s32[2048]{0:T(1024)S(1)} %add_add_fusion, bf16[2048,9]{0,1:T(8,128)(2,1)S(1)} %get-tuple-element.88, bf16[2048,9]{0,1:T(8,128)(2,1)S(1)} %get-tuple-element.89, bf16[2048,9]{0,1:T(8,128)(2,1)S(1)} %get-tuple-element.87), kind=kOutput, calls=%fused_computation.16 | convolution fusion | flops 461705216 | bytes 561152 | tf_op jit(solution)/shard_map/cs,cq->sq/dot_general | solution.py:91
  511.3 12.3 %all-to-all-start.15 = ((f32[128,1,288]{2,1,0:T(1,128)}), f32[128,1,288]{2,1,0:T(1,128)S(1)}, u32[]{:S(2)}, u32[]{:S(2)}) async-start(f32[128,1,288]{2,1,0:T(1,128)} %reshape.573), calls=%async_computation.15 | async-start | bytes 393216 | tf_op jit(solution)/shard_map/all_to_all | solution.py:95
  524.5 9.7 %all-to-all-done.15 = f32[128,1,288]{2,1,0:T(1,128)S(1)} async-done(((f32[128,1,288]{2,1,0:T(1,128)}), f32[128,1,288]{2,1,0:T(1,128)S(1)}, u32[]{:S(2)}, u32[]{:S(2)}) %all-to-all-start.15) | async-done | bytes 147488 | tf_op jit(solution)/shard_map/all_to_all | solution.py:95
  (235 shorter events, 218.8 us)
Async XLA Ops:
  2.3 9.4 %copy-start.5 = (s32[1,32,16]{1,2,0:T(8,128)S(1)}, s32[1,32,16]{1,2,0:T(8,128)}, u32[]{:S(2)}) copy-start(s32[1,32,16]{1,2,0:T(8,128)} %param.10) | copy-start | bytes 6148
  4.1 23.1 %all-to-all-start = ((bf16[16,32,8,128]{3,2,1,0:T(8,128)(2,1)}), bf16[16,32,8,128]{3,2,1,0:T(8,128)(2,1)S(1)}, u32[]{:S(2)}, u32[]{:S(2)}) async-start(bf16[16,32,8,128]{3,2,1,0:T(8,128)(2,1)} %broadcast_in_dim.134), calls=%async_computation | async-start | bytes 2097152 | tf_op jit(solution)/shard_map/all_to_all | solution.py:38
  11.9 17.6 %copy-start.1 = (s32[1024]{0:T(1024)}, s32[1024]{0:T(1024)S(1)}, u32[]{:S(2)}) copy-start(s32[1024]{0:T(1024)S(1)} %pad_clamp_fusion) | copy-start | bytes 12292
  30.6 11.9 %copy-start = (f32[1,2048]{1,0:T(1,128)S(1)}, f32[1,2048]{1,0:T(1,128)}, u32[]{:S(2)}) copy-start(f32[1,2048]{1,0:T(1,128)} %param.8) | copy-start | bytes 24580
  36.5 6.0 %collective-permute-start = (bf16[8,2,2048]{2,0,1:T(8,128)(2,1)S(1)}, bf16[8,2,2048]{2,0,1:T(8,128)(2,1)S(1)}, u32[]{:S(2)}, u32[]{:S(2)}) collective-permute-start(bf16[8,2,2048]{2,0,1:T(8,128)(2,1)S(1)} %convert_element_type.264), channel_id=1, source_target_pairs={{0,16},{16,32},{32,48},{48,64},{64,80},{80,96},{96,112},{112,0},{1... | collective-permute-start | bytes 196616 | tf_op jit(solution)/shard_map/ppermute | solution.py:12
  70.4 6.0 %collective-permute-start.1 = (bf16[8,2,2048]{2,0,1:T(8,128)(2,1)S(1)}, bf16[8,2,2048]{2,0,1:T(8,128)(2,1)S(1)}, u32[]{:S(2)}, u32[]{:S(2)}) collective-permute-start(bf16[8,2,2048]{2,0,1:T(8,128)(2,1)S(1)} %convert_element_type.269), channel_id=1, source_target_pairs={{0,16},{16,32},{32,48},{48,64},{64,80},{80,96},{96,112},{112,0},{1... | collective-permute-start | bytes 196616 | tf_op jit(solution)/shard_map/ppermute | solution.py:12
  104.6 5.7 %collective-permute-start.2 = (bf16[8,2,2048]{2,0,1:T(8,128)(2,1)S(1)}, bf16[8,2,2048]{2,0,1:T(8,128)(2,1)S(1)}, u32[]{:S(2)}, u32[]{:S(2)}) collective-permute-start(bf16[8,2,2048]{2,0,1:T(8,128)(2,1)S(1)} %convert_element_type.274), channel_id=1, source_target_pairs={{0,16},{16,32},{32,48},{48,64},{64,80},{80,96},{96,112},{112,0},{1... | collective-permute-start | bytes 196616 | tf_op jit(solution)/shard_map/ppermute | solution.py:12
  136.8 5.5 %collective-permute-start.3 = (bf16[8,2,2048]{2,0,1:T(8,128)(2,1)S(1)}, bf16[8,2,2048]{2,0,1:T(8,128)(2,1)S(1)}, u32[]{:S(2)}, u32[]{:S(2)}) collective-permute-start(bf16[8,2,2048]{2,0,1:T(8,128)(2,1)S(1)} %convert_element_type.279), channel_id=1, source_target_pairs={{0,16},{16,32},{32,48},{48,64},{64,80},{80,96},{96,112},{112,0},{1... | collective-permute-start | bytes 196616 | tf_op jit(solution)/shard_map/ppermute | solution.py:12
  167.4 8.7 %collective-permute-start.4 = (bf16[8,2,2048]{2,0,1:T(8,128)(2,1)S(1)}, bf16[8,2,2048]{2,0,1:T(8,128)(2,1)S(1)}, u32[]{:S(2)}, u32[]{:S(2)}) collective-permute-start(bf16[8,2,2048]{2,0,1:T(8,128)(2,1)S(1)} %convert_element_type.284), channel_id=1, source_target_pairs={{0,16},{16,32},{32,48},{48,64},{64,80},{80,96},{96,112},{112,0},{1... | collective-permute-start | bytes 196616 | tf_op jit(solution)/shard_map/ppermute | solution.py:12
  202.3 7.9 %collective-permute-start.5 = (bf16[8,2,2048]{2,0,1:T(8,128)(2,1)S(1)}, bf16[8,2,2048]{2,0,1:T(8,128)(2,1)S(1)}, u32[]{:S(2)}, u32[]{:S(2)}) collective-permute-start(bf16[8,2,2048]{2,0,1:T(8,128)(2,1)S(1)} %convert_element_type.289), channel_id=1, source_target_pairs={{0,16},{16,32},{32,48},{48,64},{64,80},{80,96},{96,112},{112,0},{1... | collective-permute-start | bytes 196616 | tf_op jit(solution)/shard_map/ppermute | solution.py:12
  238.7 5.2 collective-permute-start.6
  270.2 24.6 %copy-start.2 = (s32[1024]{0:T(1024)S(1)}, s32[1024]{0:T(1024)}, u32[]{:S(2)}) copy-start(s32[1024]{0:T(1024)} %copy-done.1) | copy-start | bytes 12292
  270.2 6.3 %collective-permute-start.7 = (bf16[8,2,2048]{2,0,1:T(8,128)(2,1)S(1)}, bf16[8,2,2048]{2,0,1:T(8,128)(2,1)S(1)}, u32[]{:S(2)}, u32[]{:S(2)}) collective-permute-start(bf16[8,2,2048]{2,0,1:T(8,128)(2,1)S(1)} %multiply_convert_fusion.6), channel_id=1, source_target_pairs={{0,112},{16,0},{32,16},{48,32},{64,48},{80,64},{96,80},{112,96},{1... | collective-permute-start | bytes 196616 | tf_op jit(solution)/shard_map/ppermute | solution.py:12
  304.1 5.7 %collective-permute-start.8 = (bf16[8,2,2048]{2,0,1:T(8,128)(2,1)S(1)}, bf16[8,2,2048]{2,0,1:T(8,128)(2,1)S(1)}, u32[]{:S(2)}, u32[]{:S(2)}) collective-permute-start(bf16[8,2,2048]{2,0,1:T(8,128)(2,1)S(1)} %multiply_convert_fusion.5), channel_id=1, source_target_pairs={{0,112},{16,0},{32,16},{48,32},{64,48},{80,64},{96,80},{112,96},{1... | collective-permute-start | bytes 196616 | tf_op jit(solution)/shard_map/ppermute | solution.py:12
  336.5 5.7 %collective-permute-start.9 = (bf16[8,2,2048]{2,0,1:T(8,128)(2,1)S(1)}, bf16[8,2,2048]{2,0,1:T(8,128)(2,1)S(1)}, u32[]{:S(2)}, u32[]{:S(2)}) collective-permute-start(bf16[8,2,2048]{2,0,1:T(8,128)(2,1)S(1)} %multiply_convert_fusion.4), channel_id=1, source_target_pairs={{0,112},{16,0},{32,16},{48,32},{64,48},{80,64},{96,80},{112,96},{1... | collective-permute-start | bytes 196616 | tf_op jit(solution)/shard_map/ppermute | solution.py:12
  371.4 4.6 collective-permute-start.10
  405.1 4.3 collective-permute-start.11
  437.2 5.7 %collective-permute-start.12 = (bf16[8,2,2048]{2,0,1:T(8,128)(2,1)S(1)}, bf16[8,2,2048]{2,0,1:T(8,128)(2,1)S(1)}, u32[]{:S(2)}, u32[]{:S(2)}) collective-permute-start(bf16[8,2,2048]{2,0,1:T(8,128)(2,1)S(1)} %multiply_convert_fusion.1), channel_id=1, source_target_pairs={{0,112},{16,0},{32,16},{48,32},{64,48},{80,64},{96,80},{112,96},{1... | collective-permute-start | bytes 196616 | tf_op jit(solution)/shard_map/ppermute | solution.py:12
  464.1 10.8 %copy-start.4 = (s32[1,2048]{1,0:T(1,128)S(1)}, s32[1,2048]{1,0:T(1,128)}, u32[]{:S(2)}) copy-start(s32[1,2048]{1,0:T(1,128)} %param.11) | copy-start | bytes 24580
  470.1 6.1 %collective-permute-start.13 = (bf16[8,2,2048]{2,0,1:T(8,128)(2,1)S(1)}, bf16[8,2,2048]{2,0,1:T(8,128)(2,1)S(1)}, u32[]{:S(2)}, u32[]{:S(2)}) collective-permute-start(bf16[8,2,2048]{2,0,1:T(8,128)(2,1)S(1)} %multiply_convert_fusion), channel_id=1, source_target_pairs={{0,112},{16,0},{32,16},{48,32},{64,48},{80,64},{96,80},{112,96},{1... | collective-permute-start | bytes 196616 | tf_op jit(solution)/shard_map/ppermute | solution.py:12
  477.8 15.6 %all-to-all-start.14 = ((bf16[16,32,8,128]{3,2,1,0:T(8,128)(2,1)}), bf16[16,32,8,128]{3,2,1,0:T(8,128)(2,1)S(1)}, u32[]{:S(2)}, u32[]{:S(2)}) async-start(bf16[16,32,8,128]{3,2,1,0:T(8,128)(2,1)} %broadcast_in_dim.163), calls=%async_computation.14 | async-start | bytes 2097152 | tf_op jit(solution)/shard_map/all_to_all | solution.py:38
  497.0 5.9 %copy-start.3 = (bf16[1,8,2,2048]{3,2,1,0:T(2,128)(2,1)S(1)}, bf16[1,8,2,2048]{3,2,1,0:T(2,128)(2,1)}, u32[]{:S(2)}) copy-start(bf16[1,8,2,2048]{3,2,1,0:T(2,128)(2,1)} %param.6) | copy-start | bytes 196612
  511.3 22.9 %all-to-all-start.15 = ((f32[128,1,288]{2,1,0:T(1,128)}), f32[128,1,288]{2,1,0:T(1,128)S(1)}, u32[]{:S(2)}, u32[]{:S(2)}) async-start(f32[128,1,288]{2,1,0:T(1,128)} %reshape.573), calls=%async_computation.15 | async-start | bytes 393216 | tf_op jit(solution)/shard_map/all_to_all | solution.py:95

commit v12 on v7

--- a/solution.py
+++ b/solution.py
@@ -9,8 +9,10 @@
 
 def passed_along(value, axis, steps):
     count = lax.axis_size(axis)
-    first, last = (max(0, -steps), min(count, count - steps))
-    return lax.ppermute(value, axis, [(source, source + steps) for source in range(first, last)])
+    moved = lax.ppermute(value, axis, [(source, (source + steps) % count) for source in range(count)])
+    target = lax.axis_index(axis) - steps
+    keep = (target >= 0) & (target < count)
+    return jnp.where(keep, moved, jnp.zeros_like(moved))
 
 
 def shards(toar, pml_coeff, coupling, inverse, pattern, patch_map):

time: 583 us -> 567 us (0.973)
  waiting for transfers between devices: 265 us -> 245 us
    ppermute x14, waiting for transfers between devices: 62.9 us -> 21.9 us  [passed_along(): lax.ppermute(value, axis, [(source, (source + steps) % count) for source...]
    all_to_all x15, waiting for transfers between devices: 192 us -> 214 us  [apply_layer(): gathered = lax.all_to_all(copies, 'plane', 0, 0, tiled=True)]
where the time goes in v12:
time: 567 us; the launch traced here: 565 us
  waiting for transfers between devices  245 us (43%)
  starting transfers between devices  135 us (24%)
  matrix products  94.9 us (17%)
  local copies, waits for them, and re-layouts  59.8 us (11%)
  other arithmetic  27.5 us (5%)
    all_to_all x15, waiting for transfers between devices, apply_layer(): gathered = lax.all_to_all(copies, 'plane', 0, 0, tiled=True)  214 us
    dot_general x15, matrix products, apply_layer(): jnp.einsum('rkic,rkvwc->vwri', factor, expanded, preferred_element_type=j...  84.9 us
    all_to_all x15, starting transfers between devices, apply_layer(): gathered = lax.all_to_all(copies, 'plane', 0, 0, tiled=True)  61.1 us
    ppermute x14, starting transfers between devices, passed_along(): lax.ppermute(value, axis, [(source, (source + steps) % count) for source...  60.1 us
    gather x15, local copies, waits for them, and re-layouts, apply_layer(): chosen = jnp.take(gathered, pattern_flat, axis=0, mode='clip')  27 us
    ppermute x14, waiting for transfers between devices, passed_along(): lax.ppermute(value, axis, [(source, (source + steps) % count) for source...  21.9 us
    broadcast_in_dim x30, local copies, waits for them, and re-layouts, apply_layer(): jnp.broadcast_to(local_blocks[None], (plane_count,) + local_blocks.shape)  19.4 us
    another operation x15, other arithmetic, apply_layer(): jnp.stack([jnp.concatenate([x_re, -x_im], axis=-1), jnp.concatenate([x_im...  17.3 us
  transfers between devices with their start and end apart: 30, of which 30 were waited for; matrix products, arithmetic and copies ran while one was open for 0% of the time, Pallas kernels for 0%

profile of v12, /device:TPU:1, one launch (start us, length us, event | category | flops | bytes accessed | tf_op | source)
XLA Modules:
  0.0 565.0 jit_solution(2972397121237480389)
XLA Ops:
  7.6 7.6 %all-to-all-start.2 = ((bf16[16,32,8,128]{3,2,1,0:T(8,128)(2,1)}), bf16[16,32,8,128]{3,2,1,0:T(8,128)(2,1)S(1)}, u32[]{:S(2)}, u32[]{:S(2)}) async-start(bf16[16,32,8,128]{3,2,1,0:T(8,128)(2,1)} %broadcast_in_dim.62), calls=%async_computation.2 | async-start | bytes 2097152 | tf_op jit(solution)/shard_map/all_to_all | solution.py:38
  15.3 15.4 %all-to-all-done.2 = bf16[16,32,8,128]{3,2,1,0:T(8,128)(2,1)S(1)} async-done(((bf16[16,32,8,128]{3,2,1,0:T(8,128)(2,1)}), bf16[16,32,8,128]{3,2,1,0:T(8,128)(2,1)S(1)}, u32[]{:S(2)}, u32[]{:S(2)}) %all-to-all-start.2) | async-done | bytes 1048608 | tf_op jit(solution)/shard_map/all_to_all | solution.py:38
  40.1 246.5 %while.24 = (s32[]{:T(128)}, bf16[8,2,2048]{2,0,1:T(8,128)(2,1)S(1)}, f32[1,2048]{1,0:T(1,128)S(1)}, f32[8,2,2048]{2,0,1:T(8,128)S(1)}, s32[512]{0:T(512)S(1)}, ...) while((s32[]{:T(128)}, ...), condition=%wide.region_1.2_spmd, body=%wide.region_0.1_spmd.sunk | while | flops 139920384 | bytes 24396032 | solution.py:59
  51.4 14.9 %all-to-all-done = bf16[16,32,8,128]{3,2,1,0:T(8,128)(2,1)S(1)} async-done(((bf16[16,32,8,128]{3,2,1,0:T(8,128)(2,1)}), bf16[16,32,8,128]{3,2,1,0:T(8,128)(2,1)S(1)}, u32[]{:S(2)}, u32[]{:S(2)}) %all-to-all-start) | async-done | bytes 1048608 | tf_op jit(solution)/shard_map/while/body/eval_jaxpr/all_to_all | solution.py:38
  87.6 15.2 %all-to-all-done = bf16[16,32,8,128]{3,2,1,0:T(8,128)(2,1)S(1)} async-done(((bf16[16,32,8,128]{3,2,1,0:T(8,128)(2,1)}), bf16[16,32,8,128]{3,2,1,0:T(8,128)(2,1)S(1)}, u32[]{:S(2)}, u32[]{:S(2)}) %all-to-all-start) | async-done | bytes 1048608 | tf_op jit(solution)/shard_map/while/body/eval_jaxpr/all_to_all | solution.py:38
  123.1 14.6 %all-to-all-done = bf16[16,32,8,128]{3,2,1,0:T(8,128)(2,1)S(1)} async-done(((bf16[16,32,8,128]{3,2,1,0:T(8,128)(2,1)}), bf16[16,32,8,128]{3,2,1,0:T(8,128)(2,1)S(1)}, u32[]{:S(2)}, u32[]{:S(2)}) %all-to-all-start) | async-done | bytes 1048608 | tf_op jit(solution)/shard_map/while/body/eval_jaxpr/all_to_all | solution.py:38
  156.5 12.1 %all-to-all-done = bf16[16,32,8,128]{3,2,1,0:T(8,128)(2,1)S(1)} async-done(((bf16[16,32,8,128]{3,2,1,0:T(8,128)(2,1)}), bf16[16,32,8,128]{3,2,1,0:T(8,128)(2,1)S(1)}, u32[]{:S(2)}, u32[]{:S(2)}) %all-to-all-start) | async-done | bytes 1048608 | tf_op jit(solution)/shard_map/while/body/eval_jaxpr/all_to_all | solution.py:38
  178.0 6.4 %collective-permute-start = (bf16[8,2,2048]{2,0,1:T(8,128)(2,1)S(1)}, bf16[8,2,2048]{2,0,1:T(8,128)(2,1)S(1)}, u32[]{:S(2)}, u32[]{:S(2)}) collective-permute-start(bf16[8,2,2048]{2,0,1:T(8,128)(2,1)S(1)} %get-tuple-element.315), channel_id=1, source_target_pairs={{0,16},{16,32},{32,48},{48,64},{64,80},{80,96},{96,112},{112,0},{1... | collective-permute-start | bytes 196616 | tf_op jit(solution)/shard_map/while/body/eval_jaxpr/ppermute | solution.py:12
  191.1 14.2 %all-to-all-done = bf16[16,32,8,128]{3,2,1,0:T(8,128)(2,1)S(1)} async-done(((bf16[16,32,8,128]{3,2,1,0:T(8,128)(2,1)}), bf16[16,32,8,128]{3,2,1,0:T(8,128)(2,1)S(1)}, u32[]{:S(2)}, u32[]{:S(2)}) %all-to-all-start) | async-done | bytes 1048608 | tf_op jit(solution)/shard_map/while/body/eval_jaxpr/all_to_all | solution.py:38
  227.2 15.2 %all-to-all-done = bf16[16,32,8,128]{3,2,1,0:T(8,128)(2,1)S(1)} async-done(((bf16[16,32,8,128]{3,2,1,0:T(8,128)(2,1)}), bf16[16,32,8,128]{3,2,1,0:T(8,128)(2,1)S(1)}, u32[]{:S(2)}, u32[]{:S(2)}) %all-to-all-start) | async-done | bytes 1048608 | tf_op jit(solution)/shard_map/while/body/eval_jaxpr/all_to_all | solution.py:38
  262.7 14.6 %all-to-all-done = bf16[16,32,8,128]{3,2,1,0:T(8,128)(2,1)S(1)} async-done(((bf16[16,32,8,128]{3,2,1,0:T(8,128)(2,1)}), bf16[16,32,8,128]{3,2,1,0:T(8,128)(2,1)S(1)}, u32[]{:S(2)}, u32[]{:S(2)}) %all-to-all-start) | async-done | bytes 1048608 | tf_op jit(solution)/shard_map/while/body/eval_jaxpr/all_to_all | solution.py:38
  286.6 241.7 %while.25 = (s32[]{:T(128)}, bf16[8,2,2048]{2,0,1:T(8,128)(2,1)S(1)}, bf16[8,2,2048]{2,0,1:T(8,128)(2,1)S(1)}, f32[1,2048]{1,0:T(1,128)S(1)}, s32[512]{0:T(512)S...) while((s32[]{:T(128)}, ...), condition=%wide.region_3.4_spmd, body=%wide.region_2.3_spmd.sunk | while | flops 139953152 | bytes 24985848 | solution.py:66
  296.9 14.6 %all-to-all-done.1 = bf16[16,32,8,128]{3,2,1,0:T(8,128)(2,1)S(1)} async-done(((bf16[16,32,8,128]{3,2,1,0:T(8,128)(2,1)}), bf16[16,32,8,128]{3,2,1,0:T(8,128)(2,1)S(1)}, u32[]{:S(2)}, u32[]{:S(2)}) %all-to-all-start.1) | async-done | bytes 1048608 | tf_op jit(solution)/shard_map/while/body/eval_jaxpr/all_to_all | solution.py:38
  332.7 14.6 %all-to-all-done.1 = bf16[16,32,8,128]{3,2,1,0:T(8,128)(2,1)S(1)} async-done(((bf16[16,32,8,128]{3,2,1,0:T(8,128)(2,1)}), bf16[16,32,8,128]{3,2,1,0:T(8,128)(2,1)S(1)}, u32[]{:S(2)}, u32[]{:S(2)}) %all-to-all-start.1) | async-done | bytes 1048608 | tf_op jit(solution)/shard_map/while/body/eval_jaxpr/all_to_all | solution.py:38
  368.7 17.1 %all-to-all-done.1 = bf16[16,32,8,128]{3,2,1,0:T(8,128)(2,1)S(1)} async-done(((bf16[16,32,8,128]{3,2,1,0:T(8,128)(2,1)}), bf16[16,32,8,128]{3,2,1,0:T(8,128)(2,1)S(1)}, u32[]{:S(2)}, u32[]{:S(2)}) %all-to-all-start.1) | async-done | bytes 1048608 | tf_op jit(solution)/shard_map/while/body/eval_jaxpr/all_to_all | solution.py:38
  404.2 15.4 %all-to-all-done.1 = bf16[16,32,8,128]{3,2,1,0:T(8,128)(2,1)S(1)} async-done(((bf16[16,32,8,128]{3,2,1,0:T(8,128)(2,1)}), bf16[16,32,8,128]{3,2,1,0:T(8,128)(2,1)S(1)}, u32[]{:S(2)}, u32[]{:S(2)}) %all-to-all-start.1) | async-done | bytes 1048608 | tf_op jit(solution)/shard_map/while/body/eval_jaxpr/all_to_all | solution.py:38
  438.5 12.0 %all-to-all-done.1 = bf16[16,32,8,128]{3,2,1,0:T(8,128)(2,1)S(1)} async-done(((bf16[16,32,8,128]{3,2,1,0:T(8,128)(2,1)}), bf16[16,32,8,128]{3,2,1,0:T(8,128)(2,1)S(1)}, u32[]{:S(2)}, u32[]{:S(2)}) %all-to-all-start.1) | async-done | bytes 1048608 | tf_op jit(solution)/shard_map/while/body/eval_jaxpr/all_to_all | solution.py:38
  459.8 6.1 %collective-permute-start.1 = (bf16[8,2,2048]{2,0,1:T(8,128)(2,1)S(1)}, bf16[8,2,2048]{2,0,1:T(8,128)(2,1)S(1)}, u32[]{:S(2)}, u32[]{:S(2)}) collective-permute-start(bf16[8,2,2048]{2,0,1:T(8,128)(2,1)S(1)} %multiply_convert_fusion.2), channel_id=1, source_target_pairs={{0,112},{16,0},{32,16},{48,32},{64,48},{80,64},{96,80},{112,96},{1... | collective-permute-start | bytes 196616 | tf_op jit(solution)/shard_map/while/body/eval_jaxpr/ppermute | solution.py:12
  472.8 11.9 %all-to-all-done.1 = bf16[16,32,8,128]{3,2,1,0:T(8,128)(2,1)S(1)} async-done(((bf16[16,32,8,128]{3,2,1,0:T(8,128)(2,1)}), bf16[16,32,8,128]{3,2,1,0:T(8,128)(2,1)S(1)}, u32[]{:S(2)}, u32[]{:S(2)}) %all-to-all-start.1) | async-done | bytes 1048608 | tf_op jit(solution)/shard_map/while/body/eval_jaxpr/all_to_all | solution.py:38
  494.1 6.2 %collective-permute-start.1 = (bf16[8,2,2048]{2,0,1:T(8,128)(2,1)S(1)}, bf16[8,2,2048]{2,0,1:T(8,128)(2,1)S(1)}, u32[]{:S(2)}, u32[]{:S(2)}) collective-permute-start(bf16[8,2,2048]{2,0,1:T(8,128)(2,1)S(1)} %multiply_convert_fusion.2), channel_id=1, source_target_pairs={{0,112},{16,0},{32,16},{48,32},{64,48},{80,64},{96,80},{112,96},{1... | collective-permute-start | bytes 196616 | tf_op jit(solution)/shard_map/while/body/eval_jaxpr/ppermute | solution.py:12
  507.2 11.8 %all-to-all-done.1 = bf16[16,32,8,128]{3,2,1,0:T(8,128)(2,1)S(1)} async-done(((bf16[16,32,8,128]{3,2,1,0:T(8,128)(2,1)}), bf16[16,32,8,128]{3,2,1,0:T(8,128)(2,1)S(1)}, u32[]{:S(2)}, u32[]{:S(2)}) %all-to-all-start.1) | async-done | bytes 1048608 | tf_op jit(solution)/shard_map/while/body/eval_jaxpr/all_to_all | solution.py:38
  528.4 6.5 %fusion.32 = f32[4096,27]{0,1:T(8,128)S(1)} fusion(s32[2048]{0:T(1024)S(1)} %add_add_fusion, bf16[2048,9]{0,1:T(8,128)(2,1)S(1)} %get-tuple-element.204, bf16[2048,9]{0,1:T(8,128)(2,1)S(1)} %get-tuple-element.205, bf16[2048,9]{0,1:T(8,128)(2,1)S(1)} %get-tuple-element.203), kind=kOutput, calls=%fused_computation.34 | convolution fusion | flops 461705216 | bytes 561152 | tf_op jit(solution)/shard_map/cs,cq->sq/dot_general | solution.py:88
  536.7 13.8 %all-to-all-start.3 = ((f32[128,1,288]{2,1,0:T(1,128)}), f32[128,1,288]{2,1,0:T(1,128)S(1)}, u32[]{:S(2)}, u32[]{:S(2)}) async-start(f32[128,1,288]{2,1,0:T(1,128)} %reshape.249), calls=%async_computation.3 | async-start | bytes 393216 | tf_op jit(solution)/shard_map/all_to_all | solution.py:92
  551.2 9.9 %all-to-all-done.3 = f32[128,1,288]{2,1,0:T(1,128)S(1)} async-done(((f32[128,1,288]{2,1,0:T(1,128)}), f32[128,1,288]{2,1,0:T(1,128)S(1)}, u32[]{:S(2)}, u32[]{:S(2)}) %all-to-all-start.3) | async-done | bytes 147488 | tf_op jit(solution)/shard_map/all_to_all | solution.py:92
  (266 shorter events, 292.5 us)
Async XLA Ops:
  7.6 23.1 %all-to-all-start.2 = ((bf16[16,32,8,128]{3,2,1,0:T(8,128)(2,1)}), bf16[16,32,8,128]{3,2,1,0:T(8,128)(2,1)S(1)}, u32[]{:S(2)}, u32[]{:S(2)}) async-start(bf16[16,32,8,128]{3,2,1,0:T(8,128)(2,1)} %broadcast_in_dim.62), calls=%async_computation.2 | async-start | bytes 2097152 | tf_op jit(solution)/shard_map/all_to_all | solution.py:38
  40.1 6.0 %collective-permute-start = (bf16[8,2,2048]{2,0,1:T(8,128)(2,1)S(1)}, bf16[8,2,2048]{2,0,1:T(8,128)(2,1)S(1)}, u32[]{:S(2)}, u32[]{:S(2)}) collective-permute-start(bf16[8,2,2048]{2,0,1:T(8,128)(2,1)S(1)} %get-tuple-element.315), channel_id=1, source_target_pairs={{0,16},{16,32},{32,48},{48,64},{64,80},{80,96},{96,112},{112,0},{1... | collective-permute-start | bytes 196616 | tf_op jit(solution)/shard_map/while/body/eval_jaxpr/ppermute | solution.py:12
  47.8 18.5 %all-to-all-start = ((bf16[16,32,8,128]{3,2,1,0:T(8,128)(2,1)}), bf16[16,32,8,128]{3,2,1,0:T(8,128)(2,1)S(1)}, u32[]{:S(2)}, u32[]{:S(2)}) async-start(bf16[16,32,8,128]{3,2,1,0:T(8,128)(2,1)} %broadcast_in_dim.70), calls=%async_computation | async-start | bytes 2097152 | tf_op jit(solution)/shard_map/while/body/eval_jaxpr/all_to_all | solution.py:38
  75.6 6.7 %collective-permute-start = (bf16[8,2,2048]{2,0,1:T(8,128)(2,1)S(1)}, bf16[8,2,2048]{2,0,1:T(8,128)(2,1)S(1)}, u32[]{:S(2)}, u32[]{:S(2)}) collective-permute-start(bf16[8,2,2048]{2,0,1:T(8,128)(2,1)S(1)} %get-tuple-element.315), channel_id=1, source_target_pairs={{0,16},{16,32},{32,48},{48,64},{64,80},{80,96},{96,112},{112,0},{1... | collective-permute-start | bytes 196616 | tf_op jit(solution)/shard_map/while/body/eval_jaxpr/ppermute | solution.py:12
  84.0 18.9 %all-to-all-start = ((bf16[16,32,8,128]{3,2,1,0:T(8,128)(2,1)}), bf16[16,32,8,128]{3,2,1,0:T(8,128)(2,1)S(1)}, u32[]{:S(2)}, u32[]{:S(2)}) async-start(bf16[16,32,8,128]{3,2,1,0:T(8,128)(2,1)} %broadcast_in_dim.70), calls=%async_computation | async-start | bytes 2097152 | tf_op jit(solution)/shard_map/while/body/eval_jaxpr/all_to_all | solution.py:38
  119.4 18.3 %all-to-all-start = ((bf16[16,32,8,128]{3,2,1,0:T(8,128)(2,1)}), bf16[16,32,8,128]{3,2,1,0:T(8,128)(2,1)S(1)}, u32[]{:S(2)}, u32[]{:S(2)}) async-start(bf16[16,32,8,128]{3,2,1,0:T(8,128)(2,1)} %broadcast_in_dim.70), calls=%async_computation | async-start | bytes 2097152 | tf_op jit(solution)/shard_map/while/body/eval_jaxpr/all_to_all | solution.py:38
  152.8 15.8 %all-to-all-start = ((bf16[16,32,8,128]{3,2,1,0:T(8,128)(2,1)}), bf16[16,32,8,128]{3,2,1,0:T(8,128)(2,1)S(1)}, u32[]{:S(2)}, u32[]{:S(2)}) async-start(bf16[16,32,8,128]{3,2,1,0:T(8,128)(2,1)} %broadcast_in_dim.70), calls=%async_computation | async-start | bytes 2097152 | tf_op jit(solution)/shard_map/while/body/eval_jaxpr/all_to_all | solution.py:38
  178.0 7.8 %collective-permute-start = (bf16[8,2,2048]{2,0,1:T(8,128)(2,1)S(1)}, bf16[8,2,2048]{2,0,1:T(8,128)(2,1)S(1)}, u32[]{:S(2)}, u32[]{:S(2)}) collective-permute-start(bf16[8,2,2048]{2,0,1:T(8,128)(2,1)S(1)} %get-tuple-element.315), channel_id=1, source_target_pairs={{0,16},{16,32},{32,48},{48,64},{64,80},{80,96},{96,112},{112,0},{1... | collective-permute-start | bytes 196616 | tf_op jit(solution)/shard_map/while/body/eval_jaxpr/ppermute | solution.py:12
  187.4 17.9 %all-to-all-start = ((bf16[16,32,8,128]{3,2,1,0:T(8,128)(2,1)}), bf16[16,32,8,128]{3,2,1,0:T(8,128)(2,1)S(1)}, u32[]{:S(2)}, u32[]{:S(2)}) async-start(bf16[16,32,8,128]{3,2,1,0:T(8,128)(2,1)} %broadcast_in_dim.70), calls=%async_computation | async-start | bytes 2097152 | tf_op jit(solution)/shard_map/while/body/eval_jaxpr/all_to_all | solution.py:38
  214.6 6.3 %collective-permute-start = (bf16[8,2,2048]{2,0,1:T(8,128)(2,1)S(1)}, bf16[8,2,2048]{2,0,1:T(8,128)(2,1)S(1)}, u32[]{:S(2)}, u32[]{:S(2)}) collective-permute-start(bf16[8,2,2048]{2,0,1:T(8,128)(2,1)S(1)} %get-tuple-element.315), channel_id=1, source_target_pairs={{0,16},{16,32},{32,48},{48,64},{64,80},{80,96},{96,112},{112,0},{1... | collective-permute-start | bytes 196616 | tf_op jit(solution)/shard_map/while/body/eval_jaxpr/ppermute | solution.py:12
  222.6 19.8 %all-to-all-start = ((bf16[16,32,8,128]{3,2,1,0:T(8,128)(2,1)}), bf16[16,32,8,128]{3,2,1,0:T(8,128)(2,1)S(1)}, u32[]{:S(2)}, u32[]{:S(2)}) async-start(bf16[16,32,8,128]{3,2,1,0:T(8,128)(2,1)} %broadcast_in_dim.70), calls=%async_computation | async-start | bytes 2097152 | tf_op jit(solution)/shard_map/while/body/eval_jaxpr/all_to_all | solution.py:38
  259.0 18.3 %all-to-all-start = ((bf16[16,32,8,128]{3,2,1,0:T(8,128)(2,1)}), bf16[16,32,8,128]{3,2,1,0:T(8,128)(2,1)S(1)}, u32[]{:S(2)}, u32[]{:S(2)}) async-start(bf16[16,32,8,128]{3,2,1,0:T(8,128)(2,1)} %broadcast_in_dim.70), calls=%async_computation | async-start | bytes 2097152 | tf_op jit(solution)/shard_map/while/body/eval_jaxpr/all_to_all | solution.py:38
  293.3 18.3 %all-to-all-start.1 = ((bf16[16,32,8,128]{3,2,1,0:T(8,128)(2,1)}), bf16[16,32,8,128]{3,2,1,0:T(8,128)(2,1)S(1)}, u32[]{:S(2)}, u32[]{:S(2)}) async-start(bf16[16,32,8,128]{3,2,1,0:T(8,128)(2,1)} %broadcast_in_dim.72), calls=%async_computation.1 | async-start | bytes 2097152 | tf_op jit(solution)/shard_map/while/body/eval_jaxpr/all_to_all | solution.py:38
  320.9 6.5 %collective-permute-start.1 = (bf16[8,2,2048]{2,0,1:T(8,128)(2,1)S(1)}, bf16[8,2,2048]{2,0,1:T(8,128)(2,1)S(1)}, u32[]{:S(2)}, u32[]{:S(2)}) collective-permute-start(bf16[8,2,2048]{2,0,1:T(8,128)(2,1)S(1)} %multiply_convert_fusion.2), channel_id=1, source_target_pairs={{0,112},{16,0},{32,16},{48,32},{64,48},{80,64},{96,80},{112,96},{1... | collective-permute-start | bytes 196616 | tf_op jit(solution)/shard_map/while/body/eval_jaxpr/ppermute | solution.py:12
  329.0 18.3 %all-to-all-start.1 = ((bf16[16,32,8,128]{3,2,1,0:T(8,128)(2,1)}), bf16[16,32,8,128]{3,2,1,0:T(8,128)(2,1)S(1)}, u32[]{:S(2)}, u32[]{:S(2)}) async-start(bf16[16,32,8,128]{3,2,1,0:T(8,128)(2,1)} %broadcast_in_dim.72), calls=%async_computation.1 | async-start | bytes 2097152 | tf_op jit(solution)/shard_map/while/body/eval_jaxpr/all_to_all | solution.py:38
  356.6 6.7 %collective-permute-start.1 = (bf16[8,2,2048]{2,0,1:T(8,128)(2,1)S(1)}, bf16[8,2,2048]{2,0,1:T(8,128)(2,1)S(1)}, u32[]{:S(2)}, u32[]{:S(2)}) collective-permute-start(bf16[8,2,2048]{2,0,1:T(8,128)(2,1)S(1)} %multiply_convert_fusion.2), channel_id=1, source_target_pairs={{0,112},{16,0},{32,16},{48,32},{64,48},{80,64},{96,80},{112,96},{1... | collective-permute-start | bytes 196616 | tf_op jit(solution)/shard_map/while/body/eval_jaxpr/ppermute | solution.py:12
  365.0 20.8 %all-to-all-start.1 = ((bf16[16,32,8,128]{3,2,1,0:T(8,128)(2,1)}), bf16[16,32,8,128]{3,2,1,0:T(8,128)(2,1)S(1)}, u32[]{:S(2)}, u32[]{:S(2)}) async-start(bf16[16,32,8,128]{3,2,1,0:T(8,128)(2,1)} %broadcast_in_dim.72), calls=%async_computation.1 | async-start | bytes 2097152 | tf_op jit(solution)/shard_map/while/body/eval_jaxpr/all_to_all | solution.py:38
  400.5 19.1 %all-to-all-start.1 = ((bf16[16,32,8,128]{3,2,1,0:T(8,128)(2,1)}), bf16[16,32,8,128]{3,2,1,0:T(8,128)(2,1)S(1)}, u32[]{:S(2)}, u32[]{:S(2)}) async-start(bf16[16,32,8,128]{3,2,1,0:T(8,128)(2,1)} %broadcast_in_dim.72), calls=%async_computation.1 | async-start | bytes 2097152 | tf_op jit(solution)/shard_map/while/body/eval_jaxpr/all_to_all | solution.py:38
  434.6 15.9 %all-to-all-start.1 = ((bf16[16,32,8,128]{3,2,1,0:T(8,128)(2,1)}), bf16[16,32,8,128]{3,2,1,0:T(8,128)(2,1)S(1)}, u32[]{:S(2)}, u32[]{:S(2)}) async-start(bf16[16,32,8,128]{3,2,1,0:T(8,128)(2,1)} %broadcast_in_dim.72), calls=%async_computation.1 | async-start | bytes 2097152 | tf_op jit(solution)/shard_map/while/body/eval_jaxpr/all_to_all | solution.py:38
  459.8 7.0 %collective-permute-start.1 = (bf16[8,2,2048]{2,0,1:T(8,128)(2,1)S(1)}, bf16[8,2,2048]{2,0,1:T(8,128)(2,1)S(1)}, u32[]{:S(2)}, u32[]{:S(2)}) collective-permute-start(bf16[8,2,2048]{2,0,1:T(8,128)(2,1)S(1)} %multiply_convert_fusion.2), channel_id=1, source_target_pairs={{0,112},{16,0},{32,16},{48,32},{64,48},{80,64},{96,80},{112,96},{1... | collective-permute-start | bytes 196616 | tf_op jit(solution)/shard_map/while/body/eval_jaxpr/ppermute | solution.py:12
  468.4 16.3 %all-to-all-start.1 = ((bf16[16,32,8,128]{3,2,1,0:T(8,128)(2,1)}), bf16[16,32,8,128]{3,2,1,0:T(8,128)(2,1)S(1)}, u32[]{:S(2)}, u32[]{:S(2)}) async-start(bf16[16,32,8,128]{3,2,1,0:T(8,128)(2,1)} %broadcast_in_dim.72), calls=%async_computation.1 | async-start | bytes 2097152 | tf_op jit(solution)/shard_map/while/body/eval_jaxpr/all_to_all | solution.py:38
  494.1 7.1 %collective-permute-start.1 = (bf16[8,2,2048]{2,0,1:T(8,128)(2,1)S(1)}, bf16[8,2,2048]{2,0,1:T(8,128)(2,1)S(1)}, u32[]{:S(2)}, u32[]{:S(2)}) collective-permute-start(bf16[8,2,2048]{2,0,1:T(8,128)(2,1)S(1)} %multiply_convert_fusion.2), channel_id=1, source_target_pairs={{0,112},{16,0},{32,16},{48,32},{64,48},{80,64},{96,80},{112,96},{1... | collective-permute-start | bytes 196616 | tf_op jit(solution)/shard_map/while/body/eval_jaxpr/ppermute | solution.py:12
  502.9 16.1 %all-to-all-start.1 = ((bf16[16,32,8,128]{3,2,1,0:T(8,128)(2,1)}), bf16[16,32,8,128]{3,2,1,0:T(8,128)(2,1)S(1)}, u32[]{:S(2)}, u32[]{:S(2)}) async-start(bf16[16,32,8,128]{3,2,1,0:T(8,128)(2,1)} %broadcast_in_dim.72), calls=%async_computation.1 | async-start | bytes 2097152 | tf_op jit(solution)/shard_map/while/body/eval_jaxpr/all_to_all | solution.py:38
  536.7 24.4 %all-to-all-start.3 = ((f32[128,1,288]{2,1,0:T(1,128)}), f32[128,1,288]{2,1,0:T(1,128)S(1)}, u32[]{:S(2)}, u32[]{:S(2)}) async-start(f32[128,1,288]{2,1,0:T(1,128)} %reshape.249), calls=%async_computation.3 | async-start | bytes 393216 | tf_op jit(solution)/shard_map/all_to_all | solution.py:92
  (9 other events, 284.3 us)

commit v13 on v11

--- a/solution.py
+++ b/solution.py
@@ -67,9 +67,6 @@
     precond = swept
     for turn_index in range(depth_count - 1):
         precond = up_turn(turn_index, precond)
-    product = precond.astype(jnp.float32) * toar_f32
-    contrib = product[:, 0] + product[:, 1]
-
     cell_patch = patch_map[0]
     cell_count = cell_patch.shape[0]
     owner_count = depth_count * plane_count
@@ -81,16 +78,16 @@
     rank = jnp.sum(running * hits.astype(jnp.float32), axis=1).astype(jnp.int32) - 1
     slot = owner * CAP + rank
     placed = (slot[:, None] == jnp.arange(owner_count * CAP, dtype=jnp.int32)[None, :]).astype(jnp.bfloat16)
-    local_patch = (cell_patch % PATCH_DEV).astype(jnp.float32)
-    rows = jnp.concatenate([contrib.T, local_patch[:, None]], axis=1)
-    high = lax.reduce_precision(rows, exponent_bits=8, mantissa_bits=7)
-    rest = rows - high
-    middle = lax.reduce_precision(rest, exponent_bits=8, mantissa_bits=7)
-    low = rest - middle
-    parts = jnp.concatenate([high, middle, low], axis=1).astype(jnp.bfloat16)
-    moved = jnp.einsum("cs,cq->sq", placed, parts, preferred_element_type=jnp.float32)
+    local_patch = (cell_patch % PATCH_DEV).astype(jnp.bfloat16)
+    toar_rows = jnp.concatenate([toar_local.reshape(-1, cell_count).T, local_patch[:, None]], axis=1)
+    toar_moved = jnp.einsum("cs,cq->sq", placed, toar_rows, preferred_element_type=jnp.float32)
+    precond_rows = precond.reshape(-1, cell_count).T
+    precond_moved = jnp.einsum("cs,cq->sq", placed, precond_rows, preferred_element_type=jnp.float32)
+    slots = owner_count * CAP
+    product = precond_moved.reshape(slots, vec_count, 2) * toar_moved[:, :-1].reshape(slots, vec_count, 2)
+    contrib = product[..., 0] + product[..., 1]
+    packed = jnp.concatenate([contrib, toar_moved[:, -1:]], axis=1)
     width = vec_count + 1
-    packed = (moved[:, :width] + moved[:, width:2 * width]) + moved[:, 2 * width:]
     packed = packed.reshape(owner_count, CAP, width)
     received = lax.all_to_all(packed, ("depth", "plane"), 0, 0, tiled=True)
     received = received.reshape(owner_count * CAP, vec_count + 1)

time: 547 us -> 549 us (level)
  blocking collectives: 225 us -> 208 us
  waiting for transfers between devices: 52.9 us -> 64.4 us
    all_to_all x13 -> x12, blocking collectives: 225 us -> 208 us  [apply_layer(): gathered = lax.all_to_all(copies, 'plane', 0, 0, tiled=True)]
    all_to_all x2 -> x3, waiting for transfers between devices: 25 us -> 37.6 us  [apply_layer(): gathered = lax.all_to_all(copies, 'plane', 0, 0, tiled=True)]
    dot_general x1 -> x2, matrix products: 6.48 us -> 11.8 us  [the longest x1 5.92 us: shards(): jnp.einsum('cs,cq->sq', placed, toar_rows, preferred_element_type=jnp.flo...]
    all_to_all x2 -> x3, starting transfers between devices: 11.5 us -> 15.7 us  [apply_layer(): gathered = lax.all_to_all(copies, 'plane', 0, 0, tiled=True)]
  transfers between devices with their start and end apart: 17 -> 18, of which waited for: 17 -> 17; matrix products, arithmetic and copies ran while one was open for 1% -> 2% of each run, Pallas kernels for 0% -> 0%
where the time goes in v13:
time: 549 us; the launch traced here: 540 us
  blocking collectives  208 us (38%)
  matrix products  100 us (18%)
  starting transfers between devices  90 us (16%)
  waiting for transfers between devices  64.4 us (12%)
  local copies, waits for them, and re-layouts  48.8 us (9%)
  other arithmetic  26.5 us (5%)
    all_to_all x12, blocking collectives, apply_layer(): gathered = lax.all_to_all(copies, 'plane', 0, 0, tiled=True)  208 us
    dot_general x15, matrix products, apply_layer(): jnp.einsum('rkic,rkvwc->vwri', factor, expanded, preferred_element_type=j...  84.9 us
    ppermute x14, starting transfers between devices, passed_along(): lax.ppermute(value, axis, [(source, (source + steps) % count) for source...  64.3 us
    all_to_all x3, waiting for transfers between devices, apply_layer(): gathered = lax.all_to_all(copies, 'plane', 0, 0, tiled=True)  37.6 us
    gather x15, local copies, waits for them, and re-layouts, apply_layer(): chosen = jnp.take(gathered, pattern_flat, axis=0, mode='clip')  28.1 us
    another operation x15, other arithmetic, apply_layer(): jnp.stack([jnp.concatenate([x_re, -x_im], axis=-1), jnp.concatenate([x_im...  17.3 us
    ppermute x14, waiting for transfers between devices, passed_along(): lax.ppermute(value, axis, [(source, (source + steps) % count) for source...  17 us
    all_to_all x3, starting transfers between devices, apply_layer(): gathered = lax.all_to_all(copies, 'plane', 0, 0, tiled=True)  15.7 us
  transfers between devices with their start and end apart: 18, of which 17 were waited for; matrix products, arithmetic and copies ran while one was open for 2% of the time, Pallas kernels for 0%

profile of v13, /device:TPU:1, one launch (start us, length us, event | category | flops | bytes accessed | tf_op | source)
XLA Modules:
  0.0 540.5 jit_solution(892718504435606333)
XLA Ops:
  4.1 7.6 %all-to-all-start = ((bf16[16,32,8,128]{3,2,1,0:T(8,128)(2,1)}), bf16[16,32,8,128]{3,2,1,0:T(8,128)(2,1)S(1)}, u32[]{:S(2)}, u32[]{:S(2)}) async-start(bf16[16,32,8,128]{3,2,1,0:T(8,128)(2,1)} %broadcast_in_dim.134), calls=%async_computation | async-start | bytes 2097152 | tf_op jit(solution)/shard_map/all_to_all | solution.py:38
  11.9 15.3 %all-to-all-done = bf16[16,32,8,128]{3,2,1,0:T(8,128)(2,1)S(1)} async-done(((bf16[16,32,8,128]{3,2,1,0:T(8,128)(2,1)}), bf16[16,32,8,128]{3,2,1,0:T(8,128)(2,1)S(1)}, u32[]{:S(2)}, u32[]{:S(2)}) %all-to-all-start) | async-done | bytes 1048608 | tf_op jit(solution)/shard_map/all_to_all | solution.py:38
  30.7 5.7 %fusion.213 = bf16[8,2,32,64]{3,0,1,2:T(8,128)(2,1)S(1)} fusion(bf16[1,32,16,64,128]{4,3,2,1,0:T(8,128)(2,1)} %param.9, bf16[32,16,8,1,128]{4,2,1,3,0:T(8,128)(2,1)S(1)} %get-tuple-element.81, bf16[32,16,8,1,128]{4,2,1,3,0:T(8,128)(2,1)S(1)} %get-tuple-element.80), kind=kOutput, calls=%fused_computation.128 | convolution fusion | flops 135299072 | bytes 10551296 | tf_op jit(solution)/shard_map/rkic,rkvwc->vwri/dot_general | solution.py:48
  43.3 17.7 %all_to_all.80 = bf16[16,32,8,128]{3,2,1,0:T(8,128)(2,1)S(1)} all-to-all(bf16[16,32,8,128]{3,2,1,0:T(8,128)(2,1)S(1)} %broadcast_in_dim.137), channel_id=1, replica_groups=mesh['depth'=8,'plane'=16] {'plane'}, dimensions={0} | all-to-all | bytes 2097152 | tf_op jit(solution)/shard_map/all_to_all | solution.py:38
  77.1 18.1 %all_to_all.81 = bf16[16,32,8,128]{3,2,1,0:T(8,128)(2,1)S(1)} all-to-all(bf16[16,32,8,128]{3,2,1,0:T(8,128)(2,1)S(1)} %broadcast_in_dim.139), channel_id=1, replica_groups=mesh['depth'=8,'plane'=16] {'plane'}, dimensions={0} | all-to-all | bytes 2097152 | tf_op jit(solution)/shard_map/all_to_all | solution.py:38
  111.0 16.3 %all_to_all.82 = bf16[16,32,8,128]{3,2,1,0:T(8,128)(2,1)S(1)} all-to-all(bf16[16,32,8,128]{3,2,1,0:T(8,128)(2,1)S(1)} %broadcast_in_dim.141), channel_id=1, replica_groups=mesh['depth'=8,'plane'=16] {'plane'}, dimensions={0} | all-to-all | bytes 2097152 | tf_op jit(solution)/shard_map/all_to_all | solution.py:38
  142.9 15.1 %all_to_all.83 = bf16[16,32,8,128]{3,2,1,0:T(8,128)(2,1)S(1)} all-to-all(bf16[16,32,8,128]{3,2,1,0:T(8,128)(2,1)S(1)} %broadcast_in_dim.143), channel_id=1, replica_groups=mesh['depth'=8,'plane'=16] {'plane'}, dimensions={0} | all-to-all | bytes 2097152 | tf_op jit(solution)/shard_map/all_to_all | solution.py:38
  167.5 7.3 %collective-permute-start.4 = (bf16[8,2,2048]{2,0,1:T(8,128)(2,1)S(1)}, bf16[8,2,2048]{2,0,1:T(8,128)(2,1)S(1)}, u32[]{:S(2)}, u32[]{:S(2)}) collective-permute-start(bf16[8,2,2048]{2,0,1:T(8,128)(2,1)S(1)} %convert_element_type.286), channel_id=1, source_target_pairs={{0,16},{16,32},{32,48},{48,64},{64,80},{80,96},{96,112},{112,0},{1... | collective-permute-start | bytes 196616 | tf_op jit(solution)/shard_map/ppermute | solution.py:12
  176.8 16.0 %all_to_all.84 = bf16[16,32,8,128]{3,2,1,0:T(8,128)(2,1)S(1)} all-to-all(bf16[16,32,8,128]{3,2,1,0:T(8,128)(2,1)S(1)} %broadcast_in_dim.145), channel_id=1, replica_groups=mesh['depth'=8,'plane'=16] {'plane'}, dimensions={0} | all-to-all | bytes 2097152 | tf_op jit(solution)/shard_map/all_to_all | solution.py:38
  202.3 6.6 %collective-permute-start.5 = (bf16[8,2,2048]{2,0,1:T(8,128)(2,1)S(1)}, bf16[8,2,2048]{2,0,1:T(8,128)(2,1)S(1)}, u32[]{:S(2)}, u32[]{:S(2)}) collective-permute-start(bf16[8,2,2048]{2,0,1:T(8,128)(2,1)S(1)} %convert_element_type.291), channel_id=1, source_target_pairs={{0,16},{16,32},{32,48},{48,64},{64,80},{80,96},{96,112},{112,0},{1... | collective-permute-start | bytes 196616 | tf_op jit(solution)/shard_map/ppermute | solution.py:12
  210.9 18.4 %all_to_all.85 = bf16[16,32,8,128]{3,2,1,0:T(8,128)(2,1)S(1)} all-to-all(bf16[16,32,8,128]{3,2,1,0:T(8,128)(2,1)S(1)} %broadcast_in_dim.147), channel_id=1, replica_groups=mesh['depth'=8,'plane'=16] {'plane'}, dimensions={0} | all-to-all | bytes 2097152 | tf_op jit(solution)/shard_map/all_to_all | solution.py:38
  244.6 16.1 %all_to_all.86 = bf16[16,32,8,128]{3,2,1,0:T(8,128)(2,1)S(1)} all-to-all(bf16[16,32,8,128]{3,2,1,0:T(8,128)(2,1)S(1)} %broadcast_in_dim.149), channel_id=1, replica_groups=mesh['depth'=8,'plane'=16] {'plane'}, dimensions={0} | all-to-all | bytes 2097152 | tf_op jit(solution)/shard_map/all_to_all | solution.py:38
  277.2 17.7 %all_to_all.87 = bf16[16,32,8,128]{3,2,1,0:T(8,128)(2,1)S(1)} all-to-all(bf16[16,32,8,128]{3,2,1,0:T(8,128)(2,1)S(1)} %broadcast_in_dim.151), channel_id=1, replica_groups=mesh['depth'=8,'plane'=16] {'plane'}, dimensions={0} | all-to-all | bytes 2097152 | tf_op jit(solution)/shard_map/all_to_all | solution.py:38
  310.6 16.7 %all_to_all.88 = bf16[16,32,8,128]{3,2,1,0:T(8,128)(2,1)S(1)} all-to-all(bf16[16,32,8,128]{3,2,1,0:T(8,128)(2,1)S(1)} %broadcast_in_dim.153), channel_id=1, replica_groups=mesh['depth'=8,'plane'=16] {'plane'}, dimensions={0} | all-to-all | bytes 2097152 | tf_op jit(solution)/shard_map/all_to_all | solution.py:38
  342.9 19.2 %all_to_all.89 = bf16[16,32,8,128]{3,2,1,0:T(8,128)(2,1)S(1)} all-to-all(bf16[16,32,8,128]{3,2,1,0:T(8,128)(2,1)S(1)} %broadcast_in_dim.155), channel_id=1, replica_groups=mesh['depth'=8,'plane'=16] {'plane'}, dimensions={0} | all-to-all | bytes 2097152 | tf_op jit(solution)/shard_map/all_to_all | solution.py:38
  376.7 19.1 %all_to_all.90 = bf16[16,32,8,128]{3,2,1,0:T(8,128)(2,1)S(1)} all-to-all(bf16[16,32,8,128]{3,2,1,0:T(8,128)(2,1)S(1)} %broadcast_in_dim.157), channel_id=1, replica_groups=mesh['depth'=8,'plane'=16] {'plane'}, dimensions={0} | all-to-all | bytes 2097152 | tf_op jit(solution)/shard_map/all_to_all | solution.py:38
  410.1 17.8 %all_to_all.91 = bf16[16,32,8,128]{3,2,1,0:T(8,128)(2,1)S(1)} all-to-all(bf16[16,32,8,128]{3,2,1,0:T(8,128)(2,1)S(1)} %broadcast_in_dim.159), channel_id=1, replica_groups=mesh['depth'=8,'plane'=16] {'plane'}, dimensions={0} | all-to-all | bytes 2097152 | tf_op jit(solution)/shard_map/all_to_all | solution.py:38
  448.9 14.3 %all-to-all-done.13 = bf16[16,32,8,128]{3,2,1,0:T(8,128)(2,1)S(1)} async-done(((bf16[16,32,8,128]{3,2,1,0:T(8,128)(2,1)}), bf16[16,32,8,128]{3,2,1,0:T(8,128)(2,1)S(1)}, u32[]{:S(2)}, u32[]{:S(2)}) %all-to-all-start.13) | async-done | bytes 1048608 | tf_op jit(solution)/shard_map/all_to_all | solution.py:38
  484.1 5.9 %fusion = f32[4096,17]{0,1:T(8,128)S(1)} fusion(s32[2048]{0:T(1024)S(1)} %add_add_fusion, bf16[2048,1]{0,1:T(2,128)(2,1)S(1)} %fusion.257, bf16[2048,16]{0,1:T(8,128)(2,1)S(1)} %bitcast.557), kind=kOutput, calls=%fused_computation.16 | convolution fusion | flops 293740544 | bytes 356352 | tf_op jit(solution)/shard_map/cs,cq->sq/dot_general | solution.py:83
  490.2 8.0 %all-to-all-done.14 = bf16[16,32,8,128]{3,2,1,0:T(8,128)(2,1)S(1)} async-done(((bf16[16,32,8,128]{3,2,1,0:T(8,128)(2,1)}), bf16[16,32,8,128]{3,2,1,0:T(8,128)(2,1)S(1)}, u32[]{:S(2)}, u32[]{:S(2)}) %all-to-all-start.14) | async-done | bytes 1048608 | tf_op jit(solution)/shard_map/all_to_all | solution.py:38
  501.9 5.7 %add_convert_fusion = (bf16[8,2,32,64]{3,0,1,2:T(8,128)(2,1)S(1)}, f32[8,2,32,64]{3,0,1,2:T(8,128)S(1)}) fusion(f32[8,2,32,64]{3,0,1,2:T(8,128)S(1)} %fusion.173, bf16[1,32,16,64,128]{4,3,2,1,0:T(8,128)(2,1)} %param.9, bf16[32,16,8,1,128]{4,2,1,3,0:T(8,128)(2,1)S(1)} %get-tuple-element.11, bf16[32,16,8,1,128]{4,2,1,3,0:T(8,128)(2,1)S(1)} %get-tuple-element.10), kind=kOutput, calls=%fused_computation.170 | convolution fusion | flops 135331840 | bytes 10813440 | tf_op jit(solution)/shard_map/rkic,rkvwc->vwri/dot_general | solution.py:48
  507.8 5.9 %fusion.37 = f32[4096,8,2]{0,1,2:T(8,128)S(1)} fusion(s32[2048]{0:T(1024)S(1)} %add_add_fusion, f32[4096,8,2]{0,2,1:T(2,128)S(1)} %reshape.427, f32[8,2,2048]{2,0,1:T(8,128)S(1)} %reshape.431, f32[8,2,2048]{2,0,1:T(8,128)S(1)} %reshape.426), kind=kOutput, calls=%fused_computation.53 | convolution fusion | flops 276955136 | bytes 794624 | tf_op jit(solution)/shard_map/cs,cq->sq/dot_general | solution.py:85
  515.5 10.0 %all-to-all-start.15 = ((f32[128,1,288]{2,1,0:T(1,128)}), f32[128,1,288]{2,1,0:T(1,128)S(1)}, u32[]{:S(2)}, u32[]{:S(2)}) async-start(f32[128,1,288]{2,1,0:T(1,128)} %reshape.585), calls=%async_computation.15 | async-start | bytes 393216 | tf_op jit(solution)/shard_map/all_to_all | solution.py:92
  526.3 9.7 %all-to-all-done.15 = f32[128,1,288]{2,1,0:T(1,128)S(1)} async-done(((f32[128,1,288]{2,1,0:T(1,128)}), f32[128,1,288]{2,1,0:T(1,128)S(1)}, u32[]{:S(2)}, u32[]{:S(2)}) %all-to-all-start.15) | async-done | bytes 147488 | tf_op jit(solution)/shard_map/all_to_all | solution.py:92
  (242 shorter events, 227.9 us)
Async XLA Ops:
  2.3 9.4 %copy-start.6 = (s32[1,32,16]{1,2,0:T(8,128)S(1)}, s32[1,32,16]{1,2,0:T(8,128)}, u32[]{:S(2)}) copy-start(s32[1,32,16]{1,2,0:T(8,128)} %param.10) | copy-start | bytes 6148
  4.1 23.1 %all-to-all-start = ((bf16[16,32,8,128]{3,2,1,0:T(8,128)(2,1)}), bf16[16,32,8,128]{3,2,1,0:T(8,128)(2,1)S(1)}, u32[]{:S(2)}, u32[]{:S(2)}) async-start(bf16[16,32,8,128]{3,2,1,0:T(8,128)(2,1)} %broadcast_in_dim.134), calls=%async_computation | async-start | bytes 2097152 | tf_op jit(solution)/shard_map/all_to_all | solution.py:38
  11.9 17.6 %copy-start.1 = (s32[1024]{0:T(1024)}, s32[1024]{0:T(1024)S(1)}, u32[]{:S(2)}) copy-start(s32[1024]{0:T(1024)S(1)} %pad_clamp_fusion) | copy-start | bytes 12292
  30.7 11.9 %copy-start = (f32[1,2048]{1,0:T(1,128)S(1)}, f32[1,2048]{1,0:T(1,128)}, u32[]{:S(2)}) copy-start(f32[1,2048]{1,0:T(1,128)} %param.8) | copy-start | bytes 24580
  36.6 6.0 %collective-permute-start = (bf16[8,2,2048]{2,0,1:T(8,128)(2,1)S(1)}, bf16[8,2,2048]{2,0,1:T(8,128)(2,1)S(1)}, u32[]{:S(2)}, u32[]{:S(2)}) collective-permute-start(bf16[8,2,2048]{2,0,1:T(8,128)(2,1)S(1)} %convert_element_type.266), channel_id=1, source_target_pairs={{0,16},{16,32},{32,48},{48,64},{64,80},{80,96},{96,112},{112,0},{1... | collective-permute-start | bytes 196616 | tf_op jit(solution)/shard_map/ppermute | solution.py:12
  70.4 6.0 %collective-permute-start.1 = (bf16[8,2,2048]{2,0,1:T(8,128)(2,1)S(1)}, bf16[8,2,2048]{2,0,1:T(8,128)(2,1)S(1)}, u32[]{:S(2)}, u32[]{:S(2)}) collective-permute-start(bf16[8,2,2048]{2,0,1:T(8,128)(2,1)S(1)} %convert_element_type.271), channel_id=1, source_target_pairs={{0,16},{16,32},{32,48},{48,64},{64,80},{80,96},{96,112},{112,0},{1... | collective-permute-start | bytes 196616 | tf_op jit(solution)/shard_map/ppermute | solution.py:12
  104.6 5.7 %collective-permute-start.2 = (bf16[8,2,2048]{2,0,1:T(8,128)(2,1)S(1)}, bf16[8,2,2048]{2,0,1:T(8,128)(2,1)S(1)}, u32[]{:S(2)}, u32[]{:S(2)}) collective-permute-start(bf16[8,2,2048]{2,0,1:T(8,128)(2,1)S(1)} %convert_element_type.276), channel_id=1, source_target_pairs={{0,16},{16,32},{32,48},{48,64},{64,80},{80,96},{96,112},{112,0},{1... | collective-permute-start | bytes 196616 | tf_op jit(solution)/shard_map/ppermute | solution.py:12
  136.8 5.5 %collective-permute-start.3 = (bf16[8,2,2048]{2,0,1:T(8,128)(2,1)S(1)}, bf16[8,2,2048]{2,0,1:T(8,128)(2,1)S(1)}, u32[]{:S(2)}, u32[]{:S(2)}) collective-permute-start(bf16[8,2,2048]{2,0,1:T(8,128)(2,1)S(1)} %convert_element_type.281), channel_id=1, source_target_pairs={{0,16},{16,32},{32,48},{48,64},{64,80},{80,96},{96,112},{112,0},{1... | collective-permute-start | bytes 196616 | tf_op jit(solution)/shard_map/ppermute | solution.py:12
  167.5 8.7 %collective-permute-start.4 = (bf16[8,2,2048]{2,0,1:T(8,128)(2,1)S(1)}, bf16[8,2,2048]{2,0,1:T(8,128)(2,1)S(1)}, u32[]{:S(2)}, u32[]{:S(2)}) collective-permute-start(bf16[8,2,2048]{2,0,1:T(8,128)(2,1)S(1)} %convert_element_type.286), channel_id=1, source_target_pairs={{0,16},{16,32},{32,48},{48,64},{64,80},{80,96},{96,112},{112,0},{1... | collective-permute-start | bytes 196616 | tf_op jit(solution)/shard_map/ppermute | solution.py:12
  202.3 7.9 %collective-permute-start.5 = (bf16[8,2,2048]{2,0,1:T(8,128)(2,1)S(1)}, bf16[8,2,2048]{2,0,1:T(8,128)(2,1)S(1)}, u32[]{:S(2)}, u32[]{:S(2)}) collective-permute-start(bf16[8,2,2048]{2,0,1:T(8,128)(2,1)S(1)} %convert_element_type.291), channel_id=1, source_target_pairs={{0,16},{16,32},{32,48},{48,64},{64,80},{80,96},{96,112},{112,0},{1... | collective-permute-start | bytes 196616 | tf_op jit(solution)/shard_map/ppermute | solution.py:12
  238.8 5.2 collective-permute-start.6
  270.2 24.6 %copy-start.2 = (s32[1024]{0:T(1024)S(1)}, s32[1024]{0:T(1024)}, u32[]{:S(2)}) copy-start(s32[1024]{0:T(1024)} %copy-done.1) | copy-start | bytes 12292
  270.2 6.3 %collective-permute-start.7 = (bf16[8,2,2048]{2,0,1:T(8,128)(2,1)S(1)}, bf16[8,2,2048]{2,0,1:T(8,128)(2,1)S(1)}, u32[]{:S(2)}, u32[]{:S(2)}) collective-permute-start(bf16[8,2,2048]{2,0,1:T(8,128)(2,1)S(1)} %multiply_convert_fusion.6), channel_id=1, source_target_pairs={{0,112},{16,0},{32,16},{48,32},{64,48},{80,64},{96,80},{112,96},{1... | collective-permute-start | bytes 196616 | tf_op jit(solution)/shard_map/ppermute | solution.py:12
  304.2 5.7 %collective-permute-start.8 = (bf16[8,2,2048]{2,0,1:T(8,128)(2,1)S(1)}, bf16[8,2,2048]{2,0,1:T(8,128)(2,1)S(1)}, u32[]{:S(2)}, u32[]{:S(2)}) collective-permute-start(bf16[8,2,2048]{2,0,1:T(8,128)(2,1)S(1)} %multiply_convert_fusion.5), channel_id=1, source_target_pairs={{0,112},{16,0},{32,16},{48,32},{64,48},{80,64},{96,80},{112,96},{1... | collective-permute-start | bytes 196616 | tf_op jit(solution)/shard_map/ppermute | solution.py:12
  336.6 5.7 %collective-permute-start.9 = (bf16[8,2,2048]{2,0,1:T(8,128)(2,1)S(1)}, bf16[8,2,2048]{2,0,1:T(8,128)(2,1)S(1)}, u32[]{:S(2)}, u32[]{:S(2)}) collective-permute-start(bf16[8,2,2048]{2,0,1:T(8,128)(2,1)S(1)} %multiply_convert_fusion.4), channel_id=1, source_target_pairs={{0,112},{16,0},{32,16},{48,32},{64,48},{80,64},{96,80},{112,96},{1... | collective-permute-start | bytes 196616 | tf_op jit(solution)/shard_map/ppermute | solution.py:12
  371.4 4.6 collective-permute-start.10
  405.1 4.3 collective-permute-start.11
  437.2 11.7 %copy-start.5 = (s32[1,2048]{1,0:T(1,128)S(1)}, s32[1,2048]{1,0:T(1,128)}, u32[]{:S(2)}) copy-start(s32[1,2048]{1,0:T(1,128)} %param.11) | copy-start | bytes 24580
  437.2 5.7 %collective-permute-start.12 = (bf16[8,2,2048]{2,0,1:T(8,128)(2,1)S(1)}, bf16[8,2,2048]{2,0,1:T(8,128)(2,1)S(1)}, u32[]{:S(2)}, u32[]{:S(2)}) collective-permute-start(bf16[8,2,2048]{2,0,1:T(8,128)(2,1)S(1)} %multiply_convert_fusion.1), channel_id=1, source_target_pairs={{0,112},{16,0},{32,16},{48,32},{64,48},{80,64},{96,80},{112,96},{1... | collective-permute-start | bytes 196616 | tf_op jit(solution)/shard_map/ppermute | solution.py:12
  444.6 18.6 %all-to-all-start.13 = ((bf16[16,32,8,128]{3,2,1,0:T(8,128)(2,1)}), bf16[16,32,8,128]{3,2,1,0:T(8,128)(2,1)S(1)}, u32[]{:S(2)}, u32[]{:S(2)}) async-start(bf16[16,32,8,128]{3,2,1,0:T(8,128)(2,1)} %broadcast_in_dim.161), calls=%async_computation.13 | async-start | bytes 2097152 | tf_op jit(solution)/shard_map/all_to_all | solution.py:38
  472.5 6.0 %collective-permute-start.13 = (bf16[8,2,2048]{2,0,1:T(8,128)(2,1)S(1)}, bf16[8,2,2048]{2,0,1:T(8,128)(2,1)S(1)}, u32[]{:S(2)}, u32[]{:S(2)}) collective-permute-start(bf16[8,2,2048]{2,0,1:T(8,128)(2,1)S(1)} %multiply_convert_fusion), channel_id=1, source_target_pairs={{0,112},{16,0},{32,16},{48,32},{64,48},{80,64},{96,80},{112,96},{1... | collective-permute-start | bytes 196616 | tf_op jit(solution)/shard_map/ppermute | solution.py:12
  480.1 18.1 %all-to-all-start.14 = ((bf16[16,32,8,128]{3,2,1,0:T(8,128)(2,1)}), bf16[16,32,8,128]{3,2,1,0:T(8,128)(2,1)S(1)}, u32[]{:S(2)}, u32[]{:S(2)}) async-start(bf16[16,32,8,128]{3,2,1,0:T(8,128)(2,1)} %broadcast_in_dim.163), calls=%async_computation.14 | async-start | bytes 2097152 | tf_op jit(solution)/shard_map/all_to_all | solution.py:38
  490.0 10.7 %copy-start.4 = (f32[4096,17]{0,1:T(8,128)}, f32[4096,17]{0,1:T(8,128)S(1)}, u32[]{:S(2)}) copy-start(f32[4096,17]{0,1:T(8,128)S(1)} %fusion) | copy-start | bytes 835588
  515.5 20.6 %all-to-all-start.15 = ((f32[128,1,288]{2,1,0:T(1,128)}), f32[128,1,288]{2,1,0:T(1,128)S(1)}, u32[]{:S(2)}, u32[]{:S(2)}) async-start(f32[128,1,288]{2,1,0:T(1,128)} %reshape.585), calls=%async_computation.15 | async-start | bytes 393216 | tf_op jit(solution)/shard_map/all_to_all | solution.py:92
  (2 other events, 11.5 us)

commit v14 on v11

--- a/solution.py
+++ b/solution.py
@@ -30,6 +30,19 @@
     real_part = coeff[0] * toar_f32[:, 0] - coeff[1] * toar_f32[:, 1]
     imag_part = coeff[0] * toar_f32[:, 1] + coeff[1] * toar_f32[:, 0]
     source = jnp.stack([real_part, imag_part], axis=1)
+
+    cell_patch = patch_map[0]
+    cell_count = cell_patch.shape[0]
+    owner_count = depth_count * plane_count
+    owner = cell_patch // PATCH_DEV
+    hits = (owner[:, None] == jnp.arange(owner_count, dtype=owner.dtype)[None, :]).astype(jnp.bfloat16)
+    cells = jnp.arange(cell_count, dtype=jnp.int32)
+    lower = (cells[:, None] >= cells[None, :]).astype(jnp.bfloat16)
+    running = jnp.dot(lower, hits, preferred_element_type=jnp.float32)
+    rank = jnp.sum(running * hits.astype(jnp.float32), axis=1).astype(jnp.int32) - 1
+    slot = owner * CAP + rank
+    placed = (slot[:, None] == jnp.arange(owner_count * CAP, dtype=jnp.int32)[None, :]).astype(jnp.bfloat16)
+    source, placed = lax.optimization_barrier((source, placed))
 
     def apply_layer(incoming):
         local_blocks = incoming.reshape(vec_count, 2, block_rows, block_cells).transpose(2, 0, 1, 3)
@@ -70,17 +83,6 @@
     product = precond.astype(jnp.float32) * toar_f32
     contrib = product[:, 0] + product[:, 1]
 
-    cell_patch = patch_map[0]
-    cell_count = cell_patch.shape[0]
-    owner_count = depth_count * plane_count
-    owner = cell_patch // PATCH_DEV
-    hits = (owner[:, None] == jnp.arange(owner_count, dtype=owner.dtype)[None, :]).astype(jnp.bfloat16)
-    cells = jnp.arange(cell_count, dtype=jnp.int32)
-    lower = (cells[:, None] >= cells[None, :]).astype(jnp.bfloat16)
-    running = jnp.dot(lower, hits, preferred_element_type=jnp.float32)
-    rank = jnp.sum(running * hits.astype(jnp.float32), axis=1).astype(jnp.int32) - 1
-    slot = owner * CAP + rank
-    placed = (slot[:, None] == jnp.arange(owner_count * CAP, dtype=jnp.int32)[None, :]).astype(jnp.bfloat16)
     local_patch = (cell_patch % PATCH_DEV).astype(jnp.float32)
     rows = jnp.concatenate([contrib.T, local_patch[:, None]], axis=1)
     high = lax.reduce_precision(rows, exponent_bits=8, mantissa_bits=7)

time: 547 us -> 561 us (1.026)
  other arithmetic: 26.6 us -> 33.9 us
    convert_element_type x0 -> x2, other arithmetic: none -> 6.58 us  [the longest x1 6.57 us: shards(): (slot[:, None] == jnp.arange(owner_count * CAP, dtype=jnp.int32)[None, :]...]
  transfers between devices with their start and end apart: 17 -> 17, of which waited for: 17 -> 17; matrix products, arithmetic and copies ran while one was open for 1% -> 0% of each run, Pallas kernels for 0% -> 0%
where the time goes in v14:
time: 561 us; the launch traced here: 551 us
  blocking collectives  226 us (40%)
  matrix products  97.1 us (17%)
  starting transfers between devices  88.8 us (16%)
  waiting for transfers between devices  55 us (10%)
  local copies, waits for them, and re-layouts  47.9 us (9%)
  other arithmetic  33.9 us (6%)
    all_to_all x13, blocking collectives, apply_layer(): gathered = lax.all_to_all(copies, 'plane', 0, 0, tiled=True)  226 us
    dot_general x15, matrix products, apply_layer(): jnp.einsum('rkic,rkvwc->vwri', factor, expanded, preferred_element_type=j...  84.9 us
    ppermute x14, starting transfers between devices, passed_along(): lax.ppermute(value, axis, [(source, (source + steps) % count) for source...  64.7 us
    gather x15, local copies, waits for them, and re-layouts, apply_layer(): chosen = jnp.take(gathered, pattern_flat, axis=0, mode='clip')  28.6 us
    all_to_all x2, waiting for transfers between devices, apply_layer(): gathered = lax.all_to_all(copies, 'plane', 0, 0, tiled=True)  27 us
    ppermute x14, waiting for transfers between devices, passed_along(): lax.ppermute(value, axis, [(source, (source + steps) % count) for source...  18.2 us
    another operation x15, other arithmetic, apply_layer(): jnp.stack([jnp.concatenate([x_re, -x_im], axis=-1), jnp.concatenate([x_im...  17.3 us
    all_to_all x1, starting transfers between devices, shards(): received = lax.all_to_all(packed, ('depth', 'plane'), 0, 0, tiled=True)  12.4 us
  transfers between devices with their start and end apart: 17, of which 17 were waited for; matrix products, arithmetic and copies ran while one was open for 0% of the time, Pallas kernels for 0%

profile of v14, /device:TPU:1, one launch (start us, length us, event | category | flops | bytes accessed | tf_op | source)
XLA Modules:
  0.0 550.5 jit_solution(4509347869329630141)
XLA Ops:
  5.0 6.6 %fusion = bf16[2048,4096]{1,0:T(8,128)(2,1)} fusion(s32[2048]{0:T(1024)S(1)} %add_add_fusion), kind=kLoop, calls=%fused_computation.16 | loop fusion | flops 16777216 | bytes 16785408 | tf_op jit(solution)/shard_map/convert_element_type | solution.py:44
  13.3 7.6 %all-to-all-start = ((bf16[16,32,8,128]{3,2,1,0:T(8,128)(2,1)}), bf16[16,32,8,128]{3,2,1,0:T(8,128)(2,1)S(1)}, u32[]{:S(2)}, u32[]{:S(2)}) async-start(bf16[16,32,8,128]{3,2,1,0:T(8,128)(2,1)} %broadcast_in_dim.134), calls=%async_computation | async-start | bytes 2097152 | tf_op jit(solution)/shard_map/all_to_all | solution.py:51
  21.1 15.3 %all-to-all-done = bf16[16,32,8,128]{3,2,1,0:T(8,128)(2,1)S(1)} async-done(((bf16[16,32,8,128]{3,2,1,0:T(8,128)(2,1)}), bf16[16,32,8,128]{3,2,1,0:T(8,128)(2,1)S(1)}, u32[]{:S(2)}, u32[]{:S(2)}) %all-to-all-start) | async-done | bytes 1048608 | tf_op jit(solution)/shard_map/all_to_all | solution.py:51
  39.8 5.7 %fusion.205 = bf16[8,2,32,64]{3,0,1,2:T(8,128)(2,1)S(1)} fusion(bf16[1,32,16,64,128]{4,3,2,1,0:T(8,128)(2,1)} %param.9, bf16[32,16,8,1,128]{4,2,1,3,0:T(8,128)(2,1)S(1)} %get-tuple-element.81, bf16[32,16,8,1,128]{4,2,1,3,0:T(8,128)(2,1)S(1)} %get-tuple-element.80), kind=kOutput, calls=%fused_computation.123 | convolution fusion | flops 135299072 | bytes 10551296 | tf_op jit(solution)/shard_map/rkic,rkvwc->vwri/dot_general | solution.py:61
  52.4 17.7 %all_to_all.80 = bf16[16,32,8,128]{3,2,1,0:T(8,128)(2,1)S(1)} all-to-all(bf16[16,32,8,128]{3,2,1,0:T(8,128)(2,1)S(1)} %broadcast_in_dim.137), channel_id=1, replica_groups=mesh['depth'=8,'plane'=16] {'plane'}, dimensions={0} | all-to-all | bytes 2097152 | tf_op jit(solution)/shard_map/all_to_all | solution.py:51
  86.3 17.9 %all_to_all.81 = bf16[16,32,8,128]{3,2,1,0:T(8,128)(2,1)S(1)} all-to-all(bf16[16,32,8,128]{3,2,1,0:T(8,128)(2,1)S(1)} %broadcast_in_dim.139), channel_id=1, replica_groups=mesh['depth'=8,'plane'=16] {'plane'}, dimensions={0} | all-to-all | bytes 2097152 | tf_op jit(solution)/shard_map/all_to_all | solution.py:51
  120.0 16.4 %all_to_all.82 = bf16[16,32,8,128]{3,2,1,0:T(8,128)(2,1)S(1)} all-to-all(bf16[16,32,8,128]{3,2,1,0:T(8,128)(2,1)S(1)} %broadcast_in_dim.141), channel_id=1, replica_groups=mesh['depth'=8,'plane'=16] {'plane'}, dimensions={0} | all-to-all | bytes 2097152 | tf_op jit(solution)/shard_map/all_to_all | solution.py:51
  151.9 14.9 %all_to_all.83 = bf16[16,32,8,128]{3,2,1,0:T(8,128)(2,1)S(1)} all-to-all(bf16[16,32,8,128]{3,2,1,0:T(8,128)(2,1)S(1)} %broadcast_in_dim.143), channel_id=1, replica_groups=mesh['depth'=8,'plane'=16] {'plane'}, dimensions={0} | all-to-all | bytes 2097152 | tf_op jit(solution)/shard_map/all_to_all | solution.py:51
  176.2 7.3 %collective-permute-start.4 = (bf16[8,2,2048]{2,0,1:T(8,128)(2,1)S(1)}, bf16[8,2,2048]{2,0,1:T(8,128)(2,1)S(1)}, u32[]{:S(2)}, u32[]{:S(2)}) collective-permute-start(bf16[8,2,2048]{2,0,1:T(8,128)(2,1)S(1)} %convert_element_type.292), channel_id=1, source_target_pairs={{0,16},{16,32},{32,48},{48,64},{64,80},{80,96},{96,112},{112,0},{1... | collective-permute-start | bytes 196616 | tf_op jit(solution)/shard_map/ppermute | solution.py:12
  185.6 16.1 %all_to_all.84 = bf16[16,32,8,128]{3,2,1,0:T(8,128)(2,1)S(1)} all-to-all(bf16[16,32,8,128]{3,2,1,0:T(8,128)(2,1)S(1)} %broadcast_in_dim.145), channel_id=1, replica_groups=mesh['depth'=8,'plane'=16] {'plane'}, dimensions={0} | all-to-all | bytes 2097152 | tf_op jit(solution)/shard_map/all_to_all | solution.py:51
  211.1 6.6 %collective-permute-start.5 = (bf16[8,2,2048]{2,0,1:T(8,128)(2,1)S(1)}, bf16[8,2,2048]{2,0,1:T(8,128)(2,1)S(1)}, u32[]{:S(2)}, u32[]{:S(2)}) collective-permute-start(bf16[8,2,2048]{2,0,1:T(8,128)(2,1)S(1)} %convert_element_type.297), channel_id=1, source_target_pairs={{0,16},{16,32},{32,48},{48,64},{64,80},{80,96},{96,112},{112,0},{1... | collective-permute-start | bytes 196616 | tf_op jit(solution)/shard_map/ppermute | solution.py:12
  219.6 18.5 %all_to_all.85 = bf16[16,32,8,128]{3,2,1,0:T(8,128)(2,1)S(1)} all-to-all(bf16[16,32,8,128]{3,2,1,0:T(8,128)(2,1)S(1)} %broadcast_in_dim.147), channel_id=1, replica_groups=mesh['depth'=8,'plane'=16] {'plane'}, dimensions={0} | all-to-all | bytes 2097152 | tf_op jit(solution)/shard_map/all_to_all | solution.py:51
  253.5 16.2 %all_to_all.86 = bf16[16,32,8,128]{3,2,1,0:T(8,128)(2,1)S(1)} all-to-all(bf16[16,32,8,128]{3,2,1,0:T(8,128)(2,1)S(1)} %broadcast_in_dim.149), channel_id=1, replica_groups=mesh['depth'=8,'plane'=16] {'plane'}, dimensions={0} | all-to-all | bytes 2097152 | tf_op jit(solution)/shard_map/all_to_all | solution.py:51
  286.0 17.9 %all_to_all.87 = bf16[16,32,8,128]{3,2,1,0:T(8,128)(2,1)S(1)} all-to-all(bf16[16,32,8,128]{3,2,1,0:T(8,128)(2,1)S(1)} %broadcast_in_dim.151), channel_id=1, replica_groups=mesh['depth'=8,'plane'=16] {'plane'}, dimensions={0} | all-to-all | bytes 2097152 | tf_op jit(solution)/shard_map/all_to_all | solution.py:51
  319.8 17.1 %all_to_all.88 = bf16[16,32,8,128]{3,2,1,0:T(8,128)(2,1)S(1)} all-to-all(bf16[16,32,8,128]{3,2,1,0:T(8,128)(2,1)S(1)} %broadcast_in_dim.153), channel_id=1, replica_groups=mesh['depth'=8,'plane'=16] {'plane'}, dimensions={0} | all-to-all | bytes 2097152 | tf_op jit(solution)/shard_map/all_to_all | solution.py:51
  352.3 19.0 %all_to_all.89 = bf16[16,32,8,128]{3,2,1,0:T(8,128)(2,1)S(1)} all-to-all(bf16[16,32,8,128]{3,2,1,0:T(8,128)(2,1)S(1)} %broadcast_in_dim.155), channel_id=1, replica_groups=mesh['depth'=8,'plane'=16] {'plane'}, dimensions={0} | all-to-all | bytes 2097152 | tf_op jit(solution)/shard_map/all_to_all | solution.py:51
  386.0 19.1 %all_to_all.90 = bf16[16,32,8,128]{3,2,1,0:T(8,128)(2,1)S(1)} all-to-all(bf16[16,32,8,128]{3,2,1,0:T(8,128)(2,1)S(1)} %broadcast_in_dim.157), channel_id=1, replica_groups=mesh['depth'=8,'plane'=16] {'plane'}, dimensions={0} | all-to-all | bytes 2097152 | tf_op jit(solution)/shard_map/all_to_all | solution.py:51
  419.4 17.8 %all_to_all.91 = bf16[16,32,8,128]{3,2,1,0:T(8,128)(2,1)S(1)} all-to-all(bf16[16,32,8,128]{3,2,1,0:T(8,128)(2,1)S(1)} %broadcast_in_dim.159), channel_id=1, replica_groups=mesh['depth'=8,'plane'=16] {'plane'}, dimensions={0} | all-to-all | bytes 2097152 | tf_op jit(solution)/shard_map/all_to_all | solution.py:51
  453.1 17.2 %all_to_all.92 = bf16[16,32,8,128]{3,2,1,0:T(8,128)(2,1)S(1)} all-to-all(bf16[16,32,8,128]{3,2,1,0:T(8,128)(2,1)S(1)} %broadcast_in_dim.161), channel_id=1, replica_groups=mesh['depth'=8,'plane'=16] {'plane'}, dimensions={0} | all-to-all | bytes 2097152 | tf_op jit(solution)/shard_map/all_to_all | solution.py:51
  491.7 11.7 %all-to-all-done.14 = bf16[16,32,8,128]{3,2,1,0:T(8,128)(2,1)S(1)} async-done(((bf16[16,32,8,128]{3,2,1,0:T(8,128)(2,1)}), bf16[16,32,8,128]{3,2,1,0:T(8,128)(2,1)S(1)}, u32[]{:S(2)}, u32[]{:S(2)}) %all-to-all-start.14) | async-done | bytes 1048608 | tf_op jit(solution)/shard_map/all_to_all | solution.py:51
  506.7 5.7 %add_convert_fusion = (bf16[8,2,32,64]{3,0,1,2:T(8,128)(2,1)S(1)}, f32[8,2,32,64]{3,0,1,2:T(8,128)S(1)}) fusion(f32[8,2,32,64]{3,0,1,2:T(8,128)S(1)} %fusion.165, bf16[1,32,16,64,128]{4,3,2,1,0:T(8,128)(2,1)} %param.9, bf16[32,16,8,1,128]{4,2,1,3,0:T(8,128)(2,1)S(1)} %get-tuple-element.11, bf16[32,16,8,1,128]{4,2,1,3,0:T(8,128)(2,1)S(1)} %get-tuple-element.10), kind=kOutput, calls=%fused_computation.166 | convolution fusion | flops 135331840 | bytes 10813440 | tf_op jit(solution)/shard_map/rkic,rkvwc->vwri/dot_general | solution.py:61
  512.8 8.6 %fusion.245 = f32[4096,27]{0,1:T(8,128)S(1)} fusion(bf16[2048,4096]{1,0:T(8,128)(2,1)} %fusion, bf16[2048,9]{0,1:T(8,128)(2,1)S(1)} %get-tuple-element.88, bf16[2048,9]{0,1:T(8,128)(2,1)S(1)} %get-tuple-element.89, bf16[2048,9]{0,1:T(8,128)(2,1)S(1)} %get-tuple-element.87), kind=kOutput, calls=%fused_computation.175 | convolution fusion | flops 453316608 | bytes 17330176 | tf_op jit(solution)/shard_map/cs,cq->sq/dot_general | solution.py:93
  523.2 12.4 %all-to-all-start.15 = ((f32[128,1,288]{2,1,0:T(1,128)}), f32[128,1,288]{2,1,0:T(1,128)S(1)}, u32[]{:S(2)}, u32[]{:S(2)}) async-start(f32[128,1,288]{2,1,0:T(1,128)} %reshape.572), calls=%async_computation.15 | async-start | bytes 393216 | tf_op jit(solution)/shard_map/all_to_all | solution.py:97
  536.4 9.7 %all-to-all-done.15 = f32[128,1,288]{2,1,0:T(1,128)S(1)} async-done(((f32[128,1,288]{2,1,0:T(1,128)}), f32[128,1,288]{2,1,0:T(1,128)S(1)}, u32[]{:S(2)}, u32[]{:S(2)}) %all-to-all-start.15) | async-done | bytes 147488 | tf_op jit(solution)/shard_map/all_to_all | solution.py:97
  (236 shorter events, 225.5 us)
Async XLA Ops:
  3.0 2.0 copy-start.4
  11.6 9.3 %copy-start.5 = (s32[1,32,16]{1,2,0:T(8,128)S(1)}, s32[1,32,16]{1,2,0:T(8,128)}, u32[]{:S(2)}) copy-start(s32[1,32,16]{1,2,0:T(8,128)} %param.10) | copy-start | bytes 6148
  13.3 23.1 %all-to-all-start = ((bf16[16,32,8,128]{3,2,1,0:T(8,128)(2,1)}), bf16[16,32,8,128]{3,2,1,0:T(8,128)(2,1)S(1)}, u32[]{:S(2)}, u32[]{:S(2)}) async-start(bf16[16,32,8,128]{3,2,1,0:T(8,128)(2,1)} %broadcast_in_dim.134), calls=%async_computation | async-start | bytes 2097152 | tf_op jit(solution)/shard_map/all_to_all | solution.py:51
  21.1 17.6 %copy-start.1 = (s32[1024]{0:T(1024)}, s32[1024]{0:T(1024)S(1)}, u32[]{:S(2)}) copy-start(s32[1024]{0:T(1024)S(1)} %pad_clamp_fusion) | copy-start | bytes 12292
  39.8 11.9 %copy-start = (f32[1,2048]{1,0:T(1,128)S(1)}, f32[1,2048]{1,0:T(1,128)}, u32[]{:S(2)}) copy-start(f32[1,2048]{1,0:T(1,128)} %param.8) | copy-start | bytes 24580
  45.7 6.0 %collective-permute-start = (bf16[8,2,2048]{2,0,1:T(8,128)(2,1)S(1)}, bf16[8,2,2048]{2,0,1:T(8,128)(2,1)S(1)}, u32[]{:S(2)}, u32[]{:S(2)}) collective-permute-start(bf16[8,2,2048]{2,0,1:T(8,128)(2,1)S(1)} %convert_element_type.272), channel_id=1, source_target_pairs={{0,16},{16,32},{32,48},{48,64},{64,80},{80,96},{96,112},{112,0},{1... | collective-permute-start | bytes 196616 | tf_op jit(solution)/shard_map/ppermute | solution.py:12
  79.6 6.0 %collective-permute-start.1 = (bf16[8,2,2048]{2,0,1:T(8,128)(2,1)S(1)}, bf16[8,2,2048]{2,0,1:T(8,128)(2,1)S(1)}, u32[]{:S(2)}, u32[]{:S(2)}) collective-permute-start(bf16[8,2,2048]{2,0,1:T(8,128)(2,1)S(1)} %convert_element_type.277), channel_id=1, source_target_pairs={{0,16},{16,32},{32,48},{48,64},{64,80},{80,96},{96,112},{112,0},{1... | collective-permute-start | bytes 196616 | tf_op jit(solution)/shard_map/ppermute | solution.py:12
  113.6 5.8 %collective-permute-start.2 = (bf16[8,2,2048]{2,0,1:T(8,128)(2,1)S(1)}, bf16[8,2,2048]{2,0,1:T(8,128)(2,1)S(1)}, u32[]{:S(2)}, u32[]{:S(2)}) collective-permute-start(bf16[8,2,2048]{2,0,1:T(8,128)(2,1)S(1)} %convert_element_type.282), channel_id=1, source_target_pairs={{0,16},{16,32},{32,48},{48,64},{64,80},{80,96},{96,112},{112,0},{1... | collective-permute-start | bytes 196616 | tf_op jit(solution)/shard_map/ppermute | solution.py:12
  145.8 5.4 collective-permute-start.3
  176.2 8.6 %collective-permute-start.4 = (bf16[8,2,2048]{2,0,1:T(8,128)(2,1)S(1)}, bf16[8,2,2048]{2,0,1:T(8,128)(2,1)S(1)}, u32[]{:S(2)}, u32[]{:S(2)}) collective-permute-start(bf16[8,2,2048]{2,0,1:T(8,128)(2,1)S(1)} %convert_element_type.292), channel_id=1, source_target_pairs={{0,16},{16,32},{32,48},{48,64},{64,80},{80,96},{96,112},{112,0},{1... | collective-permute-start | bytes 196616 | tf_op jit(solution)/shard_map/ppermute | solution.py:12
  211.1 7.9 %collective-permute-start.5 = (bf16[8,2,2048]{2,0,1:T(8,128)(2,1)S(1)}, bf16[8,2,2048]{2,0,1:T(8,128)(2,1)S(1)}, u32[]{:S(2)}, u32[]{:S(2)}) collective-permute-start(bf16[8,2,2048]{2,0,1:T(8,128)(2,1)S(1)} %convert_element_type.297), channel_id=1, source_target_pairs={{0,16},{16,32},{32,48},{48,64},{64,80},{80,96},{96,112},{112,0},{1... | collective-permute-start | bytes 196616 | tf_op jit(solution)/shard_map/ppermute | solution.py:12
  247.6 5.2 collective-permute-start.6
  279.1 6.3 %collective-permute-start.7 = (bf16[8,2,2048]{2,0,1:T(8,128)(2,1)S(1)}, bf16[8,2,2048]{2,0,1:T(8,128)(2,1)S(1)}, u32[]{:S(2)}, u32[]{:S(2)}) collective-permute-start(bf16[8,2,2048]{2,0,1:T(8,128)(2,1)S(1)} %multiply_convert_fusion.6), channel_id=1, source_target_pairs={{0,112},{16,0},{32,16},{48,32},{64,48},{80,64},{96,80},{112,96},{1... | collective-permute-start | bytes 196616 | tf_op jit(solution)/shard_map/ppermute | solution.py:12
  313.4 5.8 %collective-permute-start.8 = (bf16[8,2,2048]{2,0,1:T(8,128)(2,1)S(1)}, bf16[8,2,2048]{2,0,1:T(8,128)(2,1)S(1)}, u32[]{:S(2)}, u32[]{:S(2)}) collective-permute-start(bf16[8,2,2048]{2,0,1:T(8,128)(2,1)S(1)} %multiply_convert_fusion.5), channel_id=1, source_target_pairs={{0,112},{16,0},{32,16},{48,32},{64,48},{80,64},{96,80},{112,96},{1... | collective-permute-start | bytes 196616 | tf_op jit(solution)/shard_map/ppermute | solution.py:12
  346.3 5.3 collective-permute-start.9
  380.7 4.6 collective-permute-start.10
  414.5 4.3 collective-permute-start.11
  446.7 5.7 %collective-permute-start.12 = (bf16[8,2,2048]{2,0,1:T(8,128)(2,1)S(1)}, bf16[8,2,2048]{2,0,1:T(8,128)(2,1)S(1)}, u32[]{:S(2)}, u32[]{:S(2)}) collective-permute-start(bf16[8,2,2048]{2,0,1:T(8,128)(2,1)S(1)} %multiply_convert_fusion.1), channel_id=1, source_target_pairs={{0,112},{16,0},{32,16},{48,32},{64,48},{80,64},{96,80},{112,96},{1... | collective-permute-start | bytes 196616 | tf_op jit(solution)/shard_map/ppermute | solution.py:12
  479.7 23.6 %copy-start.2 = (s32[1024]{0:T(1024)S(1)}, s32[1024]{0:T(1024)}, u32[]{:S(2)}) copy-start(s32[1024]{0:T(1024)} %copy-done.1) | copy-start | bytes 12292
  479.7 6.1 %collective-permute-start.13 = (bf16[8,2,2048]{2,0,1:T(8,128)(2,1)S(1)}, bf16[8,2,2048]{2,0,1:T(8,128)(2,1)S(1)}, u32[]{:S(2)}, u32[]{:S(2)}) collective-permute-start(bf16[8,2,2048]{2,0,1:T(8,128)(2,1)S(1)} %multiply_convert_fusion), channel_id=1, source_target_pairs={{0,112},{16,0},{32,16},{48,32},{64,48},{80,64},{96,80},{112,96},{1... | collective-permute-start | bytes 196616 | tf_op jit(solution)/shard_map/ppermute | solution.py:12
  487.4 15.9 %all-to-all-start.14 = ((bf16[16,32,8,128]{3,2,1,0:T(8,128)(2,1)}), bf16[16,32,8,128]{3,2,1,0:T(8,128)(2,1)S(1)}, u32[]{:S(2)}, u32[]{:S(2)}) async-start(bf16[16,32,8,128]{3,2,1,0:T(8,128)(2,1)} %broadcast_in_dim.163), calls=%async_computation.14 | async-start | bytes 2097152 | tf_op jit(solution)/shard_map/all_to_all | solution.py:51
  506.7 5.9 %copy-start.3 = (bf16[1,8,2,2048]{3,2,1,0:T(2,128)(2,1)S(1)}, bf16[1,8,2,2048]{3,2,1,0:T(2,128)(2,1)}, u32[]{:S(2)}) copy-start(bf16[1,8,2,2048]{3,2,1,0:T(2,128)(2,1)} %param.6) | copy-start | bytes 196612
  523.2 22.9 %all-to-all-start.15 = ((f32[128,1,288]{2,1,0:T(1,128)}), f32[128,1,288]{2,1,0:T(1,128)S(1)}, u32[]{:S(2)}, u32[]{:S(2)}) async-start(f32[128,1,288]{2,1,0:T(1,128)} %reshape.572), calls=%async_computation.15 | async-start | bytes 393216 | tf_op jit(solution)/shard_map/all_to_all | solution.py:97

commit v15 on v9

--- a/solution.py
+++ b/solution.py
@@ -9,8 +9,7 @@
 
 def passed_along(value, axis, steps):
     count = lax.axis_size(axis)
-    first, last = (max(0, -steps), min(count, count - steps))
-    return lax.ppermute(value, axis, [(source, source + steps) for source in range(first, last)])
+    return lax.ppermute(value, axis, [(source, (source + steps) % count) for source in range(count)])
 
 
 def shards(toar, pml_coeff, coupling, inverse, pattern, patch_map):
@@ -48,9 +47,12 @@
         )
         return out.reshape(vec_count, 2, block_rows * block_cells)
 
+    layer = lax.axis_index("depth")
+    coupler_edge = jnp.where(layer > 0, coupler, jnp.zeros_like(coupler))
+
     def down_turn(turn_index, current):
         arrived = passed_along(current, "depth", 1)
-        down_in = (source + coupler * arrived.astype(jnp.float32)).astype(jnp.bfloat16)
+        down_in = (source + coupler_edge * arrived.astype(jnp.float32)).astype(jnp.bfloat16)
         return apply_layer(down_in).astype(jnp.bfloat16)
 
     swept = apply_layer(source.astype(jnp.bfloat16)).astype(jnp.bfloat16)
@@ -58,7 +60,7 @@
         swept = down_turn(turn_index, swept)
 
     def up_turn(turn_index, current):
-        outgoing = (coupler * current.astype(jnp.float32)).astype(jnp.bfloat16)
+        outgoing = (coupler_edge * current.astype(jnp.float32)).astype(jnp.bfloat16)
         arrived = passed_along(outgoing, "depth", -1)
         return (swept.astype(jnp.float32) + apply_layer(arrived)).astype(jnp.bfloat16)
 

time: 566 us -> 547 us (0.966)
  waiting for transfers between devices: 78.7 us -> 52.9 us
  starting transfers between devices: 75.9 us -> 89 us
  blocking collectives: 231 us -> 225 us
    ppermute x14, waiting for transfers between devices: 43.9 us -> 18.2 us  [passed_along(): lax.ppermute(value, axis, [(source, (source + steps) % count) for source...]
    ppermute x14, starting transfers between devices: 53.9 us -> 65.2 us  [passed_along(): lax.ppermute(value, axis, [(source, (source + steps) % count) for source...]
where the time goes in v15:
time: 547 us; the launch traced here: 538 us
  blocking collectives  225 us (41%)
  matrix products  94.9 us (17%)
  starting transfers between devices  89 us (16%)
  waiting for transfers between devices  52.9 us (10%)
  local copies, waits for them, and re-layouts  47.4 us (9%)
  other arithmetic  26.6 us (5%)
    all_to_all x13, blocking collectives, apply_layer(): gathered = lax.all_to_all(copies, 'plane', 0, 0, tiled=True)  225 us
    dot_general x15, matrix products, apply_layer(): jnp.einsum('rkic,rkvwc->vwri', factor, expanded, preferred_element_type=j...  84.9 us
    ppermute x14, starting transfers between devices, passed_along(): lax.ppermute(value, axis, [(source, (source + steps) % count) for source...  65.2 us
    gather x15, local copies, waits for them, and re-layouts, apply_layer(): chosen = jnp.take(gathered, pattern_flat, axis=0, mode='clip')  28.1 us
    all_to_all x2, waiting for transfers between devices, apply_layer(): gathered = lax.all_to_all(copies, 'plane', 0, 0, tiled=True)  25 us
    ppermute x14, waiting for transfers between devices, passed_along(): lax.ppermute(value, axis, [(source, (source + steps) % count) for source...  18.2 us
    another operation x15, other arithmetic, apply_layer(): jnp.stack([jnp.concatenate([x_re, -x_im], axis=-1), jnp.concatenate([x_im...  17.3 us
    all_to_all x1, starting transfers between devices, shards(): received = lax.all_to_all(packed, ('depth', 'plane'), 0, 0, tiled=True)  12.3 us
  transfers between devices with their start and end apart: 17, of which 17 were waited for; matrix products, arithmetic and copies ran while one was open for 1% of the time, Pallas kernels for 0%

profile of v15, /device:TPU:1, one launch (start us, length us, event | category | flops | bytes accessed | tf_op | source)
XLA Modules:
  0.0 538.3 jit_solution(12194108294202413964)
XLA Ops:
  4.1 7.6 %all-to-all-start = ((bf16[16,32,8,128]{3,2,1,0:T(8,128)(2,1)}), bf16[16,32,8,128]{3,2,1,0:T(8,128)(2,1)S(1)}, u32[]{:S(2)}, u32[]{:S(2)}) async-start(bf16[16,32,8,128]{3,2,1,0:T(8,128)(2,1)} %broadcast_in_dim.152), calls=%async_computation | async-start | bytes 2097152 | tf_op jit(solution)/shard_map/all_to_all | solution.py:35
  11.9 15.3 %all-to-all-done = bf16[16,32,8,128]{3,2,1,0:T(8,128)(2,1)S(1)} async-done(((bf16[16,32,8,128]{3,2,1,0:T(8,128)(2,1)}), bf16[16,32,8,128]{3,2,1,0:T(8,128)(2,1)S(1)}, u32[]{:S(2)}, u32[]{:S(2)}) %all-to-all-start) | async-done | bytes 1048608 | tf_op jit(solution)/shard_map/all_to_all | solution.py:35
  30.7 5.7 %fusion.206 = bf16[8,2,32,64]{3,0,1,2:T(8,128)(2,1)S(1)} fusion(bf16[1,32,16,64,128]{4,3,2,1,0:T(8,128)(2,1)} %param.9, bf16[32,16,8,1,128]{4,2,1,3,0:T(8,128)(2,1)S(1)} %get-tuple-element.81, bf16[32,16,8,1,128]{4,2,1,3,0:T(8,128)(2,1)S(1)} %get-tuple-element.80), kind=kOutput, calls=%fused_computation.124 | convolution fusion | flops 135299072 | bytes 10551296 | tf_op jit(solution)/shard_map/rkic,rkvwc->vwri/dot_general | solution.py:45
  43.2 17.7 %all_to_all.80 = bf16[16,32,8,128]{3,2,1,0:T(8,128)(2,1)S(1)} all-to-all(bf16[16,32,8,128]{3,2,1,0:T(8,128)(2,1)S(1)} %broadcast_in_dim.155), channel_id=1, replica_groups=mesh['depth'=8,'plane'=16] {'plane'}, dimensions={0} | all-to-all | bytes 2097152 | tf_op jit(solution)/shard_map/all_to_all | solution.py:35
  77.1 18.1 %all_to_all.81 = bf16[16,32,8,128]{3,2,1,0:T(8,128)(2,1)S(1)} all-to-all(bf16[16,32,8,128]{3,2,1,0:T(8,128)(2,1)S(1)} %broadcast_in_dim.157), channel_id=1, replica_groups=mesh['depth'=8,'plane'=16] {'plane'}, dimensions={0} | all-to-all | bytes 2097152 | tf_op jit(solution)/shard_map/all_to_all | solution.py:35
  111.0 16.3 %all_to_all.82 = bf16[16,32,8,128]{3,2,1,0:T(8,128)(2,1)S(1)} all-to-all(bf16[16,32,8,128]{3,2,1,0:T(8,128)(2,1)S(1)} %broadcast_in_dim.159), channel_id=1, replica_groups=mesh['depth'=8,'plane'=16] {'plane'}, dimensions={0} | all-to-all | bytes 2097152 | tf_op jit(solution)/shard_map/all_to_all | solution.py:35
  142.9 15.1 %all_to_all.83 = bf16[16,32,8,128]{3,2,1,0:T(8,128)(2,1)S(1)} all-to-all(bf16[16,32,8,128]{3,2,1,0:T(8,128)(2,1)S(1)} %broadcast_in_dim.161), channel_id=1, replica_groups=mesh['depth'=8,'plane'=16] {'plane'}, dimensions={0} | all-to-all | bytes 2097152 | tf_op jit(solution)/shard_map/all_to_all | solution.py:35
  167.4 7.3 %collective-permute-start.4 = (bf16[8,2,2048]{2,0,1:T(8,128)(2,1)S(1)}, bf16[8,2,2048]{2,0,1:T(8,128)(2,1)S(1)}, u32[]{:S(2)}, u32[]{:S(2)}) collective-permute-start(bf16[8,2,2048]{2,0,1:T(8,128)(2,1)S(1)} %convert_element_type.284), channel_id=1, source_target_pairs={{0,16},{16,32},{32,48},{48,64},{64,80},{80,96},{96,112},{112,0},{1... | collective-permute-start | bytes 196616 | tf_op jit(solution)/shard_map/ppermute | solution.py:12
  176.8 16.0 %all_to_all.84 = bf16[16,32,8,128]{3,2,1,0:T(8,128)(2,1)S(1)} all-to-all(bf16[16,32,8,128]{3,2,1,0:T(8,128)(2,1)S(1)} %broadcast_in_dim.163), channel_id=1, replica_groups=mesh['depth'=8,'plane'=16] {'plane'}, dimensions={0} | all-to-all | bytes 2097152 | tf_op jit(solution)/shard_map/all_to_all | solution.py:35
  202.2 6.6 %collective-permute-start.5 = (bf16[8,2,2048]{2,0,1:T(8,128)(2,1)S(1)}, bf16[8,2,2048]{2,0,1:T(8,128)(2,1)S(1)}, u32[]{:S(2)}, u32[]{:S(2)}) collective-permute-start(bf16[8,2,2048]{2,0,1:T(8,128)(2,1)S(1)} %convert_element_type.289), channel_id=1, source_target_pairs={{0,16},{16,32},{32,48},{48,64},{64,80},{80,96},{96,112},{112,0},{1... | collective-permute-start | bytes 196616 | tf_op jit(solution)/shard_map/ppermute | solution.py:12
  210.8 18.4 %all_to_all.85 = bf16[16,32,8,128]{3,2,1,0:T(8,128)(2,1)S(1)} all-to-all(bf16[16,32,8,128]{3,2,1,0:T(8,128)(2,1)S(1)} %broadcast_in_dim.165), channel_id=1, replica_groups=mesh['depth'=8,'plane'=16] {'plane'}, dimensions={0} | all-to-all | bytes 2097152 | tf_op jit(solution)/shard_map/all_to_all | solution.py:35
  244.6 16.1 %all_to_all.86 = bf16[16,32,8,128]{3,2,1,0:T(8,128)(2,1)S(1)} all-to-all(bf16[16,32,8,128]{3,2,1,0:T(8,128)(2,1)S(1)} %broadcast_in_dim.167), channel_id=1, replica_groups=mesh['depth'=8,'plane'=16] {'plane'}, dimensions={0} | all-to-all | bytes 2097152 | tf_op jit(solution)/shard_map/all_to_all | solution.py:35
  277.1 17.7 %all_to_all.87 = bf16[16,32,8,128]{3,2,1,0:T(8,128)(2,1)S(1)} all-to-all(bf16[16,32,8,128]{3,2,1,0:T(8,128)(2,1)S(1)} %broadcast_in_dim.169), channel_id=1, replica_groups=mesh['depth'=8,'plane'=16] {'plane'}, dimensions={0} | all-to-all | bytes 2097152 | tf_op jit(solution)/shard_map/all_to_all | solution.py:35
  310.5 16.7 %all_to_all.88 = bf16[16,32,8,128]{3,2,1,0:T(8,128)(2,1)S(1)} all-to-all(bf16[16,32,8,128]{3,2,1,0:T(8,128)(2,1)S(1)} %broadcast_in_dim.171), channel_id=1, replica_groups=mesh['depth'=8,'plane'=16] {'plane'}, dimensions={0} | all-to-all | bytes 2097152 | tf_op jit(solution)/shard_map/all_to_all | solution.py:35
  342.8 19.2 %all_to_all.89 = bf16[16,32,8,128]{3,2,1,0:T(8,128)(2,1)S(1)} all-to-all(bf16[16,32,8,128]{3,2,1,0:T(8,128)(2,1)S(1)} %broadcast_in_dim.173), channel_id=1, replica_groups=mesh['depth'=8,'plane'=16] {'plane'}, dimensions={0} | all-to-all | bytes 2097152 | tf_op jit(solution)/shard_map/all_to_all | solution.py:35
  376.6 19.1 %all_to_all.90 = bf16[16,32,8,128]{3,2,1,0:T(8,128)(2,1)S(1)} all-to-all(bf16[16,32,8,128]{3,2,1,0:T(8,128)(2,1)S(1)} %broadcast_in_dim.175), channel_id=1, replica_groups=mesh['depth'=8,'plane'=16] {'plane'}, dimensions={0} | all-to-all | bytes 2097152 | tf_op jit(solution)/shard_map/all_to_all | solution.py:35
  410.0 17.8 %all_to_all.91 = bf16[16,32,8,128]{3,2,1,0:T(8,128)(2,1)S(1)} all-to-all(bf16[16,32,8,128]{3,2,1,0:T(8,128)(2,1)S(1)} %broadcast_in_dim.177), channel_id=1, replica_groups=mesh['depth'=8,'plane'=16] {'plane'}, dimensions={0} | all-to-all | bytes 2097152 | tf_op jit(solution)/shard_map/all_to_all | solution.py:35
  443.4 17.2 %all_to_all.92 = bf16[16,32,8,128]{3,2,1,0:T(8,128)(2,1)S(1)} all-to-all(bf16[16,32,8,128]{3,2,1,0:T(8,128)(2,1)S(1)} %broadcast_in_dim.179), channel_id=1, replica_groups=mesh['depth'=8,'plane'=16] {'plane'}, dimensions={0} | all-to-all | bytes 2097152 | tf_op jit(solution)/shard_map/all_to_all | solution.py:35
  464.0 5.7 %fusion.146 = f32[8,2,32,64]{3,0,1,2:T(8,128)S(1)} fusion(bf16[1,32,16,64,128]{4,3,2,1,0:T(8,128)(2,1)} %param.9, bf16[32,16,8,1,128]{4,2,1,3,0:T(8,128)(2,1)S(1)} %get-tuple-element.16, bf16[32,16,8,1,128]{4,2,1,3,0:T(8,128)(2,1)S(1)} %get-tuple-element.15), kind=kOutput, calls=%fused_computation.112 | convolution fusion | flops 135266304 | bytes 10616832 | tf_op jit(solution)/shard_map/rkic,rkvwc->vwri/dot_general | solution.py:45
  483.6 9.7 %all-to-all-done.14 = bf16[16,32,8,128]{3,2,1,0:T(8,128)(2,1)S(1)} async-done(((bf16[16,32,8,128]{3,2,1,0:T(8,128)(2,1)}), bf16[16,32,8,128]{3,2,1,0:T(8,128)(2,1)S(1)}, u32[]{:S(2)}, u32[]{:S(2)}) %all-to-all-start.14) | async-done | bytes 1048608 | tf_op jit(solution)/shard_map/all_to_all | solution.py:35
  496.9 5.7 %add_convert_fusion = (bf16[8,2,32,64]{3,0,1,2:T(8,128)(2,1)S(1)}, f32[8,2,32,64]{3,0,1,2:T(8,128)S(1)}) fusion(f32[8,2,32,64]{3,0,1,2:T(8,128)S(1)} %fusion.166, bf16[1,32,16,64,128]{4,3,2,1,0:T(8,128)(2,1)} %param.9, bf16[32,16,8,1,128]{4,2,1,3,0:T(8,128)(2,1)S(1)} %get-tuple-element.11, bf16[32,16,8,1,128]{4,2,1,3,0:T(8,128)(2,1)S(1)} %get-tuple-element.10), kind=kOutput, calls=%fused_computation.167 | convolution fusion | flops 135331840 | bytes 10813440 | tf_op jit(solution)/shard_map/rkic,rkvwc->vwri/dot_general | solution.py:45
  503.0 6.5 %fusion = f32[4096,27]{0,1:T(8,128)S(1)} fusion(s32[2048]{0:T(1024)S(1)} %add_add_fusion, bf16[2048,9]{0,1:T(8,128)(2,1)S(1)} %get-tuple-element.88, bf16[2048,9]{0,1:T(8,128)(2,1)S(1)} %get-tuple-element.89, bf16[2048,9]{0,1:T(8,128)(2,1)S(1)} %get-tuple-element.87), kind=kOutput, calls=%fused_computation.16 | convolution fusion | flops 461705216 | bytes 561152 | tf_op jit(solution)/shard_map/cs,cq->sq/dot_general | solution.py:91
  511.2 12.3 %all-to-all-start.15 = ((f32[128,1,288]{2,1,0:T(1,128)}), f32[128,1,288]{2,1,0:T(1,128)S(1)}, u32[]{:S(2)}, u32[]{:S(2)}) async-start(f32[128,1,288]{2,1,0:T(1,128)} %reshape.580), calls=%async_computation.15 | async-start | bytes 393216 | tf_op jit(solution)/shard_map/all_to_all | solution.py:95
  524.4 9.7 %all-to-all-done.15 = f32[128,1,288]{2,1,0:T(1,128)S(1)} async-done(((f32[128,1,288]{2,1,0:T(1,128)}), f32[128,1,288]{2,1,0:T(1,128)S(1)}, u32[]{:S(2)}, u32[]{:S(2)}) %all-to-all-start.15) | async-done | bytes 147488 | tf_op jit(solution)/shard_map/all_to_all | solution.py:95
  (229 shorter events, 218.7 us)
Async XLA Ops:
  2.3 9.4 %copy-start.4 = (s32[1,32,16]{1,2,0:T(8,128)S(1)}, s32[1,32,16]{1,2,0:T(8,128)}, u32[]{:S(2)}) copy-start(s32[1,32,16]{1,2,0:T(8,128)} %param.10) | copy-start | bytes 6148
  4.1 23.1 %all-to-all-start = ((bf16[16,32,8,128]{3,2,1,0:T(8,128)(2,1)}), bf16[16,32,8,128]{3,2,1,0:T(8,128)(2,1)S(1)}, u32[]{:S(2)}, u32[]{:S(2)}) async-start(bf16[16,32,8,128]{3,2,1,0:T(8,128)(2,1)} %broadcast_in_dim.152), calls=%async_computation | async-start | bytes 2097152 | tf_op jit(solution)/shard_map/all_to_all | solution.py:35
  11.9 17.6 %copy-start = (s32[1024]{0:T(1024)}, s32[1024]{0:T(1024)S(1)}, u32[]{:S(2)}) copy-start(s32[1024]{0:T(1024)S(1)} %pad_clamp_fusion) | copy-start | bytes 12292
  30.6 10.6 %copy-start.5 = (f32[1,2048]{1,0:T(1,128)S(1)}, f32[1,2048]{1,0:T(1,128)}, u32[]{:S(2)}) copy-start(f32[1,2048]{1,0:T(1,128)} %param.8) | copy-start | bytes 24580
  36.5 6.0 %collective-permute-start = (bf16[8,2,2048]{2,0,1:T(8,128)(2,1)S(1)}, bf16[8,2,2048]{2,0,1:T(8,128)(2,1)S(1)}, u32[]{:S(2)}, u32[]{:S(2)}) collective-permute-start(bf16[8,2,2048]{2,0,1:T(8,128)(2,1)S(1)} %convert_element_type.264), channel_id=1, source_target_pairs={{0,16},{16,32},{32,48},{48,64},{64,80},{80,96},{96,112},{112,0},{1... | collective-permute-start | bytes 196616 | tf_op jit(solution)/shard_map/ppermute | solution.py:12
  70.4 6.0 %collective-permute-start.1 = (bf16[8,2,2048]{2,0,1:T(8,128)(2,1)S(1)}, bf16[8,2,2048]{2,0,1:T(8,128)(2,1)S(1)}, u32[]{:S(2)}, u32[]{:S(2)}) collective-permute-start(bf16[8,2,2048]{2,0,1:T(8,128)(2,1)S(1)} %convert_element_type.269), channel_id=1, source_target_pairs={{0,16},{16,32},{32,48},{48,64},{64,80},{80,96},{96,112},{112,0},{1... | collective-permute-start | bytes 196616 | tf_op jit(solution)/shard_map/ppermute | solution.py:12
  104.6 5.7 %collective-permute-start.2 = (bf16[8,2,2048]{2,0,1:T(8,128)(2,1)S(1)}, bf16[8,2,2048]{2,0,1:T(8,128)(2,1)S(1)}, u32[]{:S(2)}, u32[]{:S(2)}) collective-permute-start(bf16[8,2,2048]{2,0,1:T(8,128)(2,1)S(1)} %convert_element_type.274), channel_id=1, source_target_pairs={{0,16},{16,32},{32,48},{48,64},{64,80},{80,96},{96,112},{112,0},{1... | collective-permute-start | bytes 196616 | tf_op jit(solution)/shard_map/ppermute | solution.py:12
  136.8 5.5 %collective-permute-start.3 = (bf16[8,2,2048]{2,0,1:T(8,128)(2,1)S(1)}, bf16[8,2,2048]{2,0,1:T(8,128)(2,1)S(1)}, u32[]{:S(2)}, u32[]{:S(2)}) collective-permute-start(bf16[8,2,2048]{2,0,1:T(8,128)(2,1)S(1)} %convert_element_type.279), channel_id=1, source_target_pairs={{0,16},{16,32},{32,48},{48,64},{64,80},{80,96},{96,112},{112,0},{1... | collective-permute-start | bytes 196616 | tf_op jit(solution)/shard_map/ppermute | solution.py:12
  167.4 8.7 %collective-permute-start.4 = (bf16[8,2,2048]{2,0,1:T(8,128)(2,1)S(1)}, bf16[8,2,2048]{2,0,1:T(8,128)(2,1)S(1)}, u32[]{:S(2)}, u32[]{:S(2)}) collective-permute-start(bf16[8,2,2048]{2,0,1:T(8,128)(2,1)S(1)} %convert_element_type.284), channel_id=1, source_target_pairs={{0,16},{16,32},{32,48},{48,64},{64,80},{80,96},{96,112},{112,0},{1... | collective-permute-start | bytes 196616 | tf_op jit(solution)/shard_map/ppermute | solution.py:12
  202.2 7.9 %collective-permute-start.5 = (bf16[8,2,2048]{2,0,1:T(8,128)(2,1)S(1)}, bf16[8,2,2048]{2,0,1:T(8,128)(2,1)S(1)}, u32[]{:S(2)}, u32[]{:S(2)}) collective-permute-start(bf16[8,2,2048]{2,0,1:T(8,128)(2,1)S(1)} %convert_element_type.289), channel_id=1, source_target_pairs={{0,16},{16,32},{32,48},{48,64},{64,80},{80,96},{96,112},{112,0},{1... | collective-permute-start | bytes 196616 | tf_op jit(solution)/shard_map/ppermute | solution.py:12
  238.7 5.2 collective-permute-start.6
  270.1 24.6 %copy-start.1 = (s32[1024]{0:T(1024)S(1)}, s32[1024]{0:T(1024)}, u32[]{:S(2)}) copy-start(s32[1024]{0:T(1024)} %copy-done) | copy-start | bytes 12292
  270.2 6.3 %collective-permute-start.7 = (bf16[8,2,2048]{2,0,1:T(8,128)(2,1)S(1)}, bf16[8,2,2048]{2,0,1:T(8,128)(2,1)S(1)}, u32[]{:S(2)}, u32[]{:S(2)}) collective-permute-start(bf16[8,2,2048]{2,0,1:T(8,128)(2,1)S(1)} %multiply_convert_fusion.6), channel_id=1, source_target_pairs={{0,112},{16,0},{32,16},{48,32},{64,48},{80,64},{96,80},{112,96},{1... | collective-permute-start | bytes 196616 | tf_op jit(solution)/shard_map/ppermute | solution.py:12
  304.1 5.7 %collective-permute-start.8 = (bf16[8,2,2048]{2,0,1:T(8,128)(2,1)S(1)}, bf16[8,2,2048]{2,0,1:T(8,128)(2,1)S(1)}, u32[]{:S(2)}, u32[]{:S(2)}) collective-permute-start(bf16[8,2,2048]{2,0,1:T(8,128)(2,1)S(1)} %multiply_convert_fusion.5), channel_id=1, source_target_pairs={{0,112},{16,0},{32,16},{48,32},{64,48},{80,64},{96,80},{112,96},{1... | collective-permute-start | bytes 196616 | tf_op jit(solution)/shard_map/ppermute | solution.py:12
  336.5 5.7 %collective-permute-start.9 = (bf16[8,2,2048]{2,0,1:T(8,128)(2,1)S(1)}, bf16[8,2,2048]{2,0,1:T(8,128)(2,1)S(1)}, u32[]{:S(2)}, u32[]{:S(2)}) collective-permute-start(bf16[8,2,2048]{2,0,1:T(8,128)(2,1)S(1)} %multiply_convert_fusion.4), channel_id=1, source_target_pairs={{0,112},{16,0},{32,16},{48,32},{64,48},{80,64},{96,80},{112,96},{1... | collective-permute-start | bytes 196616 | tf_op jit(solution)/shard_map/ppermute | solution.py:12
  371.3 4.6 collective-permute-start.10
  405.0 4.3 collective-permute-start.11
  437.1 5.7 %collective-permute-start.12 = (bf16[8,2,2048]{2,0,1:T(8,128)(2,1)S(1)}, bf16[8,2,2048]{2,0,1:T(8,128)(2,1)S(1)}, u32[]{:S(2)}, u32[]{:S(2)}) collective-permute-start(bf16[8,2,2048]{2,0,1:T(8,128)(2,1)S(1)} %multiply_convert_fusion.1), channel_id=1, source_target_pairs={{0,112},{16,0},{32,16},{48,32},{64,48},{80,64},{96,80},{112,96},{1... | collective-permute-start | bytes 196616 | tf_op jit(solution)/shard_map/ppermute | solution.py:12
  464.0 10.8 %copy-start.3 = (s32[1,2048]{1,0:T(1,128)S(1)}, s32[1,2048]{1,0:T(1,128)}, u32[]{:S(2)}) copy-start(s32[1,2048]{1,0:T(1,128)} %param.11) | copy-start | bytes 24580
  470.0 6.1 %collective-permute-start.13 = (bf16[8,2,2048]{2,0,1:T(8,128)(2,1)S(1)}, bf16[8,2,2048]{2,0,1:T(8,128)(2,1)S(1)}, u32[]{:S(2)}, u32[]{:S(2)}) collective-permute-start(bf16[8,2,2048]{2,0,1:T(8,128)(2,1)S(1)} %multiply_convert_fusion), channel_id=1, source_target_pairs={{0,112},{16,0},{32,16},{48,32},{64,48},{80,64},{96,80},{112,96},{1... | collective-permute-start | bytes 196616 | tf_op jit(solution)/shard_map/ppermute | solution.py:12
  477.7 15.6 %all-to-all-start.14 = ((bf16[16,32,8,128]{3,2,1,0:T(8,128)(2,1)}), bf16[16,32,8,128]{3,2,1,0:T(8,128)(2,1)S(1)}, u32[]{:S(2)}, u32[]{:S(2)}) async-start(bf16[16,32,8,128]{3,2,1,0:T(8,128)(2,1)} %broadcast_in_dim.181), calls=%async_computation.14 | async-start | bytes 2097152 | tf_op jit(solution)/shard_map/all_to_all | solution.py:35
  496.9 5.9 %copy-start.2 = (bf16[1,8,2,2048]{3,2,1,0:T(2,128)(2,1)S(1)}, bf16[1,8,2,2048]{3,2,1,0:T(2,128)(2,1)}, u32[]{:S(2)}) copy-start(bf16[1,8,2,2048]{3,2,1,0:T(2,128)(2,1)} %param.6) | copy-start | bytes 196612
  511.2 22.9 %all-to-all-start.15 = ((f32[128,1,288]{2,1,0:T(1,128)}), f32[128,1,288]{2,1,0:T(1,128)S(1)}, u32[]{:S(2)}, u32[]{:S(2)}) async-start(f32[128,1,288]{2,1,0:T(1,128)} %reshape.580), calls=%async_computation.15 | async-start | bytes 393216 | tf_op jit(solution)/shard_map/all_to_all | solution.py:95

commit v16 on v15

--- a/solution.py
+++ b/solution.py
@@ -95,11 +95,14 @@
     received = lax.all_to_all(packed, ("depth", "plane"), 0, 0, tiled=True)
     received = received.reshape(owner_count * CAP, vec_count + 1)
     target = received[:, vec_count].astype(jnp.int32)
-    choose = (target[:, None] == jnp.arange(PATCH_DEV, dtype=jnp.int32)[None, :]).astype(jnp.float32)
-    owned = jnp.einsum(
-        "sv,sp->vp", received[:, :vec_count], choose, precision=lax.Precision.HIGHEST,
-        preferred_element_type=jnp.float32,
-    )
+    choose = (target[:, None] == jnp.arange(PATCH_DEV, dtype=jnp.int32)[None, :]).astype(jnp.bfloat16)
+    values = received[:, :vec_count]
+    top = lax.reduce_precision(values, exponent_bits=8, mantissa_bits=7)
+    remainder = values - top
+    mid = lax.reduce_precision(remainder, exponent_bits=8, mantissa_bits=7)
+    pieces = jnp.concatenate([top, mid, remainder - mid], axis=1).astype(jnp.bfloat16)
+    summed = jnp.einsum("sq,sp->qp", pieces, choose, preferred_element_type=jnp.float32)
+    owned = (summed[:vec_count] + summed[vec_count:2 * vec_count]) + summed[2 * vec_count:]
     return (precond[None], owned)
 
 

time: 547 us -> 547 us (level)
  no operation moved by 1% of the time
where the time goes in v16:
time: 547 us; the launch traced here: 538 us
  blocking collectives  225 us (41%)
  matrix products  94.1 us (17%)
  starting transfers between devices  89 us (16%)
  waiting for transfers between devices  52.9 us (10%)
  local copies, waits for them, and re-layouts  47.4 us (9%)
  other arithmetic  27.2 us (5%)
    all_to_all x13, blocking collectives, apply_layer(): gathered = lax.all_to_all(copies, 'plane', 0, 0, tiled=True)  225 us
    dot_general x15, matrix products, apply_layer(): jnp.einsum('rkic,rkvwc->vwri', factor, expanded, preferred_element_type=j...  84.9 us
    ppermute x14, starting transfers between devices, passed_along(): lax.ppermute(value, axis, [(source, (source + steps) % count) for source...  65.2 us
    gather x15, local copies, waits for them, and re-layouts, apply_layer(): chosen = jnp.take(gathered, pattern_flat, axis=0, mode='clip')  28.1 us
    all_to_all x2, waiting for transfers between devices, apply_layer(): gathered = lax.all_to_all(copies, 'plane', 0, 0, tiled=True)  25 us
    ppermute x14, waiting for transfers between devices, passed_along(): lax.ppermute(value, axis, [(source, (source + steps) % count) for source...  18.2 us
    another operation x15, other arithmetic, apply_layer(): jnp.stack([jnp.concatenate([x_re, -x_im], axis=-1), jnp.concatenate([x_im...  17.3 us
    all_to_all x1, starting transfers between devices, shards(): received = lax.all_to_all(packed, ('depth', 'plane'), 0, 0, tiled=True)  12.3 us
  transfers between devices with their start and end apart: 17, of which 17 were waited for; matrix products, arithmetic and copies ran while one was open for 1% of the time, Pallas kernels for 0%

profile of v16, /device:TPU:1, one launch (start us, length us, event | category | flops | bytes accessed | tf_op | source)
XLA Modules:
  0.0 538.2 jit_solution(5109356161676613798)
XLA Ops:
  4.1 7.6 %all-to-all-start = ((bf16[16,32,8,128]{3,2,1,0:T(8,128)(2,1)}), bf16[16,32,8,128]{3,2,1,0:T(8,128)(2,1)S(1)}, u32[]{:S(2)}, u32[]{:S(2)}) async-start(bf16[16,32,8,128]{3,2,1,0:T(8,128)(2,1)} %broadcast_in_dim.152), calls=%async_computation | async-start | bytes 2097152 | tf_op jit(solution)/shard_map/all_to_all | solution.py:35
  11.9 15.3 %all-to-all-done = bf16[16,32,8,128]{3,2,1,0:T(8,128)(2,1)S(1)} async-done(((bf16[16,32,8,128]{3,2,1,0:T(8,128)(2,1)}), bf16[16,32,8,128]{3,2,1,0:T(8,128)(2,1)S(1)}, u32[]{:S(2)}, u32[]{:S(2)}) %all-to-all-start) | async-done | bytes 1048608 | tf_op jit(solution)/shard_map/all_to_all | solution.py:35
  30.7 5.7 %fusion.206 = bf16[8,2,32,64]{3,0,1,2:T(8,128)(2,1)S(1)} fusion(bf16[1,32,16,64,128]{4,3,2,1,0:T(8,128)(2,1)} %param.9, bf16[32,16,8,1,128]{4,2,1,3,0:T(8,128)(2,1)S(1)} %get-tuple-element.81, bf16[32,16,8,1,128]{4,2,1,3,0:T(8,128)(2,1)S(1)} %get-tuple-element.80), kind=kOutput, calls=%fused_computation.124 | convolution fusion | flops 135299072 | bytes 10551296 | tf_op jit(solution)/shard_map/rkic,rkvwc->vwri/dot_general | solution.py:45
  43.2 17.7 %all_to_all.80 = bf16[16,32,8,128]{3,2,1,0:T(8,128)(2,1)S(1)} all-to-all(bf16[16,32,8,128]{3,2,1,0:T(8,128)(2,1)S(1)} %broadcast_in_dim.155), channel_id=1, replica_groups=mesh['depth'=8,'plane'=16] {'plane'}, dimensions={0} | all-to-all | bytes 2097152 | tf_op jit(solution)/shard_map/all_to_all | solution.py:35
  77.1 18.1 %all_to_all.81 = bf16[16,32,8,128]{3,2,1,0:T(8,128)(2,1)S(1)} all-to-all(bf16[16,32,8,128]{3,2,1,0:T(8,128)(2,1)S(1)} %broadcast_in_dim.157), channel_id=1, replica_groups=mesh['depth'=8,'plane'=16] {'plane'}, dimensions={0} | all-to-all | bytes 2097152 | tf_op jit(solution)/shard_map/all_to_all | solution.py:35
  111.0 16.3 %all_to_all.82 = bf16[16,32,8,128]{3,2,1,0:T(8,128)(2,1)S(1)} all-to-all(bf16[16,32,8,128]{3,2,1,0:T(8,128)(2,1)S(1)} %broadcast_in_dim.159), channel_id=1, replica_groups=mesh['depth'=8,'plane'=16] {'plane'}, dimensions={0} | all-to-all | bytes 2097152 | tf_op jit(solution)/shard_map/all_to_all | solution.py:35
  142.9 15.1 %all_to_all.83 = bf16[16,32,8,128]{3,2,1,0:T(8,128)(2,1)S(1)} all-to-all(bf16[16,32,8,128]{3,2,1,0:T(8,128)(2,1)S(1)} %broadcast_in_dim.161), channel_id=1, replica_groups=mesh['depth'=8,'plane'=16] {'plane'}, dimensions={0} | all-to-all | bytes 2097152 | tf_op jit(solution)/shard_map/all_to_all | solution.py:35
  167.4 7.3 %collective-permute-start.4 = (bf16[8,2,2048]{2,0,1:T(8,128)(2,1)S(1)}, bf16[8,2,2048]{2,0,1:T(8,128)(2,1)S(1)}, u32[]{:S(2)}, u32[]{:S(2)}) collective-permute-start(bf16[8,2,2048]{2,0,1:T(8,128)(2,1)S(1)} %convert_element_type.285), channel_id=1, source_target_pairs={{0,16},{16,32},{32,48},{48,64},{64,80},{80,96},{96,112},{112,0},{1... | collective-permute-start | bytes 196616 | tf_op jit(solution)/shard_map/ppermute | solution.py:12
  176.8 16.0 %all_to_all.84 = bf16[16,32,8,128]{3,2,1,0:T(8,128)(2,1)S(1)} all-to-all(bf16[16,32,8,128]{3,2,1,0:T(8,128)(2,1)S(1)} %broadcast_in_dim.163), channel_id=1, replica_groups=mesh['depth'=8,'plane'=16] {'plane'}, dimensions={0} | all-to-all | bytes 2097152 | tf_op jit(solution)/shard_map/all_to_all | solution.py:35
  202.3 6.6 %collective-permute-start.5 = (bf16[8,2,2048]{2,0,1:T(8,128)(2,1)S(1)}, bf16[8,2,2048]{2,0,1:T(8,128)(2,1)S(1)}, u32[]{:S(2)}, u32[]{:S(2)}) collective-permute-start(bf16[8,2,2048]{2,0,1:T(8,128)(2,1)S(1)} %convert_element_type.290), channel_id=1, source_target_pairs={{0,16},{16,32},{32,48},{48,64},{64,80},{80,96},{96,112},{112,0},{1... | collective-permute-start | bytes 196616 | tf_op jit(solution)/shard_map/ppermute | solution.py:12
  210.9 18.4 %all_to_all.85 = bf16[16,32,8,128]{3,2,1,0:T(8,128)(2,1)S(1)} all-to-all(bf16[16,32,8,128]{3,2,1,0:T(8,128)(2,1)S(1)} %broadcast_in_dim.165), channel_id=1, replica_groups=mesh['depth'=8,'plane'=16] {'plane'}, dimensions={0} | all-to-all | bytes 2097152 | tf_op jit(solution)/shard_map/all_to_all | solution.py:35
  244.6 16.1 %all_to_all.86 = bf16[16,32,8,128]{3,2,1,0:T(8,128)(2,1)S(1)} all-to-all(bf16[16,32,8,128]{3,2,1,0:T(8,128)(2,1)S(1)} %broadcast_in_dim.167), channel_id=1, replica_groups=mesh['depth'=8,'plane'=16] {'plane'}, dimensions={0} | all-to-all | bytes 2097152 | tf_op jit(solution)/shard_map/all_to_all | solution.py:35
  277.1 17.7 %all_to_all.87 = bf16[16,32,8,128]{3,2,1,0:T(8,128)(2,1)S(1)} all-to-all(bf16[16,32,8,128]{3,2,1,0:T(8,128)(2,1)S(1)} %broadcast_in_dim.169), channel_id=1, replica_groups=mesh['depth'=8,'plane'=16] {'plane'}, dimensions={0} | all-to-all | bytes 2097152 | tf_op jit(solution)/shard_map/all_to_all | solution.py:35
  310.5 16.7 %all_to_all.88 = bf16[16,32,8,128]{3,2,1,0:T(8,128)(2,1)S(1)} all-to-all(bf16[16,32,8,128]{3,2,1,0:T(8,128)(2,1)S(1)} %broadcast_in_dim.171), channel_id=1, replica_groups=mesh['depth'=8,'plane'=16] {'plane'}, dimensions={0} | all-to-all | bytes 2097152 | tf_op jit(solution)/shard_map/all_to_all | solution.py:35
  342.9 19.2 %all_to_all.89 = bf16[16,32,8,128]{3,2,1,0:T(8,128)(2,1)S(1)} all-to-all(bf16[16,32,8,128]{3,2,1,0:T(8,128)(2,1)S(1)} %broadcast_in_dim.173), channel_id=1, replica_groups=mesh['depth'=8,'plane'=16] {'plane'}, dimensions={0} | all-to-all | bytes 2097152 | tf_op jit(solution)/shard_map/all_to_all | solution.py:35
  376.6 19.1 %all_to_all.90 = bf16[16,32,8,128]{3,2,1,0:T(8,128)(2,1)S(1)} all-to-all(bf16[16,32,8,128]{3,2,1,0:T(8,128)(2,1)S(1)} %broadcast_in_dim.175), channel_id=1, replica_groups=mesh['depth'=8,'plane'=16] {'plane'}, dimensions={0} | all-to-all | bytes 2097152 | tf_op jit(solution)/shard_map/all_to_all | solution.py:35
  410.0 17.8 %all_to_all.91 = bf16[16,32,8,128]{3,2,1,0:T(8,128)(2,1)S(1)} all-to-all(bf16[16,32,8,128]{3,2,1,0:T(8,128)(2,1)S(1)} %broadcast_in_dim.177), channel_id=1, replica_groups=mesh['depth'=8,'plane'=16] {'plane'}, dimensions={0} | all-to-all | bytes 2097152 | tf_op jit(solution)/shard_map/all_to_all | solution.py:35
  443.4 17.2 %all_to_all.92 = bf16[16,32,8,128]{3,2,1,0:T(8,128)(2,1)S(1)} all-to-all(bf16[16,32,8,128]{3,2,1,0:T(8,128)(2,1)S(1)} %broadcast_in_dim.179), channel_id=1, replica_groups=mesh['depth'=8,'plane'=16] {'plane'}, dimensions={0} | all-to-all | bytes 2097152 | tf_op jit(solution)/shard_map/all_to_all | solution.py:35
  464.1 5.7 %fusion.146 = f32[8,2,32,64]{3,0,1,2:T(8,128)S(1)} fusion(bf16[1,32,16,64,128]{4,3,2,1,0:T(8,128)(2,1)} %param.9, bf16[32,16,8,1,128]{4,2,1,3,0:T(8,128)(2,1)S(1)} %get-tuple-element.16, bf16[32,16,8,1,128]{4,2,1,3,0:T(8,128)(2,1)S(1)} %get-tuple-element.15), kind=kOutput, calls=%fused_computation.112 | convolution fusion | flops 135266304 | bytes 10616832 | tf_op jit(solution)/shard_map/rkic,rkvwc->vwri/dot_general | solution.py:45
  483.6 9.7 %all-to-all-done.14 = bf16[16,32,8,128]{3,2,1,0:T(8,128)(2,1)S(1)} async-done(((bf16[16,32,8,128]{3,2,1,0:T(8,128)(2,1)}), bf16[16,32,8,128]{3,2,1,0:T(8,128)(2,1)S(1)}, u32[]{:S(2)}, u32[]{:S(2)}) %all-to-all-start.14) | async-done | bytes 1048608 | tf_op jit(solution)/shard_map/all_to_all | solution.py:35
  497.0 5.7 %add_convert_fusion = (bf16[8,2,32,64]{3,0,1,2:T(8,128)(2,1)S(1)}, f32[8,2,32,64]{3,0,1,2:T(8,128)S(1)}) fusion(f32[8,2,32,64]{3,0,1,2:T(8,128)S(1)} %fusion.166, bf16[1,32,16,64,128]{4,3,2,1,0:T(8,128)(2,1)} %param.9, bf16[32,16,8,1,128]{4,2,1,3,0:T(8,128)(2,1)S(1)} %get-tuple-element.11, bf16[32,16,8,1,128]{4,2,1,3,0:T(8,128)(2,1)S(1)} %get-tuple-element.10), kind=kOutput, calls=%fused_computation.167 | convolution fusion | flops 135331840 | bytes 10813440 | tf_op jit(solution)/shard_map/rkic,rkvwc->vwri/dot_general | solution.py:45
  503.0 6.5 %fusion = f32[4096,27]{0,1:T(8,128)S(1)} fusion(s32[2048]{0:T(1024)S(1)} %add_add_fusion, bf16[2048,9]{0,1:T(8,128)(2,1)S(1)} %get-tuple-element.91, bf16[2048,9]{0,1:T(8,128)(2,1)S(1)} %get-tuple-element.92, bf16[2048,9]{0,1:T(8,128)(2,1)S(1)} %get-tuple-element.90), kind=kOutput, calls=%fused_computation.16 | convolution fusion | flops 461705216 | bytes 561152 | tf_op jit(solution)/shard_map/cs,cq->sq/dot_general | solution.py:91
  511.2 12.3 %all-to-all-start.15 = ((f32[128,1,288]{2,1,0:T(1,128)}), f32[128,1,288]{2,1,0:T(1,128)S(1)}, u32[]{:S(2)}, u32[]{:S(2)}) async-start(f32[128,1,288]{2,1,0:T(1,128)} %reshape.580), calls=%async_computation.15 | async-start | bytes 393216 | tf_op jit(solution)/shard_map/all_to_all | solution.py:95
  524.4 9.7 %all-to-all-done.15 = f32[128,1,288]{2,1,0:T(1,128)S(1)} async-done(((f32[128,1,288]{2,1,0:T(1,128)}), f32[128,1,288]{2,1,0:T(1,128)S(1)}, u32[]{:S(2)}, u32[]{:S(2)}) %all-to-all-start.15) | async-done | bytes 147488 | tf_op jit(solution)/shard_map/all_to_all | solution.py:95
  (231 shorter events, 218.6 us)
Async XLA Ops:
  2.3 9.4 %copy-start.4 = (s32[1,32,16]{1,2,0:T(8,128)S(1)}, s32[1,32,16]{1,2,0:T(8,128)}, u32[]{:S(2)}) copy-start(s32[1,32,16]{1,2,0:T(8,128)} %param.10) | copy-start | bytes 6148
  4.1 23.1 %all-to-all-start = ((bf16[16,32,8,128]{3,2,1,0:T(8,128)(2,1)}), bf16[16,32,8,128]{3,2,1,0:T(8,128)(2,1)S(1)}, u32[]{:S(2)}, u32[]{:S(2)}) async-start(bf16[16,32,8,128]{3,2,1,0:T(8,128)(2,1)} %broadcast_in_dim.152), calls=%async_computation | async-start | bytes 2097152 | tf_op jit(solution)/shard_map/all_to_all | solution.py:35
  11.9 17.6 %copy-start = (s32[1024]{0:T(1024)}, s32[1024]{0:T(1024)S(1)}, u32[]{:S(2)}) copy-start(s32[1024]{0:T(1024)S(1)} %pad_clamp_fusion) | copy-start | bytes 12292
  30.7 10.6 %copy-start.5 = (f32[1,2048]{1,0:T(1,128)S(1)}, f32[1,2048]{1,0:T(1,128)}, u32[]{:S(2)}) copy-start(f32[1,2048]{1,0:T(1,128)} %param.8) | copy-start | bytes 24580
  36.6 6.0 %collective-permute-start = (bf16[8,2,2048]{2,0,1:T(8,128)(2,1)S(1)}, bf16[8,2,2048]{2,0,1:T(8,128)(2,1)S(1)}, u32[]{:S(2)}, u32[]{:S(2)}) collective-permute-start(bf16[8,2,2048]{2,0,1:T(8,128)(2,1)S(1)} %convert_element_type.265), channel_id=1, source_target_pairs={{0,16},{16,32},{32,48},{48,64},{64,80},{80,96},{96,112},{112,0},{1... | collective-permute-start | bytes 196616 | tf_op jit(solution)/shard_map/ppermute | solution.py:12
  70.4 6.0 %collective-permute-start.1 = (bf16[8,2,2048]{2,0,1:T(8,128)(2,1)S(1)}, bf16[8,2,2048]{2,0,1:T(8,128)(2,1)S(1)}, u32[]{:S(2)}, u32[]{:S(2)}) collective-permute-start(bf16[8,2,2048]{2,0,1:T(8,128)(2,1)S(1)} %convert_element_type.270), channel_id=1, source_target_pairs={{0,16},{16,32},{32,48},{48,64},{64,80},{80,96},{96,112},{112,0},{1... | collective-permute-start | bytes 196616 | tf_op jit(solution)/shard_map/ppermute | solution.py:12
  104.6 5.7 %collective-permute-start.2 = (bf16[8,2,2048]{2,0,1:T(8,128)(2,1)S(1)}, bf16[8,2,2048]{2,0,1:T(8,128)(2,1)S(1)}, u32[]{:S(2)}, u32[]{:S(2)}) collective-permute-start(bf16[8,2,2048]{2,0,1:T(8,128)(2,1)S(1)} %convert_element_type.275), channel_id=1, source_target_pairs={{0,16},{16,32},{32,48},{48,64},{64,80},{80,96},{96,112},{112,0},{1... | collective-permute-start | bytes 196616 | tf_op jit(solution)/shard_map/ppermute | solution.py:12
  136.8 5.5 %collective-permute-start.3 = (bf16[8,2,2048]{2,0,1:T(8,128)(2,1)S(1)}, bf16[8,2,2048]{2,0,1:T(8,128)(2,1)S(1)}, u32[]{:S(2)}, u32[]{:S(2)}) collective-permute-start(bf16[8,2,2048]{2,0,1:T(8,128)(2,1)S(1)} %convert_element_type.280), channel_id=1, source_target_pairs={{0,16},{16,32},{32,48},{48,64},{64,80},{80,96},{96,112},{112,0},{1... | collective-permute-start | bytes 196616 | tf_op jit(solution)/shard_map/ppermute | solution.py:12
  167.4 8.7 %collective-permute-start.4 = (bf16[8,2,2048]{2,0,1:T(8,128)(2,1)S(1)}, bf16[8,2,2048]{2,0,1:T(8,128)(2,1)S(1)}, u32[]{:S(2)}, u32[]{:S(2)}) collective-permute-start(bf16[8,2,2048]{2,0,1:T(8,128)(2,1)S(1)} %convert_element_type.285), channel_id=1, source_target_pairs={{0,16},{16,32},{32,48},{48,64},{64,80},{80,96},{96,112},{112,0},{1... | collective-permute-start | bytes 196616 | tf_op jit(solution)/shard_map/ppermute | solution.py:12
  202.3 7.9 %collective-permute-start.5 = (bf16[8,2,2048]{2,0,1:T(8,128)(2,1)S(1)}, bf16[8,2,2048]{2,0,1:T(8,128)(2,1)S(1)}, u32[]{:S(2)}, u32[]{:S(2)}) collective-permute-start(bf16[8,2,2048]{2,0,1:T(8,128)(2,1)S(1)} %convert_element_type.290), channel_id=1, source_target_pairs={{0,16},{16,32},{32,48},{48,64},{64,80},{80,96},{96,112},{112,0},{1... | collective-permute-start | bytes 196616 | tf_op jit(solution)/shard_map/ppermute | solution.py:12
  238.7 5.2 collective-permute-start.6
  270.2 24.6 %copy-start.1 = (s32[1024]{0:T(1024)S(1)}, s32[1024]{0:T(1024)}, u32[]{:S(2)}) copy-start(s32[1024]{0:T(1024)} %copy-done) | copy-start | bytes 12292
  270.2 6.3 %collective-permute-start.7 = (bf16[8,2,2048]{2,0,1:T(8,128)(2,1)S(1)}, bf16[8,2,2048]{2,0,1:T(8,128)(2,1)S(1)}, u32[]{:S(2)}, u32[]{:S(2)}) collective-permute-start(bf16[8,2,2048]{2,0,1:T(8,128)(2,1)S(1)} %multiply_convert_fusion.6), channel_id=1, source_target_pairs={{0,112},{16,0},{32,16},{48,32},{64,48},{80,64},{96,80},{112,96},{1... | collective-permute-start | bytes 196616 | tf_op jit(solution)/shard_map/ppermute | solution.py:12
  304.1 5.7 %collective-permute-start.8 = (bf16[8,2,2048]{2,0,1:T(8,128)(2,1)S(1)}, bf16[8,2,2048]{2,0,1:T(8,128)(2,1)S(1)}, u32[]{:S(2)}, u32[]{:S(2)}) collective-permute-start(bf16[8,2,2048]{2,0,1:T(8,128)(2,1)S(1)} %multiply_convert_fusion.5), channel_id=1, source_target_pairs={{0,112},{16,0},{32,16},{48,32},{64,48},{80,64},{96,80},{112,96},{1... | collective-permute-start | bytes 196616 | tf_op jit(solution)/shard_map/ppermute | solution.py:12
  336.5 5.7 %collective-permute-start.9 = (bf16[8,2,2048]{2,0,1:T(8,128)(2,1)S(1)}, bf16[8,2,2048]{2,0,1:T(8,128)(2,1)S(1)}, u32[]{:S(2)}, u32[]{:S(2)}) collective-permute-start(bf16[8,2,2048]{2,0,1:T(8,128)(2,1)S(1)} %multiply_convert_fusion.4), channel_id=1, source_target_pairs={{0,112},{16,0},{32,16},{48,32},{64,48},{80,64},{96,80},{112,96},{1... | collective-permute-start | bytes 196616 | tf_op jit(solution)/shard_map/ppermute | solution.py:12
  371.4 4.6 collective-permute-start.10
  405.0 4.3 collective-permute-start.11
  437.1 5.7 %collective-permute-start.12 = (bf16[8,2,2048]{2,0,1:T(8,128)(2,1)S(1)}, bf16[8,2,2048]{2,0,1:T(8,128)(2,1)S(1)}, u32[]{:S(2)}, u32[]{:S(2)}) collective-permute-start(bf16[8,2,2048]{2,0,1:T(8,128)(2,1)S(1)} %multiply_convert_fusion.1), channel_id=1, source_target_pairs={{0,112},{16,0},{32,16},{48,32},{64,48},{80,64},{96,80},{112,96},{1... | collective-permute-start | bytes 196616 | tf_op jit(solution)/shard_map/ppermute | solution.py:12
  464.1 10.8 %copy-start.3 = (s32[1,2048]{1,0:T(1,128)S(1)}, s32[1,2048]{1,0:T(1,128)}, u32[]{:S(2)}) copy-start(s32[1,2048]{1,0:T(1,128)} %param.11) | copy-start | bytes 24580
  470.0 6.1 %collective-permute-start.13 = (bf16[8,2,2048]{2,0,1:T(8,128)(2,1)S(1)}, bf16[8,2,2048]{2,0,1:T(8,128)(2,1)S(1)}, u32[]{:S(2)}, u32[]{:S(2)}) collective-permute-start(bf16[8,2,2048]{2,0,1:T(8,128)(2,1)S(1)} %multiply_convert_fusion), channel_id=1, source_target_pairs={{0,112},{16,0},{32,16},{48,32},{64,48},{80,64},{96,80},{112,96},{1... | collective-permute-start | bytes 196616 | tf_op jit(solution)/shard_map/ppermute | solution.py:12
  477.7 15.6 %all-to-all-start.14 = ((bf16[16,32,8,128]{3,2,1,0:T(8,128)(2,1)}), bf16[16,32,8,128]{3,2,1,0:T(8,128)(2,1)S(1)}, u32[]{:S(2)}, u32[]{:S(2)}) async-start(bf16[16,32,8,128]{3,2,1,0:T(8,128)(2,1)} %broadcast_in_dim.181), calls=%async_computation.14 | async-start | bytes 2097152 | tf_op jit(solution)/shard_map/all_to_all | solution.py:35
  496.9 5.9 %copy-start.2 = (bf16[1,8,2,2048]{3,2,1,0:T(2,128)(2,1)S(1)}, bf16[1,8,2,2048]{3,2,1,0:T(2,128)(2,1)}, u32[]{:S(2)}) copy-start(bf16[1,8,2,2048]{3,2,1,0:T(2,128)(2,1)} %param.6) | copy-start | bytes 196612
  511.2 22.9 %all-to-all-start.15 = ((f32[128,1,288]{2,1,0:T(1,128)}), f32[128,1,288]{2,1,0:T(1,128)S(1)}, u32[]{:S(2)}, u32[]{:S(2)}) async-start(f32[128,1,288]{2,1,0:T(1,128)} %reshape.580), calls=%async_computation.15 | async-start | bytes 393216 | tf_op jit(solution)/shard_map/all_to_all | solution.py:95
